TPU v7x, 128 devices: a whole 4x4x4 slice. The times are simulated.
128 devices in a mesh: row: 8 (over z, core), col: 8 (over y_lo, x), dep: 2 (over y_hi).
Axes of the slice: x: 4, y: 4 (y_hi: 2, y_lo: 2; y = y_hi * 2 + y_lo), z: 4, core: 2. Of those that a mesh axis runs over, the one named last changes fastest.
Arguments:
- tokens: bfloat16 [2048, 8192], P(('dep', 'col'), 'row'), may hold values from -6 to 6
- gate_weight: bfloat16 [8192, 14336], P('row', 'col'), may hold values from -0.0625 to 0.0625
- up_weight: bfloat16 [8192, 14336], P('row', 'col'), may hold values from -0.0625 to 0.0625
- cotangent: bfloat16 [2048, 14336], P(('dep', 'row'), 'col'), may hold values from -6 to 6
Outputs:
- hidden: bfloat16 [2048, 14336], P(('dep', 'row'), 'col')
- grad_tokens: bfloat16 [2048, 8192], P(('dep', 'col'), 'row')
- grad_gate_weight: bfloat16 [8192, 14336], P('row', ('col', 'dep'))
- grad_up_weight: bfloat16 [8192, 14336], P('row', ('col', 'dep'))
All inputs are finite; a program needn't handle non-finite values.
Results may differ from a plain program's by a relative error of at most 0.02.
Values may be sent and summed in bfloat16 or wider, within the bound.
No kernel may reach another device: no remote copies, remote signals or barrier semaphores. Data moves between devices by JAX's collectives and lax.ppermute only.
A program may use at most 128 MiB of HBM per device.

v0:
```python
import jax
import jax.numpy as jnp
from jax import lax
from jax.sharding import PartitionSpec as P


def on_device(tokens, gate_weight, up_weight, cotangent):
    width = gate_weight.shape[1]
    gathered = lax.all_gather(tokens, "col", axis=0, tiled=True)
    first = jnp.dot(gathered, gate_weight, preferred_element_type=jnp.float32)
    second = jnp.dot(gathered, up_weight, preferred_element_type=jnp.float32)
    joined = lax.psum_scatter(
        jnp.concatenate([first, second], axis=1).astype(jnp.bfloat16),
        "row",
        scatter_dimension=0,
        tiled=True,
    ).astype(jnp.float32)
    gate = joined[:, :width]
    up = joined[:, width:]
    sigma = jax.nn.sigmoid(gate)
    active = gate * sigma
    hidden = (active * up).astype(jnp.bfloat16)
    upstream = cotangent.astype(jnp.float32)
    grad_gate = (upstream * up * sigma * (1.0 + gate * (1.0 - sigma))).astype(jnp.bfloat16)
    grad_up = (upstream * active).astype(jnp.bfloat16)
    full_gate, full_up = (
        lax.all_gather(grad_gate, "row", axis=0, tiled=True),
        lax.all_gather(grad_up, "row", axis=0, tiled=True),
    )
    transposed = (((1,), (1,)), ((), ()))
    term = lax.dot_general(full_gate, gate_weight, transposed, preferred_element_type=jnp.float32)
    grad_tokens = lax.psum_scatter(
        (
            term
            + lax.dot_general(full_up, up_weight, transposed, preferred_element_type=jnp.float32)
        ).astype(jnp.bfloat16),
        "col",
        scatter_dimension=0,
        tiled=True,
    )
    contract = (((0,), (0,)), ((), ()))
    part_gate = lax.dot_general(gathered, full_gate, contract, preferred_element_type=jnp.float32)
    part_up = lax.dot_general(gathered, full_up, contract, preferred_element_type=jnp.float32)
    sum_gate, sum_up = (
        lax.psum_scatter(
            part_gate.astype(jnp.bfloat16), "dep", scatter_dimension=1, tiled=True
        ).astype(jnp.float32),
        lax.psum_scatter(
            part_up.astype(jnp.bfloat16), "dep", scatter_dimension=1, tiled=True
        ).astype(jnp.float32),
    )
    return (hidden, grad_tokens, sum_gate.astype(jnp.bfloat16), sum_up.astype(jnp.bfloat16))


def solution(mesh):
    return jax.shard_map(
        on_device,
        mesh=mesh,
        in_specs=(
            P(("dep", "col"), "row"),
            P("row", "col"),
            P("row", "col"),
            P(("dep", "row"), "col"),
        ),
        out_specs=(
            P(("dep", "row"), "col"),
            P(("dep", "col"), "row"),
            P("row", ("col", "dep")),
            P("row", ("col", "dep")),
        ),
        check_vma=False,
    )
```

profile of v0, /device:TPU:6, one launch (start us, length us, event | category | flops | bytes accessed | tf_op | source)
XLA Modules:
  0.0 343.0 jit_solution(17824594205613971684)
XLA Ops:
  7.2 0.0 all-gather.4.cloned.1.call-start
  7.2 0.7 all-gather.4.cloned.1.call-update
  7.9 0.0 reduce-scatter.5.cloned.1.call-start
  7.9 42.8 %all-gather.4.cloned.1.call-done = bf16[1024,1024]{1,0:T(8,128)(2,1)} async-done(((bf16[128,1024]{1,0:T(8,128)(2,1)}), bf16[1024,1024]{1,0:T(8,128)(2,1)}) %all-gather.4.cloned.1.call-update) | async-done | bytes 2097168 | tf_op jit(solution)/shard_map/all_gather | solution.py:9
  50.8 0.0 copy-start.1
  50.8 0.0 copy-start.4
  50.8 6.8 %convolution_convert_fusion.2 = bf16[1024,1792]{1,0:T(8,128)(2,1)S(1)} fusion(bf16[1024,1024]{1,0:T(8,128)(2,1)} %all-gather.4.cloned.1.call-done, bf16[1024,1792]{1,0:T(8,128)(2,1)} %param.6), kind=kOutput, calls=%fused_computation.4 | convolution fusion | flops 3759931392 | bytes 9437184 | tf_op jit(solution)/shard_map/dot_general | solution.py:11
  57.5 0.0 copy-done.1
  57.5 0.0 copy-done.4
  57.6 5.4 %convolution_convert_fusion.3 = bf16[1024,1792]{1,0:T(8,128)(2,1)} fusion(bf16[1024,1024]{1,0:T(8,128)(2,1)S(1)} %copy-done.4, bf16[1024,1792]{1,0:T(8,128)(2,1)S(1)} %copy-done.1), kind=kOutput, calls=%fused_computation.5 | convolution fusion | flops 3759931392 | bytes 9437184 | tf_op jit(solution)/shard_map/dot_general | solution.py:10
  62.9 5.5 %pad_maximum_fusion = bf16[1024,3584]{1,0:T(8,128)(2,1)} fusion(bf16[1024,1792]{1,0:T(8,128)(2,1)S(1)} %convolution_convert_fusion.2, bf16[1024,1792]{1,0:T(8,128)(2,1)} %convolution_convert_fusion.3), kind=kLoop, calls=%fused_computation | loop fusion | flops 14680064 | bytes 14680064 | tf_op jit(solution)/shard_map/concatenate | solution.py:13
  68.5 0.0 copy-start
  68.5 0.0 reduce-scatter.5.cloned.1.call-update
  68.5 0.0 copy-start.5
  68.5 0.0 all-gather.6.cloned.1.call-start
  68.6 49.6 %reduce-scatter.5.cloned.1.call-done = bf16[128,3584]{1,0:T(8,128)(2,1)} async-done(((bf16[1024,3584]{1,0:T(8,128)(2,1)}), bf16[128,3584]{1,0:T(8,128)(2,1)}) %reduce-scatter.5.cloned.1.call-update) | async-done | bytes 917520 | tf_op jit(solution)/shard_map/reduce_scatter | solution.py:12
  118.1 1.4 convert_element_type.35
  119.5 0.0 copy-done
  119.5 1.6 fusion.5
  121.1 0.0 all-gather.6.cloned.1.call-update
  121.1 0.0 all-gather.8.cloned.1.call-start
  121.2 0.5 all-gather.8.cloned.1.call-update
  121.7 0.0 reduce-scatter.9.cloned.1.call-start
  121.8 29.1 %all-gather.6.cloned.1.call-done = bf16[1024,1792]{1,0:T(8,128)(2,1)} async-done(((bf16[128,1792]{1,0:T(8,128)(2,1)}), bf16[1024,1792]{1,0:T(8,128)(2,1)}) %all-gather.6.cloned.1.call-update) | async-done | bytes 3670032 | tf_op jit(solution)/shard_map/all_gather | solution.py:27
  150.9 0.0 copy-done.5
  150.9 7.6 %fusion = bf16[1024,1792]{0,1:T(8,128)(2,1)} fusion(bf16[1024,1792]{1,0:T(8,128)(2,1)} %all-gather.6.cloned.1.call-done, bf16[1024,1024]{1,0:T(8,128)(2,1)S(1)} %copy-done.5), kind=kOutput, calls=%fused_computation.6 | convolution fusion | flops 3759931392 | bytes 9437184 | tf_op jit(solution)/shard_map/dot_general | solution.py:42
  158.5 0.0 reduce-scatter.9.cloned.1.call-update
  158.5 0.0 reduce-scatter.11.cloned.1.call-start
  158.6 24.3 %all-gather.8.cloned.1.call-done = bf16[1024,1792]{1,0:T(8,128)(2,1)} async-done(((bf16[128,1792]{1,0:T(8,128)(2,1)}), bf16[1024,1792]{1,0:T(8,128)(2,1)}) %all-gather.8.cloned.1.call-update) | async-done | bytes 3670032 | tf_op jit(solution)/shard_map/all_gather | solution.py:28
  182.9 7.6 %fusion.1 = bf16[1024,1792]{0,1:T(8,128)(2,1)} fusion(bf16[1024,1792]{1,0:T(8,128)(2,1)} %all-gather.8.cloned.1.call-done, bf16[1024,1024]{1,0:T(8,128)(2,1)S(1)} %copy-done.5), kind=kOutput, calls=%fused_computation.7 | convolution fusion | flops 3759931392 | bytes 9437184 | tf_op jit(solution)/shard_map/dot_general | solution.py:43
  190.4 0.0 reduce-scatter.11.cloned.1.call-update
  190.4 0.2 reduce-scatter.7.cloned.1.call-start
  190.7 0.0 copy-start.2
  190.7 0.0 copy-start.3
  190.7 7.6 %fusion.7 = f32[1024,1024]{1,0:T(8,128)S(1)} fusion(bf16[1024,1792]{1,0:T(8,128)(2,1)} %all-gather.6.cloned.1.call-done, bf16[1024,1792]{1,0:T(8,128)(2,1)} %param.5), kind=kOutput, calls=%fused_computation.17 | convolution fusion | flops 3758096384 | bytes 11534336 | tf_op jit(solution)/shard_map/dot_general | solution.py:31
  198.3 0.0 copy-done.2
  198.3 0.0 copy-done.3
  198.4 5.3 %add_convert_fusion = bf16[1024,1024]{1,0:T(8,128)(2,1)} fusion(f32[1024,1024]{1,0:T(8,128)S(1)} %fusion.7, bf16[1024,1792]{1,0:T(8,128)(2,1)S(1)} %copy-done.3, bf16[1024,1792]{1,0:T(8,128)(2,1)S(1)} %copy-done.2), kind=kOutput, calls=%fused_computation.1 | convolution fusion | flops 3760193536 | bytes 13631488 | tf_op jit(solution)/shard_map/dot_general | solution.py:35
  203.6 0.0 reduce-scatter.7.cloned.1.call-update
  203.7 34.4 %reduce-scatter.9.cloned.1.call-done = bf16[1024,896]{0,1:T(8,128)(2,1)} async-done(((bf16[1024,1792]{0,1:T(8,128)(2,1)}), bf16[1024,896]{0,1:T(8,128)(2,1)}) %reduce-scatter.9.cloned.1.call-update) | async-done | bytes 1835024 | tf_op jit(solution)/shard_map/reduce_scatter | solution.py:45
  238.1 3.8 %copy.8 = bf16[1024,896]{1,0:T(8,128)(2,1)} copy(bf16[1024,896]{0,1:T(8,128)(2,1)} %reduce-scatter.9.cloned.1.call-done) | data formatting | bytes 3670016
  241.9 51.1 %reduce-scatter.11.cloned.1.call-done = bf16[1024,896]{0,1:T(8,128)(2,1)} async-done(((bf16[1024,1792]{0,1:T(8,128)(2,1)}), bf16[1024,896]{0,1:T(8,128)(2,1)}) %reduce-scatter.11.cloned.1.call-update) | async-done | bytes 1835024 | tf_op jit(solution)/shard_map/reduce_scatter | solution.py:48
  292.9 3.8 %copy.9 = bf16[1024,896]{1,0:T(8,128)(2,1)} copy(bf16[1024,896]{0,1:T(8,128)(2,1)} %reduce-scatter.11.cloned.1.call-done) | data formatting | bytes 3670016
  296.7 39.4 %reduce-scatter.7.cloned.1.call-done = bf16[128,1024]{1,0:T(8,128)(2,1)} async-done(((bf16[1024,1024]{1,0:T(8,128)(2,1)}), bf16[128,1024]{1,0:T(8,128)(2,1)}) %reduce-scatter.7.cloned.1.call-update) | async-done | bytes 262160 | tf_op jit(solution)/shard_map/reduce_scatter | solution.py:32
Async XLA Ops:
  7.2 43.6 %all-gather.4.cloned.1.call-start = ((), (), s32[]{:S(2)}) async-start(), calls=%async_computation.4 | async-start | bytes 2359296 | tf_op jit(solution)/shard_map/all_gather | solution.py:9
  7.9 110.2 %reduce-scatter.5.cloned.1.call-start = ((), (), s32[]{:S(2)}) async-start(), calls=%async_computation.5 | async-start | bytes 8257536 | tf_op jit(solution)/shard_map/reduce_scatter | solution.py:12
  50.8 6.8 %copy-start.1 = (bf16[1024,1792]{1,0:T(8,128)(2,1)S(1)}, bf16[1024,1792]{1,0:T(8,128)(2,1)}, u32[]{:S(2)}) copy-start(bf16[1024,1792]{1,0:T(8,128)(2,1)} %param.5) | copy-start | bytes 11010052
  50.8 6.8 %copy-start.4 = (bf16[1024,1024]{1,0:T(8,128)(2,1)S(1)}, bf16[1024,1024]{1,0:T(8,128)(2,1)}, u32[]{:S(2)}) copy-start(bf16[1024,1024]{1,0:T(8,128)(2,1)} %all-gather.4.cloned.1.call-done) | copy-start | bytes 6291460
  68.5 51.0 %copy-start = (bf16[128,1792]{1,0:T(8,128)(2,1)S(1)}, bf16[128,1792]{1,0:T(8,128)(2,1)}, u32[]{:S(2)}) copy-start(bf16[128,1792]{1,0:T(8,128)(2,1)} %param.7) | copy-start | bytes 1376260
  68.5 82.4 %copy-start.5 = (bf16[1024,1024]{1,0:T(8,128)(2,1)S(1)}, bf16[1024,1024]{1,0:T(8,128)(2,1)}, u32[]{:S(2)}) copy-start(bf16[1024,1024]{1,0:T(8,128)(2,1)} %all-gather.4.cloned.1.call-done) | copy-start | bytes 6291460
  68.5 82.4 %all-gather.6.cloned.1.call-start = ((), (), s32[]{:S(2)}) async-start(), calls=%async_computation.6 | async-start | bytes 4128768 | tf_op jit(solution)/shard_map/all_gather | solution.py:27
  121.1 61.7 %all-gather.8.cloned.1.call-start = ((), (), s32[]{:S(2)}) async-start(), calls=%async_computation.7 | async-start | bytes 4128768 | tf_op jit(solution)/shard_map/all_gather | solution.py:28
  121.7 116.3 %reduce-scatter.9.cloned.1.call-start = ((), (), s32[]{:S(2)}) async-start(), calls=%async_computation.9 | async-start | bytes 5505024 | tf_op jit(solution)/shard_map/reduce_scatter | solution.py:45
  158.5 134.4 %reduce-scatter.11.cloned.1.call-start = ((), (), s32[]{:S(2)}) async-start(), calls=%async_computation.10 | async-start | bytes 5505024 | tf_op jit(solution)/shard_map/reduce_scatter | solution.py:48
  190.4 145.7 %reduce-scatter.7.cloned.1.call-start = ((), (), s32[]{:S(2)}) async-start(), calls=%async_computation.8 | async-start | bytes 2359296 | tf_op jit(solution)/shard_map/reduce_scatter | solution.py:32
  190.7 7.7 %copy-start.2 = (bf16[1024,1792]{1,0:T(8,128)(2,1)S(1)}, bf16[1024,1792]{1,0:T(8,128)(2,1)}, u32[]{:S(2)}) copy-start(bf16[1024,1792]{1,0:T(8,128)(2,1)} %param.6) | copy-start | bytes 11010052
  190.7 7.7 %copy-start.3 = (bf16[1024,1792]{1,0:T(8,128)(2,1)S(1)}, bf16[1024,1792]{1,0:T(8,128)(2,1)}, u32[]{:S(2)}) copy-start(bf16[1024,1792]{1,0:T(8,128)(2,1)} %all-gather.8.cloned.1.call-done) | copy-start | bytes 11010052
Sparse Core Ops, SparseCore 0:
  9.6 41.0 all-gather.3
  68.6 49.4 reduce-scatter.4
  121.3 29.5 all-gather.5
  153.0 29.8 all-gather.7
  185.0 52.9 reduce-scatter.8
  240.3 52.6 reduce-scatter.10
  295.9 40.1 reduce-scatter.6
where the time goes:
time: 346 us; the launch traced here: 343 us
  waiting for transfers between devices  272 us (79%)
  matrix products  40.2 us (12%)
  between operations  14.2 us (4%)
  other arithmetic  8.53 us (2%)
  local copies, waits for them, and re-layouts  7.62 us (2%)
    reduce_scatter x1, waiting for transfers between devices, on_device(): lax.psum_scatter(part_up.astype(jnp.bfloat16), 'dep', scatter_dimension=1...  51.1 us
    reduce_scatter x1, waiting for transfers between devices, on_device(): lax.psum_scatter(jnp.concatenate([first, second], axis=1).astype(jnp.bflo...  49.6 us
    all_gather x1, waiting for transfers between devices, on_device(): gathered = lax.all_gather(tokens, 'col', axis=0, tiled=True)  42.8 us
    reduce_scatter x1, waiting for transfers between devices, on_device(): lax.psum_scatter((term + lax.dot_general(full_up, up_weight, transposed,...  39.4 us
    reduce_scatter x1, waiting for transfers between devices, on_device(): lax.psum_scatter(part_gate.astype(jnp.bfloat16), 'dep', scatter_dimension...  34.4 us
    all_gather x1, waiting for transfers between devices, on_device(): lax.all_gather(grad_gate, 'row', axis=0, tiled=True)  29.1 us
    all_gather x1, waiting for transfers between devices, on_device(): lax.all_gather(grad_up, 'row', axis=0, tiled=True)  24.3 us
    dot_general x1, matrix products, on_device(): lax.dot_general(full_gate, gate_weight, transposed, preferred_element_typ...  7.63 us
  transfers between devices with their start and end apart: 7, of which 7 were waited for; matrix products, arithmetic and copies ran while one was open for 10% of the time, Pallas kernels for 0%

commit v1 on v0

--- a/solution.py
+++ b/solution.py
@@ -4,8 +4,21 @@
 from jax.sharding import PartitionSpec as P
 
 
+def weight_grad(gathered, full, dep):
+    contract = (((0,), (0,)), ((), ()))
+    half = full.shape[1] // 2
+    other = lax.dynamic_slice_in_dim(full, (1 - dep) * half, half, axis=1)
+    own = lax.dynamic_slice_in_dim(full, dep * half, half, axis=1)
+    send = lax.dot_general(gathered, other, contract, preferred_element_type=jnp.float32)
+    recv = lax.ppermute(send.astype(jnp.bfloat16), "dep", [(0, 1), (1, 0)])
+    mine = lax.dot_general(gathered, own, contract, preferred_element_type=jnp.float32)
+    total = mine.astype(jnp.bfloat16).astype(jnp.float32) + recv.astype(jnp.float32)
+    return total.astype(jnp.bfloat16)
+
+
 def on_device(tokens, gate_weight, up_weight, cotangent):
     width = gate_weight.shape[1]
+    dep = lax.axis_index("dep")
     gathered = lax.all_gather(tokens, "col", axis=0, tiled=True)
     first = jnp.dot(gathered, gate_weight, preferred_element_type=jnp.float32)
     second = jnp.dot(gathered, up_weight, preferred_element_type=jnp.float32)
@@ -23,10 +36,10 @@
     upstream = cotangent.astype(jnp.float32)
     grad_gate = (upstream * up * sigma * (1.0 + gate * (1.0 - sigma))).astype(jnp.bfloat16)
     grad_up = (upstream * active).astype(jnp.bfloat16)
-    full_gate, full_up = (
-        lax.all_gather(grad_gate, "row", axis=0, tiled=True),
-        lax.all_gather(grad_up, "row", axis=0, tiled=True),
-    )
+    full_gate = lax.all_gather(grad_gate, "row", axis=0, tiled=True)
+    sum_gate = weight_grad(gathered, full_gate, dep)
+    full_up = lax.all_gather(grad_up, "row", axis=0, tiled=True)
+    sum_up = weight_grad(gathered, full_up, dep)
     transposed = (((1,), (1,)), ((), ()))
     term = lax.dot_general(full_gate, gate_weight, transposed, preferred_element_type=jnp.float32)
     grad_tokens = lax.psum_scatter(
@@ -38,18 +51,7 @@
         scatter_dimension=0,
         tiled=True,
     )
-    contract = (((0,), (0,)), ((), ()))
-    part_gate = lax.dot_general(gathered, full_gate, contract, preferred_element_type=jnp.float32)
-    part_up = lax.dot_general(gathered, full_up, contract, preferred_element_type=jnp.float32)
-    sum_gate, sum_up = (
-        lax.psum_scatter(
-            part_gate.astype(jnp.bfloat16), "dep", scatter_dimension=1, tiled=True
-        ).astype(jnp.float32),
-        lax.psum_scatter(
-            part_up.astype(jnp.bfloat16), "dep", scatter_dimension=1, tiled=True
-        ).astype(jnp.float32),
-    )
-    return (hidden, grad_tokens, sum_gate.astype(jnp.bfloat16), sum_up.astype(jnp.bfloat16))
+    return (hidden, grad_tokens, sum_gate, sum_up)
 
 
 def solution(mesh):

time: 346 us -> 315 us (0.910)
  waiting for transfers between devices: 272 us -> 234 us
  matrix products: 40.2 us -> 48.8 us
  starting transfers between devices: 0.46 us -> 3.92 us
    ppermute x0 -> x2, waiting for transfers between devices: none -> 88.8 us  [weight_grad(): recv = lax.ppermute(send.astype(jnp.bfloat16), 'dep', [(0, 1), (1, 0)])]
    reduce_scatter x2 -> x0, waiting for transfers between devices: 85.5 us -> none  [the longest x1 51.1 us: on_device(): lax.psum_scatter(part_up.astype(jnp.bfloat16), 'dep', scatter_dimension=1...]
    reduce_scatter x1, waiting for transfers between devices: 39.4 us -> 0.01 us  [on_device(): lax.psum_scatter((term + lax.dot_general(full_up, up_weight, transposed,...]
    dot_general x1, matrix products: 5.28 us -> 9.64 us  [on_device(): lax.dot_general(full_up, up_weight, transposed, preferred_element_type=jn...]
    ppermute x0 -> x2, starting transfers between devices: none -> 3.55 us  [weight_grad(): recv = lax.ppermute(send.astype(jnp.bfloat16), 'dep', [(0, 1), (1, 0)])]
    dot_general x2 -> x4, matrix products: 15.2 us -> 17.9 us  [the longest x2 9.56 us: weight_grad(): lax.dot_general(gathered, own, contract, preferred_element_type=jnp.float32)]
    unnamed x14 -> x12, local copies, waits for them, and re-layouts: 7.62 us -> 4.95 us
  transfers between devices with their start and end apart: 7 -> 7, of which waited for: 7 -> 6; matrix products, arithmetic and copies ran while one was open for 10% -> 10% of each run, Pallas kernels for 0% -> 0%
where the time goes in v1:
time: 315 us; the launch traced here: 314 us
  waiting for transfers between devices  234 us (74%)
  matrix products  48.8 us (15%)
  between operations  13.9 us (4%)
  other arithmetic  8.54 us (3%)
  local copies, waits for them, and re-layouts  4.95 us (2%)
  starting transfers between devices  3.92 us (1%)
    ppermute x2, waiting for transfers between devices, weight_grad(): recv = lax.ppermute(send.astype(jnp.bfloat16), 'dep', [(0, 1), (1, 0)])  88.8 us
    reduce_scatter x1, waiting for transfers between devices, on_device(): lax.psum_scatter(jnp.concatenate([first, second], axis=1).astype(jnp.bflo...  49.6 us
    all_gather x1, waiting for transfers between devices, on_device(): gathered = lax.all_gather(tokens, 'col', axis=0, tiled=True)  42.8 us
    all_gather x1, waiting for transfers between devices, on_device(): full_gate = lax.all_gather(grad_gate, 'row', axis=0, tiled=True)  28.9 us
    all_gather x1, waiting for transfers between devices, on_device(): full_up = lax.all_gather(grad_up, 'row', axis=0, tiled=True)  22.9 us
    dot_general x1, matrix products, on_device(): lax.dot_general(full_up, up_weight, transposed, preferred_element_type=jn...  9.64 us
    dot_general x2, matrix products, weight_grad(): lax.dot_general(gathered, own, contract, preferred_element_type=jnp.float32)  9.56 us
    dot_general x1, matrix products, on_device(): lax.dot_general(full_gate, gate_weight, transposed, preferred_element_typ...  9.1 us
  transfers between devices with their start and end apart: 7, of which 6 were waited for; matrix products, arithmetic and copies ran while one was open for 10% of the time, Pallas kernels for 0%

profile of v1, /device:TPU:6, one launch (start us, length us, event | category | flops | bytes accessed | tf_op | source)
XLA Modules:
  0.0 314.3 jit_solution(1308986221624515131)
XLA Ops:
  7.2 0.0 all-gather.4.cloned.1.call-start
  7.2 0.7 all-gather.4.cloned.1.call-update
  7.9 0.0 reduce-scatter.3.cloned.1.call-start
  7.9 42.8 %all-gather.4.cloned.1.call-done = bf16[1024,1024]{1,0:T(8,128)(2,1)} async-done(((bf16[128,1024]{1,0:T(8,128)(2,1)}), bf16[1024,1024]{1,0:T(8,128)(2,1)}) %all-gather.4.cloned.1.call-update) | async-done | bytes 2097168 | tf_op jit(solution)/shard_map/all_gather | solution.py:22
  50.8 0.0 copy-start.1
  50.8 0.0 copy-start.3
  50.8 6.8 %convolution_convert_fusion = bf16[1024,1792]{1,0:T(8,128)(2,1)S(1)} fusion(bf16[1024,1024]{1,0:T(8,128)(2,1)} %all-gather.4.cloned.1.call-done, bf16[1024,1792]{1,0:T(8,128)(2,1)} %param.6), kind=kOutput, calls=%fused_computation.2 | convolution fusion | flops 3759931392 | bytes 9437184 | tf_op jit(solution)/shard_map/dot_general | solution.py:24
  57.5 0.0 copy-done.1
  57.5 0.0 copy-done.3
  57.6 5.4 %convolution_convert_fusion.1 = bf16[1024,1792]{1,0:T(8,128)(2,1)} fusion(bf16[1024,1024]{1,0:T(8,128)(2,1)S(1)} %copy-done.3, bf16[1024,1792]{1,0:T(8,128)(2,1)S(1)} %copy-done.1), kind=kOutput, calls=%fused_computation.3 | convolution fusion | flops 3759931392 | bytes 9437184 | tf_op jit(solution)/shard_map/dot_general | solution.py:23
  62.9 5.6 %pad_maximum_fusion = bf16[1024,3584]{1,0:T(8,128)(2,1)} fusion(bf16[1024,1792]{1,0:T(8,128)(2,1)S(1)} %convolution_convert_fusion, bf16[1024,1792]{1,0:T(8,128)(2,1)} %convolution_convert_fusion.1), kind=kLoop, calls=%fused_computation | loop fusion | flops 14680064 | bytes 14680064 | tf_op jit(solution)/shard_map/concatenate | solution.py:26
  68.5 0.0 copy-start
  68.5 0.0 reduce-scatter.3.cloned.1.call-update
  68.5 0.0 all-gather.6.cloned.1.call-start
  68.5 49.6 %reduce-scatter.3.cloned.1.call-done = bf16[128,3584]{1,0:T(8,128)(2,1)} async-done(((bf16[1024,3584]{1,0:T(8,128)(2,1)}), bf16[128,3584]{1,0:T(8,128)(2,1)}) %reduce-scatter.3.cloned.1.call-update) | async-done | bytes 917520 | tf_op jit(solution)/shard_map/reduce_scatter | solution.py:25
  118.1 1.4 convert_element_type.63
  119.5 0.0 copy-done
  119.5 1.6 fusion.21
  121.1 0.0 all-gather.6.cloned.1.call-update
  121.2 0.0 all-gather.8.cloned.1.call-start
  121.2 0.5 all-gather.8.cloned.1.call-update
  121.7 0.2 reduce-scatter.5.cloned.1.call-start
  122.0 28.9 %all-gather.6.cloned.1.call-done = bf16[1024,1792]{1,0:T(8,128)(2,1)} async-done(((bf16[128,1792]{1,0:T(8,128)(2,1)}), bf16[1024,1792]{1,0:T(8,128)(2,1)}) %all-gather.6.cloned.1.call-update) | async-done | bytes 3670032 | tf_op jit(solution)/shard_map/all_gather | solution.py:39
  150.9 9.1 %fusion.27 = f32[1024,1024]{1,0:T(8,128)} fusion(bf16[1024,1792]{1,0:T(8,128)(2,1)} %all-gather.6.cloned.1.call-done, bf16[1024,1792]{1,0:T(8,128)(2,1)} %param.5), kind=kOutput, calls=%fused_computation.31 | convolution fusion | flops 3758096384 | bytes 11534336 | tf_op jit(solution)/shard_map/dot_general | solution.py:44
  160.0 0.0 copy-start.4
  160.0 22.9 %all-gather.8.cloned.1.call-done = bf16[1024,1792]{1,0:T(8,128)(2,1)} async-done(((bf16[128,1792]{1,0:T(8,128)(2,1)}), bf16[1024,1792]{1,0:T(8,128)(2,1)}) %all-gather.8.cloned.1.call-update) | async-done | bytes 3670032 | tf_op jit(solution)/shard_map/all_gather | solution.py:41
  182.9 9.6 %add_convert_fusion = bf16[1024,1024]{1,0:T(8,128)(2,1)} fusion(f32[1024,1024]{1,0:T(8,128)} %fusion.27, bf16[1024,1792]{1,0:T(8,128)(2,1)} %all-gather.8.cloned.1.call-done, bf16[1024,1792]{1,0:T(8,128)(2,1)} %param.6), kind=kOutput, calls=%fused_computation.1 | convolution fusion | flops 3760193536 | bytes 13631488 | tf_op jit(solution)/shard_map/dot_general | solution.py:48
  192.5 0.0 reduce-scatter.5.cloned.1.call-update
  192.5 0.0 copy-done.4
  192.5 0.0 copy-start.2
  192.6 5.0 %convert_bitcast_fusion = bf16[1024,896]{0,1:T(8,128)(2,1)} fusion(bf16[1024,1024]{1,0:T(8,128)(2,1)S(1)} %copy-done.4, bf16[1024,1792]{1,0:T(8,128)(2,1)} %all-gather.8.cloned.1.call-done, s32[]{:T(128)S(6)} %select_n.9), kind=kOutput, calls=%fused_computation.8 | convolution fusion | flops 1879965696 | bytes 5767172 | tf_op jit(solution)/shard_map/dot_general | solution.py:12
  197.5 3.0 collective-permute-start.1
  200.5 0.0 copy-done.2
  200.5 3.4 %convert_bitcast_fusion.1 = bf16[1024,896]{0,1:T(8,128)(2,1)} fusion(bf16[1024,1024]{1,0:T(8,128)(2,1)S(1)} %copy-done.4, bf16[1024,1792]{1,0:T(8,128)(2,1)S(1)} %copy-done.2, s32[]{:T(128)S(6)} %select_n.9), kind=kOutput, calls=%fused_computation.13 | convolution fusion | flops 1879965696 | bytes 5767172 | tf_op jit(solution)/shard_map/dot_general | solution.py:12
  203.9 0.5 collective-permute-start
  204.4 57.5 %collective-permute-done.1 = bf16[1024,896]{0,1:T(8,128)(2,1)} collective-permute-done((bf16[1024,896]{0,1:T(8,128)(2,1)}, bf16[1024,896]{0,1:T(8,128)(2,1)}, u32[]{:S(2)}, u32[]{:S(2)}) %collective-permute-start.1) | collective-permute-done | bytes 1835040 | tf_op jit(solution)/shard_map/ppermute | solution.py:13
  261.9 4.8 %fusion = bf16[1024,896]{0,1:T(8,128)(2,1)S(1)} fusion(bf16[1024,896]{0,1:T(8,128)(2,1)} %collective-permute-done.1, bf16[1024,1024]{1,0:T(8,128)(2,1)} %all-gather.4.cloned.1.call-done, bf16[1024,1792]{1,0:T(8,128)(2,1)} %all-gather.8.cloned.1.call-done, s32[]{:T(128)S(6)} %select_n.8), kind=kOutput, calls=%fused_computation.5 | convolution fusion | flops 1883635712 | bytes 7602180 | tf_op jit(solution)/shard_map/dot_general | solution.py:14
  266.7 2.5 copy.9
  269.2 31.3 %collective-permute-done = bf16[1024,896]{0,1:T(8,128)(2,1)} collective-permute-done((bf16[1024,896]{0,1:T(8,128)(2,1)}, bf16[1024,896]{0,1:T(8,128)(2,1)}, u32[]{:S(2)}, u32[]{:S(2)}) %collective-permute-start) | collective-permute-done | bytes 1835040 | tf_op jit(solution)/shard_map/ppermute | solution.py:13
  300.5 4.8 %fusion.1 = bf16[1024,896]{0,1:T(8,128)(2,1)S(1)} fusion(bf16[1024,896]{0,1:T(8,128)(2,1)} %collective-permute-done, bf16[1024,1024]{1,0:T(8,128)(2,1)} %all-gather.4.cloned.1.call-done, bf16[1024,1792]{1,0:T(8,128)(2,1)} %all-gather.6.cloned.1.call-done, s32[]{:T(128)S(6)} %select_n.8), kind=kOutput, calls=%fused_computation.7 | convolution fusion | flops 1883635712 | bytes 7602180 | tf_op jit(solution)/shard_map/dot_general | solution.py:14
  305.3 2.5 copy.8
  307.7 0.0 reduce-scatter.5.cloned.1.call-done
Async XLA Ops:
  7.2 43.6 %all-gather.4.cloned.1.call-start = ((), (), s32[]{:S(2)}) async-start(), calls=%async_computation.2 | async-start | bytes 2359296 | tf_op jit(solution)/shard_map/all_gather | solution.py:22
  7.9 110.2 %reduce-scatter.3.cloned.1.call-start = ((), (), s32[]{:S(2)}) async-start(), calls=%async_computation.3 | async-start | bytes 8257536 | tf_op jit(solution)/shard_map/reduce_scatter | solution.py:25
  50.8 6.8 %copy-start.1 = (bf16[1024,1792]{1,0:T(8,128)(2,1)S(1)}, bf16[1024,1792]{1,0:T(8,128)(2,1)}, u32[]{:S(2)}) copy-start(bf16[1024,1792]{1,0:T(8,128)(2,1)} %param.5) | copy-start | bytes 11010052
  50.8 6.8 %copy-start.3 = (bf16[1024,1024]{1,0:T(8,128)(2,1)S(1)}, bf16[1024,1024]{1,0:T(8,128)(2,1)}, u32[]{:S(2)}) copy-start(bf16[1024,1024]{1,0:T(8,128)(2,1)} %all-gather.4.cloned.1.call-done) | copy-start | bytes 6291460
  68.5 51.0 %copy-start = (bf16[128,1792]{1,0:T(8,128)(2,1)S(1)}, bf16[128,1792]{1,0:T(8,128)(2,1)}, u32[]{:S(2)}) copy-start(bf16[128,1792]{1,0:T(8,128)(2,1)} %param.7) | copy-start | bytes 1376260
  68.5 82.4 %all-gather.6.cloned.1.call-start = ((), (), s32[]{:S(2)}) async-start(), calls=%async_computation.4 | async-start | bytes 4128768 | tf_op jit(solution)/shard_map/all_gather | solution.py:39
  121.2 61.7 %all-gather.8.cloned.1.call-start = ((), (), s32[]{:S(2)}) async-start(), calls=%async_computation.5 | async-start | bytes 4128768 | tf_op jit(solution)/shard_map/all_gather | solution.py:41
  121.7 186.0 %reduce-scatter.5.cloned.1.call-start = ((), (), s32[]{:S(2)}) async-start(), calls=%async_computation.6 | async-start | bytes 2359296 | tf_op jit(solution)/shard_map/reduce_scatter | solution.py:45
  160.0 32.6 %copy-start.4 = (bf16[1024,1024]{1,0:T(8,128)(2,1)S(1)}, bf16[1024,1024]{1,0:T(8,128)(2,1)}, u32[]{:S(2)}) copy-start(bf16[1024,1024]{1,0:T(8,128)(2,1)} %all-gather.4.cloned.1.call-done) | copy-start | bytes 6291460
  192.5 8.0 %copy-start.2 = (bf16[1024,1792]{1,0:T(8,128)(2,1)S(1)}, bf16[1024,1792]{1,0:T(8,128)(2,1)}, u32[]{:S(2)}) copy-start(bf16[1024,1792]{1,0:T(8,128)(2,1)} %all-gather.6.cloned.1.call-done) | copy-start | bytes 11010052
  197.5 64.4 %collective-permute-start.1 = (bf16[1024,896]{0,1:T(8,128)(2,1)}, bf16[1024,896]{0,1:T(8,128)(2,1)}, u32[]{:S(2)}, u32[]{:S(2)}) collective-permute-start(bf16[1024,896]{0,1:T(8,128)(2,1)} %convert_bitcast_fusion), channel_id=1, source_target_pairs={{0,1},{1,0},{2,3},{3,2},{4,5},{5,4},{6,7},{7,6},{8,9},{9,8},{10,11... | collective-permute-start | bytes 5505032 | tf_op jit(solution)/shard_map/ppermute | solution.py:13
  203.9 96.6 %collective-permute-start = (bf16[1024,896]{0,1:T(8,128)(2,1)}, bf16[1024,896]{0,1:T(8,128)(2,1)}, u32[]{:S(2)}, u32[]{:S(2)}) collective-permute-start(bf16[1024,896]{0,1:T(8,128)(2,1)} %convert_bitcast_fusion.1), channel_id=1, source_target_pairs={{0,1},{1,0},{2,3},{3,2},{4,5},{5,4},{6,7},{7,6},{8,9},{9,8},{10,11... | collective-permute-start | bytes 5505032 | tf_op jit(solution)/shard_map/ppermute | solution.py:13
Sparse Core Ops, SparseCore 0:
  9.6 41.0 all-gather.3
  68.6 49.4 reduce-scatter.2
  121.3 29.5 all-gather.5
  153.0 29.8 all-gather.7
  192.6 40.6 reduce-scatter.4

commit v2 on v1

v2 whole, which is shorter than its diff:
```python
import jax
import jax.numpy as jnp
from jax import lax
from jax.sharding import PartitionSpec as P


def halves(x, dep, half):
    own = lax.dynamic_slice_in_dim(x, dep * half, half, axis=1)
    other = lax.dynamic_slice_in_dim(x, (1 - dep) * half, half, axis=1)
    return own, other


def on_device(tokens, gate_weight, up_weight, cotangent):
    width = gate_weight.shape[1]
    half = width // 2
    dep = lax.axis_index("dep")
    gathered = lax.all_gather(tokens, "col", axis=0, tiled=True)
    first = jnp.dot(gathered, gate_weight, preferred_element_type=jnp.float32)
    second = jnp.dot(gathered, up_weight, preferred_element_type=jnp.float32)
    joined = lax.psum_scatter(
        jnp.concatenate([first, second], axis=1).astype(jnp.bfloat16),
        "row",
        scatter_dimension=0,
        tiled=True,
    ).astype(jnp.float32)
    gate = joined[:, :width]
    up = joined[:, width:]
    sigma = jax.nn.sigmoid(gate)
    active = gate * sigma
    hidden = (active * up).astype(jnp.bfloat16)
    upstream = cotangent.astype(jnp.float32)
    grad_gate = (upstream * up * sigma * (1.0 + gate * (1.0 - sigma))).astype(jnp.bfloat16)
    grad_up = (upstream * active).astype(jnp.bfloat16)

    gate_own, gate_other = halves(grad_gate, dep, half)
    up_own, up_other = halves(grad_up, dep, half)
    contract = (((0,), (0,)), ((), ()))
    transposed = (((1,), (1,)), ((), ()))

    full_other = lax.all_gather(
        jnp.concatenate([gate_other, up_other], axis=1), "row", axis=0, tiled=True
    )
    send = lax.dot_general(gathered, full_other, contract, preferred_element_type=jnp.float32)
    recv = lax.ppermute(send.astype(jnp.bfloat16), "dep", [(0, 1), (1, 0)])

    full_own = lax.all_gather(
        jnp.concatenate([gate_own, up_own], axis=1), "row", axis=0, tiled=True
    )
    mine = lax.dot_general(gathered, full_own, contract, preferred_element_type=jnp.float32)

    wg_own, wg_other = halves(gate_weight, dep, half)
    wu_own, wu_other = halves(up_weight, dep, half)
    term = lax.dot_general(
        full_other, jnp.concatenate([wg_other, wu_other], axis=1), transposed,
        preferred_element_type=jnp.float32,
    ) + lax.dot_general(
        full_own, jnp.concatenate([wg_own, wu_own], axis=1), transposed,
        preferred_element_type=jnp.float32,
    )
    grad_tokens = lax.psum_scatter(
        term.astype(jnp.bfloat16), "col", scatter_dimension=0, tiled=True
    )

    total = (mine.astype(jnp.bfloat16).astype(jnp.float32) + recv.astype(jnp.float32)).astype(
        jnp.bfloat16
    )
    return (hidden, grad_tokens, total[:, :half], total[:, half:])


def solution(mesh):
    return jax.shard_map(
        on_device,
        mesh=mesh,
        in_specs=(
            P(("dep", "col"), "row"),
            P("row", "col"),
            P("row", "col"),
            P(("dep", "row"), "col"),
        ),
        out_specs=(
            P(("dep", "row"), "col"),
            P(("dep", "col"), "row"),
            P("row", ("col", "dep")),
            P("row", ("col", "dep")),
        ),
        check_vma=False,
    )
```

time: 315 us -> 286 us (0.908)
  waiting for transfers between devices: 234 us -> 201 us
  local copies, waits for them, and re-layouts: 4.95 us -> 13.7 us
  matrix products: 48.8 us -> 43.3 us
    ppermute x2 -> x1, waiting for transfers between devices: 88.8 us -> 71.1 us  [on_device(): recv = lax.ppermute(send.astype(jnp.bfloat16), 'dep', [(0, 1), (1, 0)])]
    all_gather x2, waiting for transfers between devices: 51.8 us -> 37.1 us  [the longest x1 23 us: on_device(): lax.all_gather(jnp.concatenate([gate_other, up_other], axis=1), 'row', ax...]
    dynamic_slice x0 -> x2, local copies, waits for them, and re-layouts: none -> 5.85 us  [halves(): own = lax.dynamic_slice_in_dim(x, dep * half, half, axis=1)]
    dot_general x6 -> x4, matrix products: 36.6 us -> 31.2 us  [the longest x1 9.15 us: on_device(): lax.dot_general(full_own, jnp.concatenate([wg_own, wu_own], axis=1), tran...]
  transfers between devices with their start and end apart: 7 -> 6, of which waited for: 6 -> 5; matrix products, arithmetic and copies ran while one was open for 10% -> 16% of each run, Pallas kernels for 0% -> 0%
where the time goes in v2:
time: 286 us; the launch traced here: 285 us
  waiting for transfers between devices  201 us (70%)
  matrix products  43.3 us (15%)
  between operations  13.8 us (5%)
  local copies, waits for them, and re-layouts  13.7 us (5%)
  other arithmetic  9.85 us (3%)
  starting transfers between devices  3.21 us (1%)
    ppermute x1, waiting for transfers between devices, on_device(): recv = lax.ppermute(send.astype(jnp.bfloat16), 'dep', [(0, 1), (1, 0)])  71.1 us
    reduce_scatter x1, waiting for transfers between devices, on_device(): lax.psum_scatter(jnp.concatenate([first, second], axis=1).astype(jnp.bflo...  49.6 us
    all_gather x1, waiting for transfers between devices, on_device(): gathered = lax.all_gather(tokens, 'col', axis=0, tiled=True)  42.8 us
    all_gather x1, waiting for transfers between devices, on_device(): lax.all_gather(jnp.concatenate([gate_other, up_other], axis=1), 'row', ax...  23 us
    all_gather x1, waiting for transfers between devices, on_device(): lax.all_gather(jnp.concatenate([gate_own, up_own], axis=1), 'row', axis=0...  14.1 us
    dot_general x1, matrix products, on_device(): lax.dot_general(full_own, jnp.concatenate([wg_own, wu_own], axis=1), tran...  9.15 us
    dot_general x1, matrix products, on_device(): lax.dot_general(gathered, full_other, contract, preferred_element_type=jn...  8.76 us
    dot_general x1, matrix products, on_device(): lax.dot_general(gathered, full_own, contract, preferred_element_type=jnp....  7.76 us
  transfers between devices with their start and end apart: 6, of which 5 were waited for; matrix products, arithmetic and copies ran while one was open for 16% of the time, Pallas kernels for 0%

profile of v2, /device:TPU:6, one launch (start us, length us, event | category | flops | bytes accessed | tf_op | source)
XLA Modules:
  0.0 285.3 jit_solution(5544611367054668596)
XLA Ops:
  7.2 0.0 all-gather.4.cloned.1.call-start
  7.2 0.7 all-gather.4.cloned.1.call-update
  7.9 0.0 reduce-scatter.3.cloned.1.call-start
  7.9 42.8 %all-gather.4.cloned.1.call-done = bf16[1024,1024]{1,0:T(8,128)(2,1)} async-done(((bf16[128,1024]{1,0:T(8,128)(2,1)}), bf16[1024,1024]{1,0:T(8,128)(2,1)}) %all-gather.4.cloned.1.call-update) | async-done | bytes 2097168 | tf_op jit(solution)/shard_map/all_gather | solution.py:17
  50.8 0.0 copy-start
  50.8 0.0 copy-start.5
  50.8 6.8 %convolution_convert_fusion.2 = bf16[1024,1792]{1,0:T(8,128)(2,1)S(1)} fusion(bf16[1024,1024]{1,0:T(8,128)(2,1)} %all-gather.4.cloned.1.call-done, bf16[1024,1792]{1,0:T(8,128)(2,1)} %param.6), kind=kOutput, calls=%fused_computation.6 | convolution fusion | flops 3759931392 | bytes 9437184 | tf_op jit(solution)/shard_map/dot_general | solution.py:19
  57.5 0.0 copy-done
  57.5 0.0 copy-done.5
  57.6 5.4 %convolution_convert_fusion.3 = bf16[1024,1792]{1,0:T(8,128)(2,1)} fusion(bf16[1024,1024]{1,0:T(8,128)(2,1)S(1)} %copy-done.5, bf16[1024,1792]{1,0:T(8,128)(2,1)S(1)} %copy-done), kind=kOutput, calls=%fused_computation.7 | convolution fusion | flops 3759931392 | bytes 9437184 | tf_op jit(solution)/shard_map/dot_general | solution.py:18
  62.9 5.6 %pad_maximum_fusion = bf16[1024,3584]{1,0:T(8,128)(2,1)} fusion(bf16[1024,1792]{1,0:T(8,128)(2,1)S(1)} %convolution_convert_fusion.2, bf16[1024,1792]{1,0:T(8,128)(2,1)} %convolution_convert_fusion.3), kind=kLoop, calls=%fused_computation | loop fusion | flops 14680064 | bytes 14680064 | tf_op jit(solution)/shard_map/concatenate | solution.py:21
  68.5 0.0 copy-start.3
  68.5 0.0 reduce-scatter.3.cloned.1.call-update
  68.5 0.0 all-gather.6.cloned.1.call-start
  68.6 49.6 %reduce-scatter.3.cloned.1.call-done = bf16[128,3584]{1,0:T(8,128)(2,1)} async-done(((bf16[1024,3584]{1,0:T(8,128)(2,1)}), bf16[128,3584]{1,0:T(8,128)(2,1)}) %reduce-scatter.3.cloned.1.call-update) | async-done | bytes 917520 | tf_op jit(solution)/shard_map/reduce_scatter | solution.py:20
  118.1 1.4 convert_element_type.41
  119.5 0.0 copy-done.3
  119.5 1.3 fusion.14
  120.8 0.1 constant_dynamic-slice_fusion.2
  120.9 0.8 pad_maximum_fusion.1
  121.7 0.0 all-gather.6.cloned.1.call-update
  121.8 0.0 all-gather.8.cloned.1.call-start
  121.8 0.8 pad_maximum_fusion.2
  122.6 0.0 all-gather.8.cloned.1.call-update
  122.6 0.0 reduce-scatter.5.cloned.1.call-start
  122.7 5.8 %constant_dynamic-slice_fusion = (bf16[1024,896]{1,0:T(8,128)(2,1)S(1)}, bf16[1024,896]{1,0:T(8,128)(2,1)}, bf16[1024,896]{1,0:T(8,128)(2,1)}, bf16[1024,896]{1,0:T(8,128)(2,1)}) fusion(bf16[1024,1792]{1,0:T(8,128)(2,1)} %param.6, s32[]{:T(128)S(6)} %select_n.5, s32[]{:T(128)S(6)} %select_n.4, bf16[1024,1792]{1,0:T(8,128)(2,1)} %param.5), kind=kLoop, calls=%fused_computation.28 | loop fusion | bytes 14680072 | tf_op jit(solution)/shard_map/dynamic_slice | solution.py:8
  128.5 23.0 %all-gather.6.cloned.1.call-done = bf16[1024,1792]{1,0:T(8,128)(2,1)} async-done(((bf16[128,1792]{1,0:T(8,128)(2,1)}), bf16[1024,1792]{1,0:T(8,128)(2,1)}) %all-gather.6.cloned.1.call-update) | async-done | bytes 3670032 | tf_op jit(solution)/shard_map/all_gather | solution.py:40
  151.5 0.0 copy-start.1
  151.5 0.0 copy-start.2
  151.5 0.0 copy-start.4
  151.5 8.8 %fusion.9 = bf16[1024,1792]{0,1:T(8,128)(2,1)} fusion(bf16[1024,1792]{1,0:T(8,128)(2,1)} %all-gather.6.cloned.1.call-done, bf16[1024,1024]{1,0:T(8,128)(2,1)} %all-gather.4.cloned.1.call-done), kind=kOutput, calls=%fused_computation.16 | convolution fusion | flops 3759931392 | bytes 9437184 | tf_op jit(solution)/shard_map/dot_general | solution.py:43
  160.2 3.0 %collective-permute-start = (bf16[1024,1792]{0,1:T(8,128)(2,1)}, bf16[1024,1792]{0,1:T(8,128)(2,1)}, u32[]{:S(2)}, u32[]{:S(2)}) collective-permute-start(bf16[1024,1792]{0,1:T(8,128)(2,1)} %fusion.9), channel_id=1, source_target_pairs={{0,1},{1,0},{2,3},{3,2},{4,5},{5,4},{6,7},{7,6},{8,9},{9,8},{10,11... | collective-permute-start | bytes 11010056 | tf_op jit(solution)/shard_map/ppermute | solution.py:44
  163.2 0.0 copy-done.1
  163.2 0.0 copy-done.2
  163.2 0.0 copy-done.4
  163.2 5.5 %fusion.1 = f32[1024,1024]{1,0:T(8,128)} fusion(bf16[1024,1792]{1,0:T(8,128)(2,1)S(1)} %copy-done.4, bf16[1024,896]{1,0:T(8,128)(2,1)S(1)} %copy-done.1, bf16[1024,896]{1,0:T(8,128)(2,1)S(1)} %copy-done.2), kind=kOutput, calls=%fused_computation.8 | convolution fusion | flops 3765436416 | bytes 11534336 | tf_op jit(solution)/shard_map/dot_general | solution.py:53
  168.8 14.1 %all-gather.8.cloned.1.call-done = bf16[1024,1792]{1,0:T(8,128)(2,1)} async-done(((bf16[128,1792]{1,0:T(8,128)(2,1)}), bf16[1024,1792]{1,0:T(8,128)(2,1)}) %all-gather.8.cloned.1.call-update) | async-done | bytes 3670032 | tf_op jit(solution)/shard_map/all_gather | solution.py:46
  182.9 9.1 %add_convert_fusion = bf16[1024,1024]{1,0:T(8,128)(2,1)} fusion(f32[1024,1024]{1,0:T(8,128)} %fusion.1, bf16[1024,1792]{1,0:T(8,128)(2,1)} %all-gather.8.cloned.1.call-done, bf16[1024,896]{1,0:T(8,128)(2,1)S(1)} %get-tuple-element.12, bf16[1024,896]{1,0:T(8,128)(2,1)} %get-tuple-element.24), kind=kOutput, calls=%fused_computation.3 | convolution fusion | flops 3767533568 | bytes 13631488 | tf_op jit(solution)/shard_map/dot_general | solution.py:56
  192.0 0.0 reduce-scatter.5.cloned.1.call-update
  192.1 71.1 %collective-permute-done = bf16[1024,1792]{0,1:T(8,128)(2,1)} collective-permute-done((bf16[1024,1792]{0,1:T(8,128)(2,1)}, bf16[1024,1792]{0,1:T(8,128)(2,1)}, u32[]{:S(2)}, u32[]{:S(2)}) %collective-permute-start) | collective-permute-done | bytes 3670048 | tf_op jit(solution)/shard_map/ppermute | solution.py:44
  263.2 7.8 %fusion = bf16[1024,1792]{0,1:T(8,128)(2,1)S(1)} fusion(bf16[1024,1792]{0,1:T(8,128)(2,1)} %collective-permute-done, bf16[1024,1792]{1,0:T(8,128)(2,1)} %all-gather.8.cloned.1.call-done, bf16[1024,1024]{1,0:T(8,128)(2,1)} %all-gather.4.cloned.1.call-done), kind=kOutput, calls=%fused_computation.2 | convolution fusion | flops 3767271424 | bytes 13107200 | tf_op jit(solution)/shard_map/dot_general | solution.py:49
  271.0 1.6 fusion.19
  272.6 3.8 %copy.8 = bf16[1024,896]{1,0:T(8,128)(2,1)} copy(bf16[1024,896]{0,1:T(8,128)(2,1)} %get-tuple-element.9) | data formatting | bytes 3670016
  276.4 2.4 copy.9
  278.8 0.0 reduce-scatter.5.cloned.1.call-done
Async XLA Ops:
  7.2 43.6 %all-gather.4.cloned.1.call-start = ((), (), s32[]{:S(2)}) async-start(), calls=%async_computation.2 | async-start | bytes 2359296 | tf_op jit(solution)/shard_map/all_gather | solution.py:17
  7.9 110.2 %reduce-scatter.3.cloned.1.call-start = ((), (), s32[]{:S(2)}) async-start(), calls=%async_computation.3 | async-start | bytes 8257536 | tf_op jit(solution)/shard_map/reduce_scatter | solution.py:20
  50.8 6.8 %copy-start = (bf16[1024,1792]{1,0:T(8,128)(2,1)S(1)}, bf16[1024,1792]{1,0:T(8,128)(2,1)}, u32[]{:S(2)}) copy-start(bf16[1024,1792]{1,0:T(8,128)(2,1)} %param.5) | copy-start | bytes 11010052
  50.8 6.8 %copy-start.5 = (bf16[1024,1024]{1,0:T(8,128)(2,1)S(1)}, bf16[1024,1024]{1,0:T(8,128)(2,1)}, u32[]{:S(2)}) copy-start(bf16[1024,1024]{1,0:T(8,128)(2,1)} %all-gather.4.cloned.1.call-done) | copy-start | bytes 6291460
  68.5 51.0 %copy-start.3 = (bf16[128,1792]{1,0:T(8,128)(2,1)S(1)}, bf16[128,1792]{1,0:T(8,128)(2,1)}, u32[]{:S(2)}) copy-start(bf16[128,1792]{1,0:T(8,128)(2,1)} %param.7) | copy-start | bytes 1376260
  68.5 83.0 %all-gather.6.cloned.1.call-start = ((), (), s32[]{:S(2)}) async-start(), calls=%async_computation.4 | async-start | bytes 4128768 | tf_op jit(solution)/shard_map/all_gather | solution.py:40
  121.8 61.1 %all-gather.8.cloned.1.call-start = ((), (), s32[]{:S(2)}) async-start(), calls=%async_computation.5 | async-start | bytes 4128768 | tf_op jit(solution)/shard_map/all_gather | solution.py:46
  122.6 156.2 %reduce-scatter.5.cloned.1.call-start = ((), (), s32[]{:S(2)}) async-start(), calls=%async_computation.6 | async-start | bytes 2359296 | tf_op jit(solution)/shard_map/reduce_scatter | solution.py:60
  151.5 11.8 %copy-start.1 = (bf16[1024,896]{1,0:T(8,128)(2,1)S(1)}, bf16[1024,896]{1,0:T(8,128)(2,1)}, u32[]{:S(2)}) copy-start(bf16[1024,896]{1,0:T(8,128)(2,1)} %get-tuple-element.13) | copy-start | bytes 5505028
  151.5 11.8 %copy-start.2 = (bf16[1024,896]{1,0:T(8,128)(2,1)S(1)}, bf16[1024,896]{1,0:T(8,128)(2,1)}, u32[]{:S(2)}) copy-start(bf16[1024,896]{1,0:T(8,128)(2,1)} %get-tuple-element.23) | copy-start | bytes 5505028
  151.5 11.8 %copy-start.4 = (bf16[1024,1792]{1,0:T(8,128)(2,1)S(1)}, bf16[1024,1792]{1,0:T(8,128)(2,1)}, u32[]{:S(2)}) copy-start(bf16[1024,1792]{1,0:T(8,128)(2,1)} %all-gather.6.cloned.1.call-done) | copy-start | bytes 11010052
  160.2 103.0 %collective-permute-start = (bf16[1024,1792]{0,1:T(8,128)(2,1)}, bf16[1024,1792]{0,1:T(8,128)(2,1)}, u32[]{:S(2)}, u32[]{:S(2)}) collective-permute-start(bf16[1024,1792]{0,1:T(8,128)(2,1)} %fusion.9), channel_id=1, source_target_pairs={{0,1},{1,0},{2,3},{3,2},{4,5},{5,4},{6,7},{7,6},{8,9},{9,8},{10,11... | collective-permute-start | bytes 11010056 | tf_op jit(solution)/shard_map/ppermute | solution.py:44
Sparse Core Ops, SparseCore 0:
  9.6 41.0 all-gather.3
  68.6 49.4 reduce-scatter.2
  121.9 29.5 all-gather.5
  153.0 29.8 all-gather.7
  192.2 40.6 reduce-scatter.4

commit v3 on v2

--- a/solution.py
+++ b/solution.py
@@ -14,7 +14,10 @@
     width = gate_weight.shape[1]
     half = width // 2
     dep = lax.axis_index("dep")
-    gathered = lax.all_gather(tokens, "col", axis=0, tiled=True)
+    n_col = lax.axis_size("col")
+    gathered = lax.all_to_all(
+        jnp.tile(tokens, (n_col, 1)), "col", 0, 0, tiled=True
+    )
     first = jnp.dot(gathered, gate_weight, preferred_element_type=jnp.float32)
     second = jnp.dot(gathered, up_weight, preferred_element_type=jnp.float32)
     joined = lax.psum_scatter(

time: 286 us -> 270 us (0.944)
  waiting for transfers between devices: 201 us -> 157 us
  blocking collectives: 0 us -> 30.7 us
  matrix products: 43.3 us -> 39.3 us
    all_gather x1 -> x0, waiting for transfers between devices: 42.8 us -> none  [on_device(): gathered = lax.all_gather(tokens, 'col', axis=0, tiled=True)]
    all_to_all x0 -> x1, blocking collectives: none -> 30.7 us  [on_device(): lax.all_to_all(jnp.tile(tokens, (n_col, 1)), 'col', 0, 0, tiled=True)]
    unnamed x14 -> x18, local copies, waits for them, and re-layouts: 6.26 us -> 6.27 us
  transfers between devices with their start and end apart: 6 -> 5, of which waited for: 5 -> 4; matrix products, arithmetic and copies ran while one was open for 16% -> 17% of each run, Pallas kernels for 0% -> 0%
where the time goes in v3:
time: 270 us; the launch traced here: 269 us
  waiting for transfers between devices  157 us (58%)
  matrix products  39.3 us (15%)
  blocking collectives  30.7 us (11%)
  local copies, waits for them, and re-layouts  15.8 us (6%)
  between operations  13.9 us (5%)
  other arithmetic  9.85 us (4%)
  starting transfers between devices  3.18 us (1%)
    ppermute x1, waiting for transfers between devices, on_device(): recv = lax.ppermute(send.astype(jnp.bfloat16), 'dep', [(0, 1), (1, 0)])  69.5 us
    reduce_scatter x1, waiting for transfers between devices, on_device(): lax.psum_scatter(jnp.concatenate([first, second], axis=1).astype(jnp.bflo...  49.5 us
    all_to_all x1, blocking collectives, on_device(): lax.all_to_all(jnp.tile(tokens, (n_col, 1)), 'col', 0, 0, tiled=True)  30.7 us
    all_gather x1, waiting for transfers between devices, on_device(): lax.all_gather(jnp.concatenate([gate_other, up_other], axis=1), 'row', ax...  22.2 us
    all_gather x1, waiting for transfers between devices, on_device(): lax.all_gather(jnp.concatenate([gate_own, up_own], axis=1), 'row', axis=0...  15.2 us
    dot_general x1, matrix products, on_device(): lax.dot_general(full_own, jnp.concatenate([wg_own, wu_own], axis=1), tran...  9.64 us
    dot_general x1, matrix products, on_device(): lax.dot_general(gathered, full_other, contract, preferred_element_type=jn...  7.74 us
    dot_general x1, matrix products, on_device(): lax.dot_general(gathered, full_own, contract, preferred_element_type=jnp....  6.85 us
  transfers between devices with their start and end apart: 5, of which 4 were waited for; matrix products, arithmetic and copies ran while one was open for 17% of the time, Pallas kernels for 0%

profile of v3, /device:TPU:6, one launch (start us, length us, event | category | flops | bytes accessed | tf_op | source)
XLA Modules:
  0.0 269.3 jit_solution(16045401155451193586)
XLA Ops:
  7.2 0.0 reduce-scatter.3.cloned.1.call-start
  7.2 0.0 copy-start
  7.2 1.4 tile.2
  8.6 30.7 %all_to_all.9 = bf16[8,128,1024]{2,1,0:T(8,128)(2,1)S(1)} all-to-all(bf16[8,128,1024]{2,1,0:T(8,128)(2,1)S(1)} %tile.2), channel_id=1, replica_groups=mesh['row'=8,'col'=8,'dep'=2] {'col'}, dimensions={0} | all-to-all | bytes 4194304 | tf_op jit(solution)/shard_map/all_to_all | solution.py:18
  39.2 0.0 copy-start.2
  39.2 0.0 copy-done
  39.2 0.0 copy-start.1
  39.2 4.1 %convolution_convert_fusion.2 = bf16[1024,1792]{1,0:T(8,128)(2,1)S(1)} fusion(bf16[1024,1024]{1,0:T(8,128)(2,1)S(1)} %bitcast.17, bf16[1024,1792]{1,0:T(8,128)(2,1)S(1)} %copy-done), kind=kOutput, calls=%fused_computation.6 | convolution fusion | flops 3759931392 | bytes 9437184 | tf_op jit(solution)/shard_map/dot_general | solution.py:22
  43.4 0.0 copy-done.2
  43.4 0.0 copy-done.1
  43.4 5.4 %convolution_convert_fusion.3 = bf16[1024,1792]{1,0:T(8,128)(2,1)} fusion(bf16[1024,1024]{1,0:T(8,128)(2,1)S(1)} %bitcast.18, bf16[1024,1792]{1,0:T(8,128)(2,1)S(1)} %copy-done.1), kind=kOutput, calls=%fused_computation.7 | convolution fusion | flops 3759931392 | bytes 9437184 | tf_op jit(solution)/shard_map/dot_general | solution.py:21
  48.8 5.5 %pad_maximum_fusion = bf16[1024,3584]{1,0:T(8,128)(2,1)} fusion(bf16[1024,1792]{1,0:T(8,128)(2,1)S(1)} %convolution_convert_fusion.2, bf16[1024,1792]{1,0:T(8,128)(2,1)} %convolution_convert_fusion.3), kind=kLoop, calls=%fused_computation | loop fusion | flops 14680064 | bytes 14680064 | tf_op jit(solution)/shard_map/concatenate | solution.py:24
  54.3 0.0 copy-start.6
  54.3 0.0 reduce-scatter.3.cloned.1.call-update
  54.4 0.0 all-gather.3.cloned.1.call-start
  54.4 49.5 %reduce-scatter.3.cloned.1.call-done = bf16[128,3584]{1,0:T(8,128)(2,1)} async-done(((bf16[1024,3584]{1,0:T(8,128)(2,1)}), bf16[128,3584]{1,0:T(8,128)(2,1)}) %reduce-scatter.3.cloned.1.call-update) | async-done | bytes 917520 | tf_op jit(solution)/shard_map/reduce_scatter | solution.py:23
  104.0 1.4 convert_element_type.41
  105.3 0.0 copy-done.6
  105.3 1.3 fusion.14
  106.7 0.1 constant_dynamic-slice_fusion.2
  106.7 0.8 pad_maximum_fusion.1
  107.6 0.0 all-gather.3.cloned.1.call-update
  107.6 0.0 all-gather.5.cloned.1.call-start
  107.6 0.8 pad_maximum_fusion.2
  108.5 0.0 all-gather.5.cloned.1.call-update
  108.5 0.0 copy-start.3
  108.5 0.0 reduce-scatter.5.cloned.1.call-start
  108.5 6.5 %constant_dynamic-slice_fusion = (bf16[1024,896]{1,0:T(8,128)(2,1)}, bf16[1024,896]{1,0:T(8,128)(2,1)}, bf16[1024,896]{1,0:T(8,128)(2,1)}, bf16[1024,896]{1,0:T(8,128)(2,1)}) fusion(bf16[1024,1792]{1,0:T(8,128)(2,1)} %param.6, s32[]{:T(128)S(6)} %select_n.5, s32[]{:T(128)S(6)} %select_n.4, bf16[1024,1792]{1,0:T(8,128)(2,1)} %param.5), kind=kLoop, calls=%fused_computation.28 | loop fusion | bytes 14680072 | tf_op jit(solution)/shard_map/dynamic_slice | solution.py:8
  115.1 22.2 %all-gather.3.cloned.1.call-done = bf16[1024,1792]{1,0:T(8,128)(2,1)} async-done(((bf16[128,1792]{1,0:T(8,128)(2,1)}), bf16[1024,1792]{1,0:T(8,128)(2,1)}) %all-gather.3.cloned.1.call-update) | async-done | bytes 3670032 | tf_op jit(solution)/shard_map/all_gather | solution.py:43
  137.3 0.0 copy-done.3
  137.3 0.0 copy-start.4
  137.3 0.0 copy-start.5
  137.3 0.0 copy-start.7
  137.3 7.7 %fusion.9 = bf16[1024,1792]{0,1:T(8,128)(2,1)} fusion(bf16[1024,1792]{1,0:T(8,128)(2,1)} %all-gather.3.cloned.1.call-done, bf16[1024,1024]{1,0:T(8,128)(2,1)S(1)} %bitcast.19), kind=kOutput, calls=%fused_computation.16 | convolution fusion | flops 3759931392 | bytes 9437184 | tf_op jit(solution)/shard_map/dot_general | solution.py:46
  145.1 3.0 %collective-permute-start = (bf16[1024,1792]{0,1:T(8,128)(2,1)}, bf16[1024,1792]{0,1:T(8,128)(2,1)}, u32[]{:S(2)}, u32[]{:S(2)}) collective-permute-start(bf16[1024,1792]{0,1:T(8,128)(2,1)} %fusion.9), channel_id=1, source_target_pairs={{0,1},{1,0},{2,3},{3,2},{4,5},{5,4},{6,7},{7,6},{8,9},{9,8},{10,11... | collective-permute-start | bytes 11010056 | tf_op jit(solution)/shard_map/ppermute | solution.py:47
  148.1 0.0 copy-done.4
  148.1 0.0 copy-done.5
  148.1 0.0 copy-done.7
  148.1 5.6 %fusion.1 = f32[1024,1024]{1,0:T(8,128)} fusion(bf16[1024,1792]{1,0:T(8,128)(2,1)S(1)} %copy-done.7, bf16[1024,896]{1,0:T(8,128)(2,1)S(1)} %copy-done.4, bf16[1024,896]{1,0:T(8,128)(2,1)S(1)} %copy-done.5), kind=kOutput, calls=%fused_computation.8 | convolution fusion | flops 3765436416 | bytes 11534336 | tf_op jit(solution)/shard_map/dot_general | solution.py:56
  153.7 15.2 %all-gather.5.cloned.1.call-done = bf16[1024,1792]{1,0:T(8,128)(2,1)} async-done(((bf16[128,1792]{1,0:T(8,128)(2,1)}), bf16[1024,1792]{1,0:T(8,128)(2,1)}) %all-gather.5.cloned.1.call-update) | async-done | bytes 3670032 | tf_op jit(solution)/shard_map/all_gather | solution.py:49
  168.9 9.6 %add_convert_fusion = bf16[1024,1024]{1,0:T(8,128)(2,1)} fusion(f32[1024,1024]{1,0:T(8,128)} %fusion.1, bf16[1024,1792]{1,0:T(8,128)(2,1)} %all-gather.5.cloned.1.call-done, bf16[1024,896]{1,0:T(8,128)(2,1)} %get-tuple-element.12, bf16[1024,896]{1,0:T(8,128)(2,1)} %get-tuple-element.24), kind=kOutput, calls=%fused_computation.3 | convolution fusion | flops 3767533568 | bytes 13631488 | tf_op jit(solution)/shard_map/dot_general | solution.py:59
  178.5 0.0 reduce-scatter.5.cloned.1.call-update
  178.5 69.5 %collective-permute-done = bf16[1024,1792]{0,1:T(8,128)(2,1)} collective-permute-done((bf16[1024,1792]{0,1:T(8,128)(2,1)}, bf16[1024,1792]{0,1:T(8,128)(2,1)}, u32[]{:S(2)}, u32[]{:S(2)}) %collective-permute-start) | collective-permute-done | bytes 3670048 | tf_op jit(solution)/shard_map/ppermute | solution.py:47
  248.0 6.8 %fusion = bf16[1024,1792]{0,1:T(8,128)(2,1)S(1)} fusion(bf16[1024,1792]{0,1:T(8,128)(2,1)} %collective-permute-done, bf16[1024,1792]{1,0:T(8,128)(2,1)} %all-gather.5.cloned.1.call-done, bf16[1024,1024]{1,0:T(8,128)(2,1)S(1)} %bitcast.20), kind=kOutput, calls=%fused_computation.2 | convolution fusion | flops 3767271424 | bytes 13107200 | tf_op jit(solution)/shard_map/dot_general | solution.py:52
  254.9 1.6 fusion.19
  256.5 3.8 %copy.8 = bf16[1024,896]{1,0:T(8,128)(2,1)} copy(bf16[1024,896]{0,1:T(8,128)(2,1)} %get-tuple-element.9) | data formatting | bytes 3670016
  260.3 2.4 copy.9
  262.7 0.0 reduce-scatter.5.cloned.1.call-done
Async XLA Ops:
  7.2 96.8 %reduce-scatter.3.cloned.1.call-start = ((), (), s32[]{:S(2)}) async-start(), calls=%async_computation.3 | async-start | bytes 8257536 | tf_op jit(solution)/shard_map/reduce_scatter | solution.py:23
  7.2 32.0 %copy-start = (bf16[1024,1792]{1,0:T(8,128)(2,1)S(1)}, bf16[1024,1792]{1,0:T(8,128)(2,1)}, u32[]{:S(2)}) copy-start(bf16[1024,1792]{1,0:T(8,128)(2,1)} %param.6) | copy-start | bytes 11010052
  39.2 4.2 %copy-start.2 = (bf16[8,128,1024]{2,1,0:T(8,128)(2,1)}, bf16[8,128,1024]{2,1,0:T(8,128)(2,1)S(1)}, u32[]{:S(2)}) copy-start(bf16[8,128,1024]{2,1,0:T(8,128)(2,1)S(1)} %all_to_all.9) | copy-start | bytes 6291460
  39.2 4.2 %copy-start.1 = (bf16[1024,1792]{1,0:T(8,128)(2,1)S(1)}, bf16[1024,1792]{1,0:T(8,128)(2,1)}, u32[]{:S(2)}) copy-start(bf16[1024,1792]{1,0:T(8,128)(2,1)} %param.5) | copy-start | bytes 11010052
  54.3 51.0 %copy-start.6 = (bf16[128,1792]{1,0:T(8,128)(2,1)S(1)}, bf16[128,1792]{1,0:T(8,128)(2,1)}, u32[]{:S(2)}) copy-start(bf16[128,1792]{1,0:T(8,128)(2,1)} %param.7) | copy-start | bytes 1376260
  54.4 82.9 %all-gather.3.cloned.1.call-start = ((), (), s32[]{:S(2)}) async-start(), calls=%async_computation.4 | async-start | bytes 4128768 | tf_op jit(solution)/shard_map/all_gather | solution.py:43
  107.6 61.3 %all-gather.5.cloned.1.call-start = ((), (), s32[]{:S(2)}) async-start(), calls=%async_computation.5 | async-start | bytes 4128768 | tf_op jit(solution)/shard_map/all_gather | solution.py:49
  108.5 28.8 %copy-start.3 = (bf16[8,128,1024]{2,1,0:T(8,128)(2,1)S(1)}, bf16[8,128,1024]{2,1,0:T(8,128)(2,1)}, u32[]{:S(2)}) copy-start(bf16[8,128,1024]{2,1,0:T(8,128)(2,1)} %copy-done.2) | copy-start | bytes 6291460
  108.5 154.2 %reduce-scatter.5.cloned.1.call-start = ((), (), s32[]{:S(2)}) async-start(), calls=%async_computation.6 | async-start | bytes 2359296 | tf_op jit(solution)/shard_map/reduce_scatter | solution.py:63
  137.3 10.8 %copy-start.4 = (bf16[1024,896]{1,0:T(8,128)(2,1)S(1)}, bf16[1024,896]{1,0:T(8,128)(2,1)}, u32[]{:S(2)}) copy-start(bf16[1024,896]{1,0:T(8,128)(2,1)} %get-tuple-element.13) | copy-start | bytes 5505028
  137.3 10.8 %copy-start.5 = (bf16[1024,896]{1,0:T(8,128)(2,1)S(1)}, bf16[1024,896]{1,0:T(8,128)(2,1)}, u32[]{:S(2)}) copy-start(bf16[1024,896]{1,0:T(8,128)(2,1)} %get-tuple-element.23) | copy-start | bytes 5505028
  137.3 10.8 %copy-start.7 = (bf16[1024,1792]{1,0:T(8,128)(2,1)S(1)}, bf16[1024,1792]{1,0:T(8,128)(2,1)}, u32[]{:S(2)}) copy-start(bf16[1024,1792]{1,0:T(8,128)(2,1)} %all-gather.3.cloned.1.call-done) | copy-start | bytes 11010052
  145.1 103.0 %collective-permute-start = (bf16[1024,1792]{0,1:T(8,128)(2,1)}, bf16[1024,1792]{0,1:T(8,128)(2,1)}, u32[]{:S(2)}, u32[]{:S(2)}) collective-permute-start(bf16[1024,1792]{0,1:T(8,128)(2,1)} %fusion.9), channel_id=1, source_target_pairs={{0,1},{1,0},{2,3},{3,2},{4,5},{5,4},{6,7},{7,6},{8,9},{9,8},{10,11... | collective-permute-start | bytes 11010056 | tf_op jit(solution)/shard_map/ppermute | solution.py:47
Sparse Core Ops, SparseCore 0:
  54.5 49.4 reduce-scatter.2
  107.7 29.5 all-gather.2
  139.0 29.8 all-gather.4
  178.7 40.8 reduce-scatter.4

commit v4 on v3

--- a/solution.py
+++ b/solution.py
@@ -18,16 +18,14 @@
     gathered = lax.all_to_all(
         jnp.tile(tokens, (n_col, 1)), "col", 0, 0, tiled=True
     )
-    first = jnp.dot(gathered, gate_weight, preferred_element_type=jnp.float32)
-    second = jnp.dot(gathered, up_weight, preferred_element_type=jnp.float32)
-    joined = lax.psum_scatter(
-        jnp.concatenate([first, second], axis=1).astype(jnp.bfloat16),
-        "row",
-        scatter_dimension=0,
-        tiled=True,
-    ).astype(jnp.float32)
-    gate = joined[:, :width]
-    up = joined[:, width:]
+    def project(weight):
+        part = jnp.dot(gathered, weight, preferred_element_type=jnp.float32)
+        return lax.psum_scatter(
+            part.astype(jnp.bfloat16), "row", scatter_dimension=0, tiled=True
+        ).astype(jnp.float32)
+
+    gate = project(gate_weight)
+    up = project(up_weight)
     sigma = jax.nn.sigmoid(gate)
     active = gate * sigma
     hidden = (active * up).astype(jnp.bfloat16)

time: 270 us -> 287 us (1.063)
  waiting for transfers between devices: 157 us -> 176 us
  other arithmetic: 9.85 us -> 4.1 us
  matrix products: 39.3 us -> 42.6 us
    reduce_scatter x1 -> x2, waiting for transfers between devices: 49.5 us -> 69.8 us  [project(): lax.psum_scatter(part.astype(jnp.bfloat16), 'row', scatter_dimension=0, t...]
    concatenate x1 -> x0, other arithmetic: 5.55 us -> none  [on_device(): jnp.concatenate([first, second], axis=1).astype(jnp.bfloat16)]
    dot_general x2, matrix products: 9.52 us -> 12.8 us  [project(): part = jnp.dot(gathered, weight, preferred_element_type=jnp.float32)]
    dynamic_slice x2 -> x3, local copies, waits for them, and re-layouts: 6.6 us -> 6.75 us  [halves(): own = lax.dynamic_slice_in_dim(x, dep * half, half, axis=1)]
    unnamed x18 -> x14, local copies, waits for them, and re-layouts: 6.27 us -> 6.27 us
  transfers between devices with their start and end apart: 5 -> 6, of which waited for: 4 -> 5; matrix products, arithmetic and copies ran while one was open for 17% -> 18% of each run, Pallas kernels for 0% -> 0%
where the time goes in v4:
time: 287 us; the launch traced here: 286 us
  waiting for transfers between devices  176 us (61%)
  matrix products  42.6 us (15%)
  blocking collectives  30.7 us (11%)
  local copies, waits for them, and re-layouts  16 us (6%)
  between operations  13.8 us (5%)
  other arithmetic  4.1 us (1%)
  starting transfers between devices  3.22 us (1%)
    reduce_scatter x2, waiting for transfers between devices, project(): lax.psum_scatter(part.astype(jnp.bfloat16), 'row', scatter_dimension=0, t...  69.8 us
    ppermute x1, waiting for transfers between devices, on_device(): recv = lax.ppermute(send.astype(jnp.bfloat16), 'dep', [(0, 1), (1, 0)])  69.6 us
    all_to_all x1, blocking collectives, on_device(): lax.all_to_all(jnp.tile(tokens, (n_col, 1)), 'col', 0, 0, tiled=True)  30.7 us
    all_gather x1, waiting for transfers between devices, on_device(): lax.all_gather(jnp.concatenate([gate_other, up_other], axis=1), 'row', ax...  21.3 us
    all_gather x1, waiting for transfers between devices, on_device(): lax.all_gather(jnp.concatenate([gate_own, up_own], axis=1), 'row', axis=0...  15.1 us
    dot_general x2, matrix products, project(): part = jnp.dot(gathered, weight, preferred_element_type=jnp.float32)  12.8 us
    dot_general x1, matrix products, on_device(): lax.dot_general(full_own, jnp.concatenate([wg_own, wu_own], axis=1), tran...  9.65 us
    dot_general x1, matrix products, on_device(): lax.dot_general(gathered, full_other, contract, preferred_element_type=jn...  7.72 us
  transfers between devices with their start and end apart: 6, of which 5 were waited for; matrix products, arithmetic and copies ran while one was open for 18% of the time, Pallas kernels for 0%

profile of v4, /device:TPU:6, one launch (start us, length us, event | category | flops | bytes accessed | tf_op | source)
XLA Modules:
  0.0 286.3 jit_solution(6115646312491956288)
XLA Ops:
  7.2 0.0 reduce-scatter.6.cloned.1.call-start
  7.2 0.0 copy-start
  7.2 1.4 tile.2
  8.6 30.7 %all_to_all.9 = bf16[8,128,1024]{2,1,0:T(8,128)(2,1)S(1)} all-to-all(bf16[8,128,1024]{2,1,0:T(8,128)(2,1)S(1)} %tile.2), channel_id=1, replica_groups=mesh['row'=8,'col'=8,'dep'=2] {'col'}, dimensions={0} | all-to-all | bytes 4194304 | tf_op jit(solution)/shard_map/all_to_all | solution.py:18
  39.2 0.0 copy-done
  39.2 5.4 %convolution_convert_fusion.2 = bf16[1024,1792]{1,0:T(8,128)(2,1)} fusion(bf16[1024,1024]{1,0:T(8,128)(2,1)S(1)} %bitcast.17, bf16[1024,1792]{1,0:T(8,128)(2,1)S(1)} %copy-done), kind=kOutput, calls=%fused_computation.5 | convolution fusion | flops 3759931392 | bytes 9437184 | tf_op jit(solution)/shard_map/dot_general | solution.py:22
  44.6 0.0 reduce-scatter.6.cloned.1.call-update
  44.6 0.0 reduce-scatter.4.cloned.1.call-start
  44.7 7.4 %convolution_convert_fusion.3 = bf16[1024,1792]{1,0:T(8,128)(2,1)} fusion(bf16[1024,1024]{1,0:T(8,128)(2,1)S(1)} %bitcast.18, bf16[1024,1792]{1,0:T(8,128)(2,1)} %param.5), kind=kOutput, calls=%fused_computation.6 | convolution fusion | flops 3759931392 | bytes 9437184 | tf_op jit(solution)/shard_map/dot_general | solution.py:22
  52.1 0.0 copy-start.4
  52.1 0.0 reduce-scatter.4.cloned.1.call-update
  52.2 0.0 all-gather.3.cloned.1.call-start
  52.2 31.5 %reduce-scatter.6.cloned.1.call-done = bf16[128,1792]{1,0:T(8,128)(2,1)} async-done(((bf16[1024,1792]{1,0:T(8,128)(2,1)}), bf16[128,1792]{1,0:T(8,128)(2,1)}) %reduce-scatter.6.cloned.1.call-update) | async-done | bytes 458768 | tf_op jit(solution)/shard_map/reduce_scatter | solution.py:23
  83.7 38.3 %reduce-scatter.4.cloned.1.call-done = bf16[128,1792]{1,0:T(8,128)(2,1)} async-done(((bf16[1024,1792]{1,0:T(8,128)(2,1)}), bf16[128,1792]{1,0:T(8,128)(2,1)}) %reduce-scatter.4.cloned.1.call-update) | async-done | bytes 458768 | tf_op jit(solution)/shard_map/reduce_scatter | solution.py:23
  122.0 0.0 copy-done.4
  122.0 2.5 fusion.15
  124.5 0.1 constant_dynamic-slice_fusion.2
  124.6 0.8 pad_maximum_fusion
  125.4 0.0 all-gather.3.cloned.1.call-update
  125.4 0.0 all-gather.5.cloned.1.call-start
  125.5 0.8 pad_maximum_fusion.1
  126.3 0.0 all-gather.5.cloned.1.call-update
  126.3 0.0 reduce-scatter.8.cloned.1.call-start
  126.3 0.0 copy-start.1
  126.4 4.3 %constant_dynamic-slice_fusion = (bf16[1024,896]{1,0:T(8,128)(2,1)}, bf16[1024,896]{1,0:T(8,128)(2,1)}) fusion(bf16[1024,1792]{1,0:T(8,128)(2,1)} %param.6, s32[]{:T(128)S(6)} %select_n.5, s32[]{:T(128)S(6)} %select_n.4), kind=kLoop, calls=%fused_computation.33 | loop fusion | bytes 7340040 | tf_op jit(solution)/shard_map/dynamic_slice | solution.py:8
  130.7 0.0 copy-done.1
  130.7 2.3 constant_dynamic-slice_fusion.1
  133.0 21.3 %all-gather.3.cloned.1.call-done = bf16[1024,1792]{1,0:T(8,128)(2,1)} async-done(((bf16[128,1792]{1,0:T(8,128)(2,1)}), bf16[1024,1792]{1,0:T(8,128)(2,1)}) %all-gather.3.cloned.1.call-update) | async-done | bytes 3670032 | tf_op jit(solution)/shard_map/all_gather | solution.py:41
  154.3 0.0 copy-start.2
  154.3 0.0 copy-start.3
  154.3 0.0 copy-start.5
  154.3 7.7 %fusion.9 = bf16[1024,1792]{0,1:T(8,128)(2,1)} fusion(bf16[1024,1792]{1,0:T(8,128)(2,1)} %all-gather.3.cloned.1.call-done, bf16[1024,1024]{1,0:T(8,128)(2,1)S(1)} %bitcast.19), kind=kOutput, calls=%fused_computation.15 | convolution fusion | flops 3759931392 | bytes 9437184 | tf_op jit(solution)/shard_map/dot_general | solution.py:44
  162.1 3.0 %collective-permute-start = (bf16[1024,1792]{0,1:T(8,128)(2,1)}, bf16[1024,1792]{0,1:T(8,128)(2,1)}, u32[]{:S(2)}, u32[]{:S(2)}) collective-permute-start(bf16[1024,1792]{0,1:T(8,128)(2,1)} %fusion.9), channel_id=1, source_target_pairs={{0,1},{1,0},{2,3},{3,2},{4,5},{5,4},{6,7},{7,6},{8,9},{9,8},{10,11... | collective-permute-start | bytes 11010056 | tf_op jit(solution)/shard_map/ppermute | solution.py:45
  165.1 0.0 copy-done.2
  165.1 0.0 copy-done.3
  165.1 0.0 copy-done.5
  165.1 5.6 %fusion.1 = f32[1024,1024]{1,0:T(8,128)} fusion(bf16[1024,1792]{1,0:T(8,128)(2,1)S(1)} %copy-done.5, bf16[1024,896]{1,0:T(8,128)(2,1)S(1)} %copy-done.2, bf16[1024,896]{1,0:T(8,128)(2,1)S(1)} %copy-done.3), kind=kOutput, calls=%fused_computation.7 | convolution fusion | flops 3765436416 | bytes 11534336 | tf_op jit(solution)/shard_map/dot_general | solution.py:54
  170.6 15.1 %all-gather.5.cloned.1.call-done = bf16[1024,1792]{1,0:T(8,128)(2,1)} async-done(((bf16[128,1792]{1,0:T(8,128)(2,1)}), bf16[1024,1792]{1,0:T(8,128)(2,1)}) %all-gather.5.cloned.1.call-update) | async-done | bytes 3670032 | tf_op jit(solution)/shard_map/all_gather | solution.py:47
  185.8 9.6 %add_convert_fusion = bf16[1024,1024]{1,0:T(8,128)(2,1)} fusion(f32[1024,1024]{1,0:T(8,128)} %fusion.1, bf16[1024,1792]{1,0:T(8,128)(2,1)} %all-gather.5.cloned.1.call-done, bf16[1024,896]{1,0:T(8,128)(2,1)} %get-tuple-element.12, bf16[1024,896]{1,0:T(8,128)(2,1)} %get-tuple-element.10), kind=kOutput, calls=%fused_computation.2 | convolution fusion | flops 3767533568 | bytes 13631488 | tf_op jit(solution)/shard_map/dot_general | solution.py:57
  195.4 0.0 reduce-scatter.8.cloned.1.call-update
  195.4 69.6 %collective-permute-done = bf16[1024,1792]{0,1:T(8,128)(2,1)} collective-permute-done((bf16[1024,1792]{0,1:T(8,128)(2,1)}, bf16[1024,1792]{0,1:T(8,128)(2,1)}, u32[]{:S(2)}, u32[]{:S(2)}) %collective-permute-start) | collective-permute-done | bytes 3670048 | tf_op jit(solution)/shard_map/ppermute | solution.py:45
  265.0 6.8 %fusion = bf16[1024,1792]{0,1:T(8,128)(2,1)S(1)} fusion(bf16[1024,1792]{0,1:T(8,128)(2,1)} %collective-permute-done, bf16[1024,1792]{1,0:T(8,128)(2,1)} %all-gather.5.cloned.1.call-done, bf16[1024,1024]{1,0:T(8,128)(2,1)S(1)} %bitcast.20), kind=kOutput, calls=%fused_computation.1 | convolution fusion | flops 3767271424 | bytes 13107200 | tf_op jit(solution)/shard_map/dot_general | solution.py:50
  271.9 1.6 fusion.23
  273.5 3.8 %copy.8 = bf16[1024,896]{1,0:T(8,128)(2,1)} copy(bf16[1024,896]{0,1:T(8,128)(2,1)} %get-tuple-element.9) | data formatting | bytes 3670016
  277.3 2.4 copy.9
  279.7 0.0 reduce-scatter.8.cloned.1.call-done
Async XLA Ops:
  7.2 76.6 %reduce-scatter.6.cloned.1.call-start = ((), (), s32[]{:S(2)}) async-start(), calls=%async_computation.5 | async-start | bytes 4128768 | tf_op jit(solution)/shard_map/reduce_scatter | solution.py:23
  7.2 32.0 %copy-start = (bf16[1024,1792]{1,0:T(8,128)(2,1)S(1)}, bf16[1024,1792]{1,0:T(8,128)(2,1)}, u32[]{:S(2)}) copy-start(bf16[1024,1792]{1,0:T(8,128)(2,1)} %param.6) | copy-start | bytes 11010052
  44.6 77.4 %reduce-scatter.4.cloned.1.call-start = ((), (), s32[]{:S(2)}) async-start(), calls=%async_computation.4 | async-start | bytes 4128768 | tf_op jit(solution)/shard_map/reduce_scatter | solution.py:23
  52.1 69.9 %copy-start.4 = (bf16[128,1792]{1,0:T(8,128)(2,1)S(1)}, bf16[128,1792]{1,0:T(8,128)(2,1)}, u32[]{:S(2)}) copy-start(bf16[128,1792]{1,0:T(8,128)(2,1)} %param.7) | copy-start | bytes 1376260
  52.2 102.2 %all-gather.3.cloned.1.call-start = ((), (), s32[]{:S(2)}) async-start(), calls=%async_computation.6 | async-start | bytes 4128768 | tf_op jit(solution)/shard_map/all_gather | solution.py:41
  125.4 60.4 %all-gather.5.cloned.1.call-start = ((), (), s32[]{:S(2)}) async-start(), calls=%async_computation.7 | async-start | bytes 4128768 | tf_op jit(solution)/shard_map/all_gather | solution.py:47
  126.3 153.4 %reduce-scatter.8.cloned.1.call-start = ((), (), s32[]{:S(2)}) async-start(), calls=%async_computation.8 | async-start | bytes 2359296 | tf_op jit(solution)/shard_map/reduce_scatter | solution.py:61
  126.3 4.3 %copy-start.1 = (bf16[1024,1792]{1,0:T(8,128)(2,1)S(1)}, bf16[1024,1792]{1,0:T(8,128)(2,1)}, u32[]{:S(2)}) copy-start(bf16[1024,1792]{1,0:T(8,128)(2,1)} %param.5) | copy-start | bytes 11010052
  154.3 10.7 %copy-start.2 = (bf16[1024,896]{1,0:T(8,128)(2,1)S(1)}, bf16[1024,896]{1,0:T(8,128)(2,1)}, u32[]{:S(2)}) copy-start(bf16[1024,896]{1,0:T(8,128)(2,1)} %get-tuple-element.13) | copy-start | bytes 5505028
  154.3 10.7 %copy-start.3 = (bf16[1024,896]{1,0:T(8,128)(2,1)S(1)}, bf16[1024,896]{1,0:T(8,128)(2,1)}, u32[]{:S(2)}) copy-start(bf16[1024,896]{1,0:T(8,128)(2,1)} %get-tuple-element.11) | copy-start | bytes 5505028
  154.3 10.7 %copy-start.5 = (bf16[1024,1792]{1,0:T(8,128)(2,1)S(1)}, bf16[1024,1792]{1,0:T(8,128)(2,1)}, u32[]{:S(2)}) copy-start(bf16[1024,1792]{1,0:T(8,128)(2,1)} %all-gather.3.cloned.1.call-done) | copy-start | bytes 11010052
  162.1 103.0 %collective-permute-start = (bf16[1024,1792]{0,1:T(8,128)(2,1)}, bf16[1024,1792]{0,1:T(8,128)(2,1)}, u32[]{:S(2)}, u32[]{:S(2)}) collective-permute-start(bf16[1024,1792]{0,1:T(8,128)(2,1)} %fusion.9), channel_id=1, source_target_pairs={{0,1},{1,0},{2,3},{3,2},{4,5},{5,4},{6,7},{7,6},{8,9},{9,8},{10,11... | collective-permute-start | bytes 11010056 | tf_op jit(solution)/shard_map/ppermute | solution.py:45
Sparse Core Ops, SparseCore 0:
  44.8 38.9 reduce-scatter.5
  86.1 35.8 reduce-scatter.3
  125.5 28.7 all-gather.2
  155.9 29.8 all-gather.4
  195.5 40.8 reduce-scatter.7

commit v5 on v2

v5 whole, which is shorter than its diff:
```python
import jax
import jax.numpy as jnp
from jax import lax
from jax.sharding import PartitionSpec as P


def halves(x, dep, half):
    own = lax.dynamic_slice_in_dim(x, dep * half, half, axis=1)
    other = lax.dynamic_slice_in_dim(x, (1 - dep) * half, half, axis=1)
    return own, other


def on_device(tokens, gate_weight, up_weight, cotangent):
    width = gate_weight.shape[1]
    half = width // 2
    dep = lax.axis_index("dep")
    n_col = lax.axis_size("col")
    contract = (((0,), (0,)), ((), ()))
    transposed = (((1,), (1,)), ((), ()))
    pair = [(0, 1), (1, 0)]

    def gather_col(block):
        return lax.all_to_all(jnp.tile(block, (n_col, 1)), "col", 0, 0, tiled=True)

    partner_tokens = lax.ppermute(tokens, "dep", pair)
    gathered = gather_col(tokens)
    first = jnp.dot(gathered, gate_weight, preferred_element_type=jnp.float32)
    second = jnp.dot(gathered, up_weight, preferred_element_type=jnp.float32)
    joined = lax.psum_scatter(
        jnp.concatenate([first, second], axis=1).astype(jnp.bfloat16),
        "row",
        scatter_dimension=0,
        tiled=True,
    )
    gathered_partner = gather_col(partner_tokens)
    joined, gathered_partner = lax.optimization_barrier((joined, gathered_partner))
    joined = joined.astype(jnp.float32)
    gate = joined[:, :width]
    up = joined[:, width:]
    sigma = jax.nn.sigmoid(gate)
    active = gate * sigma
    hidden = (active * up).astype(jnp.bfloat16)
    upstream = cotangent.astype(jnp.float32)
    grad_gate = (upstream * up * sigma * (1.0 + gate * (1.0 - sigma))).astype(jnp.bfloat16)
    grad_up = (upstream * active).astype(jnp.bfloat16)

    gate_own, gate_other = halves(grad_gate, dep, half)
    up_own, up_other = halves(grad_up, dep, half)
    partner_grads = lax.ppermute(
        jnp.concatenate([gate_other, up_other], axis=1), "dep", pair
    )
    full = lax.all_gather(
        jnp.concatenate([grad_gate, grad_up, partner_grads], axis=1),
        "row", axis=0, tiled=True,
    )
    full_gate = full[:, :width]
    full_up = full[:, width:2 * width]
    full_partner = full[:, 2 * width:]

    term = lax.dot_general(full_gate, gate_weight, transposed, preferred_element_type=jnp.float32)
    term = term + lax.dot_general(full_up, up_weight, transposed, preferred_element_type=jnp.float32)
    grad_tokens = lax.psum_scatter(
        term.astype(jnp.bfloat16), "col", scatter_dimension=0, tiled=True
    )

    own_cols = jnp.concatenate(
        [lax.dynamic_slice_in_dim(full_gate, dep * half, half, axis=1),
         lax.dynamic_slice_in_dim(full_up, dep * half, half, axis=1)],
        axis=1,
    )
    mine = lax.dot_general(gathered, own_cols, contract, preferred_element_type=jnp.float32)
    theirs = lax.dot_general(
        gathered_partner, full_partner, contract, preferred_element_type=jnp.float32
    )
    total = (
        mine.astype(jnp.bfloat16).astype(jnp.float32)
        + theirs.astype(jnp.bfloat16).astype(jnp.float32)
    ).astype(jnp.bfloat16)
    return (hidden, grad_tokens, total[:, :half], total[:, half:])


def solution(mesh):
    return jax.shard_map(
        on_device,
        mesh=mesh,
        in_specs=(
            P(("dep", "col"), "row"),
            P("row", "col"),
            P("row", "col"),
            P(("dep", "row"), "col"),
        ),
        out_specs=(
            P(("dep", "row"), "col"),
            P(("dep", "col"), "row"),
            P("row", ("col", "dep")),
            P("row", ("col", "dep")),
        ),
        check_vma=False,
    )
```

time: 286 us -> 248 us (0.87)
  waiting for transfers between devices: 201 us -> 127 us
  blocking collectives: 0 us -> 30.7 us
  starting transfers between devices: 3.21 us -> 12.2 us
  matrix products: 43.3 us -> 35.1 us
  local copies, waits for them, and re-layouts: 13.7 us -> 17.1 us
    ppermute x1 -> x2, waiting for transfers between devices: 71.1 us -> 15.2 us  [the longest x1 10.1 us: on_device(): lax.ppermute(jnp.concatenate([gate_other, up_other], axis=1), 'dep', pair)]
    reduce_scatter x1, waiting for transfers between devices: 49.6 us -> 10.4 us  [on_device(): lax.psum_scatter(jnp.concatenate([first, second], axis=1).astype(jnp.bflo...]
    all_to_all x0 -> x1, blocking collectives: none -> 30.7 us  [gather_col(): return lax.all_to_all(jnp.tile(block, (n_col, 1)), 'col', 0, 0, tiled=True)]
    all_to_all x0 -> x1, waiting for transfers between devices: none -> 22.6 us  [gather_col(): return lax.all_to_all(jnp.tile(block, (n_col, 1)), 'col', 0, 0, tiled=True)]
    all_gather x3 -> x1, waiting for transfers between devices: 79.9 us -> 61.4 us  [on_device(): lax.all_gather(jnp.concatenate([grad_gate, grad_up, partner_grads], axis=...]
    reduce_scatter x1, waiting for transfers between devices: 0.01 us -> 17 us  [on_device(): lax.psum_scatter(term.astype(jnp.bfloat16), 'col', scatter_dimension=0, t...]
    all_to_all x0 -> x1, starting transfers between devices: none -> 5.92 us  [gather_col(): return lax.all_to_all(jnp.tile(block, (n_col, 1)), 'col', 0, 0, tiled=True)]
    dot_general x4, matrix products: 31.2 us -> 25.6 us  [the longest x1 7.28 us: on_device(): lax.dot_general(full_gate, gate_weight, transposed, preferred_element_typ...]
  transfers between devices with their start and end apart: 6 -> 6, of which waited for: 5 -> 6; matrix products, arithmetic and copies ran while one was open for 16% -> 10% of each run, Pallas kernels for 0% -> 0%
where the time goes in v5:
time: 248 us; the launch traced here: 245 us
  waiting for transfers between devices  127 us (51%)
  matrix products  35.1 us (14%)
  blocking collectives  30.7 us (12%)
  local copies, waits for them, and re-layouts  17.1 us (7%)
  between operations  13.9 us (6%)
  starting transfers between devices  12.2 us (5%)
  other arithmetic  9.42 us (4%)
    all_gather x1, waiting for transfers between devices, on_device(): lax.all_gather(jnp.concatenate([grad_gate, grad_up, partner_grads], axis=...  61.4 us
    all_to_all x1, blocking collectives, gather_col(): return lax.all_to_all(jnp.tile(block, (n_col, 1)), 'col', 0, 0, tiled=True)  30.7 us
    all_to_all x1, waiting for transfers between devices, gather_col(): return lax.all_to_all(jnp.tile(block, (n_col, 1)), 'col', 0, 0, tiled=True)  22.6 us
    reduce_scatter x1, waiting for transfers between devices, on_device(): lax.psum_scatter(term.astype(jnp.bfloat16), 'col', scatter_dimension=0, t...  17 us
    reduce_scatter x1, waiting for transfers between devices, on_device(): lax.psum_scatter(jnp.concatenate([first, second], axis=1).astype(jnp.bflo...  10.4 us
    ppermute x1, waiting for transfers between devices, on_device(): lax.ppermute(jnp.concatenate([gate_other, up_other], axis=1), 'dep', pair)  10.1 us
    unnamed x16, local copies, waits for them, and re-layouts  8.46 us
    dot_general x1, matrix products, on_device(): lax.dot_general(full_gate, gate_weight, transposed, preferred_element_typ...  7.28 us
  transfers between devices with their start and end apart: 6, of which 6 were waited for; matrix products, arithmetic and copies ran while one was open for 10% of the time, Pallas kernels for 0%

profile of v5, /device:TPU:6, one launch (start us, length us, event | category | flops | bytes accessed | tf_op | source)
XLA Modules:
  0.0 244.9 jit_solution(11439976136826247197)
XLA Ops:
  7.2 0.0 reduce-scatter.3.cloned.1.call-start
  7.2 0.0 copy-start.4
  7.2 1.4 tile.4
  8.6 30.7 %all_to_all.18 = bf16[8,128,1024]{2,1,0:T(8,128)(2,1)S(1)} all-to-all(bf16[8,128,1024]{2,1,0:T(8,128)(2,1)S(1)} %tile.4), channel_id=1, replica_groups=mesh['row'=8,'col'=8,'dep'=2] {'col'}, dimensions={0} | all-to-all | bytes 4194304 | tf_op jit(solution)/shard_map/all_to_all | solution.py:23
  39.2 0.0 copy-start
  39.2 0.0 copy-done.4
  39.2 0.0 copy-start.5
  39.2 4.1 %convolution_convert_fusion.2 = bf16[1024,1792]{1,0:T(8,128)(2,1)S(1)} fusion(bf16[1024,1024]{1,0:T(8,128)(2,1)S(1)} %bitcast.14, bf16[1024,1792]{1,0:T(8,128)(2,1)S(1)} %copy-done.4), kind=kOutput, calls=%fused_computation.6 | convolution fusion | flops 3759931392 | bytes 9437184 | tf_op jit(solution)/shard_map/dot_general | solution.py:28
  43.4 0.0 copy-done
  43.4 0.0 copy-done.5
  43.4 5.4 %convolution_convert_fusion.3 = bf16[1024,1792]{1,0:T(8,128)(2,1)} fusion(bf16[1024,1024]{1,0:T(8,128)(2,1)S(1)} %bitcast.15, bf16[1024,1792]{1,0:T(8,128)(2,1)S(1)} %copy-done.5), kind=kOutput, calls=%fused_computation.7 | convolution fusion | flops 3759931392 | bytes 9437184 | tf_op jit(solution)/shard_map/dot_general | solution.py:27
  48.8 5.5 %pad_maximum_fusion = bf16[1024,3584]{1,0:T(8,128)(2,1)} fusion(bf16[1024,1792]{1,0:T(8,128)(2,1)S(1)} %convolution_convert_fusion.2, bf16[1024,1792]{1,0:T(8,128)(2,1)} %convolution_convert_fusion.3), kind=kLoop, calls=%fused_computation | loop fusion | flops 14680064 | bytes 14680064 | tf_op jit(solution)/shard_map/concatenate | solution.py:30
  54.4 0.0 copy-start.3
  54.4 0.0 reduce-scatter.3.cloned.1.call-update
  54.4 0.9 copy-done.3
  55.3 2.9 %collective-permute-start = (bf16[128,1024]{1,0:T(8,128)(2,1)S(1)}, bf16[128,1024]{1,0:T(8,128)(2,1)S(1)}, u32[]{:S(2)}, u32[]{:S(2)}) collective-permute-start(bf16[128,1024]{1,0:T(8,128)(2,1)S(1)} %copy-done.3), channel_id=1, source_target_pairs={{0,1},{1,0},{2,3},{3,2},{4,5},{5,4},{6,7},{7,6},{8,9},{9,8},{10,11... | collective-permute-start | bytes 786440 | tf_op jit(solution)/shard_map/ppermute | solution.py:25
  58.2 5.2 %collective-permute-done = bf16[128,1024]{1,0:T(8,128)(2,1)S(1)} collective-permute-done((bf16[128,1024]{1,0:T(8,128)(2,1)S(1)}, bf16[128,1024]{1,0:T(8,128)(2,1)S(1)}, u32[]{:S(2)}, u32[]{:S(2)}) %collective-permute-start) | collective-permute-done | bytes 262176 | tf_op jit(solution)/shard_map/ppermute | solution.py:25
  63.4 1.6 tile.5
  65.0 0.0 copy-start.2
  65.0 5.9 %all-to-all-start.1 = ((bf16[8,128,1024]{2,1,0:T(8,128)(2,1)}), bf16[8,128,1024]{2,1,0:T(8,128)(2,1)S(1)}, u32[]{:S(2)}, u32[]{:S(2)}) async-start(bf16[8,128,1024]{2,1,0:T(8,128)(2,1)} %tile.5), calls=%async_computation.2 | async-start | bytes 4194304 | tf_op jit(solution)/shard_map/all_to_all | solution.py:23
  70.9 0.0 all-gather.2.cloned.1.call-start
  70.9 22.6 %all-to-all-done.1 = bf16[8,128,1024]{2,1,0:T(8,128)(2,1)S(1)} async-done(((bf16[8,128,1024]{2,1,0:T(8,128)(2,1)}), bf16[8,128,1024]{2,1,0:T(8,128)(2,1)S(1)}, u32[]{:S(2)}, u32[]{:S(2)}) %all-to-all-start.1) | async-done | bytes 2097184 | tf_op jit(solution)/shard_map/all_to_all | solution.py:23
  93.6 10.4 %reduce-scatter.3.cloned.1.call-done = bf16[128,3584]{1,0:T(8,128)(2,1)} async-done(((bf16[1024,3584]{1,0:T(8,128)(2,1)}), bf16[128,3584]{1,0:T(8,128)(2,1)}) %reduce-scatter.3.cloned.1.call-update) | async-done | bytes 917520 | tf_op jit(solution)/shard_map/reduce_scatter | solution.py:29
  104.0 1.4 convert_element_type.38
  105.3 0.0 copy-done.2
  105.4 1.3 fusion.9
  106.8 3.1 %collective-permute-start.1 = (bf16[128,1792]{1,0:T(8,128)(2,1)S(1)}, bf16[128,1792]{1,0:T(8,128)(2,1)S(1)}, u32[]{:S(2)}, u32[]{:S(2)}) collective-permute-start(bf16[128,1792]{1,0:T(8,128)(2,1)S(1)} %pad_maximum_fusion.2), channel_id=1, source_target_pairs={{0,1},{1,0},{2,3},{3,2},{4,5},{5,4},{6,7},{7,6},{8,9},{9,8},{10,11... | collective-permute-start | bytes 1376264 | tf_op jit(solution)/shard_map/ppermute | solution.py:49
  109.8 10.1 %collective-permute-done.1 = bf16[128,1792]{1,0:T(8,128)(2,1)S(1)} collective-permute-done((bf16[128,1792]{1,0:T(8,128)(2,1)S(1)}, bf16[128,1792]{1,0:T(8,128)(2,1)S(1)}, u32[]{:S(2)}, u32[]{:S(2)}) %collective-permute-start.1) | collective-permute-done | bytes 458784 | tf_op jit(solution)/shard_map/ppermute | solution.py:49
  119.9 1.2 pad_maximum_fusion.1
  121.1 0.0 all-gather.2.cloned.1.call-update
  121.1 0.2 reduce-scatter.5.cloned.1.call-start
  121.3 61.4 %all-gather.2.cloned.1.call-done = bf16[1024,5376]{1,0:T(8,128)(2,1)} async-done(((bf16[128,5376]{1,0:T(8,128)(2,1)}), bf16[1024,5376]{1,0:T(8,128)(2,1)}) %all-gather.2.cloned.1.call-update) | async-done | bytes 11010064 | tf_op jit(solution)/shard_map/all_gather | solution.py:52
  182.7 0.0 copy-start.6
  182.7 7.3 %fusion.13 = f32[1024,1024]{1,0:T(8,128)S(1)} fusion(bf16[1024,1792]{1,0:T(8,128)(2,1)} %param.6, bf16[1024,5376]{1,0:T(8,128)(2,1)} %all-gather.2.cloned.1.call-done), kind=kOutput, calls=%fused_computation.28 | convolution fusion | flops 3758096384 | bytes 11534336 | tf_op jit(solution)/shard_map/dot_general | solution.py:61
  190.0 0.0 copy-done.6
  190.0 7.3 %add_convert_fusion = bf16[1024,1024]{1,0:T(8,128)(2,1)} fusion(f32[1024,1024]{1,0:T(8,128)S(1)} %fusion.13, bf16[1024,1792]{1,0:T(8,128)(2,1)S(1)} %copy-done.6, bf16[1024,5376]{1,0:T(8,128)(2,1)} %all-gather.2.cloned.1.call-done), kind=kOutput, calls=%fused_computation.3 | convolution fusion | flops 3760193536 | bytes 13631488 | tf_op jit(solution)/shard_map/dot_general | solution.py:60
  197.2 0.0 reduce-scatter.5.cloned.1.call-update
  197.3 3.6 %fusion.16 = (bf16[1024,1792]{1,0:T(8,128)(2,1)S(1)}, bf16[1024,1792]{1,0:T(8,128)(2,1)S(1)}) fusion(bf16[1024,5376]{1,0:T(8,128)(2,1)} %all-gather.2.cloned.1.call-done), kind=kLoop, calls=%fused_computation.31 | loop fusion | bytes 14680064 | tf_op jit(solution)/shard_map/slice | solution.py:56
  200.9 0.0 copy-start.1
  200.9 0.2 constant_dynamic-slice_fusion
  201.1 0.2 constant_dynamic-slice_fusion.1
  201.3 1.3 copy-done.1
  202.5 4.5 %convolution_convert_fusion.1 = bf16[1792,1024]{1,0:T(8,128)(2,1)S(1)} fusion(bf16[1024,1024]{1,0:T(8,128)(2,1)S(1)} %bitcast.16, bf16[1024,896]{1,0:T(8,128)(2,1)S(1)} %constant_dynamic-slice_fusion, bf16[1024,896]{1,0:T(8,128)(2,1)S(1)} %constant_dynamic-slice_fusion.1), kind=kOutput, calls=%fused_computation.5 | convolution fusion | flops 3767271424 | bytes 9437184 | tf_op jit(solution)/shard_map/dot_general | solution.py:71
  207.0 6.6 %fusion = bf16[1024,1792]{0,1:T(8,128)(2,1)S(1)} fusion(bf16[1792,1024]{1,0:T(8,128)(2,1)S(1)} %convolution_convert_fusion.1, bf16[1024,1024]{1,0:T(8,128)(2,1)S(1)} %bitcast.17, bf16[1024,5376]{1,0:T(8,128)(2,1)} %all-gather.2.cloned.1.call-done), kind=kOutput, calls=%fused_computation.2 | convolution fusion | flops 3767271424 | bytes 13107200 | tf_op jit(solution)/shard_map/dot_general | solution.py:72
  213.5 1.6 fusion.17
  215.1 3.8 %copy.10 = bf16[1024,896]{1,0:T(8,128)(2,1)} copy(bf16[1024,896]{0,1:T(8,128)(2,1)} %get-tuple-element.14) | data formatting | bytes 3670016
  219.0 2.4 copy.9
  221.4 17.0 %reduce-scatter.5.cloned.1.call-done = bf16[128,1024]{1,0:T(8,128)(2,1)} async-done(((bf16[1024,1024]{1,0:T(8,128)(2,1)}), bf16[128,1024]{1,0:T(8,128)(2,1)}) %reduce-scatter.5.cloned.1.call-update) | async-done | bytes 262160 | tf_op jit(solution)/shard_map/reduce_scatter | solution.py:62
  (2 shorter events, 0.1 us)
Async XLA Ops:
  7.2 96.8 %reduce-scatter.3.cloned.1.call-start = ((), (), s32[]{:S(2)}) async-start(), calls=%async_computation.4 | async-start | bytes 8257536 | tf_op jit(solution)/shard_map/reduce_scatter | solution.py:29
  7.2 32.0 %copy-start.4 = (bf16[1024,1792]{1,0:T(8,128)(2,1)S(1)}, bf16[1024,1792]{1,0:T(8,128)(2,1)}, u32[]{:S(2)}) copy-start(bf16[1024,1792]{1,0:T(8,128)(2,1)} %param.6) | copy-start | bytes 11010052
  39.2 4.2 %copy-start = (bf16[8,128,1024]{2,1,0:T(8,128)(2,1)}, bf16[8,128,1024]{2,1,0:T(8,128)(2,1)S(1)}, u32[]{:S(2)}) copy-start(bf16[8,128,1024]{2,1,0:T(8,128)(2,1)S(1)} %all_to_all.18) | copy-start | bytes 6291460
  39.2 4.2 %copy-start.5 = (bf16[1024,1792]{1,0:T(8,128)(2,1)S(1)}, bf16[1024,1792]{1,0:T(8,128)(2,1)}, u32[]{:S(2)}) copy-start(bf16[1024,1792]{1,0:T(8,128)(2,1)} %param.5) | copy-start | bytes 11010052
  54.4 0.9 copy-start.3
  55.3 8.1 %collective-permute-start = (bf16[128,1024]{1,0:T(8,128)(2,1)S(1)}, bf16[128,1024]{1,0:T(8,128)(2,1)S(1)}, u32[]{:S(2)}, u32[]{:S(2)}) collective-permute-start(bf16[128,1024]{1,0:T(8,128)(2,1)S(1)} %copy-done.3), channel_id=1, source_target_pairs={{0,1},{1,0},{2,3},{3,2},{4,5},{5,4},{6,7},{7,6},{8,9},{9,8},{10,11... | collective-permute-start | bytes 786440 | tf_op jit(solution)/shard_map/ppermute | solution.py:25
  65.0 40.3 %copy-start.2 = (bf16[128,1792]{1,0:T(8,128)(2,1)S(1)}, bf16[128,1792]{1,0:T(8,128)(2,1)}, u32[]{:S(2)}) copy-start(bf16[128,1792]{1,0:T(8,128)(2,1)} %param.7) | copy-start | bytes 1376260
  65.0 28.5 %all-to-all-start.1 = ((bf16[8,128,1024]{2,1,0:T(8,128)(2,1)}), bf16[8,128,1024]{2,1,0:T(8,128)(2,1)S(1)}, u32[]{:S(2)}, u32[]{:S(2)}) async-start(bf16[8,128,1024]{2,1,0:T(8,128)(2,1)} %tile.5), calls=%async_computation.2 | async-start | bytes 4194304 | tf_op jit(solution)/shard_map/all_to_all | solution.py:23
  70.9 111.7 %all-gather.2.cloned.1.call-start = ((), (), s32[]{:S(2)}) async-start(), calls=%async_computation.5 | async-start | bytes 12386304 | tf_op jit(solution)/shard_map/all_gather | solution.py:52
  106.8 13.1 %collective-permute-start.1 = (bf16[128,1792]{1,0:T(8,128)(2,1)S(1)}, bf16[128,1792]{1,0:T(8,128)(2,1)S(1)}, u32[]{:S(2)}, u32[]{:S(2)}) collective-permute-start(bf16[128,1792]{1,0:T(8,128)(2,1)S(1)} %pad_maximum_fusion.2), channel_id=1, source_target_pairs={{0,1},{1,0},{2,3},{3,2},{4,5},{5,4},{6,7},{7,6},{8,9},{9,8},{10,11... | collective-permute-start | bytes 1376264 | tf_op jit(solution)/shard_map/ppermute | solution.py:49
  121.1 117.3 %reduce-scatter.5.cloned.1.call-start = ((), (), s32[]{:S(2)}) async-start(), calls=%async_computation.6 | async-start | bytes 2359296 | tf_op jit(solution)/shard_map/reduce_scatter | solution.py:62
  182.7 7.3 %copy-start.6 = (bf16[1024,1792]{1,0:T(8,128)(2,1)S(1)}, bf16[1024,1792]{1,0:T(8,128)(2,1)}, u32[]{:S(2)}) copy-start(bf16[1024,1792]{1,0:T(8,128)(2,1)} %param.5) | copy-start | bytes 11010052
  200.9 1.6 copy-start.1
Sparse Core Ops, SparseCore 0:
  54.5 49.4 reduce-scatter.2
  121.2 61.4 all-gather.1
  197.4 40.9 reduce-scatter.4

commit v6 on v5

--- a/solution.py
+++ b/solution.py
@@ -59,9 +59,10 @@
 
     term = lax.dot_general(full_gate, gate_weight, transposed, preferred_element_type=jnp.float32)
     term = term + lax.dot_general(full_up, up_weight, transposed, preferred_element_type=jnp.float32)
-    grad_tokens = lax.psum_scatter(
-        term.astype(jnp.bfloat16), "col", scatter_dimension=0, tiled=True
+    parts = lax.all_to_all(
+        term.astype(jnp.bfloat16).reshape(n_col, -1, term.shape[1]), "col", 0, 0, tiled=True
     )
+    grad_tokens = parts.astype(jnp.float32).sum(axis=0).astype(jnp.bfloat16)
 
     own_cols = jnp.concatenate(
         [lax.dynamic_slice_in_dim(full_gate, dep * half, half, axis=1),

time: 248 us -> 245 us (0.988)
  waiting for transfers between devices: 127 us -> 116 us
  local copies, waits for them, and re-layouts: 17.1 us -> 22.7 us
  starting transfers between devices: 12.2 us -> 17.7 us
  matrix products: 35.1 us -> 32.3 us
    reduce_scatter x1 -> x0, waiting for transfers between devices: 17 us -> none  [on_device(): lax.psum_scatter(term.astype(jnp.bfloat16), 'col', scatter_dimension=0, t...]
    all_to_all x0 -> x1, waiting for transfers between devices: none -> 6.33 us  [on_device(): lax.all_to_all(term.astype(jnp.bfloat16).reshape(n_col, -1, term.shape[1]...]
    all_to_all x0 -> x1, starting transfers between devices: none -> 5.72 us  [on_device(): lax.all_to_all(term.astype(jnp.bfloat16).reshape(n_col, -1, term.shape[1]...]
    dot_general x1, matrix products: 7.27 us -> 3.97 us  [on_device(): lax.dot_general(full_up, up_weight, transposed, preferred_element_type=jn...]
    unnamed x16 -> x22, local copies, waits for them, and re-layouts: 8.46 us -> 10.9 us
where the time goes in v6:
time: 245 us; the launch traced here: 244 us
  waiting for transfers between devices  116 us (47%)
  matrix products  32.3 us (13%)
  blocking collectives  30.7 us (13%)
  local copies, waits for them, and re-layouts  22.7 us (9%)
  starting transfers between devices  17.7 us (7%)
  between operations  14.2 us (6%)
  other arithmetic  10.5 us (4%)
    all_gather x1, waiting for transfers between devices, on_device(): lax.all_gather(jnp.concatenate([grad_gate, grad_up, partner_grads], axis=...  61.6 us
    all_to_all x1, blocking collectives, gather_col(): return lax.all_to_all(jnp.tile(block, (n_col, 1)), 'col', 0, 0, tiled=True)  30.7 us
    all_to_all x1, waiting for transfers between devices, gather_col(): return lax.all_to_all(jnp.tile(block, (n_col, 1)), 'col', 0, 0, tiled=True)  22.6 us
    unnamed x22, local copies, waits for them, and re-layouts  10.9 us
    reduce_scatter x1, waiting for transfers between devices, on_device(): lax.psum_scatter(jnp.concatenate([first, second], axis=1).astype(jnp.bflo...  10.4 us
    ppermute x1, waiting for transfers between devices, on_device(): lax.ppermute(jnp.concatenate([gate_other, up_other], axis=1), 'dep', pair)  10.1 us
    dot_general x1, matrix products, on_device(): lax.dot_general(gathered, own_cols, contract, preferred_element_type=jnp....  6.85 us
    dot_general x1, matrix products, on_device(): lax.dot_general(gathered_partner, full_partner, contract, preferred_eleme...  6.61 us
  transfers between devices with their start and end apart: 6, of which 6 were waited for; matrix products, arithmetic and copies ran while one was open for 10% of the time, Pallas kernels for 0%

profile of v6, /device:TPU:6, one launch (start us, length us, event | category | flops | bytes accessed | tf_op | source)
XLA Modules:
  0.0 244.2 jit_solution(12553373892392573919)
XLA Ops:
  7.2 0.0 reduce-scatter.2.cloned.1.call-start
  7.2 0.0 copy-start.6
  7.2 1.4 tile.4
  8.6 30.7 %all_to_all.23 = bf16[8,128,1024]{2,1,0:T(8,128)(2,1)S(1)} all-to-all(bf16[8,128,1024]{2,1,0:T(8,128)(2,1)S(1)} %tile.4), channel_id=1, replica_groups=mesh['row'=8,'col'=8,'dep'=2] {'col'}, dimensions={0} | all-to-all | bytes 4194304 | tf_op jit(solution)/shard_map/all_to_all | solution.py:23
  39.2 0.0 copy-start.1
  39.2 0.0 copy-done.6
  39.2 0.0 copy-start.8
  39.2 4.1 %convolution_convert_fusion.2 = bf16[1024,1792]{1,0:T(8,128)(2,1)S(1)} fusion(bf16[1024,1024]{1,0:T(8,128)(2,1)S(1)} %bitcast.15, bf16[1024,1792]{1,0:T(8,128)(2,1)S(1)} %copy-done.6), kind=kOutput, calls=%fused_computation.6 | convolution fusion | flops 3759931392 | bytes 9437184 | tf_op jit(solution)/shard_map/dot_general | solution.py:28
  43.4 0.0 copy-done.1
  43.4 0.0 copy-done.8
  43.4 5.4 %convolution_convert_fusion.3 = bf16[1024,1792]{1,0:T(8,128)(2,1)} fusion(bf16[1024,1024]{1,0:T(8,128)(2,1)S(1)} %bitcast.16, bf16[1024,1792]{1,0:T(8,128)(2,1)S(1)} %copy-done.8), kind=kOutput, calls=%fused_computation.7 | convolution fusion | flops 3759931392 | bytes 9437184 | tf_op jit(solution)/shard_map/dot_general | solution.py:27
  48.8 5.6 %pad_maximum_fusion = bf16[1024,3584]{1,0:T(8,128)(2,1)} fusion(bf16[1024,1792]{1,0:T(8,128)(2,1)S(1)} %convolution_convert_fusion.2, bf16[1024,1792]{1,0:T(8,128)(2,1)} %convolution_convert_fusion.3), kind=kLoop, calls=%fused_computation | loop fusion | flops 14680064 | bytes 14680064 | tf_op jit(solution)/shard_map/concatenate | solution.py:30
  54.4 0.0 copy-start.5
  54.4 0.0 reduce-scatter.2.cloned.1.call-update
  54.4 0.9 copy-done.5
  55.3 2.9 %collective-permute-start = (bf16[128,1024]{1,0:T(8,128)(2,1)S(1)}, bf16[128,1024]{1,0:T(8,128)(2,1)S(1)}, u32[]{:S(2)}, u32[]{:S(2)}) collective-permute-start(bf16[128,1024]{1,0:T(8,128)(2,1)S(1)} %copy-done.5), channel_id=1, source_target_pairs={{0,1},{1,0},{2,3},{3,2},{4,5},{5,4},{6,7},{7,6},{8,9},{9,8},{10,11... | collective-permute-start | bytes 786440 | tf_op jit(solution)/shard_map/ppermute | solution.py:25
  58.2 5.2 %collective-permute-done = bf16[128,1024]{1,0:T(8,128)(2,1)S(1)} collective-permute-done((bf16[128,1024]{1,0:T(8,128)(2,1)S(1)}, bf16[128,1024]{1,0:T(8,128)(2,1)S(1)}, u32[]{:S(2)}, u32[]{:S(2)}) %collective-permute-start) | collective-permute-done | bytes 262176 | tf_op jit(solution)/shard_map/ppermute | solution.py:25
  63.4 1.7 tile.5
  65.1 0.0 copy-start.4
  65.1 5.9 %all-to-all-start.1 = ((bf16[8,128,1024]{2,1,0:T(8,128)(2,1)}), bf16[8,128,1024]{2,1,0:T(8,128)(2,1)S(1)}, u32[]{:S(2)}, u32[]{:S(2)}) async-start(bf16[8,128,1024]{2,1,0:T(8,128)(2,1)} %tile.5), calls=%async_computation.2 | async-start | bytes 4194304 | tf_op jit(solution)/shard_map/all_to_all | solution.py:23
  71.0 0.0 all-gather.2.cloned.1.call-start
  71.0 22.6 %all-to-all-done.1 = bf16[8,128,1024]{2,1,0:T(8,128)(2,1)S(1)} async-done(((bf16[8,128,1024]{2,1,0:T(8,128)(2,1)}), bf16[8,128,1024]{2,1,0:T(8,128)(2,1)S(1)}, u32[]{:S(2)}, u32[]{:S(2)}) %all-to-all-start.1) | async-done | bytes 2097184 | tf_op jit(solution)/shard_map/all_to_all | solution.py:23
  93.6 0.0 copy-start.2
  93.6 10.4 %reduce-scatter.2.cloned.1.call-done = bf16[128,3584]{1,0:T(8,128)(2,1)} async-done(((bf16[1024,3584]{1,0:T(8,128)(2,1)}), bf16[128,3584]{1,0:T(8,128)(2,1)}) %reduce-scatter.2.cloned.1.call-update) | async-done | bytes 917520 | tf_op jit(solution)/shard_map/reduce_scatter | solution.py:29
  104.0 1.4 convert_element_type.40
  105.3 0.0 copy-done.4
  105.4 1.3 fusion.9
  106.7 0.0 copy-done.2
  106.8 3.1 %collective-permute-start.1 = (bf16[128,1792]{1,0:T(8,128)(2,1)S(1)}, bf16[128,1792]{1,0:T(8,128)(2,1)S(1)}, u32[]{:S(2)}, u32[]{:S(2)}) collective-permute-start(bf16[128,1792]{1,0:T(8,128)(2,1)S(1)} %pad_maximum_fusion.2), channel_id=1, source_target_pairs={{0,1},{1,0},{2,3},{3,2},{4,5},{5,4},{6,7},{7,6},{8,9},{9,8},{10,11... | collective-permute-start | bytes 1376264 | tf_op jit(solution)/shard_map/ppermute | solution.py:49
  109.9 10.1 %collective-permute-done.1 = bf16[128,1792]{1,0:T(8,128)(2,1)S(1)} collective-permute-done((bf16[128,1792]{1,0:T(8,128)(2,1)S(1)}, bf16[128,1792]{1,0:T(8,128)(2,1)S(1)}, u32[]{:S(2)}, u32[]{:S(2)}) %collective-permute-start.1) | collective-permute-done | bytes 458784 | tf_op jit(solution)/shard_map/ppermute | solution.py:49
  119.9 1.2 pad_maximum_fusion.1
  121.1 0.0 all-gather.2.cloned.1.call-update
  121.1 61.6 %all-gather.2.cloned.1.call-done = bf16[1024,5376]{1,0:T(8,128)(2,1)} async-done(((bf16[128,5376]{1,0:T(8,128)(2,1)}), bf16[1024,5376]{1,0:T(8,128)(2,1)}) %all-gather.2.cloned.1.call-update) | async-done | bytes 11010064 | tf_op jit(solution)/shard_map/all_gather | solution.py:52
  182.7 0.0 copy-start
  182.7 3.8 %fusion.16 = (bf16[1024,1792]{1,0:T(8,128)(2,1)S(1)}, bf16[1024,1792]{1,0:T(8,128)(2,1)S(1)}) fusion(bf16[1024,5376]{1,0:T(8,128)(2,1)} %all-gather.2.cloned.1.call-done), kind=kLoop, calls=%fused_computation.31 | loop fusion | bytes 14680064 | tf_op jit(solution)/shard_map/slice | solution.py:56
  186.5 0.0 copy-start.7
  186.5 1.4 constant_dynamic-slice_fusion
  187.9 1.4 constant_dynamic-slice_fusion.1
  189.2 1.1 copy-done
  190.3 1.3 copy-done.7
  191.6 0.0 copy-start.9
  191.6 4.0 %fusion.13 = f32[1024,1024]{1,0:T(8,128)S(1)} fusion(bf16[1024,1792]{1,0:T(8,128)(2,1)S(1)} %copy-done.7, bf16[1024,5376]{1,0:T(8,128)(2,1)S(1)} %copy-done), kind=kOutput, calls=%fused_computation.28 | convolution fusion | flops 3758096384 | bytes 11534336 | tf_op jit(solution)/shard_map/dot_general | solution.py:61
  195.6 0.0 copy-done.9
  195.6 5.3 %add_convert_fusion = bf16[1024,1024]{1,0:T(8,128)(2,1)} fusion(f32[1024,1024]{1,0:T(8,128)S(1)} %fusion.13, bf16[1024,1792]{1,0:T(8,128)(2,1)S(1)} %copy-done.9, bf16[1024,5376]{1,0:T(8,128)(2,1)S(1)} %copy-done), kind=kOutput, calls=%fused_computation.3 | convolution fusion | flops 3760193536 | bytes 13631488 | tf_op jit(solution)/shard_map/dot_general | solution.py:60
  200.9 5.7 %all-to-all-start.2 = ((bf16[8,128,1024]{2,1,0:T(8,128)(2,1)}), bf16[8,128,1024]{2,1,0:T(8,128)(2,1)S(1)}, u32[]{:S(2)}, u32[]{:S(2)}) async-start(bf16[8,128,1024]{2,1,0:T(8,128)(2,1)} %bitcast.19), calls=%async_computation.3 | async-start | bytes 4194304 | tf_op jit(solution)/shard_map/all_to_all | solution.py:62
  206.6 0.0 copy-start.3
  206.6 6.9 %convolution_convert_fusion.1 = bf16[1792,1024]{1,0:T(8,128)(2,1)S(1)} fusion(bf16[1024,1024]{1,0:T(8,128)(2,1)} %bitcast.17, bf16[1024,896]{1,0:T(8,128)(2,1)} %constant_dynamic-slice_fusion, bf16[1024,896]{1,0:T(8,128)(2,1)} %constant_dynamic-slice_fusion.1), kind=kOutput, calls=%fused_computation.5 | convolution fusion | flops 3767271424 | bytes 9437184 | tf_op jit(solution)/shard_map/dot_general | solution.py:72
  213.5 0.0 copy-done.3
  213.5 6.6 %fusion = bf16[1024,1792]{0,1:T(8,128)(2,1)S(1)} fusion(bf16[1792,1024]{1,0:T(8,128)(2,1)S(1)} %convolution_convert_fusion.1, bf16[1024,1024]{1,0:T(8,128)(2,1)S(1)} %bitcast.18, bf16[1024,5376]{1,0:T(8,128)(2,1)} %all-gather.2.cloned.1.call-done), kind=kOutput, calls=%fused_computation.2 | convolution fusion | flops 3767271424 | bytes 13107200 | tf_op jit(solution)/shard_map/dot_general | solution.py:73
  220.1 2.2 fusion.17
  222.3 3.8 %copy.10 = bf16[1024,896]{1,0:T(8,128)(2,1)} copy(bf16[1024,896]{0,1:T(8,128)(2,1)} %get-tuple-element.14) | data formatting | bytes 3670016
  226.1 3.8 %copy.9 = bf16[1024,896]{1,0:T(8,128)(2,1)} copy(bf16[1024,896]{0,1:T(8,128)(2,1)} %get-tuple-element.15) | data formatting | bytes 3670016
  229.9 6.3 %all-to-all-done.2 = bf16[8,128,1024]{2,1,0:T(8,128)(2,1)S(1)} async-done(((bf16[8,128,1024]{2,1,0:T(8,128)(2,1)}), bf16[8,128,1024]{2,1,0:T(8,128)(2,1)S(1)}, u32[]{:S(2)}, u32[]{:S(2)}) %all-to-all-start.2) | async-done | bytes 2097184 | tf_op jit(solution)/shard_map/all_to_all | solution.py:62
  236.3 1.1 reduce_sum.12
  (2 shorter events, 0.1 us)
Async XLA Ops:
  7.2 96.8 %reduce-scatter.2.cloned.1.call-start = ((), (), s32[]{:S(2)}) async-start(), calls=%async_computation.4 | async-start | bytes 8257536 | tf_op jit(solution)/shard_map/reduce_scatter | solution.py:29
  7.2 32.0 %copy-start.6 = (bf16[1024,1792]{1,0:T(8,128)(2,1)S(1)}, bf16[1024,1792]{1,0:T(8,128)(2,1)}, u32[]{:S(2)}) copy-start(bf16[1024,1792]{1,0:T(8,128)(2,1)} %param.6) | copy-start | bytes 11010052
  39.2 4.2 %copy-start.1 = (bf16[8,128,1024]{2,1,0:T(8,128)(2,1)}, bf16[8,128,1024]{2,1,0:T(8,128)(2,1)S(1)}, u32[]{:S(2)}) copy-start(bf16[8,128,1024]{2,1,0:T(8,128)(2,1)S(1)} %all_to_all.23) | copy-start | bytes 6291460
  39.2 4.2 %copy-start.8 = (bf16[1024,1792]{1,0:T(8,128)(2,1)S(1)}, bf16[1024,1792]{1,0:T(8,128)(2,1)}, u32[]{:S(2)}) copy-start(bf16[1024,1792]{1,0:T(8,128)(2,1)} %param.5) | copy-start | bytes 11010052
  54.4 0.9 copy-start.5
  55.3 8.1 %collective-permute-start = (bf16[128,1024]{1,0:T(8,128)(2,1)S(1)}, bf16[128,1024]{1,0:T(8,128)(2,1)S(1)}, u32[]{:S(2)}, u32[]{:S(2)}) collective-permute-start(bf16[128,1024]{1,0:T(8,128)(2,1)S(1)} %copy-done.5), channel_id=1, source_target_pairs={{0,1},{1,0},{2,3},{3,2},{4,5},{5,4},{6,7},{7,6},{8,9},{9,8},{10,11... | collective-permute-start | bytes 786440 | tf_op jit(solution)/shard_map/ppermute | solution.py:25
  65.1 40.3 %copy-start.4 = (bf16[128,1792]{1,0:T(8,128)(2,1)S(1)}, bf16[128,1792]{1,0:T(8,128)(2,1)}, u32[]{:S(2)}) copy-start(bf16[128,1792]{1,0:T(8,128)(2,1)} %param.7) | copy-start | bytes 1376260
  65.1 28.5 %all-to-all-start.1 = ((bf16[8,128,1024]{2,1,0:T(8,128)(2,1)}), bf16[8,128,1024]{2,1,0:T(8,128)(2,1)S(1)}, u32[]{:S(2)}, u32[]{:S(2)}) async-start(bf16[8,128,1024]{2,1,0:T(8,128)(2,1)} %tile.5), calls=%async_computation.2 | async-start | bytes 4194304 | tf_op jit(solution)/shard_map/all_to_all | solution.py:23
  71.0 111.7 %all-gather.2.cloned.1.call-start = ((), (), s32[]{:S(2)}) async-start(), calls=%async_computation.5 | async-start | bytes 12386304 | tf_op jit(solution)/shard_map/all_gather | solution.py:52
  93.6 13.1 %copy-start.2 = (bf16[8,128,1024]{2,1,0:T(8,128)(2,1)}, bf16[8,128,1024]{2,1,0:T(8,128)(2,1)S(1)}, u32[]{:S(2)}) copy-start(bf16[8,128,1024]{2,1,0:T(8,128)(2,1)S(1)} %all-to-all-done.1) | copy-start | bytes 6291460
  106.8 13.1 %collective-permute-start.1 = (bf16[128,1792]{1,0:T(8,128)(2,1)S(1)}, bf16[128,1792]{1,0:T(8,128)(2,1)S(1)}, u32[]{:S(2)}, u32[]{:S(2)}) collective-permute-start(bf16[128,1792]{1,0:T(8,128)(2,1)S(1)} %pad_maximum_fusion.2), channel_id=1, source_target_pairs={{0,1},{1,0},{2,3},{3,2},{4,5},{5,4},{6,7},{7,6},{8,9},{9,8},{10,11... | collective-permute-start | bytes 1376264 | tf_op jit(solution)/shard_map/ppermute | solution.py:49
  182.7 7.6 %copy-start = (bf16[1024,5376]{1,0:T(8,128)(2,1)S(1)}, bf16[1024,5376]{1,0:T(8,128)(2,1)}, u32[]{:S(2)}) copy-start(bf16[1024,5376]{1,0:T(8,128)(2,1)} %all-gather.2.cloned.1.call-done) | copy-start | bytes 33030148
  186.5 5.1 %copy-start.7 = (bf16[1024,1792]{1,0:T(8,128)(2,1)S(1)}, bf16[1024,1792]{1,0:T(8,128)(2,1)}, u32[]{:S(2)}) copy-start(bf16[1024,1792]{1,0:T(8,128)(2,1)} %param.6) | copy-start | bytes 11010052
  191.6 4.0 %copy-start.9 = (bf16[1024,1792]{1,0:T(8,128)(2,1)S(1)}, bf16[1024,1792]{1,0:T(8,128)(2,1)}, u32[]{:S(2)}) copy-start(bf16[1024,1792]{1,0:T(8,128)(2,1)} %param.5) | copy-start | bytes 11010052
  200.9 35.3 %all-to-all-start.2 = ((bf16[8,128,1024]{2,1,0:T(8,128)(2,1)}), bf16[8,128,1024]{2,1,0:T(8,128)(2,1)S(1)}, u32[]{:S(2)}, u32[]{:S(2)}) async-start(bf16[8,128,1024]{2,1,0:T(8,128)(2,1)} %bitcast.19), calls=%async_computation.3 | async-start | bytes 4194304 | tf_op jit(solution)/shard_map/all_to_all | solution.py:62
  206.6 6.9 %copy-start.3 = (bf16[8,128,1024]{2,1,0:T(8,128)(2,1)S(1)}, bf16[8,128,1024]{2,1,0:T(8,128)(2,1)}, u32[]{:S(2)}) copy-start(bf16[8,128,1024]{2,1,0:T(8,128)(2,1)} %copy-done.2) | copy-start | bytes 6291460
Sparse Core Ops, SparseCore 0:
  54.5 49.4 reduce-scatter.1
  121.2 61.4 all-gather.1

commit v7 on v5

--- a/solution.py
+++ b/solution.py
@@ -59,19 +59,22 @@
 
     term = lax.dot_general(full_gate, gate_weight, transposed, preferred_element_type=jnp.float32)
     term = term + lax.dot_general(full_up, up_weight, transposed, preferred_element_type=jnp.float32)
-    grad_tokens = lax.psum_scatter(
-        term.astype(jnp.bfloat16), "col", scatter_dimension=0, tiled=True
-    )
+    term = term.astype(jnp.bfloat16).reshape(n_col, -1, term.shape[1])
 
     own_cols = jnp.concatenate(
         [lax.dynamic_slice_in_dim(full_gate, dep * half, half, axis=1),
          lax.dynamic_slice_in_dim(full_up, dep * half, half, axis=1)],
         axis=1,
     )
-    mine = lax.dot_general(gathered, own_cols, contract, preferred_element_type=jnp.float32)
-    theirs = lax.dot_general(
-        gathered_partner, full_partner, contract, preferred_element_type=jnp.float32
-    )
+    own_cols, full_partner, term = lax.optimization_barrier((own_cols, full_partner, term))
+    parts = lax.all_to_all(term, "col", 0, 0, tiled=True)
+    grad_tokens = parts.astype(jnp.float32).sum(axis=0).astype(jnp.bfloat16)
+
+    def weight_part(grads, rows):
+        return lax.dot_general(rows, grads, contract, preferred_element_type=jnp.float32)
+
+    mine = weight_part(own_cols, gathered)
+    theirs = weight_part(full_partner, gathered_partner)
     total = (
         mine.astype(jnp.bfloat16).astype(jnp.float32)
         + theirs.astype(jnp.bfloat16).astype(jnp.float32)

time: 248 us -> 247 us (level); the launches traced: 245 us -> 247 us
  waiting for transfers between devices: 127 us -> 118 us
  local copies, waits for them, and re-layouts: 17.1 us -> 23.1 us
  starting transfers between devices: 12.2 us -> 17.7 us
  matrix products: 35.1 us -> 30 us
  other arithmetic: 9.42 us -> 12.6 us
    reduce_scatter x1 -> x0, waiting for transfers between devices: 17 us -> none  [on_device(): lax.psum_scatter(term.astype(jnp.bfloat16), 'col', scatter_dimension=0, t...]
    all_to_all x0 -> x1, waiting for transfers between devices: none -> 8.53 us  [on_device(): parts = lax.all_to_all(term, 'col', 0, 0, tiled=True)]
    all_to_all x0 -> x1, starting transfers between devices: none -> 5.72 us  [on_device(): parts = lax.all_to_all(term, 'col', 0, 0, tiled=True)]
    dot_general x1, matrix products: 7.27 us -> 3.97 us  [on_device(): lax.dot_general(full_up, up_weight, transposed, preferred_element_type=jn...]
    slice x1, local copies, waits for them, and re-layouts: 3.64 us -> 6.55 us  [on_device(): full_partner = full[:, 2 * width:]]
    unnamed x16 -> x28, local copies, waits for them, and re-layouts: 8.46 us -> 10.9 us
  transfers between devices with their start and end apart: 6 -> 6, of which waited for: 6 -> 6; matrix products, arithmetic and copies ran while one was open for 10% -> 9% of each run, Pallas kernels for 0% -> 0%
where the time goes in v7:
time: 247 us
  waiting for transfers between devices  118 us (48%)
  blocking collectives  30.7 us (12%)
  matrix products  30 us (12%)
  local copies, waits for them, and re-layouts  23.1 us (9%)
  starting transfers between devices  17.7 us (7%)
  between operations  14.2 us (6%)
  other arithmetic  12.6 us (5%)
    all_gather x1, waiting for transfers between devices, on_device(): lax.all_gather(jnp.concatenate([grad_gate, grad_up, partner_grads], axis=...  61.6 us
    all_to_all x1, blocking collectives, gather_col(): return lax.all_to_all(jnp.tile(block, (n_col, 1)), 'col', 0, 0, tiled=True)  30.7 us
    all_to_all x1, waiting for transfers between devices, gather_col(): return lax.all_to_all(jnp.tile(block, (n_col, 1)), 'col', 0, 0, tiled=True)  22.6 us
    dot_general x2, matrix products, weight_part(): lax.dot_general(rows, grads, contract, preferred_element_type=jnp.float32)  11.2 us
    unnamed x28, local copies, waits for them, and re-layouts  10.9 us
    reduce_scatter x1, waiting for transfers between devices, on_device(): lax.psum_scatter(jnp.concatenate([first, second], axis=1).astype(jnp.bflo...  10.4 us
    ppermute x1, waiting for transfers between devices, on_device(): lax.ppermute(jnp.concatenate([gate_other, up_other], axis=1), 'dep', pair)  10.1 us
    all_to_all x1, waiting for transfers between devices, on_device(): parts = lax.all_to_all(term, 'col', 0, 0, tiled=True)  8.53 us
  transfers between devices with their start and end apart: 6, of which 6 were waited for; matrix products, arithmetic and copies ran while one was open for 9% of the time, Pallas kernels for 0%

profile of v7, /device:TPU:6, one launch (start us, length us, event | category | flops | bytes accessed | tf_op | source)
XLA Modules:
  0.0 246.6 jit_solution(2063745430639261679)
XLA Ops:
  7.2 0.0 reduce-scatter.2.cloned.1.call-start
  7.2 0.0 copy-start.6
  7.2 1.4 tile.4
  8.6 30.7 %all_to_all.23 = bf16[8,128,1024]{2,1,0:T(8,128)(2,1)S(1)} all-to-all(bf16[8,128,1024]{2,1,0:T(8,128)(2,1)S(1)} %tile.4), channel_id=1, replica_groups=mesh['row'=8,'col'=8,'dep'=2] {'col'}, dimensions={0} | all-to-all | bytes 4194304 | tf_op jit(solution)/shard_map/all_to_all | solution.py:23
  39.2 0.0 copy-start.1
  39.2 0.0 copy-done.6
  39.2 0.0 copy-start.8
  39.2 4.1 %convolution_convert_fusion.2 = bf16[1024,1792]{1,0:T(8,128)(2,1)S(1)} fusion(bf16[1024,1024]{1,0:T(8,128)(2,1)S(1)} %bitcast.19, bf16[1024,1792]{1,0:T(8,128)(2,1)S(1)} %copy-done.6), kind=kOutput, calls=%fused_computation.6 | convolution fusion | flops 3759931392 | bytes 9437184 | tf_op jit(solution)/shard_map/dot_general | solution.py:28
  43.4 0.0 copy-done.1
  43.4 0.0 copy-done.8
  43.4 5.4 %convolution_convert_fusion.3 = bf16[1024,1792]{1,0:T(8,128)(2,1)} fusion(bf16[1024,1024]{1,0:T(8,128)(2,1)S(1)} %bitcast.20, bf16[1024,1792]{1,0:T(8,128)(2,1)S(1)} %copy-done.8), kind=kOutput, calls=%fused_computation.7 | convolution fusion | flops 3759931392 | bytes 9437184 | tf_op jit(solution)/shard_map/dot_general | solution.py:27
  48.8 5.6 %pad_maximum_fusion = bf16[1024,3584]{1,0:T(8,128)(2,1)} fusion(bf16[1024,1792]{1,0:T(8,128)(2,1)S(1)} %convolution_convert_fusion.2, bf16[1024,1792]{1,0:T(8,128)(2,1)} %convolution_convert_fusion.3), kind=kLoop, calls=%fused_computation | loop fusion | flops 14680064 | bytes 14680064 | tf_op jit(solution)/shard_map/concatenate | solution.py:30
  54.4 0.0 copy-start.5
  54.4 0.0 reduce-scatter.2.cloned.1.call-update
  54.4 0.9 copy-done.5
  55.3 2.9 %collective-permute-start = (bf16[128,1024]{1,0:T(8,128)(2,1)S(1)}, bf16[128,1024]{1,0:T(8,128)(2,1)S(1)}, u32[]{:S(2)}, u32[]{:S(2)}) collective-permute-start(bf16[128,1024]{1,0:T(8,128)(2,1)S(1)} %copy-done.5), channel_id=1, source_target_pairs={{0,1},{1,0},{2,3},{3,2},{4,5},{5,4},{6,7},{7,6},{8,9},{9,8},{10,11... | collective-permute-start | bytes 786440 | tf_op jit(solution)/shard_map/ppermute | solution.py:25
  58.2 5.2 %collective-permute-done = bf16[128,1024]{1,0:T(8,128)(2,1)S(1)} collective-permute-done((bf16[128,1024]{1,0:T(8,128)(2,1)S(1)}, bf16[128,1024]{1,0:T(8,128)(2,1)S(1)}, u32[]{:S(2)}, u32[]{:S(2)}) %collective-permute-start) | collective-permute-done | bytes 262176 | tf_op jit(solution)/shard_map/ppermute | solution.py:25
  63.4 1.7 tile.5
  65.1 0.0 copy-start.4
  65.1 5.9 %all-to-all-start.1 = ((bf16[8,128,1024]{2,1,0:T(8,128)(2,1)}), bf16[8,128,1024]{2,1,0:T(8,128)(2,1)S(1)}, u32[]{:S(2)}, u32[]{:S(2)}) async-start(bf16[8,128,1024]{2,1,0:T(8,128)(2,1)} %tile.5), calls=%async_computation.2 | async-start | bytes 4194304 | tf_op jit(solution)/shard_map/all_to_all | solution.py:23
  71.0 0.0 all-gather.2.cloned.1.call-start
  71.0 22.6 %all-to-all-done.1 = bf16[8,128,1024]{2,1,0:T(8,128)(2,1)S(1)} async-done(((bf16[8,128,1024]{2,1,0:T(8,128)(2,1)}), bf16[8,128,1024]{2,1,0:T(8,128)(2,1)S(1)}, u32[]{:S(2)}, u32[]{:S(2)}) %all-to-all-start.1) | async-done | bytes 2097184 | tf_op jit(solution)/shard_map/all_to_all | solution.py:23
  93.6 0.0 copy-start.3
  93.6 10.4 %reduce-scatter.2.cloned.1.call-done = bf16[128,3584]{1,0:T(8,128)(2,1)} async-done(((bf16[1024,3584]{1,0:T(8,128)(2,1)}), bf16[128,3584]{1,0:T(8,128)(2,1)}) %reduce-scatter.2.cloned.1.call-update) | async-done | bytes 917520 | tf_op jit(solution)/shard_map/reduce_scatter | solution.py:29
  104.0 1.4 convert_element_type.40
  105.3 0.0 copy-done.4
  105.4 1.3 fusion.3
  106.7 0.0 copy-done.3
  106.8 3.1 %collective-permute-start.1 = (bf16[128,1792]{1,0:T(8,128)(2,1)S(1)}, bf16[128,1792]{1,0:T(8,128)(2,1)S(1)}, u32[]{:S(2)}, u32[]{:S(2)}) collective-permute-start(bf16[128,1792]{1,0:T(8,128)(2,1)S(1)} %pad_maximum_fusion.3), channel_id=1, source_target_pairs={{0,1},{1,0},{2,3},{3,2},{4,5},{5,4},{6,7},{7,6},{8,9},{9,8},{10,11... | collective-permute-start | bytes 1376264 | tf_op jit(solution)/shard_map/ppermute | solution.py:49
  109.9 10.1 %collective-permute-done.1 = bf16[128,1792]{1,0:T(8,128)(2,1)S(1)} collective-permute-done((bf16[128,1792]{1,0:T(8,128)(2,1)S(1)}, bf16[128,1792]{1,0:T(8,128)(2,1)S(1)}, u32[]{:S(2)}, u32[]{:S(2)}) %collective-permute-start.1) | collective-permute-done | bytes 458784 | tf_op jit(solution)/shard_map/ppermute | solution.py:49
  119.9 1.2 pad_maximum_fusion.2
  121.1 0.0 all-gather.2.cloned.1.call-update
  121.1 61.6 %all-gather.2.cloned.1.call-done = bf16[1024,5376]{1,0:T(8,128)(2,1)} async-done(((bf16[128,5376]{1,0:T(8,128)(2,1)}), bf16[1024,5376]{1,0:T(8,128)(2,1)}) %all-gather.2.cloned.1.call-update) | async-done | bytes 11010064 | tf_op jit(solution)/shard_map/all_gather | solution.py:52
  182.7 0.0 slice-start
  182.7 0.0 slice-start.1
  182.7 6.6 %fusion.9 = (bf16[1024,1792]{1,0:T(8,128)(2,1)}, bf16[1024,1792]{1,0:T(8,128)(2,1)S(1)}, bf16[1024,1792]{1,0:T(8,128)(2,1)S(1)}) fusion(bf16[1024,5376]{1,0:T(8,128)(2,1)} %all-gather.2.cloned.1.call-done), kind=kLoop, calls=%fused_computation.27 | loop fusion | bytes 22020096 | tf_op jit(solution)/shard_map/slice | solution.py:58
  189.3 0.0 slice-start.2
  189.3 0.1 constant_dynamic-slice_fusion
  189.4 0.2 constant_dynamic-slice_fusion.1
  189.6 0.0 copy-start.7
  189.6 2.1 pad_maximum_fusion.1
  191.7 0.0 slice-done
  191.7 0.0 slice-done.1
  191.7 1.2 slice-done.2
  193.0 1.1 copy-done.7
  194.1 0.0 copy-start.9
  194.1 4.0 %fusion.6 = f32[1024,1024]{1,0:T(8,128)S(1)} fusion(bf16[1024,1792]{1,0:T(8,128)(2,1)S(1)} %copy-done.7, bf16[1024,5376]{1,0:T(8,128)(2,1)S(1)} %bitcast.18), kind=kOutput, calls=%fused_computation.24 | convolution fusion | flops 3758096384 | bytes 11534336 | tf_op jit(solution)/shard_map/dot_general | solution.py:61
  198.0 0.0 copy-done.9
  198.1 5.3 %add_convert_fusion = bf16[1024,1024]{1,0:T(8,128)(2,1)} fusion(f32[1024,1024]{1,0:T(8,128)S(1)} %fusion.6, bf16[1024,1792]{1,0:T(8,128)(2,1)S(1)} %copy-done.9, bf16[1024,5376]{1,0:T(8,128)(2,1)S(1)} %bitcast.18), kind=kOutput, calls=%fused_computation.3 | convolution fusion | flops 3760193536 | bytes 13631488 | tf_op jit(solution)/shard_map/dot_general | solution.py:60
  203.3 5.7 %all-to-all-start.2 = ((bf16[8,128,1024]{2,1,0:T(8,128)(2,1)}), bf16[8,128,1024]{2,1,0:T(8,128)(2,1)S(1)}, u32[]{:S(2)}, u32[]{:S(2)}) async-start(bf16[8,128,1024]{2,1,0:T(8,128)(2,1)} %bitcast.23), calls=%async_computation.3 | async-start | bytes 4194304 | tf_op jit(solution)/shard_map/all_to_all | solution.py:70
  209.1 0.0 copy-start
  209.1 0.0 copy-start.2
  209.1 6.8 %convolution_convert_fusion = bf16[1024,1792]{0,1:T(8,128)(2,1)S(1)} fusion(bf16[1024,1024]{1,0:T(8,128)(2,1)} %bitcast.22, bf16[1024,1792]{1,0:T(8,128)(2,1)} %get-tuple-element.13), kind=kOutput, calls=%fused_computation.4 | convolution fusion | flops 3759931392 | bytes 9437184 | tf_op jit(solution)/shard_map/dot_general | solution.py:74
  215.9 0.0 copy-done
  215.9 0.0 copy-done.2
  215.9 4.4 %fusion = bf16[1024,1792]{0,1:T(8,128)(2,1)S(1)} fusion(bf16[1024,1792]{0,1:T(8,128)(2,1)S(1)} %convolution_convert_fusion, bf16[1024,1792]{1,0:T(8,128)(2,1)S(1)} %copy-done, bf16[1024,1024]{1,0:T(8,128)(2,1)S(1)} %bitcast.21), kind=kOutput, calls=%fused_computation.2 | convolution fusion | flops 3767271424 | bytes 13107200 | tf_op jit(solution)/shard_map/dot_general | solution.py:74
  220.3 2.2 fusion.10
  222.6 3.8 %copy.10 = bf16[1024,896]{1,0:T(8,128)(2,1)} copy(bf16[1024,896]{0,1:T(8,128)(2,1)} %get-tuple-element.21) | data formatting | bytes 3670016
  226.4 3.8 %copy.9 = bf16[1024,896]{1,0:T(8,128)(2,1)} copy(bf16[1024,896]{0,1:T(8,128)(2,1)} %get-tuple-element.22) | data formatting | bytes 3670016
  230.2 8.5 %all-to-all-done.2 = bf16[8,128,1024]{2,1,0:T(8,128)(2,1)S(1)} async-done(((bf16[8,128,1024]{2,1,0:T(8,128)(2,1)}), bf16[8,128,1024]{2,1,0:T(8,128)(2,1)S(1)}, u32[]{:S(2)}, u32[]{:S(2)}) %all-to-all-start.2) | async-done | bytes 2097184 | tf_op jit(solution)/shard_map/all_to_all | solution.py:70
  238.7 1.1 reduce_sum.12
  (3 shorter events, 0.1 us)
Async XLA Ops:
  7.2 96.8 %reduce-scatter.2.cloned.1.call-start = ((), (), s32[]{:S(2)}) async-start(), calls=%async_computation.4 | async-start | bytes 8257536 | tf_op jit(solution)/shard_map/reduce_scatter | solution.py:29
  7.2 32.0 %copy-start.6 = (bf16[1024,1792]{1,0:T(8,128)(2,1)S(1)}, bf16[1024,1792]{1,0:T(8,128)(2,1)}, u32[]{:S(2)}) copy-start(bf16[1024,1792]{1,0:T(8,128)(2,1)} %param.6) | copy-start | bytes 11010052
  39.2 4.2 %copy-start.1 = (bf16[8,128,1024]{2,1,0:T(8,128)(2,1)}, bf16[8,128,1024]{2,1,0:T(8,128)(2,1)S(1)}, u32[]{:S(2)}) copy-start(bf16[8,128,1024]{2,1,0:T(8,128)(2,1)S(1)} %all_to_all.23) | copy-start | bytes 6291460
  39.2 4.2 %copy-start.8 = (bf16[1024,1792]{1,0:T(8,128)(2,1)S(1)}, bf16[1024,1792]{1,0:T(8,128)(2,1)}, u32[]{:S(2)}) copy-start(bf16[1024,1792]{1,0:T(8,128)(2,1)} %param.5) | copy-start | bytes 11010052
  54.4 0.9 copy-start.5
  55.3 8.1 %collective-permute-start = (bf16[128,1024]{1,0:T(8,128)(2,1)S(1)}, bf16[128,1024]{1,0:T(8,128)(2,1)S(1)}, u32[]{:S(2)}, u32[]{:S(2)}) collective-permute-start(bf16[128,1024]{1,0:T(8,128)(2,1)S(1)} %copy-done.5), channel_id=1, source_target_pairs={{0,1},{1,0},{2,3},{3,2},{4,5},{5,4},{6,7},{7,6},{8,9},{9,8},{10,11... | collective-permute-start | bytes 786440 | tf_op jit(solution)/shard_map/ppermute | solution.py:25
  65.1 40.3 %copy-start.4 = (bf16[128,1792]{1,0:T(8,128)(2,1)S(1)}, bf16[128,1792]{1,0:T(8,128)(2,1)}, u32[]{:S(2)}) copy-start(bf16[128,1792]{1,0:T(8,128)(2,1)} %param.7) | copy-start | bytes 1376260
  65.1 28.5 %all-to-all-start.1 = ((bf16[8,128,1024]{2,1,0:T(8,128)(2,1)}), bf16[8,128,1024]{2,1,0:T(8,128)(2,1)S(1)}, u32[]{:S(2)}, u32[]{:S(2)}) async-start(bf16[8,128,1024]{2,1,0:T(8,128)(2,1)} %tile.5), calls=%async_computation.2 | async-start | bytes 4194304 | tf_op jit(solution)/shard_map/all_to_all | solution.py:23
  71.0 111.7 %all-gather.2.cloned.1.call-start = ((), (), s32[]{:S(2)}) async-start(), calls=%async_computation.5 | async-start | bytes 12386304 | tf_op jit(solution)/shard_map/all_gather | solution.py:52
  93.6 13.1 %copy-start.3 = (bf16[8,128,1024]{2,1,0:T(8,128)(2,1)}, bf16[8,128,1024]{2,1,0:T(8,128)(2,1)S(1)}, u32[]{:S(2)}) copy-start(bf16[8,128,1024]{2,1,0:T(8,128)(2,1)S(1)} %all-to-all-done.1) | copy-start | bytes 6291460
  106.8 13.1 %collective-permute-start.1 = (bf16[128,1792]{1,0:T(8,128)(2,1)S(1)}, bf16[128,1792]{1,0:T(8,128)(2,1)S(1)}, u32[]{:S(2)}, u32[]{:S(2)}) collective-permute-start(bf16[128,1792]{1,0:T(8,128)(2,1)S(1)} %pad_maximum_fusion.3), channel_id=1, source_target_pairs={{0,1},{1,0},{2,3},{3,2},{4,5},{5,4},{6,7},{7,6},{8,9},{9,8},{10,11... | collective-permute-start | bytes 1376264 | tf_op jit(solution)/shard_map/ppermute | solution.py:49
  182.7 9.0 %slice-start = ((s8[11010048]{0:T(1024)(128)(4,1)}), s8[4194304]{0:T(1024)(128)(4,1)S(1)}, s32[]{:S(2)}) async-start(s8[11010048]{0:T(1024)(128)(4,1)} %bitcast.17), calls=%async_computation.6 | async-start | bytes 8388608
  182.7 9.0 %slice-start.1 = ((s8[11010048]{0:T(1024)(128)(4,1)}), s8[4194304]{0:T(1024)(128)(4,1)S(1)}, s32[]{:S(2)}) async-start(s8[11010048]{0:T(1024)(128)(4,1)} %bitcast.17), calls=%async_computation.7 | async-start | bytes 8388608
  189.3 3.7 %slice-start.2 = ((s8[11010048]{0:T(1024)(128)(4,1)}), s8[2621440]{0:T(1024)(128)(4,1)S(1)}, s32[]{:S(2)}) async-start(s8[11010048]{0:T(1024)(128)(4,1)} %bitcast.17), calls=%async_computation.8 | async-start | bytes 5242880
  189.6 4.5 %copy-start.7 = (bf16[1024,1792]{1,0:T(8,128)(2,1)S(1)}, bf16[1024,1792]{1,0:T(8,128)(2,1)}, u32[]{:S(2)}) copy-start(bf16[1024,1792]{1,0:T(8,128)(2,1)} %param.6) | copy-start | bytes 11010052
  194.1 4.0 %copy-start.9 = (bf16[1024,1792]{1,0:T(8,128)(2,1)S(1)}, bf16[1024,1792]{1,0:T(8,128)(2,1)}, u32[]{:S(2)}) copy-start(bf16[1024,1792]{1,0:T(8,128)(2,1)} %param.5) | copy-start | bytes 11010052
  203.3 35.4 %all-to-all-start.2 = ((bf16[8,128,1024]{2,1,0:T(8,128)(2,1)}), bf16[8,128,1024]{2,1,0:T(8,128)(2,1)S(1)}, u32[]{:S(2)}, u32[]{:S(2)}) async-start(bf16[8,128,1024]{2,1,0:T(8,128)(2,1)} %bitcast.23), calls=%async_computation.3 | async-start | bytes 4194304 | tf_op jit(solution)/shard_map/all_to_all | solution.py:70
  209.1 6.8 %copy-start = (bf16[1024,1792]{1,0:T(8,128)(2,1)S(1)}, bf16[1024,1792]{1,0:T(8,128)(2,1)}, u32[]{:S(2)}) copy-start(bf16[1024,1792]{1,0:T(8,128)(2,1)} %pad_maximum_fusion.1) | copy-start | bytes 11010052
  209.1 6.8 %copy-start.2 = (bf16[8,128,1024]{2,1,0:T(8,128)(2,1)S(1)}, bf16[8,128,1024]{2,1,0:T(8,128)(2,1)}, u32[]{:S(2)}) copy-start(bf16[8,128,1024]{2,1,0:T(8,128)(2,1)} %copy-done.1) | copy-start | bytes 6291460
Sparse Core Ops, SparseCore 0:
  54.5 49.4 reduce-scatter.1
  121.2 61.4 all-gather.1

commit v8 on v7

--- a/solution.py
+++ b/solution.py
@@ -50,12 +50,9 @@
         jnp.concatenate([gate_other, up_other], axis=1), "dep", pair
     )
     full = lax.all_gather(
-        jnp.concatenate([grad_gate, grad_up, partner_grads], axis=1),
-        "row", axis=0, tiled=True,
+        jnp.stack([grad_gate, grad_up, partner_grads]), "row", axis=1, tiled=True
     )
-    full_gate = full[:, :width]
-    full_up = full[:, width:2 * width]
-    full_partner = full[:, 2 * width:]
+    full_gate, full_up, full_partner = full[0], full[1], full[2]
 
     term = lax.dot_general(full_gate, gate_weight, transposed, preferred_element_type=jnp.float32)
     term = term + lax.dot_general(full_up, up_weight, transposed, preferred_element_type=jnp.float32)

time: 247 us -> 247 us (level)
    slice x1 -> x0, local copies, waits for them, and re-layouts: 6.55 us -> none  [on_device(): full_partner = full[:, 2 * width:]]
    squeeze x0 -> x1, local copies, waits for them, and re-layouts: none -> 6.12 us  [on_device(): full_gate, full_up, full_partner = (full[0], full[1], full[2])]
where the time goes in v8:
time: 247 us
  waiting for transfers between devices  118 us (48%)
  blocking collectives  30.7 us (12%)
  matrix products  30 us (12%)
  local copies, waits for them, and re-layouts  22.9 us (9%)
  starting transfers between devices  17.7 us (7%)
  between operations  14.2 us (6%)
  other arithmetic  12.7 us (5%)
    all_gather x1, waiting for transfers between devices, on_device(): lax.all_gather(jnp.stack([grad_gate, grad_up, partner_grads]), 'row', axi...  61.6 us
    all_to_all x1, blocking collectives, gather_col(): return lax.all_to_all(jnp.tile(block, (n_col, 1)), 'col', 0, 0, tiled=True)  30.7 us
    all_to_all x1, waiting for transfers between devices, gather_col(): return lax.all_to_all(jnp.tile(block, (n_col, 1)), 'col', 0, 0, tiled=True)  22.6 us
    dot_general x2, matrix products, weight_part(): lax.dot_general(rows, grads, contract, preferred_element_type=jnp.float32)  11.2 us
    unnamed x28, local copies, waits for them, and re-layouts  11.2 us
    reduce_scatter x1, waiting for transfers between devices, on_device(): lax.psum_scatter(jnp.concatenate([first, second], axis=1).astype(jnp.bflo...  10.4 us
    ppermute x1, waiting for transfers between devices, on_device(): lax.ppermute(jnp.concatenate([gate_other, up_other], axis=1), 'dep', pair)  10.1 us
    all_to_all x1, waiting for transfers between devices, on_device(): parts = lax.all_to_all(term, 'col', 0, 0, tiled=True)  8.55 us
  transfers between devices with their start and end apart: 6, of which 6 were waited for; matrix products, arithmetic and copies ran while one was open for 9% of the time, Pallas kernels for 0%

profile of v8, /device:TPU:6, one launch (start us, length us, event | category | flops | bytes accessed | tf_op | source)
XLA Modules:
  0.0 246.6 jit_solution(11426415517972651306)
XLA Ops:
  7.2 0.0 reduce-scatter.2.cloned.1.call-start
  7.2 0.0 copy-start.6
  7.2 1.4 tile.4
  8.6 30.7 %all_to_all.23 = bf16[8,128,1024]{2,1,0:T(8,128)(2,1)S(1)} all-to-all(bf16[8,128,1024]{2,1,0:T(8,128)(2,1)S(1)} %tile.4), channel_id=1, replica_groups=mesh['row'=8,'col'=8,'dep'=2] {'col'}, dimensions={0} | all-to-all | bytes 4194304 | tf_op jit(solution)/shard_map/all_to_all | solution.py:23
  39.2 0.0 copy-start.1
  39.2 0.0 copy-done.6
  39.2 0.0 copy-start.8
  39.2 4.1 %convolution_convert_fusion.2 = bf16[1024,1792]{1,0:T(8,128)(2,1)S(1)} fusion(bf16[1024,1024]{1,0:T(8,128)(2,1)S(1)} %bitcast.38, bf16[1024,1792]{1,0:T(8,128)(2,1)S(1)} %copy-done.6), kind=kOutput, calls=%fused_computation.6 | convolution fusion | flops 3759931392 | bytes 9437184 | tf_op jit(solution)/shard_map/dot_general | solution.py:28
  43.4 0.0 copy-done.1
  43.4 0.0 copy-done.8
  43.4 5.4 %convolution_convert_fusion.3 = bf16[1024,1792]{1,0:T(8,128)(2,1)} fusion(bf16[1024,1024]{1,0:T(8,128)(2,1)S(1)} %bitcast.39, bf16[1024,1792]{1,0:T(8,128)(2,1)S(1)} %copy-done.8), kind=kOutput, calls=%fused_computation.7 | convolution fusion | flops 3759931392 | bytes 9437184 | tf_op jit(solution)/shard_map/dot_general | solution.py:27
  48.8 5.6 %pad_maximum_fusion = bf16[1024,3584]{1,0:T(8,128)(2,1)} fusion(bf16[1024,1792]{1,0:T(8,128)(2,1)S(1)} %convolution_convert_fusion.2, bf16[1024,1792]{1,0:T(8,128)(2,1)} %convolution_convert_fusion.3), kind=kLoop, calls=%fused_computation | loop fusion | flops 14680064 | bytes 14680064 | tf_op jit(solution)/shard_map/concatenate | solution.py:30
  54.4 0.0 copy-start.5
  54.4 0.0 reduce-scatter.2.cloned.1.call-update
  54.4 0.9 copy-done.5
  55.3 2.9 %collective-permute-start = (bf16[128,1024]{1,0:T(8,128)(2,1)S(1)}, bf16[128,1024]{1,0:T(8,128)(2,1)S(1)}, u32[]{:S(2)}, u32[]{:S(2)}) collective-permute-start(bf16[128,1024]{1,0:T(8,128)(2,1)S(1)} %copy-done.5), channel_id=1, source_target_pairs={{0,1},{1,0},{2,3},{3,2},{4,5},{5,4},{6,7},{7,6},{8,9},{9,8},{10,11... | collective-permute-start | bytes 786440 | tf_op jit(solution)/shard_map/ppermute | solution.py:25
  58.2 5.2 %collective-permute-done = bf16[128,1024]{1,0:T(8,128)(2,1)S(1)} collective-permute-done((bf16[128,1024]{1,0:T(8,128)(2,1)S(1)}, bf16[128,1024]{1,0:T(8,128)(2,1)S(1)}, u32[]{:S(2)}, u32[]{:S(2)}) %collective-permute-start) | collective-permute-done | bytes 262176 | tf_op jit(solution)/shard_map/ppermute | solution.py:25
  63.4 1.7 tile.5
  65.1 0.0 copy-start.4
  65.1 5.9 %all-to-all-start.1 = ((bf16[8,128,1024]{2,1,0:T(8,128)(2,1)}), bf16[8,128,1024]{2,1,0:T(8,128)(2,1)S(1)}, u32[]{:S(2)}, u32[]{:S(2)}) async-start(bf16[8,128,1024]{2,1,0:T(8,128)(2,1)} %tile.5), calls=%async_computation.2 | async-start | bytes 4194304 | tf_op jit(solution)/shard_map/all_to_all | solution.py:23
  71.0 0.0 all-gather.2.cloned.1.call-start
  71.0 22.6 %all-to-all-done.1 = bf16[8,128,1024]{2,1,0:T(8,128)(2,1)S(1)} async-done(((bf16[8,128,1024]{2,1,0:T(8,128)(2,1)}), bf16[8,128,1024]{2,1,0:T(8,128)(2,1)S(1)}, u32[]{:S(2)}, u32[]{:S(2)}) %all-to-all-start.1) | async-done | bytes 2097184 | tf_op jit(solution)/shard_map/all_to_all | solution.py:23
  93.6 0.0 copy-start.3
  93.6 10.4 %reduce-scatter.2.cloned.1.call-done = bf16[128,3584]{1,0:T(8,128)(2,1)} async-done(((bf16[1024,3584]{1,0:T(8,128)(2,1)}), bf16[128,3584]{1,0:T(8,128)(2,1)}) %reduce-scatter.2.cloned.1.call-update) | async-done | bytes 917520 | tf_op jit(solution)/shard_map/reduce_scatter | solution.py:29
  104.0 1.4 convert_element_type.40
  105.3 0.0 copy-done.4
  105.4 1.3 fusion.9
  106.7 0.0 copy-done.3
  106.8 3.1 %collective-permute-start.1 = (bf16[128,1792]{1,0:T(8,128)(2,1)S(1)}, bf16[128,1792]{1,0:T(8,128)(2,1)S(1)}, u32[]{:S(2)}, u32[]{:S(2)}) collective-permute-start(bf16[128,1792]{1,0:T(8,128)(2,1)S(1)} %pad_maximum_fusion.3), channel_id=1, source_target_pairs={{0,1},{1,0},{2,3},{3,2},{4,5},{5,4},{6,7},{7,6},{8,9},{9,8},{10,11... | collective-permute-start | bytes 1376264 | tf_op jit(solution)/shard_map/ppermute | solution.py:49
  109.9 10.1 %collective-permute-done.1 = bf16[128,1792]{1,0:T(8,128)(2,1)S(1)} collective-permute-done((bf16[128,1792]{1,0:T(8,128)(2,1)S(1)}, bf16[128,1792]{1,0:T(8,128)(2,1)S(1)}, u32[]{:S(2)}, u32[]{:S(2)}) %collective-permute-start.1) | collective-permute-done | bytes 458784 | tf_op jit(solution)/shard_map/ppermute | solution.py:49
  119.9 1.2 pad_maximum_fusion.2
  121.1 0.0 all-gather.2.cloned.1.call-update
  121.2 61.6 %all-gather.2.cloned.1.call-done = bf16[3,1024,1792]{2,1,0:T(8,128)(2,1)} async-done(((bf16[3,128,1792]{2,1,0:T(8,128)(2,1)}), bf16[3,1024,1792]{2,1,0:T(8,128)(2,1)}) %all-gather.2.cloned.1.call-update) | async-done | bytes 11010064 | tf_op jit(solution)/shard_map/all_gather | solution.py:52
  182.8 0.0 slice-start
  182.8 0.0 slice-start.1
  182.8 6.1 %slice_bitcast_fusion = (bf16[1024,1792]{1,0:T(8,128)(2,1)}, bf16[1,1024,1792]{2,1,0:T(8,128)(2,1)S(1)}, bf16[1,1024,1792]{2,1,0:T(8,128)(2,1)S(1)}) fusion(bf16[3,1024,1792]{2,1,0:T(8,128)(2,1)} %all-gather.2.cloned.1.call-done), kind=kLoop, calls=%fused_computation.8 | loop fusion | bytes 22020096 | tf_op jit(solution)/shard_map/squeeze | solution.py:55
  188.9 0.0 slice-start.2
  188.9 0.1 dynamic-slice_bitcast_fusion
  189.0 0.2 dynamic-slice_bitcast_fusion.1
  189.2 0.0 copy-start.7
  189.2 2.1 pad_maximum_fusion.1
  191.3 0.0 slice-done
  191.3 0.1 slice-done.1
  191.4 1.5 slice-done.2
  192.9 1.1 copy-done.7
  194.0 0.0 copy-start.9
  194.0 4.0 %fusion.1 = f32[1024,1024]{1,0:T(8,128)S(1)} fusion(bf16[1024,1792]{1,0:T(8,128)(2,1)S(1)} %copy-done.7, bf16[3,1024,1792]{2,1,0:T(8,128)(2,1)S(1)} %bitcast.35), kind=kOutput, calls=%fused_computation.10 | convolution fusion | flops 3758096384 | bytes 11534336 | tf_op jit(solution)/shard_map/dot_general | solution.py:58
  198.0 0.0 copy-done.9
  198.0 5.3 %add_convert_fusion = bf16[1024,1024]{1,0:T(8,128)(2,1)} fusion(f32[1024,1024]{1,0:T(8,128)S(1)} %fusion.1, bf16[1024,1792]{1,0:T(8,128)(2,1)S(1)} %copy-done.9, bf16[3,1024,1792]{2,1,0:T(8,128)(2,1)S(1)} %bitcast.35), kind=kOutput, calls=%fused_computation.3 | convolution fusion | flops 3760193536 | bytes 13631488 | tf_op jit(solution)/shard_map/dot_general | solution.py:57
  203.3 5.7 %all-to-all-start.2 = ((bf16[8,128,1024]{2,1,0:T(8,128)(2,1)}), bf16[8,128,1024]{2,1,0:T(8,128)(2,1)S(1)}, u32[]{:S(2)}, u32[]{:S(2)}) async-start(bf16[8,128,1024]{2,1,0:T(8,128)(2,1)} %bitcast.42), calls=%async_computation.3 | async-start | bytes 4194304 | tf_op jit(solution)/shard_map/all_to_all | solution.py:67
  209.0 0.0 copy-start
  209.0 0.0 copy-start.2
  209.0 6.8 %convolution_convert_fusion = bf16[1024,1792]{0,1:T(8,128)(2,1)S(1)} fusion(bf16[1024,1024]{1,0:T(8,128)(2,1)} %bitcast.41, bf16[1024,1792]{1,0:T(8,128)(2,1)} %get-tuple-element.13), kind=kOutput, calls=%fused_computation.4 | convolution fusion | flops 3759931392 | bytes 9437184 | tf_op jit(solution)/shard_map/dot_general | solution.py:71
  215.8 0.0 copy-done
  215.8 0.0 copy-done.2
  215.9 4.4 %fusion = bf16[1024,1792]{0,1:T(8,128)(2,1)S(1)} fusion(bf16[1024,1792]{0,1:T(8,128)(2,1)S(1)} %convolution_convert_fusion, bf16[1024,1792]{1,0:T(8,128)(2,1)S(1)} %copy-done, bf16[1024,1024]{1,0:T(8,128)(2,1)S(1)} %bitcast.40), kind=kOutput, calls=%fused_computation.2 | convolution fusion | flops 3767271424 | bytes 13107200 | tf_op jit(solution)/shard_map/dot_general | solution.py:71
  220.3 2.2 fusion.14
  222.5 3.8 %copy.10 = bf16[1024,896]{1,0:T(8,128)(2,1)} copy(bf16[1024,896]{0,1:T(8,128)(2,1)} %get-tuple-element.21) | data formatting | bytes 3670016
  226.3 3.8 %copy.9 = bf16[1024,896]{1,0:T(8,128)(2,1)} copy(bf16[1024,896]{0,1:T(8,128)(2,1)} %get-tuple-element.22) | data formatting | bytes 3670016
  230.1 8.5 %all-to-all-done.2 = bf16[8,128,1024]{2,1,0:T(8,128)(2,1)S(1)} async-done(((bf16[8,128,1024]{2,1,0:T(8,128)(2,1)}), bf16[8,128,1024]{2,1,0:T(8,128)(2,1)S(1)}, u32[]{:S(2)}, u32[]{:S(2)}) %all-to-all-start.2) | async-done | bytes 2097184 | tf_op jit(solution)/shard_map/all_to_all | solution.py:67
  238.7 1.1 reduce_sum.12
  (3 shorter events, 0.1 us)
Async XLA Ops:
  7.2 96.8 %reduce-scatter.2.cloned.1.call-start = ((), (), s32[]{:S(2)}) async-start(), calls=%async_computation.4 | async-start | bytes 8257536 | tf_op jit(solution)/shard_map/reduce_scatter | solution.py:29
  7.2 32.0 %copy-start.6 = (bf16[1024,1792]{1,0:T(8,128)(2,1)S(1)}, bf16[1024,1792]{1,0:T(8,128)(2,1)}, u32[]{:S(2)}) copy-start(bf16[1024,1792]{1,0:T(8,128)(2,1)} %param.6) | copy-start | bytes 11010052
  39.2 4.2 %copy-start.1 = (bf16[8,128,1024]{2,1,0:T(8,128)(2,1)}, bf16[8,128,1024]{2,1,0:T(8,128)(2,1)S(1)}, u32[]{:S(2)}) copy-start(bf16[8,128,1024]{2,1,0:T(8,128)(2,1)S(1)} %all_to_all.23) | copy-start | bytes 6291460
  39.2 4.2 %copy-start.8 = (bf16[1024,1792]{1,0:T(8,128)(2,1)S(1)}, bf16[1024,1792]{1,0:T(8,128)(2,1)}, u32[]{:S(2)}) copy-start(bf16[1024,1792]{1,0:T(8,128)(2,1)} %param.5) | copy-start | bytes 11010052
  54.4 0.9 copy-start.5
  55.3 8.1 %collective-permute-start = (bf16[128,1024]{1,0:T(8,128)(2,1)S(1)}, bf16[128,1024]{1,0:T(8,128)(2,1)S(1)}, u32[]{:S(2)}, u32[]{:S(2)}) collective-permute-start(bf16[128,1024]{1,0:T(8,128)(2,1)S(1)} %copy-done.5), channel_id=1, source_target_pairs={{0,1},{1,0},{2,3},{3,2},{4,5},{5,4},{6,7},{7,6},{8,9},{9,8},{10,11... | collective-permute-start | bytes 786440 | tf_op jit(solution)/shard_map/ppermute | solution.py:25
  65.1 40.3 %copy-start.4 = (bf16[128,1792]{1,0:T(8,128)(2,1)S(1)}, bf16[128,1792]{1,0:T(8,128)(2,1)}, u32[]{:S(2)}) copy-start(bf16[128,1792]{1,0:T(8,128)(2,1)} %param.7) | copy-start | bytes 1376260
  65.1 28.5 %all-to-all-start.1 = ((bf16[8,128,1024]{2,1,0:T(8,128)(2,1)}), bf16[8,128,1024]{2,1,0:T(8,128)(2,1)S(1)}, u32[]{:S(2)}, u32[]{:S(2)}) async-start(bf16[8,128,1024]{2,1,0:T(8,128)(2,1)} %tile.5), calls=%async_computation.2 | async-start | bytes 4194304 | tf_op jit(solution)/shard_map/all_to_all | solution.py:23
  71.0 111.8 %all-gather.2.cloned.1.call-start = ((), (), s32[]{:S(2)}) async-start(), calls=%async_computation.5 | async-start | bytes 12386304 | tf_op jit(solution)/shard_map/all_gather | solution.py:52
  93.6 13.1 %copy-start.3 = (bf16[8,128,1024]{2,1,0:T(8,128)(2,1)}, bf16[8,128,1024]{2,1,0:T(8,128)(2,1)S(1)}, u32[]{:S(2)}) copy-start(bf16[8,128,1024]{2,1,0:T(8,128)(2,1)S(1)} %all-to-all-done.1) | copy-start | bytes 6291460
  106.8 13.1 %collective-permute-start.1 = (bf16[128,1792]{1,0:T(8,128)(2,1)S(1)}, bf16[128,1792]{1,0:T(8,128)(2,1)S(1)}, u32[]{:S(2)}, u32[]{:S(2)}) collective-permute-start(bf16[128,1792]{1,0:T(8,128)(2,1)S(1)} %pad_maximum_fusion.3), channel_id=1, source_target_pairs={{0,1},{1,0},{2,3},{3,2},{4,5},{5,4},{6,7},{7,6},{8,9},{9,8},{10,11... | collective-permute-start | bytes 1376264 | tf_op jit(solution)/shard_map/ppermute | solution.py:49
  182.8 8.6 %slice-start = ((s8[11010048]{0:T(1024)(128)(4,1)}), s8[4194304]{0:T(1024)(128)(4,1)S(1)}, s32[]{:S(2)}) async-start(s8[11010048]{0:T(1024)(128)(4,1)} %bitcast.34), calls=%async_computation.6 | async-start | bytes 8388608
  182.8 8.6 %slice-start.1 = ((s8[11010048]{0:T(1024)(128)(4,1)}), s8[4194304]{0:T(1024)(128)(4,1)S(1)}, s32[]{:S(2)}) async-start(s8[11010048]{0:T(1024)(128)(4,1)} %bitcast.34), calls=%async_computation.7 | async-start | bytes 8388608
  188.9 4.0 %slice-start.2 = ((s8[11010048]{0:T(1024)(128)(4,1)}), s8[2621440]{0:T(1024)(128)(4,1)S(1)}, s32[]{:S(2)}) async-start(s8[11010048]{0:T(1024)(128)(4,1)} %bitcast.34), calls=%async_computation.8 | async-start | bytes 5242880
  189.2 4.8 %copy-start.7 = (bf16[1024,1792]{1,0:T(8,128)(2,1)S(1)}, bf16[1024,1792]{1,0:T(8,128)(2,1)}, u32[]{:S(2)}) copy-start(bf16[1024,1792]{1,0:T(8,128)(2,1)} %param.6) | copy-start | bytes 11010052
  194.0 4.0 %copy-start.9 = (bf16[1024,1792]{1,0:T(8,128)(2,1)S(1)}, bf16[1024,1792]{1,0:T(8,128)(2,1)}, u32[]{:S(2)}) copy-start(bf16[1024,1792]{1,0:T(8,128)(2,1)} %param.5) | copy-start | bytes 11010052
  203.3 35.4 %all-to-all-start.2 = ((bf16[8,128,1024]{2,1,0:T(8,128)(2,1)}), bf16[8,128,1024]{2,1,0:T(8,128)(2,1)S(1)}, u32[]{:S(2)}, u32[]{:S(2)}) async-start(bf16[8,128,1024]{2,1,0:T(8,128)(2,1)} %bitcast.42), calls=%async_computation.3 | async-start | bytes 4194304 | tf_op jit(solution)/shard_map/all_to_all | solution.py:67
  209.0 6.8 %copy-start = (bf16[1024,1792]{1,0:T(8,128)(2,1)S(1)}, bf16[1024,1792]{1,0:T(8,128)(2,1)}, u32[]{:S(2)}) copy-start(bf16[1024,1792]{1,0:T(8,128)(2,1)} %pad_maximum_fusion.1) | copy-start | bytes 11010052
  209.0 6.8 %copy-start.2 = (bf16[8,128,1024]{2,1,0:T(8,128)(2,1)S(1)}, bf16[8,128,1024]{2,1,0:T(8,128)(2,1)}, u32[]{:S(2)}) copy-start(bf16[8,128,1024]{2,1,0:T(8,128)(2,1)} %copy-done.1) | copy-start | bytes 6291460
Sparse Core Ops, SparseCore 0:
  54.5 49.4 reduce-scatter.1
  121.3 61.4 all-gather.1

commit v9 on v8

--- a/solution.py
+++ b/solution.py
@@ -46,37 +46,38 @@
 
     gate_own, gate_other = halves(grad_gate, dep, half)
     up_own, up_other = halves(grad_up, dep, half)
-    partner_grads = lax.ppermute(
-        jnp.concatenate([gate_other, up_other], axis=1), "dep", pair
+    partner_gate, partner_up = jnp.split(
+        lax.ppermute(jnp.concatenate([gate_other, up_other], axis=1), "dep", pair), 2, axis=1
     )
     full = lax.all_gather(
-        jnp.stack([grad_gate, grad_up, partner_grads]), "row", axis=1, tiled=True
+        jnp.stack([gate_own, up_own, gate_other, up_other, partner_gate, partner_up]),
+        "row", axis=1, tiled=True,
     )
-    full_gate, full_up, full_partner = full[0], full[1], full[2]
 
-    term = lax.dot_general(full_gate, gate_weight, transposed, preferred_element_type=jnp.float32)
-    term = term + lax.dot_general(full_up, up_weight, transposed, preferred_element_type=jnp.float32)
+    wg_own, wg_other = halves(gate_weight, dep, half)
+    wu_own, wu_other = halves(up_weight, dep, half)
+    term = lax.dot_general(full[0], wg_own, transposed, preferred_element_type=jnp.float32)
+    term = term + lax.dot_general(full[2], wg_other, transposed, preferred_element_type=jnp.float32)
+    term = term + lax.dot_general(full[1], wu_own, transposed, preferred_element_type=jnp.float32)
+    term = term + lax.dot_general(full[3], wu_other, transposed, preferred_element_type=jnp.float32)
     term = term.astype(jnp.bfloat16).reshape(n_col, -1, term.shape[1])
-
-    own_cols = jnp.concatenate(
-        [lax.dynamic_slice_in_dim(full_gate, dep * half, half, axis=1),
-         lax.dynamic_slice_in_dim(full_up, dep * half, half, axis=1)],
-        axis=1,
-    )
-    own_cols, full_partner, term = lax.optimization_barrier((own_cols, full_partner, term))
+    term, gathered, gathered_partner = lax.optimization_barrier((term, gathered, gathered_partner))
     parts = lax.all_to_all(term, "col", 0, 0, tiled=True)
     grad_tokens = parts.astype(jnp.float32).sum(axis=0).astype(jnp.bfloat16)
 
-    def weight_part(grads, rows):
-        return lax.dot_general(rows, grads, contract, preferred_element_type=jnp.float32)
+    def weight_grad(own, partner):
+        mine = lax.dot_general(gathered, own, contract, preferred_element_type=jnp.float32)
+        theirs = lax.dot_general(
+            gathered_partner, partner, contract, preferred_element_type=jnp.float32
+        )
+        return (
+            mine.astype(jnp.bfloat16).astype(jnp.float32)
+            + theirs.astype(jnp.bfloat16).astype(jnp.float32)
+        ).astype(jnp.bfloat16)
 
-    mine = weight_part(own_cols, gathered)
-    theirs = weight_part(full_partner, gathered_partner)
-    total = (
-        mine.astype(jnp.bfloat16).astype(jnp.float32)
-        + theirs.astype(jnp.bfloat16).astype(jnp.float32)
-    ).astype(jnp.bfloat16)
-    return (hidden, grad_tokens, total[:, :half], total[:, half:])
+    sum_gate = weight_grad(full[0], full[4])
+    sum_up = weight_grad(full[1], full[5])
+    return (hidden, grad_tokens, sum_gate, sum_up)
 
 
 def solution(mesh):

time: 247 us -> 242 us (0.980)
  local copies, waits for them, and re-layouts: 22.9 us -> 5.79 us
  matrix products: 30 us -> 43.4 us
  other arithmetic: 12.7 us -> 9.36 us
    dot_general x4 -> x8, matrix products: 20.5 us -> 33.8 us  [the longest x2 10.4 us: weight_grad(): lax.dot_general(gathered_partner, partner, contract, preferred_element_ty...]
    unnamed x28 -> x29, local copies, waits for them, and re-layouts: 11.2 us -> 2.89 us
    squeeze x1 -> x0, local copies, waits for them, and re-layouts: 6.12 us -> none  [on_device(): full_gate, full_up, full_partner = (full[0], full[1], full[2])]
where the time goes in v9:
time: 242 us
  waiting for transfers between devices  120 us (50%)
  matrix products  43.4 us (18%)
  blocking collectives  30.9 us (13%)
  starting transfers between devices  17.5 us (7%)
  between operations  14.2 us (6%)
  other arithmetic  9.36 us (4%)
  local copies, waits for them, and re-layouts  5.79 us (2%)
    all_gather x1, waiting for transfers between devices, on_device(): lax.all_gather(jnp.stack([gate_own, up_own, gate_other, up_other, partner...  61.6 us
    all_to_all x1, blocking collectives, gather_col(): return lax.all_to_all(jnp.tile(block, (n_col, 1)), 'col', 0, 0, tiled=True)  30.9 us
    all_to_all x1, waiting for transfers between devices, gather_col(): return lax.all_to_all(jnp.tile(block, (n_col, 1)), 'col', 0, 0, tiled=True)  22.6 us
    reduce_scatter x1, waiting for transfers between devices, on_device(): lax.psum_scatter(jnp.concatenate([first, second], axis=1).astype(jnp.bflo...  10.6 us
    dot_general x2, matrix products, weight_grad(): lax.dot_general(gathered_partner, partner, contract, preferred_element_ty...  10.4 us
    all_to_all x1, waiting for transfers between devices, on_device(): parts = lax.all_to_all(term, 'col', 0, 0, tiled=True)  10.4 us
    ppermute x1, waiting for transfers between devices, on_device(): lax.ppermute(jnp.concatenate([gate_other, up_other], axis=1), 'dep', pair)  10.1 us
    dot_general x2, matrix products, weight_grad(): lax.dot_general(gathered, own, contract, preferred_element_type=jnp.float32)  8.73 us
  transfers between devices with their start and end apart: 6, of which 6 were waited for; matrix products, arithmetic and copies ran while one was open for 9% of the time, Pallas kernels for 0%

profile of v9, /device:TPU:6, one launch (start us, length us, event | category | flops | bytes accessed | tf_op | source)
XLA Modules:
  0.0 241.6 jit_solution(7133710134856563216)
XLA Ops:
  7.2 0.0 reduce-scatter.2.cloned.1.call-start
  7.2 1.2 tile.4
  8.4 0.0 copy-start.5
  8.4 30.9 %all_to_all.23 = bf16[8,128,1024]{2,1,0:T(8,128)(2,1)S(1)} all-to-all(bf16[8,128,1024]{2,1,0:T(8,128)(2,1)S(1)} %tile.4), channel_id=1, replica_groups=mesh['row'=8,'col'=8,'dep'=2] {'col'}, dimensions={0} | all-to-all | bytes 4194304 | tf_op jit(solution)/shard_map/all_to_all | solution.py:23
  39.4 0.0 copy-start
  39.4 0.0 copy-done.5
  39.4 0.0 copy-start.10
  39.4 4.2 %convolution_convert_fusion = bf16[1024,1792]{1,0:T(8,128)(2,1)S(1)} fusion(bf16[1024,1024]{1,0:T(8,128)(2,1)S(1)} %bitcast.52, bf16[1024,1792]{1,0:T(8,128)(2,1)S(1)} %copy-done.5), kind=kOutput, calls=%fused_computation.2 | convolution fusion | flops 3759931392 | bytes 9437184 | tf_op jit(solution)/shard_map/dot_general | solution.py:28
  43.5 0.0 copy-done
  43.5 0.0 copy-done.10
  43.5 5.4 %convolution_convert_fusion.1 = bf16[1024,1792]{1,0:T(8,128)(2,1)} fusion(bf16[1024,1024]{1,0:T(8,128)(2,1)S(1)} %bitcast.53, bf16[1024,1792]{1,0:T(8,128)(2,1)S(1)} %copy-done.10), kind=kOutput, calls=%fused_computation.3 | convolution fusion | flops 3759931392 | bytes 9437184 | tf_op jit(solution)/shard_map/dot_general | solution.py:27
  48.9 5.6 %pad_maximum_fusion = bf16[1024,3584]{1,0:T(8,128)(2,1)} fusion(bf16[1024,1792]{1,0:T(8,128)(2,1)S(1)} %convolution_convert_fusion, bf16[1024,1792]{1,0:T(8,128)(2,1)} %convolution_convert_fusion.1), kind=kLoop, calls=%fused_computation | loop fusion | flops 14680064 | bytes 14680064 | tf_op jit(solution)/shard_map/concatenate | solution.py:30
  54.5 0.0 copy-start.9
  54.5 0.0 reduce-scatter.2.cloned.1.call-update
  54.5 0.9 copy-done.9
  55.4 2.9 %collective-permute-start = (bf16[128,1024]{1,0:T(8,128)(2,1)S(1)}, bf16[128,1024]{1,0:T(8,128)(2,1)S(1)}, u32[]{:S(2)}, u32[]{:S(2)}) collective-permute-start(bf16[128,1024]{1,0:T(8,128)(2,1)S(1)} %copy-done.9), channel_id=1, source_target_pairs={{0,1},{1,0},{2,3},{3,2},{4,5},{5,4},{6,7},{7,6},{8,9},{9,8},{10,11... | collective-permute-start | bytes 786440 | tf_op jit(solution)/shard_map/ppermute | solution.py:25
  58.3 5.2 %collective-permute-done = bf16[128,1024]{1,0:T(8,128)(2,1)S(1)} collective-permute-done((bf16[128,1024]{1,0:T(8,128)(2,1)S(1)}, bf16[128,1024]{1,0:T(8,128)(2,1)S(1)}, u32[]{:S(2)}, u32[]{:S(2)}) %collective-permute-start) | collective-permute-done | bytes 262176 | tf_op jit(solution)/shard_map/ppermute | solution.py:25
  63.5 1.7 tile.5
  65.2 5.8 %all-to-all-start.1 = ((bf16[8,128,1024]{2,1,0:T(8,128)(2,1)}), bf16[8,128,1024]{2,1,0:T(8,128)(2,1)S(1)}, u32[]{:S(2)}, u32[]{:S(2)}) async-start(bf16[8,128,1024]{2,1,0:T(8,128)(2,1)} %tile.5), calls=%async_computation.2 | async-start | bytes 4194304 | tf_op jit(solution)/shard_map/all_to_all | solution.py:23
  71.0 0.0 copy-start.7
  71.0 0.0 all-gather.2.cloned.1.call-start
  71.0 22.6 %all-to-all-done.1 = bf16[8,128,1024]{2,1,0:T(8,128)(2,1)S(1)} async-done(((bf16[8,128,1024]{2,1,0:T(8,128)(2,1)}), bf16[8,128,1024]{2,1,0:T(8,128)(2,1)S(1)}, u32[]{:S(2)}, u32[]{:S(2)}) %all-to-all-start.1) | async-done | bytes 2097184 | tf_op jit(solution)/shard_map/all_to_all | solution.py:23
  93.6 0.0 copy-start.2
  93.6 10.6 %reduce-scatter.2.cloned.1.call-done = bf16[128,3584]{1,0:T(8,128)(2,1)} async-done(((bf16[1024,3584]{1,0:T(8,128)(2,1)}), bf16[128,3584]{1,0:T(8,128)(2,1)}) %reduce-scatter.2.cloned.1.call-update) | async-done | bytes 917520 | tf_op jit(solution)/shard_map/reduce_scatter | solution.py:29
  104.1 1.4 convert_element_type.51
  105.5 0.0 copy-done.7
  105.5 1.3 fusion.14
  106.8 0.0 copy-done.2
  106.9 0.1 bitcast_dynamic-update-slice_fusion.1
  106.9 0.1 bitcast_dynamic-update-slice_fusion
  107.0 3.1 %collective-permute-start.1 = (bf16[128,1792]{1,0:T(8,128)(2,1)S(1)}, bf16[128,1792]{1,0:T(8,128)(2,1)S(1)}, u32[]{:S(2)}, u32[]{:S(2)}) collective-permute-start(bf16[128,1792]{1,0:T(8,128)(2,1)S(1)} %pad_maximum_fusion.1), channel_id=1, source_target_pairs={{0,1},{1,0},{2,3},{3,2},{4,5},{5,4},{6,7},{7,6},{8,9},{9,8},{10,11... | collective-permute-start | bytes 1376264 | tf_op jit(solution)/shard_map/ppermute | solution.py:50
  110.1 10.1 %collective-permute-done.1 = bf16[128,1792]{1,0:T(8,128)(2,1)S(1)} collective-permute-done((bf16[128,1792]{1,0:T(8,128)(2,1)S(1)}, bf16[128,1792]{1,0:T(8,128)(2,1)S(1)}, u32[]{:S(2)}, u32[]{:S(2)}) %collective-permute-start.1) | collective-permute-done | bytes 458784 | tf_op jit(solution)/shard_map/ppermute | solution.py:50
  120.2 0.0 copy-start.4
  120.3 1.1 copy-done.4
  121.3 0.0 all-gather.2.cloned.1.call-update
  121.4 61.6 %all-gather.2.cloned.1.call-done = bf16[6,1024,896]{2,1,0:T(8,128)(2,1)} async-done(((bf16[6,128,896]{2,1,0:T(8,128)(2,1)}), bf16[6,1024,896]{2,1,0:T(8,128)(2,1)}) %all-gather.2.cloned.1.call-update) | async-done | bytes 11010064 | tf_op jit(solution)/shard_map/all_gather | solution.py:52
  183.0 0.0 copy-start.8
  183.0 4.6 %fusion.4 = f32[1024,1024]{1,0:T(8,128)S(1)} fusion(bf16[1024,1792]{1,0:T(8,128)(2,1)} %param.6, s32[]{:T(128)S(6)} %select_n.4, bf16[6,1024,896]{2,1,0:T(8,128)(2,1)} %all-gather.2.cloned.1.call-done), kind=kOutput, calls=%fused_computation.16 | convolution fusion | flops 1879048192 | bytes 7864324 | tf_op jit(solution)/shard_map/dot_general | solution.py:61
  187.5 0.7 copy-done.8
  188.2 0.0 copy-start.11
  188.2 4.0 %fusion.7 = f32[1024,1024]{1,0:T(8,128)S(1)} fusion(bf16[1024,1792]{1,0:T(8,128)(2,1)} %param.5, s32[]{:T(128)S(6)} %select_n.4, bf16[6,1024,896]{2,1,0:T(8,128)(2,1)S(1)} %copy-done.8), kind=kOutput, calls=%fused_computation.19 | convolution fusion | flops 1879048192 | bytes 7864324 | tf_op jit(solution)/shard_map/dot_general | solution.py:59
  192.2 0.0 copy-done.11
  192.2 0.0 copy-start.6
  192.2 2.4 fusion.2
  194.6 0.0 copy-done.6
  194.6 3.7 %add_convert_fusion = bf16[1024,1024]{1,0:T(8,128)(2,1)} fusion(f32[1024,1024]{1,0:T(8,128)S(1)} %fusion.4, f32[1024,1024]{1,0:T(8,128)S(1)} %fusion.7, f32[1024,1024]{1,0:T(8,128)S(1)} %fusion.2, bf16[6,1024,896]{2,1,0:T(8,128)(2,1)S(1)} %copy-done.8, bf16[1024,1792]{1,0:T(8,128)(2,1)S(1)} %copy-done.6, s32[]{:T(128)S(6)} %select_n.5), kind=kOutput, calls=%fused_computation.1 | convolution fusion | flops 1883242496 | bytes 18350084 | tf_op jit(solution)/shard_map/dot_general | solution.py:62
  198.3 5.7 %all-to-all-start.2 = ((bf16[8,128,1024]{2,1,0:T(8,128)(2,1)}), bf16[8,128,1024]{2,1,0:T(8,128)(2,1)S(1)}, u32[]{:S(2)}, u32[]{:S(2)}) async-start(bf16[8,128,1024]{2,1,0:T(8,128)(2,1)} %bitcast.51), calls=%async_computation.3 | async-start | bytes 4194304 | tf_op jit(solution)/shard_map/all_to_all | solution.py:65
  204.1 0.0 copy-start.1
  204.1 4.7 %fusion.10 = bf16[1024,896]{1,0:T(8,128)(2,1)S(1)} fusion(bf16[1024,1024]{1,0:T(8,128)(2,1)} %bitcast.54, bf16[6,1024,896]{2,1,0:T(8,128)(2,1)} %all-gather.2.cloned.1.call-done), kind=kOutput, calls=%fused_computation.22 | convolution fusion | flops 1879048192 | bytes 5767168 | tf_op jit(solution)/shard_map/dot_general | solution.py:69
  208.7 0.0 copy-done.1
  208.7 0.0 copy-start.3
  208.8 4.1 %fusion.9 = bf16[1024,896]{1,0:T(8,128)(2,1)S(1)} fusion(bf16[1024,1024]{1,0:T(8,128)(2,1)S(1)} %bitcast.55, bf16[6,1024,896]{2,1,0:T(8,128)(2,1)} %all-gather.2.cloned.1.call-done), kind=kOutput, calls=%fused_computation.21 | convolution fusion | flops 1879048192 | bytes 5767168 | tf_op jit(solution)/shard_map/dot_general | solution.py:69
  212.8 0.0 copy-done.3
  212.8 5.2 %add_convert_fusion.2 = bf16[1024,896]{1,0:T(8,128)(2,1)} fusion(bf16[1024,896]{1,0:T(8,128)(2,1)S(1)} %fusion.9, bf16[1024,1024]{1,0:T(8,128)(2,1)S(1)} %bitcast.56, bf16[6,1024,896]{2,1,0:T(8,128)(2,1)} %all-gather.2.cloned.1.call-done), kind=kOutput, calls=%fused_computation.5 | convolution fusion | flops 1883635712 | bytes 7602176 | tf_op jit(solution)/shard_map/dot_general | solution.py:70
  218.1 5.2 %add_convert_fusion.1 = bf16[1024,896]{1,0:T(8,128)(2,1)} fusion(bf16[1024,896]{1,0:T(8,128)(2,1)S(1)} %fusion.10, bf16[1024,1024]{1,0:T(8,128)(2,1)S(1)} %bitcast.57, bf16[6,1024,896]{2,1,0:T(8,128)(2,1)} %all-gather.2.cloned.1.call-done), kind=kOutput, calls=%fused_computation.4 | convolution fusion | flops 1883635712 | bytes 7602176 | tf_op jit(solution)/shard_map/dot_general | solution.py:70
  223.3 10.4 %all-to-all-done.2 = bf16[8,128,1024]{2,1,0:T(8,128)(2,1)S(1)} async-done(((bf16[8,128,1024]{2,1,0:T(8,128)(2,1)}), bf16[8,128,1024]{2,1,0:T(8,128)(2,1)S(1)}, u32[]{:S(2)}, u32[]{:S(2)}) %all-to-all-start.2) | async-done | bytes 2097184 | tf_op jit(solution)/shard_map/all_to_all | solution.py:65
  233.7 1.1 reduce_sum.12
  (5 shorter events, 0.1 us)
Async XLA Ops:
  7.2 96.9 %reduce-scatter.2.cloned.1.call-start = ((), (), s32[]{:S(2)}) async-start(), calls=%async_computation.4 | async-start | bytes 8257536 | tf_op jit(solution)/shard_map/reduce_scatter | solution.py:29
  8.4 30.9 %copy-start.5 = (bf16[1024,1792]{1,0:T(8,128)(2,1)S(1)}, bf16[1024,1792]{1,0:T(8,128)(2,1)}, u32[]{:S(2)}) copy-start(bf16[1024,1792]{1,0:T(8,128)(2,1)} %param.6) | copy-start | bytes 11010052
  39.4 4.2 %copy-start = (bf16[8,128,1024]{2,1,0:T(8,128)(2,1)}, bf16[8,128,1024]{2,1,0:T(8,128)(2,1)S(1)}, u32[]{:S(2)}) copy-start(bf16[8,128,1024]{2,1,0:T(8,128)(2,1)S(1)} %all_to_all.23) | copy-start | bytes 6291460
  39.4 4.2 %copy-start.10 = (bf16[1024,1792]{1,0:T(8,128)(2,1)S(1)}, bf16[1024,1792]{1,0:T(8,128)(2,1)}, u32[]{:S(2)}) copy-start(bf16[1024,1792]{1,0:T(8,128)(2,1)} %param.5) | copy-start | bytes 11010052
  54.5 0.9 copy-start.9
  55.4 8.1 %collective-permute-start = (bf16[128,1024]{1,0:T(8,128)(2,1)S(1)}, bf16[128,1024]{1,0:T(8,128)(2,1)S(1)}, u32[]{:S(2)}, u32[]{:S(2)}) collective-permute-start(bf16[128,1024]{1,0:T(8,128)(2,1)S(1)} %copy-done.9), channel_id=1, source_target_pairs={{0,1},{1,0},{2,3},{3,2},{4,5},{5,4},{6,7},{7,6},{8,9},{9,8},{10,11... | collective-permute-start | bytes 786440 | tf_op jit(solution)/shard_map/ppermute | solution.py:25
  65.2 28.4 %all-to-all-start.1 = ((bf16[8,128,1024]{2,1,0:T(8,128)(2,1)}), bf16[8,128,1024]{2,1,0:T(8,128)(2,1)S(1)}, u32[]{:S(2)}, u32[]{:S(2)}) async-start(bf16[8,128,1024]{2,1,0:T(8,128)(2,1)} %tile.5), calls=%async_computation.2 | async-start | bytes 4194304 | tf_op jit(solution)/shard_map/all_to_all | solution.py:23
  71.0 34.5 %copy-start.7 = (bf16[128,1792]{1,0:T(8,128)(2,1)S(1)}, bf16[128,1792]{1,0:T(8,128)(2,1)}, u32[]{:S(2)}) copy-start(bf16[128,1792]{1,0:T(8,128)(2,1)} %param.7) | copy-start | bytes 1376260
  71.0 112.0 %all-gather.2.cloned.1.call-start = ((), (), s32[]{:S(2)}) async-start(), calls=%async_computation.5 | async-start | bytes 12386304 | tf_op jit(solution)/shard_map/all_gather | solution.py:52
  93.6 13.2 %copy-start.2 = (bf16[8,128,1024]{2,1,0:T(8,128)(2,1)}, bf16[8,128,1024]{2,1,0:T(8,128)(2,1)S(1)}, u32[]{:S(2)}) copy-start(bf16[8,128,1024]{2,1,0:T(8,128)(2,1)S(1)} %all-to-all-done.1) | copy-start | bytes 6291460
  107.0 13.2 %collective-permute-start.1 = (bf16[128,1792]{1,0:T(8,128)(2,1)S(1)}, bf16[128,1792]{1,0:T(8,128)(2,1)S(1)}, u32[]{:S(2)}, u32[]{:S(2)}) collective-permute-start(bf16[128,1792]{1,0:T(8,128)(2,1)S(1)} %pad_maximum_fusion.1), channel_id=1, source_target_pairs={{0,1},{1,0},{2,3},{3,2},{4,5},{5,4},{6,7},{7,6},{8,9},{9,8},{10,11... | collective-permute-start | bytes 1376264 | tf_op jit(solution)/shard_map/ppermute | solution.py:50
  120.2 1.1 copy-start.4
  183.0 5.2 %copy-start.8 = (bf16[6,1024,896]{2,1,0:T(8,128)(2,1)S(1)}, bf16[6,1024,896]{2,1,0:T(8,128)(2,1)}, u32[]{:S(2)}) copy-start(bf16[6,1024,896]{2,1,0:T(8,128)(2,1)} %all-gather.2.cloned.1.call-done) | copy-start | bytes 33030148
  188.2 4.0 %copy-start.11 = (bf16[1024,1792]{1,0:T(8,128)(2,1)S(1)}, bf16[1024,1792]{1,0:T(8,128)(2,1)}, u32[]{:S(2)}) copy-start(bf16[1024,1792]{1,0:T(8,128)(2,1)} %param.5) | copy-start | bytes 11010052
  192.2 2.4 copy-start.6
  198.3 35.4 %all-to-all-start.2 = ((bf16[8,128,1024]{2,1,0:T(8,128)(2,1)}), bf16[8,128,1024]{2,1,0:T(8,128)(2,1)S(1)}, u32[]{:S(2)}, u32[]{:S(2)}) async-start(bf16[8,128,1024]{2,1,0:T(8,128)(2,1)} %bitcast.51), calls=%async_computation.3 | async-start | bytes 4194304 | tf_op jit(solution)/shard_map/all_to_all | solution.py:65
  204.1 4.7 %copy-start.1 = (bf16[8,128,1024]{2,1,0:T(8,128)(2,1)S(1)}, bf16[8,128,1024]{2,1,0:T(8,128)(2,1)}, u32[]{:S(2)}) copy-start(bf16[8,128,1024]{2,1,0:T(8,128)(2,1)} %copy-done) | copy-start | bytes 6291460
  208.7 4.1 %copy-start.3 = (bf16[8,128,1024]{2,1,0:T(8,128)(2,1)S(1)}, bf16[8,128,1024]{2,1,0:T(8,128)(2,1)}, u32[]{:S(2)}) copy-start(bf16[8,128,1024]{2,1,0:T(8,128)(2,1)} %copy-done.2) | copy-start | bytes 6291460
Sparse Core Ops, SparseCore 0:
  54.6 49.4 reduce-scatter.1
  121.5 61.4 all-gather.1

commit v10 on v9

--- a/solution.py
+++ b/solution.py
@@ -23,9 +23,14 @@
         return lax.all_to_all(jnp.tile(block, (n_col, 1)), "col", 0, 0, tiled=True)
 
     partner_tokens = lax.ppermute(tokens, "dep", pair)
-    gathered = gather_col(tokens)
-    first = jnp.dot(gathered, gate_weight, preferred_element_type=jnp.float32)
-    second = jnp.dot(gathered, up_weight, preferred_element_type=jnp.float32)
+    feat = tokens.shape[1] // 2
+    lower = gather_col(tokens[:, :feat])
+    first = jnp.dot(lower, gate_weight[:feat], preferred_element_type=jnp.float32)
+    second = jnp.dot(lower, up_weight[:feat], preferred_element_type=jnp.float32)
+    upper = gather_col(tokens[:, feat:])
+    first = first + jnp.dot(upper, gate_weight[feat:], preferred_element_type=jnp.float32)
+    second = second + jnp.dot(upper, up_weight[feat:], preferred_element_type=jnp.float32)
+    gathered = jnp.concatenate([lower, upper], axis=1)
     joined = lax.psum_scatter(
         jnp.concatenate([first, second], axis=1).astype(jnp.bfloat16),
         "row",
@@ -56,14 +61,28 @@
 
     wg_own, wg_other = halves(gate_weight, dep, half)
     wu_own, wu_other = halves(up_weight, dep, half)
-    term = lax.dot_general(full[0], wg_own, transposed, preferred_element_type=jnp.float32)
-    term = term + lax.dot_general(full[2], wg_other, transposed, preferred_element_type=jnp.float32)
-    term = term + lax.dot_general(full[1], wu_own, transposed, preferred_element_type=jnp.float32)
-    term = term + lax.dot_general(full[3], wu_other, transposed, preferred_element_type=jnp.float32)
-    term = term.astype(jnp.bfloat16).reshape(n_col, -1, term.shape[1])
-    term, gathered, gathered_partner = lax.optimization_barrier((term, gathered, gathered_partner))
-    parts = lax.all_to_all(term, "col", 0, 0, tiled=True)
-    grad_tokens = parts.astype(jnp.float32).sum(axis=0).astype(jnp.bfloat16)
+    def grad_part(lo, hi):
+        term = lax.dot_general(full[0], wg_own[lo:hi], transposed, preferred_element_type=jnp.float32)
+        term = term + lax.dot_general(
+            full[2], wg_other[lo:hi], transposed, preferred_element_type=jnp.float32
+        )
+        term = term + lax.dot_general(
+            full[1], wu_own[lo:hi], transposed, preferred_element_type=jnp.float32
+        )
+        term = term + lax.dot_general(
+            full[3], wu_other[lo:hi], transposed, preferred_element_type=jnp.float32
+        )
+        return term.astype(jnp.bfloat16).reshape(n_col, -1, hi - lo)
+
+    def reduce_part(term):
+        parts = lax.all_to_all(term, "col", 0, 0, tiled=True)
+        return parts.astype(jnp.float32).sum(axis=0).astype(jnp.bfloat16)
+
+    rows = gate_weight.shape[0]
+    low_sum = reduce_part(grad_part(0, rows // 2))
+    high = grad_part(rows // 2, rows)
+    high, gathered, gathered_partner = lax.optimization_barrier((high, gathered, gathered_partner))
+    grad_tokens = jnp.concatenate([low_sum, reduce_part(high)], axis=1)
 
     def weight_grad(own, partner):
         mine = lax.dot_general(gathered, own, contract, preferred_element_type=jnp.float32)

time: 242 us -> 262 us (1.083); the launches traced: 242 us -> 259 us
  matrix products: 43.4 us -> 66.9 us
  starting transfers between devices: 17.5 us -> 31.5 us
  blocking collectives: 30.9 us -> 19.2 us
  waiting for transfers between devices: 120 us -> 109 us
  other arithmetic: 9.36 us -> 12 us
    dot_general x6 -> x12, matrix products: 24.2 us -> 48.9 us  [the longest x2 7.75 us: grad_part(): lax.dot_general(full[3], wu_other[lo:hi], transposed, preferred_element_t...]
    all_to_all x1, blocking collectives: 30.9 us -> 19.2 us  [gather_col(): return lax.all_to_all(jnp.tile(block, (n_col, 1)), 'col', 0, 0, tiled=True)]
    all_to_all x1 -> x2, starting transfers between devices: 5.79 us -> 13.9 us  [gather_col(): return lax.all_to_all(jnp.tile(block, (n_col, 1)), 'col', 0, 0, tiled=True)]
    all_to_all x1 -> x2, waiting for transfers between devices: 10.4 us -> 2.42 us  [reduce_part(): parts = lax.all_to_all(term, 'col', 0, 0, tiled=True)]
    all_to_all x1 -> x2, starting transfers between devices: 5.72 us -> 11.4 us  [reduce_part(): parts = lax.all_to_all(term, 'col', 0, 0, tiled=True)]
    reduce_scatter x1, waiting for transfers between devices: 10.6 us -> 6.57 us  [on_device(): lax.psum_scatter(jnp.concatenate([first, second], axis=1).astype(jnp.bflo...]
    all_to_all x1 -> x2, waiting for transfers between devices: 22.6 us -> 24.9 us  [gather_col(): return lax.all_to_all(jnp.tile(block, (n_col, 1)), 'col', 0, 0, tiled=True)]
  transfers between devices with their start and end apart: 6 -> 8, of which waited for: 6 -> 7; matrix products, arithmetic and copies ran while one was open for 9% -> 18% of each run, Pallas kernels for 0% -> 0%
where the time goes in v10:
time: 262 us; the launch traced here: 259 us
  waiting for transfers between devices  109 us (42%)
  matrix products  66.9 us (26%)
  starting transfers between devices  31.5 us (12%)
  blocking collectives  19.2 us (7%)
  between operations  14.2 us (5%)
  other arithmetic  12 us (5%)
  local copies, waits for them, and re-layouts  6.06 us (2%)
    all_gather x1, waiting for transfers between devices, on_device(): lax.all_gather(jnp.stack([gate_own, up_own, gate_other, up_other, partner...  60 us
    all_to_all x2, waiting for transfers between devices, gather_col(): return lax.all_to_all(jnp.tile(block, (n_col, 1)), 'col', 0, 0, tiled=True)  24.9 us
    all_to_all x1, blocking collectives, gather_col(): return lax.all_to_all(jnp.tile(block, (n_col, 1)), 'col', 0, 0, tiled=True)  19.2 us
    all_to_all x2, starting transfers between devices, gather_col(): return lax.all_to_all(jnp.tile(block, (n_col, 1)), 'col', 0, 0, tiled=True)  13.9 us
    all_to_all x2, starting transfers between devices, reduce_part(): parts = lax.all_to_all(term, 'col', 0, 0, tiled=True)  11.4 us
    dot_general x2, matrix products, weight_grad(): lax.dot_general(gathered_partner, partner, contract, preferred_element_ty...  11.1 us
    ppermute x1, waiting for transfers between devices, on_device(): lax.ppermute(jnp.concatenate([gate_other, up_other], axis=1), 'dep', pair)  10.1 us
    dot_general x2, matrix products, grad_part(): lax.dot_general(full[3], wu_other[lo:hi], transposed, preferred_element_t...  7.75 us
  transfers between devices with their start and end apart: 8, of which 7 were waited for; matrix products, arithmetic and copies ran while one was open for 18% of the time, Pallas kernels for 0%

profile of v10, /device:TPU:6, one launch (start us, length us, event | category | flops | bytes accessed | tf_op | source)
XLA Modules:
  0.0 258.9 jit_solution(11606167829542987171)
XLA Ops:
  7.2 1.0 fusion.37
  8.2 0.1 tile.6
  8.2 19.2 %all_to_all.37 = bf16[8,128,512]{2,1,0:T(8,128)(2,1)S(1)} all-to-all(bf16[8,128,512]{2,1,0:T(8,128)(2,1)S(1)} %tile.6), channel_id=1, replica_groups=mesh['row'=8,'col'=8,'dep'=2] {'col'}, dimensions={0} | all-to-all | bytes 2097152 | tf_op jit(solution)/shard_map/all_to_all | solution.py:23
  27.5 1.1 tile.7
  28.6 5.5 %all-to-all-start.1 = ((bf16[8,128,512]{2,1,0:T(8,128)(2,1)}), bf16[8,128,512]{2,1,0:T(8,128)(2,1)S(1)}, u32[]{:S(2)}, u32[]{:S(2)}) async-start(bf16[8,128,512]{2,1,0:T(8,128)(2,1)} %tile.7), calls=%async_computation.1 | async-start | bytes 2097152 | tf_op jit(solution)/shard_map/all_to_all | solution.py:23
  34.1 0.0 reduce-scatter.2.cloned.1.call-start
  34.1 6.7 %fusion.3 = f32[1024,1792]{1,0:T(8,128)} fusion(bf16[1024,512]{1,0:T(8,128)(2,1)S(1)} %bitcast.61, bf16[1024,1792]{1,0:T(8,128)(2,1)} %param.6), kind=kOutput, calls=%fused_computation.17 | convolution fusion | flops 1879048192 | bytes 10223616 | tf_op jit(solution)/shard_map/dot_general | solution.py:29
  40.7 0.0 copy-done.4
  40.7 5.1 %fusion.6 = f32[1024,1792]{1,0:T(8,128)} fusion(bf16[1024,512]{1,0:T(8,128)(2,1)S(1)} %bitcast.62, bf16[1024,1792]{1,0:T(8,128)(2,1)S(1)} %copy-done.4), kind=kOutput, calls=%fused_computation.20 | convolution fusion | flops 1879048192 | bytes 10223616 | tf_op jit(solution)/shard_map/dot_general | solution.py:28
  45.8 0.5 all-to-all-done.1
  46.3 7.7 %add_convert_fusion = bf16[1024,1792]{1,0:T(8,128)(2,1)} fusion(f32[1024,1792]{1,0:T(8,128)} %fusion.3, bf16[1024,512]{1,0:T(8,128)(2,1)S(1)} %bitcast.64, bf16[1024,1792]{1,0:T(8,128)(2,1)} %param.6), kind=kOutput, calls=%fused_computation.1 | convolution fusion | flops 1882718208 | bytes 13893632 | tf_op jit(solution)/shard_map/dot_general | solution.py:32
  54.0 0.0 copy-done.5
  54.0 0.0 copy-done.8
  54.0 4.0 %add_convert_fusion.1 = bf16[1024,1792]{1,0:T(8,128)(2,1)} fusion(f32[1024,1792]{1,0:T(8,128)S(1)} %copy-done.8, bf16[1024,512]{1,0:T(8,128)(2,1)S(1)} %bitcast.65, bf16[1024,1792]{1,0:T(8,128)(2,1)S(1)} %copy-done.5), kind=kOutput, calls=%fused_computation.2 | convolution fusion | flops 1882718208 | bytes 13893632 | tf_op jit(solution)/shard_map/dot_general | solution.py:31
  58.0 6.6 %pad_maximum_fusion = bf16[1024,3584]{1,0:T(8,128)(2,1)} fusion(bf16[1024,1792]{1,0:T(8,128)(2,1)} %add_convert_fusion, bf16[1024,1792]{1,0:T(8,128)(2,1)} %add_convert_fusion.1), kind=kLoop, calls=%fused_computation | loop fusion | flops 14680064 | bytes 14680064 | tf_op jit(solution)/shard_map/concatenate | solution.py:35
  64.6 0.0 reduce-scatter.2.cloned.1.call-update
  64.7 0.9 copy-done.3
  65.6 2.9 %collective-permute-start = (bf16[128,1024]{1,0:T(8,128)(2,1)S(1)}, bf16[128,1024]{1,0:T(8,128)(2,1)S(1)}, u32[]{:S(2)}, u32[]{:S(2)}) collective-permute-start(bf16[128,1024]{1,0:T(8,128)(2,1)S(1)} %copy-done.3), channel_id=1, source_target_pairs={{0,1},{1,0},{2,3},{3,2},{4,5},{5,4},{6,7},{7,6},{8,9},{9,8},{10,11... | collective-permute-start | bytes 786440 | tf_op jit(solution)/shard_map/ppermute | solution.py:25
  68.5 5.0 %collective-permute-done = bf16[128,1024]{1,0:T(8,128)(2,1)S(1)} collective-permute-done((bf16[128,1024]{1,0:T(8,128)(2,1)S(1)}, bf16[128,1024]{1,0:T(8,128)(2,1)S(1)}, u32[]{:S(2)}, u32[]{:S(2)}) %collective-permute-start) | collective-permute-done | bytes 262176 | tf_op jit(solution)/shard_map/ppermute | solution.py:25
  73.5 1.7 tile.8
  75.1 8.4 %all-to-all-start.2 = ((bf16[8,128,1024]{2,1,0:T(8,128)(2,1)}), bf16[8,128,1024]{2,1,0:T(8,128)(2,1)}, u32[]{:S(2)}, u32[]{:S(2)}) async-start(bf16[8,128,1024]{2,1,0:T(8,128)(2,1)} %tile.8), calls=%async_computation.3 | async-start | bytes 4194304 | tf_op jit(solution)/shard_map/all_to_all | solution.py:23
  83.6 0.0 all-gather.2.cloned.1.call-start
  83.6 24.4 %all-to-all-done.2 = bf16[8,128,1024]{2,1,0:T(8,128)(2,1)} async-done(((bf16[8,128,1024]{2,1,0:T(8,128)(2,1)}), bf16[8,128,1024]{2,1,0:T(8,128)(2,1)}, u32[]{:S(2)}, u32[]{:S(2)}) %all-to-all-start.2) | async-done | bytes 2097184 | tf_op jit(solution)/shard_map/all_to_all | solution.py:23
  107.9 6.6 %reduce-scatter.2.cloned.1.call-done = bf16[128,3584]{1,0:T(8,128)(2,1)} async-done(((bf16[1024,3584]{1,0:T(8,128)(2,1)}), bf16[128,3584]{1,0:T(8,128)(2,1)}) %reduce-scatter.2.cloned.1.call-update) | async-done | bytes 917520 | tf_op jit(solution)/shard_map/reduce_scatter | solution.py:34
  114.5 1.4 convert_element_type.56
  115.9 0.0 copy-done.2
  115.9 1.3 fusion.21
  117.3 0.1 bitcast_dynamic-update-slice_fusion.1
  117.3 0.1 bitcast_dynamic-update-slice_fusion
  117.4 3.3 %collective-permute-start.1 = (bf16[128,1792]{1,0:T(8,128)(2,1)S(1)}, bf16[128,1792]{1,0:T(8,128)(2,1)S(1)}, u32[]{:S(2)}, u32[]{:S(2)}) collective-permute-start(bf16[128,1792]{1,0:T(8,128)(2,1)S(1)} %pad_maximum_fusion.2), channel_id=1, source_target_pairs={{0,1},{1,0},{2,3},{3,2},{4,5},{5,4},{6,7},{7,6},{8,9},{9,8},{10,11... | collective-permute-start | bytes 1376264 | tf_op jit(solution)/shard_map/ppermute | solution.py:55
  120.7 10.1 %collective-permute-done.1 = bf16[128,1792]{1,0:T(8,128)(2,1)S(1)} collective-permute-done((bf16[128,1792]{1,0:T(8,128)(2,1)S(1)}, bf16[128,1792]{1,0:T(8,128)(2,1)S(1)}, u32[]{:S(2)}, u32[]{:S(2)}) %collective-permute-start.1) | collective-permute-done | bytes 458784 | tf_op jit(solution)/shard_map/ppermute | solution.py:55
  130.8 0.0 copy-start.1
  130.8 1.1 copy-done.1
  131.9 0.0 all-gather.2.cloned.1.call-update
  131.9 1.6 pad_maximum_fusion.1
  133.5 60.0 %all-gather.2.cloned.1.call-done = bf16[6,1024,896]{2,1,0:T(8,128)(2,1)} async-done(((bf16[6,128,896]{2,1,0:T(8,128)(2,1)}), bf16[6,1024,896]{2,1,0:T(8,128)(2,1)}) %all-gather.2.cloned.1.call-update) | async-done | bytes 11010064 | tf_op jit(solution)/shard_map/all_gather | solution.py:57
  193.5 3.2 %fusion.16 = f32[1024,512]{1,0:T(8,128)S(1)} fusion(bf16[6,1024,896]{2,1,0:T(8,128)(2,1)} %all-gather.2.cloned.1.call-done, bf16[1024,1792]{1,0:T(8,128)(2,1)} %param.6, s32[]{:T(128)S(6)} %add.64, s32[]{:T(128)S(6)} %select_n.4), kind=kOutput, calls=%fused_computation.30 | convolution fusion | flops 939524096 | bytes 4849672 | tf_op jit(solution)/shard_map/dot_general | solution.py:69
  196.7 0.0 copy-done.6
  196.7 2.8 %fusion.13 = f32[1024,512]{1,0:T(8,128)S(1)} fusion(bf16[6,1024,896]{2,1,0:T(8,128)(2,1)} %all-gather.2.cloned.1.call-done, bf16[1024,1792]{1,0:T(8,128)(2,1)S(1)} %copy-done.6, s32[]{:T(128)S(6)} %add.64, s32[]{:T(128)S(6)} %select_n.4), kind=kOutput, calls=%fused_computation.27 | convolution fusion | flops 939524096 | bytes 4849672 | tf_op jit(solution)/shard_map/dot_general | solution.py:65
  199.5 2.8 %fusion.8 = f32[1024,512]{1,0:T(8,128)S(1)} fusion(bf16[6,1024,896]{2,1,0:T(8,128)(2,1)} %all-gather.2.cloned.1.call-done, bf16[1024,1792]{1,0:T(8,128)(2,1)S(1)} %copy-done.6, s32[]{:T(128)S(6)} %add.64, s32[]{:T(128)S(6)} %select_n.5), kind=kOutput, calls=%fused_computation.22 | convolution fusion | flops 939524096 | bytes 4849672 | tf_op jit(solution)/shard_map/dot_general | solution.py:66
  202.3 4.1 %add_convert_fusion.4 = bf16[1024,512]{1,0:T(8,128)(2,1)} fusion(f32[1024,512]{1,0:T(8,128)S(1)} %fusion.16, f32[1024,512]{1,0:T(8,128)S(1)} %fusion.13, f32[1024,512]{1,0:T(8,128)S(1)} %fusion.8, bf16[6,1024,896]{2,1,0:T(8,128)(2,1)} %all-gather.2.cloned.1.call-done, bf16[1024,1792]{1,0:T(8,128)(2,1)} %param.6, s32[]{:T(128)S(6)} %add.64, s32[]{:T(128)S(6)} %select_n.5), kind=kOutput, calls=%fused_computation.6 | convolution fusion | flops 941621248 | bytes 10092552 | tf_op jit(solution)/shard_map/dot_general | solution.py:72
  206.4 5.7 %all-to-all-start.4 = ((bf16[8,128,512]{2,1,0:T(8,128)(2,1)}), bf16[8,128,512]{2,1,0:T(8,128)(2,1)S(1)}, u32[]{:S(2)}, u32[]{:S(2)}) async-start(bf16[8,128,512]{2,1,0:T(8,128)(2,1)} %bitcast.14), calls=%async_computation.5 | async-start | bytes 2097152 | tf_op jit(solution)/shard_map/all_to_all | solution.py:78
  212.1 3.2 %fusion.17 = f32[1024,512]{1,0:T(8,128)S(1)} fusion(bf16[6,1024,896]{2,1,0:T(8,128)(2,1)} %all-gather.2.cloned.1.call-done, bf16[1024,1792]{1,0:T(8,128)(2,1)} %param.6, s32[]{:T(128)S(6)} %select_n.4), kind=kOutput, calls=%fused_computation.31 | convolution fusion | flops 939524096 | bytes 4849668 | tf_op jit(solution)/shard_map/dot_general | solution.py:69
  215.3 0.0 copy-done.7
  215.3 0.0 slice-start.1
  215.3 2.9 %fusion.14 = f32[1024,512]{1,0:T(8,128)S(1)} fusion(bf16[6,1024,896]{2,1,0:T(8,128)(2,1)} %all-gather.2.cloned.1.call-done, bf16[1024,1792]{1,0:T(8,128)(2,1)S(1)} %copy-done.7, s32[]{:T(128)S(6)} %select_n.4), kind=kOutput, calls=%fused_computation.28 | convolution fusion | flops 939524096 | bytes 4849668 | tf_op jit(solution)/shard_map/dot_general | solution.py:65
  218.2 0.0 slice-start.2
  218.2 2.9 %fusion.9 = f32[1024,512]{1,0:T(8,128)S(1)} fusion(bf16[6,1024,896]{2,1,0:T(8,128)(2,1)} %all-gather.2.cloned.1.call-done, bf16[1024,1792]{1,0:T(8,128)(2,1)S(1)} %copy-done.7, s32[]{:T(128)S(6)} %select_n.5), kind=kOutput, calls=%fused_computation.23 | convolution fusion | flops 939524096 | bytes 4849668 | tf_op jit(solution)/shard_map/dot_general | solution.py:66
  221.2 0.0 slice-done
  221.2 0.0 slice-done.1
  221.2 0.0 slice-done.2
  221.2 0.0 copy-start
  221.2 3.6 %add_convert_fusion.5 = bf16[1024,512]{1,0:T(8,128)(2,1)} fusion(f32[1024,512]{1,0:T(8,128)S(1)} %fusion.17, f32[1024,512]{1,0:T(8,128)S(1)} %fusion.14, f32[1024,512]{1,0:T(8,128)S(1)} %fusion.9, bf16[6,1024,896]{2,1,0:T(8,128)(2,1)S(1)} %bitcast.68, bf16[1024,1792]{1,0:T(8,128)(2,1)} %param.6, s32[]{:T(128)S(6)} %select_n.5), kind=kOutput, calls=%fused_computation.7 | convolution fusion | flops 941621248 | bytes 10092548 | tf_op jit(solution)/shard_map/dot_general | solution.py:72
  224.9 0.0 copy-done
  224.9 2.4 fusion.12
  227.3 5.3 %add_convert_fusion.3 = bf16[1024,896]{1,0:T(8,128)(2,1)} fusion(bf16[1024,896]{1,0:T(8,128)(2,1)S(1)} %fusion.12, bf16[1024,1024]{1,0:T(8,128)(2,1)} %bitcast.2, bf16[6,1024,896]{2,1,0:T(8,128)(2,1)S(1)} %bitcast.68), kind=kOutput, calls=%fused_computation.4 | convolution fusion | flops 1883635712 | bytes 7602176 | tf_op jit(solution)/shard_map/dot_general | solution.py:89
  232.6 0.0 all-to-all-done.4
  232.6 5.7 %all-to-all-start.3 = ((bf16[8,128,512]{2,1,0:T(8,128)(2,1)}), bf16[8,128,512]{2,1,0:T(8,128)(2,1)S(1)}, u32[]{:S(2)}, u32[]{:S(2)}) async-start(bf16[8,128,512]{2,1,0:T(8,128)(2,1)} %bitcast.13), calls=%async_computation.4 | async-start | bytes 2097152 | tf_op jit(solution)/shard_map/all_to_all | solution.py:78
  238.3 4.5 %fusion.15 = bf16[1024,896]{1,0:T(8,128)(2,1)S(1)} fusion(bf16[1024,1024]{1,0:T(8,128)(2,1)} %pad_maximum_fusion.1, bf16[6,1024,896]{2,1,0:T(8,128)(2,1)} %all-gather.2.cloned.1.call-done), kind=kOutput, calls=%fused_computation.29 | convolution fusion | flops 1879048192 | bytes 5767168 | tf_op jit(solution)/shard_map/dot_general | solution.py:88
  242.8 5.8 %add_convert_fusion.2 = bf16[1024,896]{1,0:T(8,128)(2,1)} fusion(bf16[1024,896]{1,0:T(8,128)(2,1)S(1)} %fusion.15, bf16[1024,1024]{1,0:T(8,128)(2,1)} %bitcast.2, bf16[6,1024,896]{2,1,0:T(8,128)(2,1)} %all-gather.2.cloned.1.call-done), kind=kOutput, calls=%fused_computation.3 | convolution fusion | flops 1883635712 | bytes 7602176 | tf_op jit(solution)/shard_map/dot_general | solution.py:89
  248.6 0.1 reduce_sum.25
  248.7 2.4 all-to-all-done.3
  251.2 0.1 reduce_sum.24
  251.3 0.7 pad_maximum_fusion.3
  (14 shorter events, 0.2 us)
Async XLA Ops:
  28.6 17.8 %all-to-all-start.1 = ((bf16[8,128,512]{2,1,0:T(8,128)(2,1)}), bf16[8,128,512]{2,1,0:T(8,128)(2,1)S(1)}, u32[]{:S(2)}, u32[]{:S(2)}) async-start(bf16[8,128,512]{2,1,0:T(8,128)(2,1)} %tile.7), calls=%async_computation.1 | async-start | bytes 2097152 | tf_op jit(solution)/shard_map/all_to_all | solution.py:23
  34.1 80.4 %reduce-scatter.2.cloned.1.call-start = ((), (), s32[]{:S(2)}) async-start(), calls=%async_computation.6 | async-start | bytes 8257536 | tf_op jit(solution)/shard_map/reduce_scatter | solution.py:34
  34.1 6.7 %copy-start.4 = (bf16[1024,1792]{1,0:T(8,128)(2,1)S(1)}, bf16[1024,1792]{1,0:T(8,128)(2,1)}, u32[]{:S(2)}) copy-start(bf16[1024,1792]{1,0:T(8,128)(2,1)} %param.5) | copy-start | bytes 11010052
  46.3 7.7 %copy-start.5 = (bf16[1024,1792]{1,0:T(8,128)(2,1)S(1)}, bf16[1024,1792]{1,0:T(8,128)(2,1)}, u32[]{:S(2)}) copy-start(bf16[1024,1792]{1,0:T(8,128)(2,1)} %param.5) | copy-start | bytes 11010052
  46.3 7.7 %copy-start.8 = (f32[1024,1792]{1,0:T(8,128)S(1)}, f32[1024,1792]{1,0:T(8,128)}, u32[]{:S(2)}) copy-start(f32[1024,1792]{1,0:T(8,128)} %fusion.6) | copy-start | bytes 22020100
  64.6 0.9 copy-start.3
  65.6 7.9 %collective-permute-start = (bf16[128,1024]{1,0:T(8,128)(2,1)S(1)}, bf16[128,1024]{1,0:T(8,128)(2,1)S(1)}, u32[]{:S(2)}, u32[]{:S(2)}) collective-permute-start(bf16[128,1024]{1,0:T(8,128)(2,1)S(1)} %copy-done.3), channel_id=1, source_target_pairs={{0,1},{1,0},{2,3},{3,2},{4,5},{5,4},{6,7},{7,6},{8,9},{9,8},{10,11... | collective-permute-start | bytes 786440 | tf_op jit(solution)/shard_map/ppermute | solution.py:25
  75.1 32.8 %all-to-all-start.2 = ((bf16[8,128,1024]{2,1,0:T(8,128)(2,1)}), bf16[8,128,1024]{2,1,0:T(8,128)(2,1)}, u32[]{:S(2)}, u32[]{:S(2)}) async-start(bf16[8,128,1024]{2,1,0:T(8,128)(2,1)} %tile.8), calls=%async_computation.3 | async-start | bytes 4194304 | tf_op jit(solution)/shard_map/all_to_all | solution.py:23
  83.6 32.3 %copy-start.2 = (bf16[128,1792]{1,0:T(8,128)(2,1)S(1)}, bf16[128,1792]{1,0:T(8,128)(2,1)}, u32[]{:S(2)}) copy-start(bf16[128,1792]{1,0:T(8,128)(2,1)} %param.7) | copy-start | bytes 1376260
  83.6 110.0 %all-gather.2.cloned.1.call-start = ((), (), s32[]{:S(2)}) async-start(), calls=%async_computation.7 | async-start | bytes 12386304 | tf_op jit(solution)/shard_map/all_gather | solution.py:57
  117.4 13.3 %collective-permute-start.1 = (bf16[128,1792]{1,0:T(8,128)(2,1)S(1)}, bf16[128,1792]{1,0:T(8,128)(2,1)S(1)}, u32[]{:S(2)}, u32[]{:S(2)}) collective-permute-start(bf16[128,1792]{1,0:T(8,128)(2,1)S(1)} %pad_maximum_fusion.2), channel_id=1, source_target_pairs={{0,1},{1,0},{2,3},{3,2},{4,5},{5,4},{6,7},{7,6},{8,9},{9,8},{10,11... | collective-permute-start | bytes 1376264 | tf_op jit(solution)/shard_map/ppermute | solution.py:55
  130.8 1.1 copy-start.1
  193.5 3.2 %copy-start.6 = (bf16[1024,1792]{1,0:T(8,128)(2,1)S(1)}, bf16[1024,1792]{1,0:T(8,128)(2,1)}, u32[]{:S(2)}) copy-start(bf16[1024,1792]{1,0:T(8,128)(2,1)} %param.5) | copy-start | bytes 11010052
  206.4 26.2 %all-to-all-start.4 = ((bf16[8,128,512]{2,1,0:T(8,128)(2,1)}), bf16[8,128,512]{2,1,0:T(8,128)(2,1)S(1)}, u32[]{:S(2)}, u32[]{:S(2)}) async-start(bf16[8,128,512]{2,1,0:T(8,128)(2,1)} %bitcast.14), calls=%async_computation.5 | async-start | bytes 2097152 | tf_op jit(solution)/shard_map/all_to_all | solution.py:78
  212.1 3.2 %copy-start.7 = (bf16[1024,1792]{1,0:T(8,128)(2,1)S(1)}, bf16[1024,1792]{1,0:T(8,128)(2,1)}, u32[]{:S(2)}) copy-start(bf16[1024,1792]{1,0:T(8,128)(2,1)} %param.5) | copy-start | bytes 11010052
  212.1 9.1 %slice-start = ((s8[11010048]{0:T(1024)(128)(4,1)}), s8[4194304]{0:T(1024)(128)(4,1)S(1)}, s32[]{:S(2)}) async-start(s8[11010048]{0:T(1024)(128)(4,1)} %bitcast.67), calls=%async_computation.8 | async-start | bytes 8388608
  215.3 5.9 %slice-start.1 = ((s8[11010048]{0:T(1024)(128)(4,1)}), s8[4194304]{0:T(1024)(128)(4,1)S(1)}, s32[]{:S(2)}) async-start(s8[11010048]{0:T(1024)(128)(4,1)} %bitcast.67), calls=%async_computation.9 | async-start | bytes 8388608
  218.2 3.0 %slice-start.2 = ((s8[11010048]{0:T(1024)(128)(4,1)}), s8[2621440]{0:T(1024)(128)(4,1)S(1)}, s32[]{:S(2)}) async-start(s8[11010048]{0:T(1024)(128)(4,1)} %bitcast.67), calls=%async_computation.10 | async-start | bytes 5242880
  221.2 3.6 %copy-start = (bf16[1024,1024]{1,0:T(8,128)(2,1)S(1)}, bf16[1024,1024]{1,0:T(8,128)(2,1)}, u32[]{:S(2)}) copy-start(bf16[1024,1024]{1,0:T(8,128)(2,1)} %pad_maximum_fusion.1) | copy-start | bytes 6291460
  232.6 18.6 %all-to-all-start.3 = ((bf16[8,128,512]{2,1,0:T(8,128)(2,1)}), bf16[8,128,512]{2,1,0:T(8,128)(2,1)S(1)}, u32[]{:S(2)}, u32[]{:S(2)}) async-start(bf16[8,128,512]{2,1,0:T(8,128)(2,1)} %bitcast.13), calls=%async_computation.4 | async-start | bytes 2097152 | tf_op jit(solution)/shard_map/all_to_all | solution.py:78
Sparse Core Ops, SparseCore 0:
  64.8 49.6 reduce-scatter.1
  132.0 61.4 all-gather.1

commit v11 on v9

--- a/solution.py
+++ b/solution.py
@@ -46,13 +46,16 @@
 
     gate_own, gate_other = halves(grad_gate, dep, half)
     up_own, up_other = halves(grad_up, dep, half)
-    partner_gate, partner_up = jnp.split(
-        lax.ppermute(jnp.concatenate([gate_other, up_other], axis=1), "dep", pair), 2, axis=1
+    full = lax.all_gather(
+        jnp.stack([gate_own, up_own, gate_other, up_other]), "row", axis=1, tiled=True
     )
-    full = lax.all_gather(
-        jnp.stack([gate_own, up_own, gate_other, up_other, partner_gate, partner_up]),
-        "row", axis=1, tiled=True,
+    n_row = lax.axis_size("row")
+    partner = lax.ppermute(jnp.stack([gate_other, up_other]), "dep", pair)
+    partner = lax.all_to_all(
+        jnp.broadcast_to(partner[None], (n_row,) + partner.shape), "row", 0, 0, tiled=True
     )
+    partner_gate = partner[:, 0].reshape(-1, half)
+    partner_up = partner[:, 1].reshape(-1, half)
 
     wg_own, wg_other = halves(gate_weight, dep, half)
     wu_own, wu_other = halves(up_weight, dep, half)
@@ -75,8 +78,8 @@
             + theirs.astype(jnp.bfloat16).astype(jnp.float32)
         ).astype(jnp.bfloat16)
 
-    sum_gate = weight_grad(full[0], full[4])
-    sum_up = weight_grad(full[1], full[5])
+    sum_gate = weight_grad(full[0], partner_gate)
+    sum_up = weight_grad(full[1], partner_up)
     return (hidden, grad_tokens, sum_gate, sum_up)
 
 

time: 242 us -> 249 us (1.029)
  blocking collectives: 30.9 us -> 100 us
  waiting for transfers between devices: 120 us -> 60.4 us
  matrix products: 43.4 us -> 38.7 us
    all_to_all x0 -> x1, blocking collectives: none -> 69.1 us  [on_device(): lax.all_to_all(jnp.broadcast_to(partner[None], (n_row,) + partner.shape),...]
    all_gather x1, waiting for transfers between devices: 61.6 us -> 0.01 us  [on_device(): lax.all_gather(jnp.stack([gate_own, up_own, gate_other, up_other]), 'row'...]
    dot_general x2, matrix products: 10.4 us -> 7.46 us  [weight_grad(): lax.dot_general(gathered_partner, partner, contract, preferred_element_ty...]
  transfers between devices with their start and end apart: 6 -> 6, of which waited for: 6 -> 5; matrix products, arithmetic and copies ran while one was open for 9% -> 8% of each run, Pallas kernels for 0% -> 0%
where the time goes in v11:
time: 249 us
  blocking collectives  100 us (40%)
  waiting for transfers between devices  60.4 us (24%)
  matrix products  38.7 us (16%)
  starting transfers between devices  17.5 us (7%)
  between operations  14.2 us (6%)
  other arithmetic  10.4 us (4%)
  local copies, waits for them, and re-layouts  7.32 us (3%)
    all_to_all x1, blocking collectives, on_device(): lax.all_to_all(jnp.broadcast_to(partner[None], (n_row,) + partner.shape),...  69.1 us
    all_to_all x1, blocking collectives, gather_col(): return lax.all_to_all(jnp.tile(block, (n_col, 1)), 'col', 0, 0, tiled=True)  30.9 us
    all_to_all x1, waiting for transfers between devices, gather_col(): return lax.all_to_all(jnp.tile(block, (n_col, 1)), 'col', 0, 0, tiled=True)  22.6 us
    all_to_all x1, waiting for transfers between devices, on_device(): parts = lax.all_to_all(term, 'col', 0, 0, tiled=True)  11.9 us
    reduce_scatter x1, waiting for transfers between devices, on_device(): lax.psum_scatter(jnp.concatenate([first, second], axis=1).astype(jnp.bflo...  10.6 us
    ppermute x1, waiting for transfers between devices, on_device(): partner = lax.ppermute(jnp.stack([gate_other, up_other]), 'dep', pair)  10.1 us
    dot_general x2, matrix products, weight_grad(): lax.dot_general(gathered, own, contract, preferred_element_type=jnp.float32)  8.74 us
    dot_general x2, matrix products, weight_grad(): lax.dot_general(gathered_partner, partner, contract, preferred_element_ty...  7.46 us
  transfers between devices with their start and end apart: 6, of which 5 were waited for; matrix products, arithmetic and copies ran while one was open for 8% of the time, Pallas kernels for 0%

profile of v11, /device:TPU:6, one launch (start us, length us, event | category | flops | bytes accessed | tf_op | source)
XLA Modules:
  0.0 248.7 jit_solution(3587974001769393307)
XLA Ops:
  7.2 0.0 reduce-scatter.2.cloned.1.call-start
  7.2 1.2 tile.4
  8.4 0.0 copy-start.6
  8.4 30.9 %all_to_all.28 = bf16[8,128,1024]{2,1,0:T(8,128)(2,1)S(1)} all-to-all(bf16[8,128,1024]{2,1,0:T(8,128)(2,1)S(1)} %tile.4), channel_id=1, replica_groups=mesh['row'=8,'col'=8,'dep'=2] {'col'}, dimensions={0} | all-to-all | bytes 4194304 | tf_op jit(solution)/shard_map/all_to_all | solution.py:23
  39.4 0.0 copy-start
  39.4 0.0 copy-done.6
  39.4 0.0 copy-start.11
  39.4 4.2 %convolution_convert_fusion = bf16[1024,1792]{1,0:T(8,128)(2,1)S(1)} fusion(bf16[1024,1024]{1,0:T(8,128)(2,1)S(1)} %bitcast.38, bf16[1024,1792]{1,0:T(8,128)(2,1)S(1)} %copy-done.6), kind=kOutput, calls=%fused_computation.2 | convolution fusion | flops 3759931392 | bytes 9437184 | tf_op jit(solution)/shard_map/dot_general | solution.py:28
  43.5 0.0 copy-done
  43.5 0.0 copy-done.11
  43.5 5.4 %convolution_convert_fusion.1 = bf16[1024,1792]{1,0:T(8,128)(2,1)} fusion(bf16[1024,1024]{1,0:T(8,128)(2,1)S(1)} %bitcast.39, bf16[1024,1792]{1,0:T(8,128)(2,1)S(1)} %copy-done.11), kind=kOutput, calls=%fused_computation.3 | convolution fusion | flops 3759931392 | bytes 9437184 | tf_op jit(solution)/shard_map/dot_general | solution.py:27
  48.9 5.6 %pad_maximum_fusion = bf16[1024,3584]{1,0:T(8,128)(2,1)} fusion(bf16[1024,1792]{1,0:T(8,128)(2,1)S(1)} %convolution_convert_fusion, bf16[1024,1792]{1,0:T(8,128)(2,1)} %convolution_convert_fusion.1), kind=kLoop, calls=%fused_computation | loop fusion | flops 14680064 | bytes 14680064 | tf_op jit(solution)/shard_map/concatenate | solution.py:30
  54.5 0.0 copy-start.10
  54.5 0.0 reduce-scatter.2.cloned.1.call-update
  54.5 0.9 copy-done.10
  55.4 2.9 %collective-permute-start = (bf16[128,1024]{1,0:T(8,128)(2,1)S(1)}, bf16[128,1024]{1,0:T(8,128)(2,1)S(1)}, u32[]{:S(2)}, u32[]{:S(2)}) collective-permute-start(bf16[128,1024]{1,0:T(8,128)(2,1)S(1)} %copy-done.10), channel_id=1, source_target_pairs={{0,1},{1,0},{2,3},{3,2},{4,5},{5,4},{6,7},{7,6},{8,9},{9,8},{10,11... | collective-permute-start | bytes 786440 | tf_op jit(solution)/shard_map/ppermute | solution.py:25
  58.3 5.2 %collective-permute-done = bf16[128,1024]{1,0:T(8,128)(2,1)S(1)} collective-permute-done((bf16[128,1024]{1,0:T(8,128)(2,1)S(1)}, bf16[128,1024]{1,0:T(8,128)(2,1)S(1)}, u32[]{:S(2)}, u32[]{:S(2)}) %collective-permute-start) | collective-permute-done | bytes 262176 | tf_op jit(solution)/shard_map/ppermute | solution.py:25
  63.5 1.7 tile.5
  65.2 5.8 %all-to-all-start.1 = ((bf16[8,128,1024]{2,1,0:T(8,128)(2,1)}), bf16[8,128,1024]{2,1,0:T(8,128)(2,1)S(1)}, u32[]{:S(2)}, u32[]{:S(2)}) async-start(bf16[8,128,1024]{2,1,0:T(8,128)(2,1)} %tile.5), calls=%async_computation.2 | async-start | bytes 4194304 | tf_op jit(solution)/shard_map/all_to_all | solution.py:23
  70.9 0.0 copy-start.8
  70.9 0.0 all-gather.2.cloned.1.call-start
  70.9 22.6 %all-to-all-done.1 = bf16[8,128,1024]{2,1,0:T(8,128)(2,1)S(1)} async-done(((bf16[8,128,1024]{2,1,0:T(8,128)(2,1)}), bf16[8,128,1024]{2,1,0:T(8,128)(2,1)S(1)}, u32[]{:S(2)}, u32[]{:S(2)}) %all-to-all-start.1) | async-done | bytes 2097184 | tf_op jit(solution)/shard_map/all_to_all | solution.py:23
  93.5 0.0 copy-start.2
  93.5 10.6 %reduce-scatter.2.cloned.1.call-done = bf16[128,3584]{1,0:T(8,128)(2,1)} async-done(((bf16[1024,3584]{1,0:T(8,128)(2,1)}), bf16[128,3584]{1,0:T(8,128)(2,1)}) %reduce-scatter.2.cloned.1.call-update) | async-done | bytes 917520 | tf_op jit(solution)/shard_map/reduce_scatter | solution.py:29
  104.1 1.4 convert_element_type.51
  105.5 0.0 copy-done.8
  105.5 1.3 fusion.11
  106.8 0.0 copy-done.2
  106.8 0.1 dynamic-slice_bitcast_fusion.2
  106.9 1.1 pad_maximum_fusion.1
  107.9 0.0 all-gather.2.cloned.1.call-update
  108.0 0.1 pad_maximum_fusion.2
  108.0 3.1 %collective-permute-start.1 = (bf16[2,128,896]{2,1,0:T(8,128)(2,1)S(1)}, bf16[2,128,896]{2,1,0:T(8,128)(2,1)S(1)}, u32[]{:S(2)}, u32[]{:S(2)}) collective-permute-start(bf16[2,128,896]{2,1,0:T(8,128)(2,1)S(1)} %pad_maximum_fusion.2), channel_id=1, source_target_pairs={{0,1},{1,0},{2,3},{3,2},{4,5},{5,4},{6,7},{7,6},{8,9},{9,8},{10,11... | collective-permute-start | bytes 1376264 | tf_op jit(solution)/shard_map/ppermute | solution.py:53
  111.1 10.1 %collective-permute-done.1 = bf16[2,128,896]{2,1,0:T(8,128)(2,1)S(1)} collective-permute-done((bf16[2,128,896]{2,1,0:T(8,128)(2,1)S(1)}, bf16[2,128,896]{2,1,0:T(8,128)(2,1)S(1)}, u32[]{:S(2)}, u32[]{:S(2)}) %collective-permute-start.1) | collective-permute-done | bytes 458784 | tf_op jit(solution)/shard_map/ppermute | solution.py:53
  121.2 0.5 broadcast_in_dim.2
  121.7 69.1 %all_to_all.29 = bf16[8,2,128,896]{3,2,1,0:T(8,128)(2,1)S(1)} all-to-all(bf16[8,2,128,896]{3,2,1,0:T(8,128)(2,1)S(1)} %broadcast_in_dim.2), channel_id=1, replica_groups=mesh['row'=8,'col'=8,'dep'=2] {'row'}, dimensions={0} | all-to-all | bytes 7340032 | tf_op jit(solution)/shard_map/all_to_all | solution.py:54
  190.8 2.2 fusion.18
  193.1 0.0 all-gather.2.cloned.1.call-done
  193.1 0.0 copy-start.9
  193.1 0.0 copy-start.12
  193.1 4.6 %fusion.2 = f32[1024,1024]{1,0:T(8,128)S(1)} fusion(bf16[1024,1792]{1,0:T(8,128)(2,1)} %param.6, s32[]{:T(128)S(6)} %select_n.4, bf16[4,1024,896]{2,1,0:T(8,128)(2,1)} %all-gather.2.cloned.1.call-done), kind=kOutput, calls=%fused_computation.12 | convolution fusion | flops 1879048192 | bytes 7864324 | tf_op jit(solution)/shard_map/dot_general | solution.py:64
  197.6 0.0 copy-done.9
  197.6 0.7 copy-done.12
  198.3 2.4 fusion.5
  200.7 0.0 copy-start.7
  200.7 2.4 fusion
  203.0 0.0 copy-done.7
  203.1 3.7 %add_convert_fusion = bf16[1024,1024]{1,0:T(8,128)(2,1)} fusion(f32[1024,1024]{1,0:T(8,128)S(1)} %fusion.2, f32[1024,1024]{1,0:T(8,128)S(1)} %fusion.5, f32[1024,1024]{1,0:T(8,128)S(1)} %fusion, bf16[4,1024,896]{2,1,0:T(8,128)(2,1)S(1)} %copy-done.9, bf16[1024,1792]{1,0:T(8,128)(2,1)S(1)} %copy-done.7, s32[]{:T(128)S(6)} %select_n.5), kind=kOutput, calls=%fused_computation.1 | convolution fusion | flops 1883242496 | bytes 18350084 | tf_op jit(solution)/shard_map/dot_general | solution.py:65
  206.8 5.7 %all-to-all-start.2 = ((bf16[8,128,1024]{2,1,0:T(8,128)(2,1)}), bf16[8,128,1024]{2,1,0:T(8,128)(2,1)S(1)}, u32[]{:S(2)}, u32[]{:S(2)}) async-start(bf16[8,128,1024]{2,1,0:T(8,128)(2,1)} %bitcast.37), calls=%async_computation.3 | async-start | bytes 4194304 | tf_op jit(solution)/shard_map/all_to_all | solution.py:68
  212.5 0.0 copy-start.1
  212.5 4.7 %fusion.7 = bf16[1024,896]{1,0:T(8,128)(2,1)S(1)} fusion(bf16[1024,1024]{1,0:T(8,128)(2,1)} %bitcast.40, bf16[4,1024,896]{2,1,0:T(8,128)(2,1)} %all-gather.2.cloned.1.call-done), kind=kOutput, calls=%fused_computation.17 | convolution fusion | flops 1879048192 | bytes 5767168 | tf_op jit(solution)/shard_map/dot_general | solution.py:72
  217.2 0.0 copy-done.1
  217.2 0.0 copy-start.3
  217.2 0.0 copy-start.5
  217.2 4.1 %fusion.8 = bf16[1024,896]{1,0:T(8,128)(2,1)S(1)} fusion(bf16[1024,1024]{1,0:T(8,128)(2,1)S(1)} %bitcast.41, bf16[4,1024,896]{2,1,0:T(8,128)(2,1)} %all-gather.2.cloned.1.call-done), kind=kOutput, calls=%fused_computation.18 | convolution fusion | flops 1879048192 | bytes 5767168 | tf_op jit(solution)/shard_map/dot_general | solution.py:72
  221.3 0.0 copy-done.3
  221.3 0.0 copy-done.5
  221.3 0.0 copy-start.4
  221.3 3.7 %add_convert_fusion.2 = bf16[1024,896]{1,0:T(8,128)(2,1)} fusion(bf16[1024,896]{1,0:T(8,128)(2,1)S(1)} %fusion.7, bf16[1024,1024]{1,0:T(8,128)(2,1)S(1)} %bitcast.42, bf16[1024,896]{1,0:T(8,128)(2,1)S(1)} %bitcast.45), kind=kOutput, calls=%fused_computation.5 | convolution fusion | flops 1883635712 | bytes 7602176 | tf_op jit(solution)/shard_map/dot_general | solution.py:73
  225.1 0.0 copy-done.4
  225.1 3.7 %add_convert_fusion.1 = bf16[1024,896]{1,0:T(8,128)(2,1)} fusion(bf16[1024,896]{1,0:T(8,128)(2,1)S(1)} %fusion.8, bf16[1024,1024]{1,0:T(8,128)(2,1)S(1)} %bitcast.43, bf16[1024,896]{1,0:T(8,128)(2,1)S(1)} %bitcast.44), kind=kOutput, calls=%fused_computation.4 | convolution fusion | flops 1883635712 | bytes 7602176 | tf_op jit(solution)/shard_map/dot_general | solution.py:73
  228.8 11.9 %all-to-all-done.2 = bf16[8,128,1024]{2,1,0:T(8,128)(2,1)S(1)} async-done(((bf16[8,128,1024]{2,1,0:T(8,128)(2,1)}), bf16[8,128,1024]{2,1,0:T(8,128)(2,1)S(1)}, u32[]{:S(2)}, u32[]{:S(2)}) %all-to-all-start.2) | async-done | bytes 2097184 | tf_op jit(solution)/shard_map/all_to_all | solution.py:68
  240.7 1.1 reduce_sum.12
Async XLA Ops:
  7.2 96.9 %reduce-scatter.2.cloned.1.call-start = ((), (), s32[]{:S(2)}) async-start(), calls=%async_computation.5 | async-start | bytes 8257536 | tf_op jit(solution)/shard_map/reduce_scatter | solution.py:29
  8.4 30.9 %copy-start.6 = (bf16[1024,1792]{1,0:T(8,128)(2,1)S(1)}, bf16[1024,1792]{1,0:T(8,128)(2,1)}, u32[]{:S(2)}) copy-start(bf16[1024,1792]{1,0:T(8,128)(2,1)} %param.6) | copy-start | bytes 11010052
  39.4 4.2 %copy-start = (bf16[8,128,1024]{2,1,0:T(8,128)(2,1)}, bf16[8,128,1024]{2,1,0:T(8,128)(2,1)S(1)}, u32[]{:S(2)}) copy-start(bf16[8,128,1024]{2,1,0:T(8,128)(2,1)S(1)} %all_to_all.28) | copy-start | bytes 6291460
  39.4 4.2 %copy-start.11 = (bf16[1024,1792]{1,0:T(8,128)(2,1)S(1)}, bf16[1024,1792]{1,0:T(8,128)(2,1)}, u32[]{:S(2)}) copy-start(bf16[1024,1792]{1,0:T(8,128)(2,1)} %param.5) | copy-start | bytes 11010052
  54.5 0.9 copy-start.10
  55.4 8.1 %collective-permute-start = (bf16[128,1024]{1,0:T(8,128)(2,1)S(1)}, bf16[128,1024]{1,0:T(8,128)(2,1)S(1)}, u32[]{:S(2)}, u32[]{:S(2)}) collective-permute-start(bf16[128,1024]{1,0:T(8,128)(2,1)S(1)} %copy-done.10), channel_id=1, source_target_pairs={{0,1},{1,0},{2,3},{3,2},{4,5},{5,4},{6,7},{7,6},{8,9},{9,8},{10,11... | collective-permute-start | bytes 786440 | tf_op jit(solution)/shard_map/ppermute | solution.py:25
  65.2 28.4 %all-to-all-start.1 = ((bf16[8,128,1024]{2,1,0:T(8,128)(2,1)}), bf16[8,128,1024]{2,1,0:T(8,128)(2,1)S(1)}, u32[]{:S(2)}, u32[]{:S(2)}) async-start(bf16[8,128,1024]{2,1,0:T(8,128)(2,1)} %tile.5), calls=%async_computation.2 | async-start | bytes 4194304 | tf_op jit(solution)/shard_map/all_to_all | solution.py:23
  70.9 34.5 %copy-start.8 = (bf16[128,1792]{1,0:T(8,128)(2,1)S(1)}, bf16[128,1792]{1,0:T(8,128)(2,1)}, u32[]{:S(2)}) copy-start(bf16[128,1792]{1,0:T(8,128)(2,1)} %param.7) | copy-start | bytes 1376260
  70.9 122.1 %all-gather.2.cloned.1.call-start = ((), (), s32[]{:S(2)}) async-start(), calls=%async_computation.6 | async-start | bytes 8257536 | tf_op jit(solution)/shard_map/all_gather | solution.py:49
  93.5 13.2 %copy-start.2 = (bf16[8,128,1024]{2,1,0:T(8,128)(2,1)}, bf16[8,128,1024]{2,1,0:T(8,128)(2,1)S(1)}, u32[]{:S(2)}) copy-start(bf16[8,128,1024]{2,1,0:T(8,128)(2,1)S(1)} %all-to-all-done.1) | copy-start | bytes 6291460
  108.0 13.2 %collective-permute-start.1 = (bf16[2,128,896]{2,1,0:T(8,128)(2,1)S(1)}, bf16[2,128,896]{2,1,0:T(8,128)(2,1)S(1)}, u32[]{:S(2)}, u32[]{:S(2)}) collective-permute-start(bf16[2,128,896]{2,1,0:T(8,128)(2,1)S(1)} %pad_maximum_fusion.2), channel_id=1, source_target_pairs={{0,1},{1,0},{2,3},{3,2},{4,5},{5,4},{6,7},{7,6},{8,9},{9,8},{10,11... | collective-permute-start | bytes 1376264 | tf_op jit(solution)/shard_map/ppermute | solution.py:53
  193.1 4.6 %copy-start.9 = (bf16[4,1024,896]{2,1,0:T(8,128)(2,1)S(1)}, bf16[4,1024,896]{2,1,0:T(8,128)(2,1)}, u32[]{:S(2)}) copy-start(bf16[4,1024,896]{2,1,0:T(8,128)(2,1)} %all-gather.2.cloned.1.call-done) | copy-start | bytes 22020100
  193.1 5.2 %copy-start.12 = (bf16[1024,1792]{1,0:T(8,128)(2,1)S(1)}, bf16[1024,1792]{1,0:T(8,128)(2,1)}, u32[]{:S(2)}) copy-start(bf16[1024,1792]{1,0:T(8,128)(2,1)} %param.5) | copy-start | bytes 11010052
  200.7 2.4 copy-start.7
  206.8 33.9 %all-to-all-start.2 = ((bf16[8,128,1024]{2,1,0:T(8,128)(2,1)}), bf16[8,128,1024]{2,1,0:T(8,128)(2,1)S(1)}, u32[]{:S(2)}, u32[]{:S(2)}) async-start(bf16[8,128,1024]{2,1,0:T(8,128)(2,1)} %bitcast.37), calls=%async_computation.3 | async-start | bytes 4194304 | tf_op jit(solution)/shard_map/all_to_all | solution.py:68
  212.5 4.7 %copy-start.1 = (bf16[8,128,1024]{2,1,0:T(8,128)(2,1)S(1)}, bf16[8,128,1024]{2,1,0:T(8,128)(2,1)}, u32[]{:S(2)}) copy-start(bf16[8,128,1024]{2,1,0:T(8,128)(2,1)} %copy-done) | copy-start | bytes 6291460
  217.2 4.1 %copy-start.3 = (bf16[8,128,1024]{2,1,0:T(8,128)(2,1)S(1)}, bf16[8,128,1024]{2,1,0:T(8,128)(2,1)}, u32[]{:S(2)}) copy-start(bf16[8,128,1024]{2,1,0:T(8,128)(2,1)} %copy-done.2) | copy-start | bytes 6291460
  217.2 4.1 %copy-start.5 = (bf16[8,1,128,896]{3,2,1,0:T(8,128)(2,1)S(1)}, bf16[8,1,128,896]{3,2,1,0:T(8,128)(2,1)}, u32[]{:S(2)}) copy-start(bf16[8,1,128,896]{3,2,1,0:T(8,128)(2,1)} %get-tuple-element.15) | copy-start | bytes 5505028
  221.3 3.7 %copy-start.4 = (bf16[8,1,128,896]{3,2,1,0:T(8,128)(2,1)S(1)}, bf16[8,1,128,896]{3,2,1,0:T(8,128)(2,1)}, u32[]{:S(2)}) copy-start(bf16[8,1,128,896]{3,2,1,0:T(8,128)(2,1)} %get-tuple-element.14) | copy-start | bytes 5505028
Sparse Core Ops, SparseCore 0:
  54.6 49.4 reduce-scatter.1
  108.1 83.1 all-gather.1

commit v12 on v9

--- a/solution.py
+++ b/solution.py
@@ -62,8 +62,13 @@
     term = term + lax.dot_general(full[3], wu_other, transposed, preferred_element_type=jnp.float32)
     term = term.astype(jnp.bfloat16).reshape(n_col, -1, term.shape[1])
     term, gathered, gathered_partner = lax.optimization_barrier((term, gathered, gathered_partner))
-    parts = lax.all_to_all(term, "col", 0, 0, tiled=True)
-    grad_tokens = parts.astype(jnp.float32).sum(axis=0).astype(jnp.bfloat16)
+    col = lax.axis_index("col")
+    summed = lax.dynamic_index_in_dim(term, col, 0, keepdims=False).astype(jnp.float32)
+    for shift in range(1, n_col):
+        block = lax.dynamic_index_in_dim(term, (col + shift) % n_col, 0, keepdims=False)
+        moved = lax.ppermute(block, "col", [(i, (i + shift) % n_col) for i in range(n_col)])
+        summed = summed + moved.astype(jnp.float32)
+    grad_tokens = summed.astype(jnp.bfloat16)
 
     def weight_grad(own, partner):
         mine = lax.dot_general(gathered, own, contract, preferred_element_type=jnp.float32)

time: 242 us -> 244 us (level); the launches traced: 242 us -> 241 us
  matrix products: 43.4 us -> 40.1 us
  starting transfers between devices: 17.5 us -> 20.7 us
    all_to_all x1 -> x0, waiting for transfers between devices: 10.4 us -> none  [on_device(): parts = lax.all_to_all(term, 'col', 0, 0, tiled=True)]
    ppermute x0 -> x7, waiting for transfers between devices: none -> 10.2 us  [on_device(): lax.ppermute(block, 'col', [(i, (i + shift) % n_col) for i in range(n_col)])]
    ppermute x0 -> x7, starting transfers between devices: none -> 8.94 us  [on_device(): lax.ppermute(block, 'col', [(i, (i + shift) % n_col) for i in range(n_col)])]
    all_to_all x1 -> x0, starting transfers between devices: 5.72 us -> none  [on_device(): parts = lax.all_to_all(term, 'col', 0, 0, tiled=True)]
    dot_general x2, matrix products: 10.4 us -> 7.38 us  [weight_grad(): lax.dot_general(gathered_partner, partner, contract, preferred_element_ty...]
  transfers between devices with their start and end apart: 6 -> 12, of which waited for: 6 -> 9; matrix products, arithmetic and copies ran while one was open for 9% -> 7% of each run, Pallas kernels for 0% -> 0%
where the time goes in v12:
time: 244 us; the launch traced here: 241 us
  waiting for transfers between devices  120 us (49%)
  matrix products  40.1 us (16%)
  blocking collectives  30.9 us (13%)
  starting transfers between devices  20.7 us (8%)
  between operations  14.4 us (6%)
  other arithmetic  9.29 us (4%)
  local copies, waits for them, and re-layouts  5.34 us (2%)
    all_gather x1, waiting for transfers between devices, on_device(): lax.all_gather(jnp.stack([gate_own, up_own, gate_other, up_other, partner...  61.5 us
    all_to_all x1, blocking collectives, gather_col(): return lax.all_to_all(jnp.tile(block, (n_col, 1)), 'col', 0, 0, tiled=True)  30.9 us
    all_to_all x1, waiting for transfers between devices, gather_col(): return lax.all_to_all(jnp.tile(block, (n_col, 1)), 'col', 0, 0, tiled=True)  22.6 us
    reduce_scatter x1, waiting for transfers between devices, on_device(): lax.psum_scatter(jnp.concatenate([first, second], axis=1).astype(jnp.bflo...  10.6 us
    ppermute x7, waiting for transfers between devices, on_device(): lax.ppermute(block, 'col', [(i, (i + shift) % n_col) for i in range(n_col)])  10.2 us
    ppermute x1, waiting for transfers between devices, on_device(): lax.ppermute(jnp.concatenate([gate_other, up_other], axis=1), 'dep', pair)  10.1 us
    ppermute x7, starting transfers between devices, on_device(): lax.ppermute(block, 'col', [(i, (i + shift) % n_col) for i in range(n_col)])  8.94 us
    dot_general x2, matrix products, weight_grad(): lax.dot_general(gathered_partner, partner, contract, preferred_element_ty...  7.38 us
  transfers between devices with their start and end apart: 12, of which 9 were waited for; matrix products, arithmetic and copies ran while one was open for 7% of the time, Pallas kernels for 0%

profile of v12, /device:TPU:6, one launch (start us, length us, event | category | flops | bytes accessed | tf_op | source)
XLA Modules:
  0.0 241.0 jit_solution(13903881225226899041)
XLA Ops:
  7.2 0.0 reduce-scatter.2.cloned.1.call-start
  7.2 1.2 tile.4
  8.4 0.0 copy-start.3
  8.4 30.9 %all_to_all.18 = bf16[8,128,1024]{2,1,0:T(8,128)(2,1)S(1)} all-to-all(bf16[8,128,1024]{2,1,0:T(8,128)(2,1)S(1)} %tile.4), channel_id=1, replica_groups=mesh['row'=8,'col'=8,'dep'=2] {'col'}, dimensions={0} | all-to-all | bytes 4194304 | tf_op jit(solution)/shard_map/all_to_all | solution.py:23
  39.4 0.0 copy-done.3
  39.4 4.2 %convolution_convert_fusion = bf16[1024,1792]{1,0:T(8,128)(2,1)S(1)} fusion(bf16[1024,1024]{1,0:T(8,128)(2,1)S(1)} %bitcast.70, bf16[1024,1792]{1,0:T(8,128)(2,1)S(1)} %copy-done.3), kind=kOutput, calls=%fused_computation.2 | convolution fusion | flops 3759931392 | bytes 9437184 | tf_op jit(solution)/shard_map/dot_general | solution.py:28
  43.5 0.0 copy-done
  43.5 0.0 copy-done.7
  43.5 5.4 %convolution_convert_fusion.1 = bf16[1024,1792]{1,0:T(8,128)(2,1)} fusion(bf16[1024,1024]{1,0:T(8,128)(2,1)S(1)} %bitcast.71, bf16[1024,1792]{1,0:T(8,128)(2,1)S(1)} %copy-done.7), kind=kOutput, calls=%fused_computation.3 | convolution fusion | flops 3759931392 | bytes 9437184 | tf_op jit(solution)/shard_map/dot_general | solution.py:27
  48.9 5.5 %pad_maximum_fusion = bf16[1024,3584]{1,0:T(8,128)(2,1)} fusion(bf16[1024,1792]{1,0:T(8,128)(2,1)S(1)} %convolution_convert_fusion, bf16[1024,1792]{1,0:T(8,128)(2,1)} %convolution_convert_fusion.1), kind=kLoop, calls=%fused_computation | loop fusion | flops 14680064 | bytes 14680064 | tf_op jit(solution)/shard_map/concatenate | solution.py:30
  54.5 0.0 reduce-scatter.2.cloned.1.call-update
  54.5 0.9 copy-done.6
  55.4 2.9 %collective-permute-start = (bf16[128,1024]{1,0:T(8,128)(2,1)S(1)}, bf16[128,1024]{1,0:T(8,128)(2,1)S(1)}, u32[]{:S(2)}, u32[]{:S(2)}) collective-permute-start(bf16[128,1024]{1,0:T(8,128)(2,1)S(1)} %copy-done.6), channel_id=1, source_target_pairs={{0,1},{1,0},{2,3},{3,2},{4,5},{5,4},{6,7},{7,6},{8,9},{9,8},{10,11... | collective-permute-start | bytes 786440 | tf_op jit(solution)/shard_map/ppermute | solution.py:25
  58.3 5.2 %collective-permute-done = bf16[128,1024]{1,0:T(8,128)(2,1)S(1)} collective-permute-done((bf16[128,1024]{1,0:T(8,128)(2,1)S(1)}, bf16[128,1024]{1,0:T(8,128)(2,1)S(1)}, u32[]{:S(2)}, u32[]{:S(2)}) %collective-permute-start) | collective-permute-done | bytes 262176 | tf_op jit(solution)/shard_map/ppermute | solution.py:25
  63.5 1.7 tile.5
  65.1 5.8 %all-to-all-start.1 = ((bf16[8,128,1024]{2,1,0:T(8,128)(2,1)}), bf16[8,128,1024]{2,1,0:T(8,128)(2,1)S(1)}, u32[]{:S(2)}, u32[]{:S(2)}) async-start(bf16[8,128,1024]{2,1,0:T(8,128)(2,1)} %tile.5), calls=%async_computation.2 | async-start | bytes 4194304 | tf_op jit(solution)/shard_map/all_to_all | solution.py:23
  70.9 0.0 all-gather.2.cloned.1.call-start
  70.9 22.6 %all-to-all-done.1 = bf16[8,128,1024]{2,1,0:T(8,128)(2,1)S(1)} async-done(((bf16[8,128,1024]{2,1,0:T(8,128)(2,1)}), bf16[8,128,1024]{2,1,0:T(8,128)(2,1)S(1)}, u32[]{:S(2)}, u32[]{:S(2)}) %all-to-all-start.1) | async-done | bytes 2097184 | tf_op jit(solution)/shard_map/all_to_all | solution.py:23
  93.5 10.6 %reduce-scatter.2.cloned.1.call-done = bf16[128,3584]{1,0:T(8,128)(2,1)} async-done(((bf16[1024,3584]{1,0:T(8,128)(2,1)}), bf16[128,3584]{1,0:T(8,128)(2,1)}) %reduce-scatter.2.cloned.1.call-update) | async-done | bytes 917520 | tf_op jit(solution)/shard_map/reduce_scatter | solution.py:29
  104.1 1.4 convert_element_type.79
  105.5 0.0 copy-done.5
  105.5 1.3 fusion.14
  106.9 0.1 bitcast_dynamic-update-slice_fusion.1
  106.9 0.1 bitcast_dynamic-update-slice_fusion
  107.0 3.1 %collective-permute-start.1 = (bf16[128,1792]{1,0:T(8,128)(2,1)S(1)}, bf16[128,1792]{1,0:T(8,128)(2,1)S(1)}, u32[]{:S(2)}, u32[]{:S(2)}) collective-permute-start(bf16[128,1792]{1,0:T(8,128)(2,1)S(1)} %pad_maximum_fusion.1), channel_id=1, source_target_pairs={{0,1},{1,0},{2,3},{3,2},{4,5},{5,4},{6,7},{7,6},{8,9},{9,8},{10,11... | collective-permute-start | bytes 1376264 | tf_op jit(solution)/shard_map/ppermute | solution.py:50
  110.1 10.1 %collective-permute-done.1 = bf16[128,1792]{1,0:T(8,128)(2,1)S(1)} collective-permute-done((bf16[128,1792]{1,0:T(8,128)(2,1)S(1)}, bf16[128,1792]{1,0:T(8,128)(2,1)S(1)}, u32[]{:S(2)}, u32[]{:S(2)}) %collective-permute-start.1) | collective-permute-done | bytes 458784 | tf_op jit(solution)/shard_map/ppermute | solution.py:50
  120.2 0.0 copy-start.2
  120.2 1.1 copy-done.2
  121.3 0.0 all-gather.2.cloned.1.call-update
  121.4 61.5 %all-gather.2.cloned.1.call-done = bf16[6,1024,896]{2,1,0:T(8,128)(2,1)} async-done(((bf16[6,128,896]{2,1,0:T(8,128)(2,1)}), bf16[6,1024,896]{2,1,0:T(8,128)(2,1)}) %all-gather.2.cloned.1.call-update) | async-done | bytes 11010064 | tf_op jit(solution)/shard_map/all_gather | solution.py:52
  182.9 4.6 %fusion.4 = f32[1024,1024]{1,0:T(8,128)S(1)} fusion(bf16[1024,1792]{1,0:T(8,128)(2,1)} %param.6, s32[]{:T(128)S(6)} %select_n.68, bf16[6,1024,896]{2,1,0:T(8,128)(2,1)} %all-gather.2.cloned.1.call-done), kind=kOutput, calls=%fused_computation.16 | convolution fusion | flops 1879048192 | bytes 7864324 | tf_op jit(solution)/shard_map/dot_general | solution.py:61
  187.5 0.0 copy-done.8
  187.5 3.9 %fusion.7 = f32[1024,1024]{1,0:T(8,128)S(1)} fusion(bf16[1024,1792]{1,0:T(8,128)(2,1)S(1)} %copy-done.8, s32[]{:T(128)S(6)} %select_n.68, bf16[6,1024,896]{2,1,0:T(8,128)(2,1)} %all-gather.2.cloned.1.call-done), kind=kOutput, calls=%fused_computation.19 | convolution fusion | flops 1879048192 | bytes 7864324 | tf_op jit(solution)/shard_map/dot_general | solution.py:59
  191.4 0.0 copy-start.4
  191.4 4.0 %fusion.2 = f32[1024,1024]{1,0:T(8,128)S(1)} fusion(bf16[6,1024,896]{2,1,0:T(8,128)(2,1)} %all-gather.2.cloned.1.call-done, bf16[1024,1792]{1,0:T(8,128)(2,1)S(1)} %copy-done.8, s32[]{:T(128)S(6)} %select_n.69), kind=kOutput, calls=%fused_computation.13 | convolution fusion | flops 1879048192 | bytes 7864324 | tf_op jit(solution)/shard_map/dot_general | solution.py:60
  195.4 0.0 copy-done.4
  195.4 0.0 slice-start
  195.4 0.0 slice-start.1
  195.5 4.1 %add_convert_fusion = bf16[1024,1024]{1,0:T(8,128)(2,1)S(1)} fusion(f32[1024,1024]{1,0:T(8,128)S(1)} %fusion.4, f32[1024,1024]{1,0:T(8,128)S(1)} %fusion.7, f32[1024,1024]{1,0:T(8,128)S(1)} %fusion.2, bf16[6,1024,896]{2,1,0:T(8,128)(2,1)} %all-gather.2.cloned.1.call-done, bf16[1024,1792]{1,0:T(8,128)(2,1)S(1)} %copy-done.4, s32[]{:T(128)S(6)} %select_n.69), kind=kOutput, calls=%fused_computation.1 | convolution fusion | flops 1883242496 | bytes 18350084 | tf_op jit(solution)/shard_map/dot_general | solution.py:62
  199.6 0.0 copy-start.1
  199.6 0.2 dynamic-slice_bitcast_fusion.6
  199.8 1.1 collective-permute-start.8
  200.9 1.2 collective-permute-start.7
  202.1 3.0 %collective-permute-start.6 = (bf16[128,1024]{1,0:T(8,128)(2,1)S(1)}, bf16[128,1024]{1,0:T(8,128)(2,1)S(1)}, u32[]{:S(2)}, u32[]{:S(2)}) collective-permute-start(bf16[128,1024]{1,0:T(8,128)(2,1)S(1)} %get-tuple-element.23), channel_id=1, source_target_pairs={{0,10},{2,12},{4,14},{6,0},{8,2},{10,4},{12,6},{14,8},{1,11},{3,13... | collective-permute-start | bytes 786440 | tf_op jit(solution)/shard_map/ppermute | solution.py:69
  205.1 0.5 collective-permute-start.5
  205.6 0.9 collective-permute-start.4
  206.5 0.0 copy-done.1
  206.6 4.2 %fusion.9 = bf16[1024,896]{1,0:T(8,128)(2,1)S(1)} fusion(bf16[1024,1024]{1,0:T(8,128)(2,1)S(1)} %bitcast.72, bf16[6,1024,896]{2,1,0:T(8,128)(2,1)} %all-gather.2.cloned.1.call-done), kind=kOutput, calls=%fused_computation.21 | convolution fusion | flops 1879048192 | bytes 5767168 | tf_op jit(solution)/shard_map/dot_general | solution.py:74
  210.8 0.0 slice-done
  210.8 0.0 slice-done.1
  210.8 0.0 slice-done.2
  210.8 3.7 %add_convert_fusion.2 = bf16[1024,896]{1,0:T(8,128)(2,1)} fusion(bf16[1024,896]{1,0:T(8,128)(2,1)S(1)} %fusion.9, bf16[1024,1024]{1,0:T(8,128)(2,1)S(1)} %bitcast.74, bf16[6,1024,896]{2,1,0:T(8,128)(2,1)S(1)} %bitcast.77), kind=kOutput, calls=%fused_computation.5 | convolution fusion | flops 1883635712 | bytes 7602176 | tf_op jit(solution)/shard_map/dot_general | solution.py:75
  214.5 2.4 %fusion.10 = bf16[1024,896]{1,0:T(8,128)(2,1)S(1)} fusion(bf16[1024,1024]{1,0:T(8,128)(2,1)S(1)} %bitcast.73, bf16[6,1024,896]{2,1,0:T(8,128)(2,1)S(1)} %bitcast.77), kind=kOutput, calls=%fused_computation.22 | convolution fusion | flops 1879048192 | bytes 5767168 | tf_op jit(solution)/shard_map/dot_general | solution.py:74
  217.0 3.1 %collective-permute-done.8 = bf16[128,1024]{1,0:T(8,128)(2,1)S(1)} collective-permute-done((bf16[128,1024]{1,0:T(8,128)(2,1)S(1)}, bf16[128,1024]{1,0:T(8,128)(2,1)S(1)}, u32[]{:S(2)}, u32[]{:S(2)}) %collective-permute-start.8) | collective-permute-done | bytes 262176 | tf_op jit(solution)/shard_map/ppermute | solution.py:69
  220.1 0.0 collective-permute-start.3
  220.1 0.0 collective-permute-done.7
  220.1 2.2 collective-permute-start.2
  222.3 3.7 %add_convert_fusion.1 = bf16[1024,896]{1,0:T(8,128)(2,1)} fusion(bf16[1024,896]{1,0:T(8,128)(2,1)S(1)} %fusion.10, bf16[1024,1024]{1,0:T(8,128)(2,1)S(1)} %bitcast.75, bf16[6,1024,896]{2,1,0:T(8,128)(2,1)S(1)} %bitcast.77), kind=kOutput, calls=%fused_computation.4 | convolution fusion | flops 1883635712 | bytes 7602176 | tf_op jit(solution)/shard_map/dot_general | solution.py:75
  226.0 0.0 collective-permute-done.6
  226.0 1.5 collective-permute-done.5
  227.5 1.8 collective-permute-done.4
  229.3 0.0 collective-permute-done.3
  229.3 3.7 %collective-permute-done.2 = bf16[128,1024]{1,0:T(8,128)(2,1)S(1)} collective-permute-done((bf16[128,1024]{1,0:T(8,128)(2,1)S(1)}, bf16[128,1024]{1,0:T(8,128)(2,1)S(1)}, u32[]{:S(2)}, u32[]{:S(2)}) %collective-permute-start.2) | collective-permute-done | bytes 262176 | tf_op jit(solution)/shard_map/ppermute | solution.py:69
  233.1 1.1 fusion.22
  (12 shorter events, 0.2 us)
Async XLA Ops:
  7.2 96.9 %reduce-scatter.2.cloned.1.call-start = ((), (), s32[]{:S(2)}) async-start(), calls=%async_computation.3 | async-start | bytes 8257536 | tf_op jit(solution)/shard_map/reduce_scatter | solution.py:29
  8.4 30.9 %copy-start.3 = (bf16[1024,1792]{1,0:T(8,128)(2,1)S(1)}, bf16[1024,1792]{1,0:T(8,128)(2,1)}, u32[]{:S(2)}) copy-start(bf16[1024,1792]{1,0:T(8,128)(2,1)} %param.6) | copy-start | bytes 11010052
  39.4 4.2 %copy-start = (bf16[8,128,1024]{2,1,0:T(8,128)(2,1)}, bf16[8,128,1024]{2,1,0:T(8,128)(2,1)S(1)}, u32[]{:S(2)}) copy-start(bf16[8,128,1024]{2,1,0:T(8,128)(2,1)S(1)} %all_to_all.18) | copy-start | bytes 6291460
  39.4 4.2 %copy-start.7 = (bf16[1024,1792]{1,0:T(8,128)(2,1)S(1)}, bf16[1024,1792]{1,0:T(8,128)(2,1)}, u32[]{:S(2)}) copy-start(bf16[1024,1792]{1,0:T(8,128)(2,1)} %param.5) | copy-start | bytes 11010052
  54.5 0.9 copy-start.6
  55.4 8.1 %collective-permute-start = (bf16[128,1024]{1,0:T(8,128)(2,1)S(1)}, bf16[128,1024]{1,0:T(8,128)(2,1)S(1)}, u32[]{:S(2)}, u32[]{:S(2)}) collective-permute-start(bf16[128,1024]{1,0:T(8,128)(2,1)S(1)} %copy-done.6), channel_id=1, source_target_pairs={{0,1},{1,0},{2,3},{3,2},{4,5},{5,4},{6,7},{7,6},{8,9},{9,8},{10,11... | collective-permute-start | bytes 786440 | tf_op jit(solution)/shard_map/ppermute | solution.py:25
  65.1 28.4 %all-to-all-start.1 = ((bf16[8,128,1024]{2,1,0:T(8,128)(2,1)}), bf16[8,128,1024]{2,1,0:T(8,128)(2,1)S(1)}, u32[]{:S(2)}, u32[]{:S(2)}) async-start(bf16[8,128,1024]{2,1,0:T(8,128)(2,1)} %tile.5), calls=%async_computation.2 | async-start | bytes 4194304 | tf_op jit(solution)/shard_map/all_to_all | solution.py:23
  70.9 34.5 %copy-start.5 = (bf16[128,1792]{1,0:T(8,128)(2,1)S(1)}, bf16[128,1792]{1,0:T(8,128)(2,1)}, u32[]{:S(2)}) copy-start(bf16[128,1792]{1,0:T(8,128)(2,1)} %param.7) | copy-start | bytes 1376260
  70.9 112.0 %all-gather.2.cloned.1.call-start = ((), (), s32[]{:S(2)}) async-start(), calls=%async_computation.4 | async-start | bytes 12386304 | tf_op jit(solution)/shard_map/all_gather | solution.py:52
  107.0 13.2 %collective-permute-start.1 = (bf16[128,1792]{1,0:T(8,128)(2,1)S(1)}, bf16[128,1792]{1,0:T(8,128)(2,1)S(1)}, u32[]{:S(2)}, u32[]{:S(2)}) collective-permute-start(bf16[128,1792]{1,0:T(8,128)(2,1)S(1)} %pad_maximum_fusion.1), channel_id=1, source_target_pairs={{0,1},{1,0},{2,3},{3,2},{4,5},{5,4},{6,7},{7,6},{8,9},{9,8},{10,11... | collective-permute-start | bytes 1376264 | tf_op jit(solution)/shard_map/ppermute | solution.py:50
  120.2 1.1 copy-start.2
  182.9 4.6 %copy-start.8 = (bf16[1024,1792]{1,0:T(8,128)(2,1)S(1)}, bf16[1024,1792]{1,0:T(8,128)(2,1)}, u32[]{:S(2)}) copy-start(bf16[1024,1792]{1,0:T(8,128)(2,1)} %param.5) | copy-start | bytes 11010052
  191.4 4.0 %copy-start.4 = (bf16[1024,1792]{1,0:T(8,128)(2,1)S(1)}, bf16[1024,1792]{1,0:T(8,128)(2,1)}, u32[]{:S(2)}) copy-start(bf16[1024,1792]{1,0:T(8,128)(2,1)} %param.6) | copy-start | bytes 11010052
  195.4 15.4 %slice-start = ((s8[11010048]{0:T(1024)(128)(4,1)}), s8[2621440]{0:T(1024)(128)(4,1)S(1)}, s32[]{:S(2)}) async-start(s8[11010048]{0:T(1024)(128)(4,1)} %bitcast.76), calls=%async_computation.5 | async-start | bytes 5242880
  195.4 15.4 %slice-start.1 = ((s8[11010048]{0:T(1024)(128)(4,1)}), s8[4194304]{0:T(1024)(128)(4,1)S(1)}, s32[]{:S(2)}) async-start(s8[11010048]{0:T(1024)(128)(4,1)} %bitcast.76), calls=%async_computation.6 | async-start | bytes 8388608
  199.6 7.0 %copy-start.1 = (bf16[8,128,1024]{2,1,0:T(8,128)(2,1)S(1)}, bf16[8,128,1024]{2,1,0:T(8,128)(2,1)}, u32[]{:S(2)}) copy-start(bf16[8,128,1024]{2,1,0:T(8,128)(2,1)} %copy-done) | copy-start | bytes 6291460
  199.8 20.3 %collective-permute-start.8 = (bf16[128,1024]{1,0:T(8,128)(2,1)S(1)}, bf16[128,1024]{1,0:T(8,128)(2,1)S(1)}, u32[]{:S(2)}, u32[]{:S(2)}) collective-permute-start(bf16[128,1024]{1,0:T(8,128)(2,1)S(1)} %get-tuple-element.21), channel_id=1, source_target_pairs={{0,14},{2,0},{4,2},{6,4},{8,6},{10,8},{12,10},{14,12},{1,15},{3,1}... | collective-permute-start | bytes 786440 | tf_op jit(solution)/shard_map/ppermute | solution.py:69
  200.9 19.2 %collective-permute-start.7 = (bf16[128,1024]{1,0:T(8,128)(2,1)S(1)}, bf16[128,1024]{1,0:T(8,128)(2,1)S(1)}, u32[]{:S(2)}, u32[]{:S(2)}) collective-permute-start(bf16[128,1024]{1,0:T(8,128)(2,1)S(1)} %get-tuple-element.22), channel_id=1, source_target_pairs={{0,12},{2,14},{4,0},{6,2},{8,4},{10,6},{12,8},{14,10},{1,13},{3,15... | collective-permute-start | bytes 786440 | tf_op jit(solution)/shard_map/ppermute | solution.py:69
  202.1 23.9 %collective-permute-start.6 = (bf16[128,1024]{1,0:T(8,128)(2,1)S(1)}, bf16[128,1024]{1,0:T(8,128)(2,1)S(1)}, u32[]{:S(2)}, u32[]{:S(2)}) collective-permute-start(bf16[128,1024]{1,0:T(8,128)(2,1)S(1)} %get-tuple-element.23), channel_id=1, source_target_pairs={{0,10},{2,12},{4,14},{6,0},{8,2},{10,4},{12,6},{14,8},{1,11},{3,13... | collective-permute-start | bytes 786440 | tf_op jit(solution)/shard_map/ppermute | solution.py:69
  205.1 22.4 %collective-permute-start.5 = (bf16[128,1024]{1,0:T(8,128)(2,1)S(1)}, bf16[128,1024]{1,0:T(8,128)(2,1)S(1)}, u32[]{:S(2)}, u32[]{:S(2)}) collective-permute-start(bf16[128,1024]{1,0:T(8,128)(2,1)S(1)} %get-tuple-element.24), channel_id=1, source_target_pairs={{0,8},{2,10},{4,12},{6,14},{8,0},{10,2},{12,4},{14,6},{1,9},{3,11}... | collective-permute-start | bytes 786440 | tf_op jit(solution)/shard_map/ppermute | solution.py:69
  205.6 5.2 %slice-start.2 = ((s8[11010048]{0:T(1024)(128)(4,1)}), s8[4194304]{0:T(1024)(128)(4,1)S(1)}, s32[]{:S(2)}) async-start(s8[11010048]{0:T(1024)(128)(4,1)} %bitcast.76), calls=%async_computation.7 | async-start | bytes 8388608
  205.6 23.7 %collective-permute-start.4 = (bf16[128,1024]{1,0:T(8,128)(2,1)S(1)}, bf16[128,1024]{1,0:T(8,128)(2,1)S(1)}, u32[]{:S(2)}, u32[]{:S(2)}) collective-permute-start(bf16[128,1024]{1,0:T(8,128)(2,1)S(1)} %get-tuple-element.25), channel_id=1, source_target_pairs={{0,6},{2,8},{4,10},{6,12},{8,14},{10,0},{12,2},{14,4},{1,7},{3,9},... | collective-permute-start | bytes 786440 | tf_op jit(solution)/shard_map/ppermute | solution.py:69
  220.1 9.2 %collective-permute-start.3 = (bf16[128,1024]{1,0:T(8,128)(2,1)S(1)}, bf16[128,1024]{1,0:T(8,128)(2,1)S(1)}, u32[]{:S(2)}, u32[]{:S(2)}) collective-permute-start(bf16[128,1024]{1,0:T(8,128)(2,1)S(1)} %get-tuple-element.26), channel_id=1, source_target_pairs={{0,4},{2,6},{4,8},{6,10},{8,12},{10,14},{12,0},{14,2},{1,5},{3,7},... | collective-permute-start | bytes 786440 | tf_op jit(solution)/shard_map/ppermute | solution.py:69
  220.1 13.0 %collective-permute-start.2 = (bf16[128,1024]{1,0:T(8,128)(2,1)S(1)}, bf16[128,1024]{1,0:T(8,128)(2,1)S(1)}, u32[]{:S(2)}, u32[]{:S(2)}) collective-permute-start(bf16[128,1024]{1,0:T(8,128)(2,1)S(1)} %get-tuple-element.20), channel_id=1, source_target_pairs={{0,2},{2,4},{4,6},{6,8},{8,10},{10,12},{12,14},{14,0},{1,3},{3,5},... | collective-permute-start | bytes 786440 | tf_op jit(solution)/shard_map/ppermute | solution.py:69
Sparse Core Ops, SparseCore 0:
  54.6 49.4 reduce-scatter.1
  121.5 61.4 all-gather.1

commit v13 on v9

--- a/solution.py
+++ b/solution.py
@@ -50,16 +50,18 @@
         lax.ppermute(jnp.concatenate([gate_other, up_other], axis=1), "dep", pair), 2, axis=1
     )
     full = lax.all_gather(
-        jnp.stack([gate_own, up_own, gate_other, up_other, partner_gate, partner_up]),
-        "row", axis=1, tiled=True,
+        jnp.concatenate(
+            [gate_own, up_own, gate_other, up_other, partner_gate, partner_up], axis=1
+        ),
+        "row", axis=0, tiled=True,
     )
 
     wg_own, wg_other = halves(gate_weight, dep, half)
     wu_own, wu_other = halves(up_weight, dep, half)
-    term = lax.dot_general(full[0], wg_own, transposed, preferred_element_type=jnp.float32)
-    term = term + lax.dot_general(full[2], wg_other, transposed, preferred_element_type=jnp.float32)
-    term = term + lax.dot_general(full[1], wu_own, transposed, preferred_element_type=jnp.float32)
-    term = term + lax.dot_general(full[3], wu_other, transposed, preferred_element_type=jnp.float32)
+    weights = jnp.concatenate([wg_own, wu_own, wg_other, wu_other], axis=1)
+    term = lax.dot_general(
+        full[:, :2 * width], weights, transposed, preferred_element_type=jnp.float32
+    )
     term = term.astype(jnp.bfloat16).reshape(n_col, -1, term.shape[1])
     term, gathered, gathered_partner = lax.optimization_barrier((term, gathered, gathered_partner))
     parts = lax.all_to_all(term, "col", 0, 0, tiled=True)
@@ -75,8 +77,8 @@
             + theirs.astype(jnp.bfloat16).astype(jnp.float32)
         ).astype(jnp.bfloat16)
 
-    sum_gate = weight_grad(full[0], full[4])
-    sum_up = weight_grad(full[1], full[5])
+    sum_gate = weight_grad(full[:, :half], full[:, 2 * width:2 * width + half])
+    sum_up = weight_grad(full[:, half:width], full[:, 2 * width + half:])
     return (hidden, grad_tokens, sum_gate, sum_up)
 
 

time: 242 us -> 240 us (level)
  local copies, waits for them, and re-layouts: 5.79 us -> 10.9 us
  waiting for transfers between devices: 120 us -> 115 us
    all_gather x1, waiting for transfers between devices: 61.6 us -> 55.8 us  [on_device(): lax.all_gather(jnp.concatenate([gate_own, up_own, gate_other, up_other, p...]
    dynamic_slice x0 -> x1, local copies, waits for them, and re-layouts: none -> 5.78 us  [halves(): own = lax.dynamic_slice_in_dim(x, dep * half, half, axis=1)]
    dot_general x4 -> x1, matrix products: 14.7 us -> 12.9 us  [on_device(): lax.dot_general(full[:, :2 * width], weights, transposed, preferred_eleme...]
  transfers between devices with their start and end apart: 6 -> 6, of which waited for: 6 -> 6; matrix products, arithmetic and copies ran while one was open for 9% -> 11% of each run, Pallas kernels for 0% -> 0%
where the time goes in v13:
time: 240 us; the launch traced here: 239 us
  waiting for transfers between devices  115 us (48%)
  matrix products  41.6 us (17%)
  blocking collectives  30.9 us (13%)
  starting transfers between devices  17.5 us (7%)
  between operations  14.2 us (6%)
  local copies, waits for them, and re-layouts  10.9 us (5%)
  other arithmetic  9.35 us (4%)
    all_gather x1, waiting for transfers between devices, on_device(): lax.all_gather(jnp.concatenate([gate_own, up_own, gate_other, up_other, p...  55.8 us
    all_to_all x1, blocking collectives, gather_col(): return lax.all_to_all(jnp.tile(block, (n_col, 1)), 'col', 0, 0, tiled=True)  30.9 us
    all_to_all x1, waiting for transfers between devices, gather_col(): return lax.all_to_all(jnp.tile(block, (n_col, 1)), 'col', 0, 0, tiled=True)  22.6 us
    dot_general x1, matrix products, on_device(): lax.dot_general(full[:, :2 * width], weights, transposed, preferred_eleme...  12.9 us
    reduce_scatter x1, waiting for transfers between devices, on_device(): lax.psum_scatter(jnp.concatenate([first, second], axis=1).astype(jnp.bflo...  10.6 us
    dot_general x2, matrix products, weight_grad(): lax.dot_general(gathered_partner, partner, contract, preferred_element_ty...  10.4 us
    all_to_all x1, waiting for transfers between devices, on_device(): parts = lax.all_to_all(term, 'col', 0, 0, tiled=True)  10.4 us
    ppermute x1, waiting for transfers between devices, on_device(): lax.ppermute(jnp.concatenate([gate_other, up_other], axis=1), 'dep', pair)  10.1 us
  transfers between devices with their start and end apart: 6, of which 6 were waited for; matrix products, arithmetic and copies ran while one was open for 11% of the time, Pallas kernels for 0%

profile of v13, /device:TPU:6, one launch (start us, length us, event | category | flops | bytes accessed | tf_op | source)
XLA Modules:
  0.0 239.1 jit_solution(14760640296373024874)
XLA Ops:
  7.2 0.0 reduce-scatter.2.cloned.1.call-start
  7.2 1.2 tile.4
  8.4 0.0 copy-start
  8.4 30.9 %all_to_all.23 = bf16[8,128,1024]{2,1,0:T(8,128)(2,1)S(1)} all-to-all(bf16[8,128,1024]{2,1,0:T(8,128)(2,1)S(1)} %tile.4), channel_id=1, replica_groups=mesh['row'=8,'col'=8,'dep'=2] {'col'}, dimensions={0} | all-to-all | bytes 4194304 | tf_op jit(solution)/shard_map/all_to_all | solution.py:23
  39.4 0.0 copy-start.2
  39.4 0.0 copy-done
  39.4 0.0 copy-start.1
  39.4 4.2 %convolution_convert_fusion = bf16[1024,1792]{1,0:T(8,128)(2,1)S(1)} fusion(bf16[1024,1024]{1,0:T(8,128)(2,1)S(1)} %bitcast.11, bf16[1024,1792]{1,0:T(8,128)(2,1)S(1)} %copy-done), kind=kOutput, calls=%fused_computation.10 | convolution fusion | flops 3759931392 | bytes 9437184 | tf_op jit(solution)/shard_map/dot_general | solution.py:28
  43.5 0.0 copy-done.2
  43.5 0.0 copy-done.1
  43.5 5.4 %convolution_convert_fusion.1 = bf16[1024,1792]{1,0:T(8,128)(2,1)} fusion(bf16[1024,1024]{1,0:T(8,128)(2,1)S(1)} %bitcast.12, bf16[1024,1792]{1,0:T(8,128)(2,1)S(1)} %copy-done.1), kind=kOutput, calls=%fused_computation.11 | convolution fusion | flops 3759931392 | bytes 9437184 | tf_op jit(solution)/shard_map/dot_general | solution.py:27
  48.9 5.5 %pad_maximum_fusion = bf16[1024,3584]{1,0:T(8,128)(2,1)} fusion(bf16[1024,1792]{1,0:T(8,128)(2,1)S(1)} %convolution_convert_fusion, bf16[1024,1792]{1,0:T(8,128)(2,1)} %convolution_convert_fusion.1), kind=kLoop, calls=%fused_computation.2 | loop fusion | flops 14680064 | bytes 14680064 | tf_op jit(solution)/shard_map/concatenate | solution.py:30
  54.5 0.0 copy-start.8
  54.5 0.0 reduce-scatter.2.cloned.1.call-update
  54.5 0.9 copy-done.8
  55.4 2.9 %collective-permute-start = (bf16[128,1024]{1,0:T(8,128)(2,1)S(1)}, bf16[128,1024]{1,0:T(8,128)(2,1)S(1)}, u32[]{:S(2)}, u32[]{:S(2)}) collective-permute-start(bf16[128,1024]{1,0:T(8,128)(2,1)S(1)} %copy-done.8), channel_id=1, source_target_pairs={{0,1},{1,0},{2,3},{3,2},{4,5},{5,4},{6,7},{7,6},{8,9},{9,8},{10,11... | collective-permute-start | bytes 786440 | tf_op jit(solution)/shard_map/ppermute | solution.py:25
  58.3 5.2 %collective-permute-done = bf16[128,1024]{1,0:T(8,128)(2,1)S(1)} collective-permute-done((bf16[128,1024]{1,0:T(8,128)(2,1)S(1)}, bf16[128,1024]{1,0:T(8,128)(2,1)S(1)}, u32[]{:S(2)}, u32[]{:S(2)}) %collective-permute-start) | collective-permute-done | bytes 262176 | tf_op jit(solution)/shard_map/ppermute | solution.py:25
  63.5 1.7 tile.5
  65.1 5.8 %all-to-all-start.1 = ((bf16[8,128,1024]{2,1,0:T(8,128)(2,1)}), bf16[8,128,1024]{2,1,0:T(8,128)(2,1)S(1)}, u32[]{:S(2)}, u32[]{:S(2)}) async-start(bf16[8,128,1024]{2,1,0:T(8,128)(2,1)} %tile.5), calls=%async_computation.2 | async-start | bytes 4194304 | tf_op jit(solution)/shard_map/all_to_all | solution.py:23
  70.9 0.0 copy-start.7
  70.9 0.0 all-gather.2.cloned.1.call-start
  70.9 22.6 %all-to-all-done.1 = bf16[8,128,1024]{2,1,0:T(8,128)(2,1)S(1)} async-done(((bf16[8,128,1024]{2,1,0:T(8,128)(2,1)}), bf16[8,128,1024]{2,1,0:T(8,128)(2,1)S(1)}, u32[]{:S(2)}, u32[]{:S(2)}) %all-to-all-start.1) | async-done | bytes 2097184 | tf_op jit(solution)/shard_map/all_to_all | solution.py:23
  93.5 0.0 copy-start.4
  93.5 10.6 %reduce-scatter.2.cloned.1.call-done = bf16[128,3584]{1,0:T(8,128)(2,1)} async-done(((bf16[1024,3584]{1,0:T(8,128)(2,1)}), bf16[128,3584]{1,0:T(8,128)(2,1)}) %reduce-scatter.2.cloned.1.call-update) | async-done | bytes 917520 | tf_op jit(solution)/shard_map/reduce_scatter | solution.py:29
  104.1 1.4 convert_element_type.51
  105.5 0.0 copy-done.7
  105.5 1.3 fusion.29
  106.8 0.0 copy-done.4
  106.9 0.1 constant_dynamic-update-slice_fusion.2
  106.9 0.1 constant_dynamic-update-slice_fusion.1
  107.0 3.1 %collective-permute-start.1 = (bf16[128,1792]{1,0:T(8,128)(2,1)S(1)}, bf16[128,1792]{1,0:T(8,128)(2,1)S(1)}, u32[]{:S(2)}, u32[]{:S(2)}) collective-permute-start(bf16[128,1792]{1,0:T(8,128)(2,1)S(1)} %pad_maximum_fusion.1), channel_id=1, source_target_pairs={{0,1},{1,0},{2,3},{3,2},{4,5},{5,4},{6,7},{7,6},{8,9},{9,8},{10,11... | collective-permute-start | bytes 1376264 | tf_op jit(solution)/shard_map/ppermute | solution.py:50
  110.1 10.1 %collective-permute-done.1 = bf16[128,1792]{1,0:T(8,128)(2,1)S(1)} collective-permute-done((bf16[128,1792]{1,0:T(8,128)(2,1)S(1)}, bf16[128,1792]{1,0:T(8,128)(2,1)S(1)}, u32[]{:S(2)}, u32[]{:S(2)}) %collective-permute-start.1) | collective-permute-done | bytes 458784 | tf_op jit(solution)/shard_map/ppermute | solution.py:50
  120.2 0.0 copy-start.6
  120.2 1.1 copy-done.6
  121.3 0.0 all-gather.2.cloned.1.call-update
  121.3 5.8 %constant_dynamic-slice_fusion.2 = (bf16[1024,896]{1,0:T(8,128)(2,1)S(1)}, bf16[1024,896]{1,0:T(8,128)(2,1)}, bf16[1024,896]{1,0:T(8,128)(2,1)}, bf16[1024,896]{1,0:T(8,128)(2,1)}) fusion(bf16[1024,1792]{1,0:T(8,128)(2,1)} %param.6, s32[]{:T(128)S(6)} %select_n.4, s32[]{:T(128)S(6)} %select_n.5, bf16[1024,1792]{1,0:T(8,128)(2,1)} %param.5), kind=kLoop, calls=%fused_computation.40 | loop fusion | bytes 14680072 | tf_op jit(solution)/shard_map/dynamic_slice | solution.py:8
  127.1 55.8 %all-gather.2.cloned.1.call-done = bf16[1024,5376]{1,0:T(8,128)(2,1)} async-done(((bf16[128,5376]{1,0:T(8,128)(2,1)}), bf16[1024,5376]{1,0:T(8,128)(2,1)}) %all-gather.2.cloned.1.call-update) | async-done | bytes 11010064 | tf_op jit(solution)/shard_map/all_gather | solution.py:52
  182.9 12.9 %fusion.9 = bf16[1024,1024]{1,0:T(8,128)(2,1)} fusion(bf16[1024,896]{1,0:T(8,128)(2,1)} %get-tuple-element.21, bf16[1024,896]{1,0:T(8,128)(2,1)} %get-tuple-element.25, bf16[1024,896]{1,0:T(8,128)(2,1)S(1)} %get-tuple-element.20, bf16[1024,896]{1,0:T(8,128)(2,1)} %get-tuple-element.26, bf16[1024,5376]{1,0:T(8,128)(2,1)} %all-gather.2.cloned.1.call-done), kind=kOutput, calls=%fused_computation.14 | convolution fusion | flops 7546601472 | bytes 16777216 | tf_op jit(solution)/shard_map/dot_general | solution.py:62
  195.8 5.7 %all-to-all-start.2 = ((bf16[8,128,1024]{2,1,0:T(8,128)(2,1)}), bf16[8,128,1024]{2,1,0:T(8,128)(2,1)S(1)}, u32[]{:S(2)}, u32[]{:S(2)}) async-start(bf16[8,128,1024]{2,1,0:T(8,128)(2,1)} %bitcast.17), calls=%async_computation.3 | async-start | bytes 4194304 | tf_op jit(solution)/shard_map/all_to_all | solution.py:67
  201.6 0.0 copy-start.3
  201.6 4.7 %fusion.16 = bf16[1024,896]{1,0:T(8,128)(2,1)S(1)} fusion(bf16[1024,1024]{1,0:T(8,128)(2,1)} %bitcast.13, bf16[1024,5376]{1,0:T(8,128)(2,1)} %all-gather.2.cloned.1.call-done), kind=kOutput, calls=%fused_computation.17 | convolution fusion | flops 1879048192 | bytes 5767168 | tf_op jit(solution)/shard_map/dot_general | solution.py:71
  206.2 0.0 copy-done.3
  206.2 0.0 copy-start.5
  206.2 4.1 %fusion.20 = bf16[1024,896]{1,0:T(8,128)(2,1)S(1)} fusion(bf16[1024,1024]{1,0:T(8,128)(2,1)S(1)} %bitcast.14, bf16[1024,5376]{1,0:T(8,128)(2,1)} %all-gather.2.cloned.1.call-done), kind=kOutput, calls=%fused_computation.21 | convolution fusion | flops 1879048192 | bytes 5767168 | tf_op jit(solution)/shard_map/dot_general | solution.py:71
  210.3 0.0 copy-done.5
  210.3 5.2 %add_convert_fusion.1 = bf16[1024,896]{1,0:T(8,128)(2,1)} fusion(bf16[1024,896]{1,0:T(8,128)(2,1)S(1)} %fusion.20, bf16[1024,1024]{1,0:T(8,128)(2,1)S(1)} %bitcast.15, bf16[1024,5376]{1,0:T(8,128)(2,1)} %all-gather.2.cloned.1.call-done), kind=kOutput, calls=%fused_computation.13 | convolution fusion | flops 1883635712 | bytes 7602176 | tf_op jit(solution)/shard_map/dot_general | solution.py:72
  215.6 5.2 %add_convert_fusion = bf16[1024,896]{1,0:T(8,128)(2,1)} fusion(bf16[1024,896]{1,0:T(8,128)(2,1)S(1)} %fusion.16, bf16[1024,1024]{1,0:T(8,128)(2,1)S(1)} %bitcast.16, bf16[1024,5376]{1,0:T(8,128)(2,1)} %all-gather.2.cloned.1.call-done), kind=kOutput, calls=%fused_computation.12 | convolution fusion | flops 1883635712 | bytes 7602176 | tf_op jit(solution)/shard_map/dot_general | solution.py:72
  220.8 10.4 %all-to-all-done.2 = bf16[8,128,1024]{2,1,0:T(8,128)(2,1)S(1)} async-done(((bf16[8,128,1024]{2,1,0:T(8,128)(2,1)}), bf16[8,128,1024]{2,1,0:T(8,128)(2,1)S(1)}, u32[]{:S(2)}, u32[]{:S(2)}) %all-to-all-start.2) | async-done | bytes 2097184 | tf_op jit(solution)/shard_map/all_to_all | solution.py:67
  231.2 1.1 reduce_sum.12
  (4 shorter events, 0.1 us)
Async XLA Ops:
  7.2 96.9 %reduce-scatter.2.cloned.1.call-start = ((), (), s32[]{:S(2)}) async-start(), calls=%async_computation.4 | async-start | bytes 8257536 | tf_op jit(solution)/shard_map/reduce_scatter | solution.py:29
  8.4 30.9 %copy-start = (bf16[1024,1792]{1,0:T(8,128)(2,1)S(1)}, bf16[1024,1792]{1,0:T(8,128)(2,1)}, u32[]{:S(2)}) copy-start(bf16[1024,1792]{1,0:T(8,128)(2,1)} %param.6) | copy-start | bytes 11010052
  39.4 4.2 %copy-start.2 = (bf16[8,128,1024]{2,1,0:T(8,128)(2,1)}, bf16[8,128,1024]{2,1,0:T(8,128)(2,1)S(1)}, u32[]{:S(2)}) copy-start(bf16[8,128,1024]{2,1,0:T(8,128)(2,1)S(1)} %all_to_all.23) | copy-start | bytes 6291460
  39.4 4.2 %copy-start.1 = (bf16[1024,1792]{1,0:T(8,128)(2,1)S(1)}, bf16[1024,1792]{1,0:T(8,128)(2,1)}, u32[]{:S(2)}) copy-start(bf16[1024,1792]{1,0:T(8,128)(2,1)} %param.5) | copy-start | bytes 11010052
  54.5 0.9 copy-start.8
  55.4 8.1 %collective-permute-start = (bf16[128,1024]{1,0:T(8,128)(2,1)S(1)}, bf16[128,1024]{1,0:T(8,128)(2,1)S(1)}, u32[]{:S(2)}, u32[]{:S(2)}) collective-permute-start(bf16[128,1024]{1,0:T(8,128)(2,1)S(1)} %copy-done.8), channel_id=1, source_target_pairs={{0,1},{1,0},{2,3},{3,2},{4,5},{5,4},{6,7},{7,6},{8,9},{9,8},{10,11... | collective-permute-start | bytes 786440 | tf_op jit(solution)/shard_map/ppermute | solution.py:25
  65.1 28.4 %all-to-all-start.1 = ((bf16[8,128,1024]{2,1,0:T(8,128)(2,1)}), bf16[8,128,1024]{2,1,0:T(8,128)(2,1)S(1)}, u32[]{:S(2)}, u32[]{:S(2)}) async-start(bf16[8,128,1024]{2,1,0:T(8,128)(2,1)} %tile.5), calls=%async_computation.2 | async-start | bytes 4194304 | tf_op jit(solution)/shard_map/all_to_all | solution.py:23
  70.9 34.5 %copy-start.7 = (bf16[128,1792]{1,0:T(8,128)(2,1)S(1)}, bf16[128,1792]{1,0:T(8,128)(2,1)}, u32[]{:S(2)}) copy-start(bf16[128,1792]{1,0:T(8,128)(2,1)} %param.7) | copy-start | bytes 1376260
  70.9 112.0 %all-gather.2.cloned.1.call-start = ((), (), s32[]{:S(2)}) async-start(), calls=%async_computation.5 | async-start | bytes 12386304 | tf_op jit(solution)/shard_map/all_gather | solution.py:52
  93.5 13.3 %copy-start.4 = (bf16[8,128,1024]{2,1,0:T(8,128)(2,1)}, bf16[8,128,1024]{2,1,0:T(8,128)(2,1)S(1)}, u32[]{:S(2)}) copy-start(bf16[8,128,1024]{2,1,0:T(8,128)(2,1)S(1)} %all-to-all-done.1) | copy-start | bytes 6291460
  107.0 13.2 %collective-permute-start.1 = (bf16[128,1792]{1,0:T(8,128)(2,1)S(1)}, bf16[128,1792]{1,0:T(8,128)(2,1)S(1)}, u32[]{:S(2)}, u32[]{:S(2)}) collective-permute-start(bf16[128,1792]{1,0:T(8,128)(2,1)S(1)} %pad_maximum_fusion.1), channel_id=1, source_target_pairs={{0,1},{1,0},{2,3},{3,2},{4,5},{5,4},{6,7},{7,6},{8,9},{9,8},{10,11... | collective-permute-start | bytes 1376264 | tf_op jit(solution)/shard_map/ppermute | solution.py:50
  120.2 1.1 copy-start.6
  195.8 35.3 %all-to-all-start.2 = ((bf16[8,128,1024]{2,1,0:T(8,128)(2,1)}), bf16[8,128,1024]{2,1,0:T(8,128)(2,1)S(1)}, u32[]{:S(2)}, u32[]{:S(2)}) async-start(bf16[8,128,1024]{2,1,0:T(8,128)(2,1)} %bitcast.17), calls=%async_computation.3 | async-start | bytes 4194304 | tf_op jit(solution)/shard_map/all_to_all | solution.py:67
  201.6 4.7 %copy-start.3 = (bf16[8,128,1024]{2,1,0:T(8,128)(2,1)S(1)}, bf16[8,128,1024]{2,1,0:T(8,128)(2,1)}, u32[]{:S(2)}) copy-start(bf16[8,128,1024]{2,1,0:T(8,128)(2,1)} %copy-done.2) | copy-start | bytes 6291460
  206.2 4.1 %copy-start.5 = (bf16[8,128,1024]{2,1,0:T(8,128)(2,1)S(1)}, bf16[8,128,1024]{2,1,0:T(8,128)(2,1)}, u32[]{:S(2)}) copy-start(bf16[8,128,1024]{2,1,0:T(8,128)(2,1)} %copy-done.4) | copy-start | bytes 6291460
Sparse Core Ops, SparseCore 0:
  54.6 49.4 reduce-scatter.1
  121.4 61.4 all-gather.1

commit v14 on v13

--- a/solution.py
+++ b/solution.py
@@ -37,18 +37,26 @@
     joined = joined.astype(jnp.float32)
     gate = joined[:, :width]
     up = joined[:, width:]
-    sigma = jax.nn.sigmoid(gate)
-    active = gate * sigma
-    hidden = (active * up).astype(jnp.bfloat16)
     upstream = cotangent.astype(jnp.float32)
-    grad_gate = (upstream * up * sigma * (1.0 + gate * (1.0 - sigma))).astype(jnp.bfloat16)
-    grad_up = (upstream * active).astype(jnp.bfloat16)
 
-    gate_own, gate_other = halves(grad_gate, dep, half)
-    up_own, up_other = halves(grad_up, dep, half)
-    partner_gate, partner_up = jnp.split(
-        lax.ppermute(jnp.concatenate([gate_other, up_other], axis=1), "dep", pair), 2, axis=1
+    def grads(gate, up, upstream):
+        sigma = jax.nn.sigmoid(gate)
+        active = gate * sigma
+        grad_gate = (upstream * up * sigma * (1.0 + gate * (1.0 - sigma))).astype(jnp.bfloat16)
+        return grad_gate, (upstream * active).astype(jnp.bfloat16)
+
+    gate_own, gate_other = halves(gate, dep, half)
+    up_own, up_other = halves(up, dep, half)
+    up_stream_own, up_stream_other = halves(upstream, dep, half)
+    grad_gate_other, grad_up_other = grads(gate_other, up_other, up_stream_other)
+    payload = jnp.concatenate([grad_gate_other, grad_up_other], axis=1)
+    payload, gate_own, up_own, up_stream_own, gate, up = lax.optimization_barrier(
+        (payload, gate_own, up_own, up_stream_own, gate, up)
     )
+    partner_gate, partner_up = jnp.split(lax.ppermute(payload, "dep", pair), 2, axis=1)
+    grad_gate_own, grad_up_own = grads(gate_own, up_own, up_stream_own)
+    hidden = (gate * jax.nn.sigmoid(gate) * up).astype(jnp.bfloat16)
+    gate_own, up_own, gate_other, up_other = grad_gate_own, grad_up_own, grad_gate_other, grad_up_other
     full = lax.all_gather(
         jnp.concatenate(
             [gate_own, up_own, gate_other, up_other, partner_gate, partner_up], axis=1

time: 240 us -> 239 us (level)
  waiting for transfers between devices: 115 us -> 111 us
  transfers between devices with their start and end apart: 6 -> 6, of which waited for: 6 -> 6; matrix products, arithmetic and copies ran while one was open for 11% -> 12% of each run, Pallas kernels for 0% -> 0%
where the time goes in v14:
time: 239 us; the launch traced here: 238 us
  waiting for transfers between devices  111 us (46%)
  matrix products  42.9 us (18%)
  blocking collectives  30.9 us (13%)
  starting transfers between devices  18.4 us (8%)
  between operations  14.2 us (6%)
  local copies, waits for them, and re-layouts  12.6 us (5%)
  other arithmetic  8.4 us (4%)
    all_gather x1, waiting for transfers between devices, on_device(): lax.all_gather(jnp.concatenate([gate_own, up_own, gate_other, up_other, p...  54.2 us
    all_to_all x1, blocking collectives, gather_col(): return lax.all_to_all(jnp.tile(block, (n_col, 1)), 'col', 0, 0, tiled=True)  30.9 us
    all_to_all x1, waiting for transfers between devices, gather_col(): return lax.all_to_all(jnp.tile(block, (n_col, 1)), 'col', 0, 0, tiled=True)  22.6 us
    dot_general x1, matrix products, on_device(): lax.dot_general(full[:, :2 * width], weights, transposed, preferred_eleme...  13.2 us
    dot_general x2, matrix products, weight_grad(): lax.dot_general(gathered_partner, partner, contract, preferred_element_ty...  11.6 us
    ppermute x1, waiting for transfers between devices, on_device(): lax.ppermute(payload, 'dep', pair)  9.66 us
    reduce_scatter x1, waiting for transfers between devices, on_device(): lax.psum_scatter(jnp.concatenate([first, second], axis=1).astype(jnp.bflo...  9.6 us
    all_to_all x1, waiting for transfers between devices, on_device(): parts = lax.all_to_all(term, 'col', 0, 0, tiled=True)  9.42 us
  transfers between devices with their start and end apart: 6, of which 6 were waited for; matrix products, arithmetic and copies ran while one was open for 12% of the time, Pallas kernels for 0%

profile of v14, /device:TPU:6, one launch (start us, length us, event | category | flops | bytes accessed | tf_op | source)
XLA Modules:
  0.0 238.1 jit_solution(402393057591845907)
XLA Ops:
  7.2 0.0 reduce-scatter.2.cloned.1.call-start
  7.2 1.2 tile.4
  8.4 0.0 copy-start
  8.4 30.9 %all_to_all.23 = bf16[8,128,1024]{2,1,0:T(8,128)(2,1)S(1)} all-to-all(bf16[8,128,1024]{2,1,0:T(8,128)(2,1)S(1)} %tile.4), channel_id=1, replica_groups=mesh['row'=8,'col'=8,'dep'=2] {'col'}, dimensions={0} | all-to-all | bytes 4194304 | tf_op jit(solution)/shard_map/all_to_all | solution.py:23
  39.4 0.0 copy-start.2
  39.4 0.0 copy-done
  39.4 0.0 copy-start.1
  39.4 4.2 %convolution_convert_fusion = bf16[1024,1792]{1,0:T(8,128)(2,1)S(1)} fusion(bf16[1024,1024]{1,0:T(8,128)(2,1)S(1)} %bitcast.11, bf16[1024,1792]{1,0:T(8,128)(2,1)S(1)} %copy-done), kind=kOutput, calls=%fused_computation.10 | convolution fusion | flops 3759931392 | bytes 9437184 | tf_op jit(solution)/shard_map/dot_general | solution.py:28
  43.5 0.0 copy-done.2
  43.5 0.0 copy-done.1
  43.5 5.4 %convolution_convert_fusion.1 = bf16[1024,1792]{1,0:T(8,128)(2,1)} fusion(bf16[1024,1024]{1,0:T(8,128)(2,1)S(1)} %bitcast.12, bf16[1024,1792]{1,0:T(8,128)(2,1)S(1)} %copy-done.1), kind=kOutput, calls=%fused_computation.11 | convolution fusion | flops 3759931392 | bytes 9437184 | tf_op jit(solution)/shard_map/dot_general | solution.py:27
  48.9 5.5 %pad_maximum_fusion = bf16[1024,3584]{1,0:T(8,128)(2,1)} fusion(bf16[1024,1792]{1,0:T(8,128)(2,1)S(1)} %convolution_convert_fusion, bf16[1024,1792]{1,0:T(8,128)(2,1)} %convolution_convert_fusion.1), kind=kLoop, calls=%fused_computation.2 | loop fusion | flops 14680064 | bytes 14680064 | tf_op jit(solution)/shard_map/concatenate | solution.py:30
  54.5 0.0 copy-start.6
  54.5 0.0 reduce-scatter.2.cloned.1.call-update
  54.5 0.9 copy-done.6
  55.4 2.9 %collective-permute-start = (bf16[128,1024]{1,0:T(8,128)(2,1)S(1)}, bf16[128,1024]{1,0:T(8,128)(2,1)S(1)}, u32[]{:S(2)}, u32[]{:S(2)}) collective-permute-start(bf16[128,1024]{1,0:T(8,128)(2,1)S(1)} %copy-done.6), channel_id=1, source_target_pairs={{0,1},{1,0},{2,3},{3,2},{4,5},{5,4},{6,7},{7,6},{8,9},{9,8},{10,11... | collective-permute-start | bytes 786440 | tf_op jit(solution)/shard_map/ppermute | solution.py:25
  58.3 5.2 %collective-permute-done = bf16[128,1024]{1,0:T(8,128)(2,1)S(1)} collective-permute-done((bf16[128,1024]{1,0:T(8,128)(2,1)S(1)}, bf16[128,1024]{1,0:T(8,128)(2,1)S(1)}, u32[]{:S(2)}, u32[]{:S(2)}) %collective-permute-start) | collective-permute-done | bytes 262176 | tf_op jit(solution)/shard_map/ppermute | solution.py:25
  63.5 1.7 tile.5
  65.1 0.0 copy-start.5
  65.1 6.6 %all-to-all-start.1 = ((bf16[8,128,1024]{2,1,0:T(8,128)(2,1)}), bf16[8,128,1024]{2,1,0:T(8,128)(2,1)}, u32[]{:S(2)}, u32[]{:S(2)}) async-start(bf16[8,128,1024]{2,1,0:T(8,128)(2,1)} %tile.5), calls=%async_computation.2 | async-start | bytes 4194304 | tf_op jit(solution)/shard_map/all_to_all | solution.py:23
  71.8 0.0 all-gather.2.cloned.1.call-start
  71.8 0.0 copy-done.5
  71.8 0.1 convert_element_type.57
  71.9 22.6 %all-to-all-done.1 = bf16[8,128,1024]{2,1,0:T(8,128)(2,1)} async-done(((bf16[8,128,1024]{2,1,0:T(8,128)(2,1)}), bf16[8,128,1024]{2,1,0:T(8,128)(2,1)}, u32[]{:S(2)}, u32[]{:S(2)}) %all-to-all-start.1) | async-done | bytes 2097184 | tf_op jit(solution)/shard_map/all_to_all | solution.py:23
  94.5 9.6 %reduce-scatter.2.cloned.1.call-done = bf16[128,3584]{1,0:T(8,128)(2,1)} async-done(((bf16[1024,3584]{1,0:T(8,128)(2,1)}), bf16[128,3584]{1,0:T(8,128)(2,1)}) %reduce-scatter.2.cloned.1.call-update) | async-done | bytes 917520 | tf_op jit(solution)/shard_map/reduce_scatter | solution.py:29
  104.1 1.3 fusion.29
  105.4 0.3 multiply_convert_fusion.4
  105.7 3.1 %collective-permute-start.1 = (bf16[128,1792]{1,0:T(8,128)(2,1)S(1)}, bf16[128,1792]{1,0:T(8,128)(2,1)S(1)}, u32[]{:S(2)}, u32[]{:S(2)}) collective-permute-start(bf16[128,1792]{1,0:T(8,128)(2,1)S(1)} %pad_maximum_fusion.1), channel_id=1, source_target_pairs={{0,1},{1,0},{2,3},{3,2},{4,5},{5,4},{6,7},{7,6},{8,9},{9,8},{10,11... | collective-permute-start | bytes 1376264 | tf_op jit(solution)/shard_map/ppermute | solution.py:56
  108.8 0.2 fusion.26
  109.0 0.2 fusion.27
  109.2 9.7 %collective-permute-done.1 = bf16[128,1792]{1,0:T(8,128)(2,1)S(1)} collective-permute-done((bf16[128,1792]{1,0:T(8,128)(2,1)S(1)}, bf16[128,1792]{1,0:T(8,128)(2,1)S(1)}, u32[]{:S(2)}, u32[]{:S(2)}) %collective-permute-start.1) | collective-permute-done | bytes 458784 | tf_op jit(solution)/shard_map/ppermute | solution.py:56
  118.9 0.0 copy-start.4
  118.9 1.1 copy-done.4
  120.0 0.0 all-gather.2.cloned.1.call-update
  120.0 6.4 %constant_dynamic-slice_fusion.1 = (bf16[1024,896]{1,0:T(8,128)(2,1)}, bf16[1024,896]{1,0:T(8,128)(2,1)}, bf16[1024,896]{1,0:T(8,128)(2,1)}, bf16[1024,896]{1,0:T(8,128)(2,1)}) fusion(bf16[1024,1792]{1,0:T(8,128)(2,1)} %param.6, s32[]{:T(128)S(6)} %select_n.5, s32[]{:T(128)S(6)} %select_n.4, bf16[1024,1792]{1,0:T(8,128)(2,1)} %param.5), kind=kLoop, calls=%fused_computation.37 | loop fusion | bytes 14680072 | tf_op jit(solution)/shard_map/dynamic_slice | solution.py:8
  126.4 1.0 multiply_convert_fusion
  127.4 54.2 %all-gather.2.cloned.1.call-done = bf16[1024,5376]{1,0:T(8,128)(2,1)} async-done(((bf16[128,5376]{1,0:T(8,128)(2,1)}), bf16[1024,5376]{1,0:T(8,128)(2,1)}) %all-gather.2.cloned.1.call-update) | async-done | bytes 11010064 | tf_op jit(solution)/shard_map/all_gather | solution.py:60
  181.6 13.2 %fusion.9 = bf16[1024,1024]{1,0:T(8,128)(2,1)} fusion(bf16[1024,896]{1,0:T(8,128)(2,1)} %get-tuple-element.29, bf16[1024,896]{1,0:T(8,128)(2,1)} %get-tuple-element.37, bf16[1024,896]{1,0:T(8,128)(2,1)} %get-tuple-element.28, bf16[1024,896]{1,0:T(8,128)(2,1)} %get-tuple-element.38, bf16[1024,5376]{1,0:T(8,128)(2,1)} %all-gather.2.cloned.1.call-done), kind=kOutput, calls=%fused_computation.14 | convolution fusion | flops 7546601472 | bytes 16777216 | tf_op jit(solution)/shard_map/dot_general | solution.py:70
  194.8 5.7 %all-to-all-start.2 = ((bf16[8,128,1024]{2,1,0:T(8,128)(2,1)}), bf16[8,128,1024]{2,1,0:T(8,128)(2,1)S(1)}, u32[]{:S(2)}, u32[]{:S(2)}) async-start(bf16[8,128,1024]{2,1,0:T(8,128)(2,1)} %bitcast.15), calls=%async_computation.3 | async-start | bytes 4194304 | tf_op jit(solution)/shard_map/all_to_all | solution.py:75
  200.5 0.0 copy-start.3
  200.5 4.7 %fusion.16 = bf16[1024,896]{1,0:T(8,128)(2,1)S(1)} fusion(bf16[1024,1024]{1,0:T(8,128)(2,1)} %bitcast.13, bf16[1024,5376]{1,0:T(8,128)(2,1)} %all-gather.2.cloned.1.call-done), kind=kOutput, calls=%fused_computation.17 | convolution fusion | flops 1879048192 | bytes 5767168 | tf_op jit(solution)/shard_map/dot_general | solution.py:79
  205.2 0.0 copy-done.3
  205.2 3.9 %fusion.20 = bf16[1024,896]{1,0:T(8,128)(2,1)S(1)} fusion(bf16[1024,1024]{1,0:T(8,128)(2,1)S(1)} %bitcast.14, bf16[1024,5376]{1,0:T(8,128)(2,1)} %all-gather.2.cloned.1.call-done), kind=kOutput, calls=%fused_computation.21 | convolution fusion | flops 1879048192 | bytes 5767168 | tf_op jit(solution)/shard_map/dot_general | solution.py:79
  209.2 5.8 %add_convert_fusion.1 = bf16[1024,896]{1,0:T(8,128)(2,1)} fusion(bf16[1024,896]{1,0:T(8,128)(2,1)S(1)} %fusion.20, bf16[1024,1024]{1,0:T(8,128)(2,1)} %bitcast.1, bf16[1024,5376]{1,0:T(8,128)(2,1)} %all-gather.2.cloned.1.call-done), kind=kOutput, calls=%fused_computation.13 | convolution fusion | flops 1883635712 | bytes 7602176 | tf_op jit(solution)/shard_map/dot_general | solution.py:80
  215.0 5.8 %add_convert_fusion = bf16[1024,896]{1,0:T(8,128)(2,1)} fusion(bf16[1024,896]{1,0:T(8,128)(2,1)S(1)} %fusion.16, bf16[1024,1024]{1,0:T(8,128)(2,1)} %bitcast.1, bf16[1024,5376]{1,0:T(8,128)(2,1)} %all-gather.2.cloned.1.call-done), kind=kOutput, calls=%fused_computation.12 | convolution fusion | flops 1883635712 | bytes 7602176 | tf_op jit(solution)/shard_map/dot_general | solution.py:80
  220.8 9.4 %all-to-all-done.2 = bf16[8,128,1024]{2,1,0:T(8,128)(2,1)S(1)} async-done(((bf16[8,128,1024]{2,1,0:T(8,128)(2,1)}), bf16[8,128,1024]{2,1,0:T(8,128)(2,1)S(1)}, u32[]{:S(2)}, u32[]{:S(2)}) %all-to-all-start.2) | async-done | bytes 2097184 | tf_op jit(solution)/shard_map/all_to_all | solution.py:75
  230.2 1.1 reduce_sum.12
  (4 shorter events, 0.1 us)
Async XLA Ops:
  7.2 96.9 %reduce-scatter.2.cloned.1.call-start = ((), (), s32[]{:S(2)}) async-start(), calls=%async_computation.4 | async-start | bytes 8257536 | tf_op jit(solution)/shard_map/reduce_scatter | solution.py:29
  8.4 30.9 %copy-start = (bf16[1024,1792]{1,0:T(8,128)(2,1)S(1)}, bf16[1024,1792]{1,0:T(8,128)(2,1)}, u32[]{:S(2)}) copy-start(bf16[1024,1792]{1,0:T(8,128)(2,1)} %param.6) | copy-start | bytes 11010052
  39.4 4.2 %copy-start.2 = (bf16[8,128,1024]{2,1,0:T(8,128)(2,1)}, bf16[8,128,1024]{2,1,0:T(8,128)(2,1)S(1)}, u32[]{:S(2)}) copy-start(bf16[8,128,1024]{2,1,0:T(8,128)(2,1)S(1)} %all_to_all.23) | copy-start | bytes 6291460
  39.4 4.2 %copy-start.1 = (bf16[1024,1792]{1,0:T(8,128)(2,1)S(1)}, bf16[1024,1792]{1,0:T(8,128)(2,1)}, u32[]{:S(2)}) copy-start(bf16[1024,1792]{1,0:T(8,128)(2,1)} %param.5) | copy-start | bytes 11010052
  54.5 0.9 copy-start.6
  55.4 8.1 %collective-permute-start = (bf16[128,1024]{1,0:T(8,128)(2,1)S(1)}, bf16[128,1024]{1,0:T(8,128)(2,1)S(1)}, u32[]{:S(2)}, u32[]{:S(2)}) collective-permute-start(bf16[128,1024]{1,0:T(8,128)(2,1)S(1)} %copy-done.6), channel_id=1, source_target_pairs={{0,1},{1,0},{2,3},{3,2},{4,5},{5,4},{6,7},{7,6},{8,9},{9,8},{10,11... | collective-permute-start | bytes 786440 | tf_op jit(solution)/shard_map/ppermute | solution.py:25
  65.1 6.7 %copy-start.5 = (bf16[128,1792]{1,0:T(8,128)(2,1)S(1)}, bf16[128,1792]{1,0:T(8,128)(2,1)}, u32[]{:S(2)}) copy-start(bf16[128,1792]{1,0:T(8,128)(2,1)} %param.7) | copy-start | bytes 1376260
  65.1 29.4 %all-to-all-start.1 = ((bf16[8,128,1024]{2,1,0:T(8,128)(2,1)}), bf16[8,128,1024]{2,1,0:T(8,128)(2,1)}, u32[]{:S(2)}, u32[]{:S(2)}) async-start(bf16[8,128,1024]{2,1,0:T(8,128)(2,1)} %tile.5), calls=%async_computation.2 | async-start | bytes 4194304 | tf_op jit(solution)/shard_map/all_to_all | solution.py:23
  71.8 109.9 %all-gather.2.cloned.1.call-start = ((), (), s32[]{:S(2)}) async-start(), calls=%async_computation.5 | async-start | bytes 12386304 | tf_op jit(solution)/shard_map/all_gather | solution.py:60
  105.7 13.2 %collective-permute-start.1 = (bf16[128,1792]{1,0:T(8,128)(2,1)S(1)}, bf16[128,1792]{1,0:T(8,128)(2,1)S(1)}, u32[]{:S(2)}, u32[]{:S(2)}) collective-permute-start(bf16[128,1792]{1,0:T(8,128)(2,1)S(1)} %pad_maximum_fusion.1), channel_id=1, source_target_pairs={{0,1},{1,0},{2,3},{3,2},{4,5},{5,4},{6,7},{7,6},{8,9},{9,8},{10,11... | collective-permute-start | bytes 1376264 | tf_op jit(solution)/shard_map/ppermute | solution.py:56
  118.9 1.1 copy-start.4
  194.8 35.3 %all-to-all-start.2 = ((bf16[8,128,1024]{2,1,0:T(8,128)(2,1)}), bf16[8,128,1024]{2,1,0:T(8,128)(2,1)S(1)}, u32[]{:S(2)}, u32[]{:S(2)}) async-start(bf16[8,128,1024]{2,1,0:T(8,128)(2,1)} %bitcast.15), calls=%async_computation.3 | async-start | bytes 4194304 | tf_op jit(solution)/shard_map/all_to_all | solution.py:75
  200.5 4.7 %copy-start.3 = (bf16[8,128,1024]{2,1,0:T(8,128)(2,1)S(1)}, bf16[8,128,1024]{2,1,0:T(8,128)(2,1)}, u32[]{:S(2)}) copy-start(bf16[8,128,1024]{2,1,0:T(8,128)(2,1)} %copy-done.2) | copy-start | bytes 6291460
Sparse Core Ops, SparseCore 0:
  54.6 49.4 reduce-scatter.1
  120.1 61.4 all-gather.1

commit v15 on v14

--- a/solution.py
+++ b/solution.py
@@ -1,6 +1,7 @@
 import jax
 import jax.numpy as jnp
 from jax import lax
+from jax.experimental.layout import Layout, with_layout_constraint
 from jax.sharding import PartitionSpec as P
 
 
@@ -66,10 +67,10 @@
 
     wg_own, wg_other = halves(gate_weight, dep, half)
     wu_own, wu_other = halves(up_weight, dep, half)
-    weights = jnp.concatenate([wg_own, wu_own, wg_other, wu_other], axis=1)
-    term = lax.dot_general(
-        full[:, :2 * width], weights, transposed, preferred_element_type=jnp.float32
+    weights = with_layout_constraint(
+        jnp.concatenate([wg_own, wu_own, wg_other, wu_other], axis=1).T, Layout((0, 1))
     )
+    term = jnp.dot(full[:, :2 * width], weights, preferred_element_type=jnp.float32)
     term = term.astype(jnp.bfloat16).reshape(n_col, -1, term.shape[1])
     term, gathered, gathered_partner = lax.optimization_barrier((term, gathered, gathered_partner))
     parts = lax.all_to_all(term, "col", 0, 0, tiled=True)

time: 239 us -> 239 us (level)
  waiting for transfers between devices: 111 us -> 95.4 us
  local copies, waits for them, and re-layouts: 12.6 us -> 28 us
    unnamed x16 -> x20, local copies, waits for them, and re-layouts: 2.09 us -> 17.5 us
    all_gather x1, waiting for transfers between devices: 54.2 us -> 38.9 us  [on_device(): lax.all_gather(jnp.concatenate([gate_own, up_own, gate_other, up_other, p...]
  transfers between devices with their start and end apart: 6 -> 6, of which waited for: 6 -> 6; matrix products, arithmetic and copies ran while one was open for 12% -> 19% of each run, Pallas kernels for 0% -> 0%
where the time goes in v15:
time: 239 us; the launch traced here: 238 us
  waiting for transfers between devices  95.4 us (40%)
  matrix products  43 us (18%)
  blocking collectives  30.9 us (13%)
  local copies, waits for them, and re-layouts  28 us (12%)
  starting transfers between devices  18.4 us (8%)
  between operations  14.2 us (6%)
  other arithmetic  8.4 us (4%)
    all_gather x1, waiting for transfers between devices, on_device(): lax.all_gather(jnp.concatenate([gate_own, up_own, gate_other, up_other, p...  38.9 us
    all_to_all x1, blocking collectives, gather_col(): return lax.all_to_all(jnp.tile(block, (n_col, 1)), 'col', 0, 0, tiled=True)  30.9 us
    all_to_all x1, waiting for transfers between devices, gather_col(): return lax.all_to_all(jnp.tile(block, (n_col, 1)), 'col', 0, 0, tiled=True)  22.6 us
    unnamed x20, local copies, waits for them, and re-layouts  17.5 us
    dot_general x1, matrix products, on_device(): jnp.dot(full[:, :2 * width], weights, preferred_element_type=jnp.float32)  13.3 us
    dot_general x2, matrix products, weight_grad(): lax.dot_general(gathered_partner, partner, contract, preferred_element_ty...  11.6 us
    ppermute x1, waiting for transfers between devices, on_device(): lax.ppermute(payload, 'dep', pair)  9.66 us
    reduce_scatter x1, waiting for transfers between devices, on_device(): lax.psum_scatter(jnp.concatenate([first, second], axis=1).astype(jnp.bflo...  9.6 us
  transfers between devices with their start and end apart: 6, of which 6 were waited for; matrix products, arithmetic and copies ran while one was open for 19% of the time, Pallas kernels for 0%

profile of v15, /device:TPU:6, one launch (start us, length us, event | category | flops | bytes accessed | tf_op | source)
XLA Modules:
  0.0 238.2 jit_solution(7619890547766901413)
XLA Ops:
  7.2 0.0 reduce-scatter.2.cloned.1.call-start
  7.2 1.2 tile.4
  8.4 0.0 copy-start
  8.4 30.9 %all_to_all.23 = bf16[8,128,1024]{2,1,0:T(8,128)(2,1)S(1)} all-to-all(bf16[8,128,1024]{2,1,0:T(8,128)(2,1)S(1)} %tile.4), channel_id=1, replica_groups=mesh['row'=8,'col'=8,'dep'=2] {'col'}, dimensions={0} | all-to-all | bytes 4194304 | tf_op jit(solution)/shard_map/all_to_all | solution.py:24
  39.4 0.0 copy-start.2
  39.4 0.0 copy-done
  39.4 0.0 copy-start.1
  39.4 4.2 %convolution_convert_fusion = bf16[1024,1792]{1,0:T(8,128)(2,1)S(1)} fusion(bf16[1024,1024]{1,0:T(8,128)(2,1)S(1)} %bitcast.16, bf16[1024,1792]{1,0:T(8,128)(2,1)S(1)} %copy-done), kind=kOutput, calls=%fused_computation.10 | convolution fusion | flops 3759931392 | bytes 9437184 | tf_op jit(solution)/shard_map/dot_general | solution.py:29
  43.5 0.0 copy-done.2
  43.5 0.0 copy-done.1
  43.5 5.4 %convolution_convert_fusion.1 = bf16[1024,1792]{1,0:T(8,128)(2,1)} fusion(bf16[1024,1024]{1,0:T(8,128)(2,1)S(1)} %bitcast.17, bf16[1024,1792]{1,0:T(8,128)(2,1)S(1)} %copy-done.1), kind=kOutput, calls=%fused_computation.11 | convolution fusion | flops 3759931392 | bytes 9437184 | tf_op jit(solution)/shard_map/dot_general | solution.py:28
  48.9 5.5 %pad_maximum_fusion = bf16[1024,3584]{1,0:T(8,128)(2,1)} fusion(bf16[1024,1792]{1,0:T(8,128)(2,1)S(1)} %convolution_convert_fusion, bf16[1024,1792]{1,0:T(8,128)(2,1)} %convolution_convert_fusion.1), kind=kLoop, calls=%fused_computation.2 | loop fusion | flops 14680064 | bytes 14680064 | tf_op jit(solution)/shard_map/concatenate | solution.py:31
  54.5 0.0 copy-start.6
  54.5 0.0 reduce-scatter.2.cloned.1.call-update
  54.5 0.9 copy-done.6
  55.4 2.9 %collective-permute-start = (bf16[128,1024]{1,0:T(8,128)(2,1)S(1)}, bf16[128,1024]{1,0:T(8,128)(2,1)S(1)}, u32[]{:S(2)}, u32[]{:S(2)}) collective-permute-start(bf16[128,1024]{1,0:T(8,128)(2,1)S(1)} %copy-done.6), channel_id=1, source_target_pairs={{0,1},{1,0},{2,3},{3,2},{4,5},{5,4},{6,7},{7,6},{8,9},{9,8},{10,11... | collective-permute-start | bytes 786440 | tf_op jit(solution)/shard_map/ppermute | solution.py:26
  58.3 5.2 %collective-permute-done = bf16[128,1024]{1,0:T(8,128)(2,1)S(1)} collective-permute-done((bf16[128,1024]{1,0:T(8,128)(2,1)S(1)}, bf16[128,1024]{1,0:T(8,128)(2,1)S(1)}, u32[]{:S(2)}, u32[]{:S(2)}) %collective-permute-start) | collective-permute-done | bytes 262176 | tf_op jit(solution)/shard_map/ppermute | solution.py:26
  63.5 1.7 tile.5
  65.1 0.0 copy-start.5
  65.1 6.6 %all-to-all-start.1 = ((bf16[8,128,1024]{2,1,0:T(8,128)(2,1)}), bf16[8,128,1024]{2,1,0:T(8,128)(2,1)}, u32[]{:S(2)}, u32[]{:S(2)}) async-start(bf16[8,128,1024]{2,1,0:T(8,128)(2,1)} %tile.5), calls=%async_computation.2 | async-start | bytes 4194304 | tf_op jit(solution)/shard_map/all_to_all | solution.py:24
  71.8 0.0 all-gather.2.cloned.1.call-start
  71.8 0.0 copy-done.5
  71.8 0.1 convert_element_type.57
  71.9 22.6 %all-to-all-done.1 = bf16[8,128,1024]{2,1,0:T(8,128)(2,1)} async-done(((bf16[8,128,1024]{2,1,0:T(8,128)(2,1)}), bf16[8,128,1024]{2,1,0:T(8,128)(2,1)}, u32[]{:S(2)}, u32[]{:S(2)}) %all-to-all-start.1) | async-done | bytes 2097184 | tf_op jit(solution)/shard_map/all_to_all | solution.py:24
  94.5 9.6 %reduce-scatter.2.cloned.1.call-done = bf16[128,3584]{1,0:T(8,128)(2,1)} async-done(((bf16[1024,3584]{1,0:T(8,128)(2,1)}), bf16[128,3584]{1,0:T(8,128)(2,1)}) %reduce-scatter.2.cloned.1.call-update) | async-done | bytes 917520 | tf_op jit(solution)/shard_map/reduce_scatter | solution.py:30
  104.1 1.3 fusion.26
  105.4 0.3 multiply_convert_fusion.4
  105.7 3.1 %collective-permute-start.1 = (bf16[128,1792]{1,0:T(8,128)(2,1)S(1)}, bf16[128,1792]{1,0:T(8,128)(2,1)S(1)}, u32[]{:S(2)}, u32[]{:S(2)}) collective-permute-start(bf16[128,1792]{1,0:T(8,128)(2,1)S(1)} %pad_maximum_fusion.1), channel_id=1, source_target_pairs={{0,1},{1,0},{2,3},{3,2},{4,5},{5,4},{6,7},{7,6},{8,9},{9,8},{10,11... | collective-permute-start | bytes 1376264 | tf_op jit(solution)/shard_map/ppermute | solution.py:57
  108.8 0.2 fusion.23
  109.0 0.2 fusion.24
  109.2 9.7 %collective-permute-done.1 = bf16[128,1792]{1,0:T(8,128)(2,1)S(1)} collective-permute-done((bf16[128,1792]{1,0:T(8,128)(2,1)S(1)}, bf16[128,1792]{1,0:T(8,128)(2,1)S(1)}, u32[]{:S(2)}, u32[]{:S(2)}) %collective-permute-start.1) | collective-permute-done | bytes 458784 | tf_op jit(solution)/shard_map/ppermute | solution.py:57
  118.9 0.0 copy-start.4
  118.9 1.1 copy-done.4
  120.0 0.0 all-gather.2.cloned.1.call-update
  120.1 6.4 %constant_dynamic-slice_fusion.1 = (bf16[1024,896]{1,0:T(8,128)(2,1)}, bf16[1024,896]{1,0:T(8,128)(2,1)}, bf16[1024,896]{1,0:T(8,128)(2,1)}, bf16[1024,896]{1,0:T(8,128)(2,1)}) fusion(bf16[1024,1792]{1,0:T(8,128)(2,1)} %param.6, s32[]{:T(128)S(6)} %select_n.5, s32[]{:T(128)S(6)} %select_n.4, bf16[1024,1792]{1,0:T(8,128)(2,1)} %param.5), kind=kLoop, calls=%fused_computation.37 | loop fusion | bytes 14680072 | tf_op jit(solution)/shard_map/dynamic_slice | solution.py:9
  126.4 3.8 %copy.13 = bf16[1024,896]{0,1:T(8,128)(2,1)} copy(bf16[1024,896]{1,0:T(8,128)(2,1)} %get-tuple-element.28) | data formatting | bytes 3670016
  130.3 3.9 %copy.15 = bf16[1024,896]{0,1:T(8,128)(2,1)} copy(bf16[1024,896]{1,0:T(8,128)(2,1)} %get-tuple-element.29) | data formatting | bytes 3670016
  134.2 3.8 %copy.14 = bf16[1024,896]{0,1:T(8,128)(2,1)} copy(bf16[1024,896]{1,0:T(8,128)(2,1)} %get-tuple-element.37) | data formatting | bytes 3670016
  138.0 3.8 %copy.12 = bf16[1024,896]{0,1:T(8,128)(2,1)} copy(bf16[1024,896]{1,0:T(8,128)(2,1)} %get-tuple-element.38) | data formatting | bytes 3670016
  141.8 1.0 multiply_convert_fusion
  142.8 38.9 %all-gather.2.cloned.1.call-done = bf16[1024,5376]{1,0:T(8,128)(2,1)} async-done(((bf16[128,5376]{1,0:T(8,128)(2,1)}), bf16[1024,5376]{1,0:T(8,128)(2,1)}) %all-gather.2.cloned.1.call-update) | async-done | bytes 11010064 | tf_op jit(solution)/shard_map/all_gather | solution.py:61
  181.7 13.3 %fusion.8 = bf16[1024,1024]{1,0:T(8,128)(2,1)} fusion(bf16[1024,896]{0,1:T(8,128)(2,1)} %copy.15, bf16[1024,896]{0,1:T(8,128)(2,1)} %copy.14, bf16[1024,896]{0,1:T(8,128)(2,1)} %copy.13, bf16[1024,896]{0,1:T(8,128)(2,1)} %copy.12, bf16[1024,5376]{1,0:T(8,128)(2,1)} %all-gather.2.cloned.1.call-done), kind=kOutput, calls=%fused_computation.14 | convolution fusion | flops 7546601472 | bytes 16777216 | tf_op jit(solution)/shard_map/dot_general | solution.py:73
  194.9 5.7 %all-to-all-start.2 = ((bf16[8,128,1024]{2,1,0:T(8,128)(2,1)}), bf16[8,128,1024]{2,1,0:T(8,128)(2,1)S(1)}, u32[]{:S(2)}, u32[]{:S(2)}) async-start(bf16[8,128,1024]{2,1,0:T(8,128)(2,1)} %bitcast.20), calls=%async_computation.3 | async-start | bytes 4194304 | tf_op jit(solution)/shard_map/all_to_all | solution.py:76
  200.7 0.0 copy-start.3
  200.7 4.7 %fusion.13 = bf16[1024,896]{1,0:T(8,128)(2,1)S(1)} fusion(bf16[1024,1024]{1,0:T(8,128)(2,1)} %bitcast.18, bf16[1024,5376]{1,0:T(8,128)(2,1)} %all-gather.2.cloned.1.call-done), kind=kOutput, calls=%fused_computation.17 | convolution fusion | flops 1879048192 | bytes 5767168 | tf_op jit(solution)/shard_map/dot_general | solution.py:80
  205.3 0.0 copy-done.3
  205.3 3.9 %fusion.17 = bf16[1024,896]{1,0:T(8,128)(2,1)S(1)} fusion(bf16[1024,1024]{1,0:T(8,128)(2,1)S(1)} %bitcast.19, bf16[1024,5376]{1,0:T(8,128)(2,1)} %all-gather.2.cloned.1.call-done), kind=kOutput, calls=%fused_computation.21 | convolution fusion | flops 1879048192 | bytes 5767168 | tf_op jit(solution)/shard_map/dot_general | solution.py:80
  209.3 5.8 %add_convert_fusion.1 = bf16[1024,896]{1,0:T(8,128)(2,1)} fusion(bf16[1024,896]{1,0:T(8,128)(2,1)S(1)} %fusion.17, bf16[1024,1024]{1,0:T(8,128)(2,1)} %bitcast.1, bf16[1024,5376]{1,0:T(8,128)(2,1)} %all-gather.2.cloned.1.call-done), kind=kOutput, calls=%fused_computation.13 | convolution fusion | flops 1883635712 | bytes 7602176 | tf_op jit(solution)/shard_map/dot_general | solution.py:81
  215.1 5.8 %add_convert_fusion = bf16[1024,896]{1,0:T(8,128)(2,1)} fusion(bf16[1024,896]{1,0:T(8,128)(2,1)S(1)} %fusion.13, bf16[1024,1024]{1,0:T(8,128)(2,1)} %bitcast.1, bf16[1024,5376]{1,0:T(8,128)(2,1)} %all-gather.2.cloned.1.call-done), kind=kOutput, calls=%fused_computation.12 | convolution fusion | flops 1883635712 | bytes 7602176 | tf_op jit(solution)/shard_map/dot_general | solution.py:81
  220.9 9.4 %all-to-all-done.2 = bf16[8,128,1024]{2,1,0:T(8,128)(2,1)S(1)} async-done(((bf16[8,128,1024]{2,1,0:T(8,128)(2,1)}), bf16[8,128,1024]{2,1,0:T(8,128)(2,1)S(1)}, u32[]{:S(2)}, u32[]{:S(2)}) %all-to-all-start.2) | async-done | bytes 2097184 | tf_op jit(solution)/shard_map/all_to_all | solution.py:76
  230.3 1.1 reduce_sum.12
  (4 shorter events, 0.1 us)
Async XLA Ops:
  7.2 96.9 %reduce-scatter.2.cloned.1.call-start = ((), (), s32[]{:S(2)}) async-start(), calls=%async_computation.4 | async-start | bytes 8257536 | tf_op jit(solution)/shard_map/reduce_scatter | solution.py:30
  8.4 30.9 %copy-start = (bf16[1024,1792]{1,0:T(8,128)(2,1)S(1)}, bf16[1024,1792]{1,0:T(8,128)(2,1)}, u32[]{:S(2)}) copy-start(bf16[1024,1792]{1,0:T(8,128)(2,1)} %param.6) | copy-start | bytes 11010052
  39.4 4.2 %copy-start.2 = (bf16[8,128,1024]{2,1,0:T(8,128)(2,1)}, bf16[8,128,1024]{2,1,0:T(8,128)(2,1)S(1)}, u32[]{:S(2)}) copy-start(bf16[8,128,1024]{2,1,0:T(8,128)(2,1)S(1)} %all_to_all.23) | copy-start | bytes 6291460
  39.4 4.2 %copy-start.1 = (bf16[1024,1792]{1,0:T(8,128)(2,1)S(1)}, bf16[1024,1792]{1,0:T(8,128)(2,1)}, u32[]{:S(2)}) copy-start(bf16[1024,1792]{1,0:T(8,128)(2,1)} %param.5) | copy-start | bytes 11010052
  54.5 0.9 copy-start.6
  55.4 8.1 %collective-permute-start = (bf16[128,1024]{1,0:T(8,128)(2,1)S(1)}, bf16[128,1024]{1,0:T(8,128)(2,1)S(1)}, u32[]{:S(2)}, u32[]{:S(2)}) collective-permute-start(bf16[128,1024]{1,0:T(8,128)(2,1)S(1)} %copy-done.6), channel_id=1, source_target_pairs={{0,1},{1,0},{2,3},{3,2},{4,5},{5,4},{6,7},{7,6},{8,9},{9,8},{10,11... | collective-permute-start | bytes 786440 | tf_op jit(solution)/shard_map/ppermute | solution.py:26
  65.1 6.7 %copy-start.5 = (bf16[128,1792]{1,0:T(8,128)(2,1)S(1)}, bf16[128,1792]{1,0:T(8,128)(2,1)}, u32[]{:S(2)}) copy-start(bf16[128,1792]{1,0:T(8,128)(2,1)} %param.7) | copy-start | bytes 1376260
  65.1 29.4 %all-to-all-start.1 = ((bf16[8,128,1024]{2,1,0:T(8,128)(2,1)}), bf16[8,128,1024]{2,1,0:T(8,128)(2,1)}, u32[]{:S(2)}, u32[]{:S(2)}) async-start(bf16[8,128,1024]{2,1,0:T(8,128)(2,1)} %tile.5), calls=%async_computation.2 | async-start | bytes 4194304 | tf_op jit(solution)/shard_map/all_to_all | solution.py:24
  71.8 109.9 %all-gather.2.cloned.1.call-start = ((), (), s32[]{:S(2)}) async-start(), calls=%async_computation.5 | async-start | bytes 12386304 | tf_op jit(solution)/shard_map/all_gather | solution.py:61
  105.7 13.2 %collective-permute-start.1 = (bf16[128,1792]{1,0:T(8,128)(2,1)S(1)}, bf16[128,1792]{1,0:T(8,128)(2,1)S(1)}, u32[]{:S(2)}, u32[]{:S(2)}) collective-permute-start(bf16[128,1792]{1,0:T(8,128)(2,1)S(1)} %pad_maximum_fusion.1), channel_id=1, source_target_pairs={{0,1},{1,0},{2,3},{3,2},{4,5},{5,4},{6,7},{7,6},{8,9},{9,8},{10,11... | collective-permute-start | bytes 1376264 | tf_op jit(solution)/shard_map/ppermute | solution.py:57
  118.9 1.1 copy-start.4
  194.9 35.3 %all-to-all-start.2 = ((bf16[8,128,1024]{2,1,0:T(8,128)(2,1)}), bf16[8,128,1024]{2,1,0:T(8,128)(2,1)S(1)}, u32[]{:S(2)}, u32[]{:S(2)}) async-start(bf16[8,128,1024]{2,1,0:T(8,128)(2,1)} %bitcast.20), calls=%async_computation.3 | async-start | bytes 4194304 | tf_op jit(solution)/shard_map/all_to_all | solution.py:76
  200.7 4.7 %copy-start.3 = (bf16[8,128,1024]{2,1,0:T(8,128)(2,1)S(1)}, bf16[8,128,1024]{2,1,0:T(8,128)(2,1)}, u32[]{:S(2)}) copy-start(bf16[8,128,1024]{2,1,0:T(8,128)(2,1)} %copy-done.2) | copy-start | bytes 6291460
Sparse Core Ops, SparseCore 0:
  54.6 49.4 reduce-scatter.1
  120.2 61.4 all-gather.1

commit v16 on v14

--- a/solution.py
+++ b/solution.py
@@ -58,17 +58,22 @@
     hidden = (gate * jax.nn.sigmoid(gate) * up).astype(jnp.bfloat16)
     gate_own, up_own, gate_other, up_other = grad_gate_own, grad_up_own, grad_gate_other, grad_up_other
     full = lax.all_gather(
-        jnp.concatenate(
-            [gate_own, up_own, gate_other, up_other, partner_gate, partner_up], axis=1
-        ),
-        "row", axis=0, tiled=True,
+        jnp.stack([
+            jnp.concatenate([gate_own, up_own], axis=1),
+            jnp.concatenate([gate_other, up_other], axis=1),
+            jnp.concatenate([partner_gate, partner_up], axis=1),
+        ]),
+        "row", axis=1, tiled=True,
     )
 
     wg_own, wg_other = halves(gate_weight, dep, half)
     wu_own, wu_other = halves(up_weight, dep, half)
-    weights = jnp.concatenate([wg_own, wu_own, wg_other, wu_other], axis=1)
     term = lax.dot_general(
-        full[:, :2 * width], weights, transposed, preferred_element_type=jnp.float32
+        full[0], jnp.concatenate([wg_own, wu_own], axis=1), transposed,
+        preferred_element_type=jnp.float32,
+    ) + lax.dot_general(
+        full[1], jnp.concatenate([wg_other, wu_other], axis=1), transposed,
+        preferred_element_type=jnp.float32,
     )
     term = term.astype(jnp.bfloat16).reshape(n_col, -1, term.shape[1])
     term, gathered, gathered_partner = lax.optimization_barrier((term, gathered, gathered_partner))
@@ -85,8 +90,8 @@
             + theirs.astype(jnp.bfloat16).astype(jnp.float32)
         ).astype(jnp.bfloat16)
 
-    sum_gate = weight_grad(full[:, :half], full[:, 2 * width:2 * width + half])
-    sum_up = weight_grad(full[:, half:width], full[:, 2 * width + half:])
+    sum_gate = weight_grad(full[0][:, :half], full[2][:, :half])
+    sum_up = weight_grad(full[0][:, half:], full[2][:, half:])
     return (hidden, grad_tokens, sum_gate, sum_up)
 
 

time: 239 us -> 240 us (level)
  matrix products: 42.9 us -> 39.4 us
  local copies, waits for them, and re-layouts: 12.6 us -> 15.3 us
    squeeze x0 -> x1, local copies, waits for them, and re-layouts: none -> 3.63 us  [on_device(): full[0]]
    dot_general x2, matrix products: 11.6 us -> 8.17 us  [weight_grad(): lax.dot_general(gathered_partner, partner, contract, preferred_element_ty...]
    dot_general x1 -> x2, matrix products: 13.2 us -> 14.2 us  [the longest x1 7.24 us: on_device(): lax.dot_general(full[1], jnp.concatenate([wg_other, wu_other], axis=1), t...]
where the time goes in v16:
time: 240 us; the launch traced here: 239 us
  waiting for transfers between devices  112 us (47%)
  matrix products  39.4 us (16%)
  blocking collectives  30.7 us (13%)
  starting transfers between devices  18.3 us (8%)
  local copies, waits for them, and re-layouts  15.3 us (6%)
  between operations  14.2 us (6%)
  other arithmetic  9.64 us (4%)
    all_gather x1, waiting for transfers between devices, on_device(): lax.all_gather(jnp.stack([jnp.concatenate([gate_own, up_own], axis=1), jn...  54.2 us
    all_to_all x1, blocking collectives, gather_col(): return lax.all_to_all(jnp.tile(block, (n_col, 1)), 'col', 0, 0, tiled=True)  30.7 us
    all_to_all x1, waiting for transfers between devices, gather_col(): return lax.all_to_all(jnp.tile(block, (n_col, 1)), 'col', 0, 0, tiled=True)  22.6 us
    all_to_all x1, waiting for transfers between devices, on_device(): parts = lax.all_to_all(term, 'col', 0, 0, tiled=True)  10.3 us
    ppermute x1, waiting for transfers between devices, on_device(): lax.ppermute(payload, 'dep', pair)  9.75 us
    reduce_scatter x1, waiting for transfers between devices, on_device(): lax.psum_scatter(jnp.concatenate([first, second], axis=1).astype(jnp.bflo...  9.67 us
    dot_general x2, matrix products, weight_grad(): lax.dot_general(gathered_partner, partner, contract, preferred_element_ty...  8.17 us
    dot_general x2, matrix products, weight_grad(): lax.dot_general(gathered, own, contract, preferred_element_type=jnp.float32)  7.47 us
  transfers between devices with their start and end apart: 6, of which 6 were waited for; matrix products, arithmetic and copies ran while one was open for 12% of the time, Pallas kernels for 0%

profile of v16, /device:TPU:6, one launch (start us, length us, event | category | flops | bytes accessed | tf_op | source)
XLA Modules:
  0.0 239.1 jit_solution(14657623888860640853)
XLA Ops:
  7.2 0.0 reduce-scatter.2.cloned.1.call-start
  7.2 0.0 copy-start
  7.2 1.4 tile.4
  8.6 30.7 %all_to_all.23 = bf16[8,128,1024]{2,1,0:T(8,128)(2,1)S(1)} all-to-all(bf16[8,128,1024]{2,1,0:T(8,128)(2,1)S(1)} %tile.4), channel_id=1, replica_groups=mesh['row'=8,'col'=8,'dep'=2] {'col'}, dimensions={0} | all-to-all | bytes 4194304 | tf_op jit(solution)/shard_map/all_to_all | solution.py:23
  39.2 0.0 copy-start.2
  39.2 0.0 copy-done
  39.2 0.0 copy-start.1
  39.2 4.1 %convolution_convert_fusion = bf16[1024,1792]{1,0:T(8,128)(2,1)S(1)} fusion(bf16[1024,1024]{1,0:T(8,128)(2,1)S(1)} %bitcast.26, bf16[1024,1792]{1,0:T(8,128)(2,1)S(1)} %copy-done), kind=kOutput, calls=%fused_computation.2 | convolution fusion | flops 3759931392 | bytes 9437184 | tf_op jit(solution)/shard_map/dot_general | solution.py:28
  43.4 0.0 copy-done.2
  43.4 0.0 copy-done.1
  43.4 5.4 %convolution_convert_fusion.1 = bf16[1024,1792]{1,0:T(8,128)(2,1)} fusion(bf16[1024,1024]{1,0:T(8,128)(2,1)S(1)} %bitcast.27, bf16[1024,1792]{1,0:T(8,128)(2,1)S(1)} %copy-done.1), kind=kOutput, calls=%fused_computation.3 | convolution fusion | flops 3759931392 | bytes 9437184 | tf_op jit(solution)/shard_map/dot_general | solution.py:27
  48.8 5.6 %pad_maximum_fusion = bf16[1024,3584]{1,0:T(8,128)(2,1)} fusion(bf16[1024,1792]{1,0:T(8,128)(2,1)S(1)} %convolution_convert_fusion, bf16[1024,1792]{1,0:T(8,128)(2,1)} %convolution_convert_fusion.1), kind=kLoop, calls=%fused_computation | loop fusion | flops 14680064 | bytes 14680064 | tf_op jit(solution)/shard_map/concatenate | solution.py:30
  54.4 0.0 copy-start.7
  54.4 0.0 reduce-scatter.2.cloned.1.call-update
  54.4 0.9 copy-done.7
  55.3 0.0 copy-start.6
  55.3 2.9 %collective-permute-start = (bf16[128,1024]{1,0:T(8,128)(2,1)S(1)}, bf16[128,1024]{1,0:T(8,128)(2,1)S(1)}, u32[]{:S(2)}, u32[]{:S(2)}) collective-permute-start(bf16[128,1024]{1,0:T(8,128)(2,1)S(1)} %copy-done.7), channel_id=1, source_target_pairs={{0,1},{1,0},{2,3},{3,2},{4,5},{5,4},{6,7},{7,6},{8,9},{9,8},{10,11... | collective-permute-start | bytes 786440 | tf_op jit(solution)/shard_map/ppermute | solution.py:25
  58.2 5.2 %collective-permute-done = bf16[128,1024]{1,0:T(8,128)(2,1)S(1)} collective-permute-done((bf16[128,1024]{1,0:T(8,128)(2,1)S(1)}, bf16[128,1024]{1,0:T(8,128)(2,1)S(1)}, u32[]{:S(2)}, u32[]{:S(2)}) %collective-permute-start) | collective-permute-done | bytes 262176 | tf_op jit(solution)/shard_map/ppermute | solution.py:25
  63.4 1.7 tile.5
  65.1 6.5 %all-to-all-start.1 = ((bf16[8,128,1024]{2,1,0:T(8,128)(2,1)}), bf16[8,128,1024]{2,1,0:T(8,128)(2,1)}, u32[]{:S(2)}, u32[]{:S(2)}) async-start(bf16[8,128,1024]{2,1,0:T(8,128)(2,1)} %tile.5), calls=%async_computation.2 | async-start | bytes 4194304 | tf_op jit(solution)/shard_map/all_to_all | solution.py:23
  71.6 0.0 all-gather.2.cloned.1.call-start
  71.6 0.0 copy-done.6
  71.6 0.1 convert_element_type.57
  71.7 22.6 %all-to-all-done.1 = bf16[8,128,1024]{2,1,0:T(8,128)(2,1)} async-done(((bf16[8,128,1024]{2,1,0:T(8,128)(2,1)}), bf16[8,128,1024]{2,1,0:T(8,128)(2,1)}, u32[]{:S(2)}, u32[]{:S(2)}) %all-to-all-start.1) | async-done | bytes 2097184 | tf_op jit(solution)/shard_map/all_to_all | solution.py:23
  94.3 9.7 %reduce-scatter.2.cloned.1.call-done = bf16[128,3584]{1,0:T(8,128)(2,1)} async-done(((bf16[1024,3584]{1,0:T(8,128)(2,1)}), bf16[128,3584]{1,0:T(8,128)(2,1)}) %reduce-scatter.2.cloned.1.call-update) | async-done | bytes 917520 | tf_op jit(solution)/shard_map/reduce_scatter | solution.py:29
  104.0 1.3 fusion.25
  105.3 0.3 multiply_convert_fusion.4
  105.6 0.1 fusion.24
  105.6 3.1 %collective-permute-start.1 = (bf16[128,1792]{1,0:T(8,128)(2,1)S(1)}, bf16[128,1792]{1,0:T(8,128)(2,1)S(1)}, u32[]{:S(2)}, u32[]{:S(2)}) collective-permute-start(bf16[128,1792]{1,0:T(8,128)(2,1)S(1)} %get-tuple-element.21), channel_id=1, source_target_pairs={{0,1},{1,0},{2,3},{3,2},{4,5},{5,4},{6,7},{7,6},{8,9},{9,8},{10,11... | collective-permute-start | bytes 1376264 | tf_op jit(solution)/shard_map/ppermute | solution.py:56
  108.7 0.3 multiply_convert_fusion.2
  109.0 9.7 %collective-permute-done.1 = bf16[128,1792]{1,0:T(8,128)(2,1)S(1)} collective-permute-done((bf16[128,1792]{1,0:T(8,128)(2,1)S(1)}, bf16[128,1792]{1,0:T(8,128)(2,1)S(1)}, u32[]{:S(2)}, u32[]{:S(2)}) %collective-permute-start.1) | collective-permute-done | bytes 458784 | tf_op jit(solution)/shard_map/ppermute | solution.py:56
  118.8 1.2 pad_maximum_fusion.1
  120.0 0.0 all-gather.2.cloned.1.call-update
  120.0 6.4 %constant_dynamic-slice_fusion = (bf16[1024,896]{1,0:T(8,128)(2,1)}, bf16[1024,896]{1,0:T(8,128)(2,1)}, bf16[1024,896]{1,0:T(8,128)(2,1)}, bf16[1024,896]{1,0:T(8,128)(2,1)}) fusion(bf16[1024,1792]{1,0:T(8,128)(2,1)} %param.5, s32[]{:T(128)S(6)} %select_n.4, s32[]{:T(128)S(6)} %select_n.5, bf16[1024,1792]{1,0:T(8,128)(2,1)} %param.6), kind=kLoop, calls=%fused_computation.35 | loop fusion | bytes 14680072 | tf_op jit(solution)/shard_map/dynamic_slice | solution.py:9
  126.4 1.0 multiply_convert_fusion
  127.4 54.2 %all-gather.2.cloned.1.call-done = bf16[3,1024,1792]{2,1,0:T(8,128)(2,1)} async-done(((bf16[3,128,1792]{2,1,0:T(8,128)(2,1)}), bf16[3,1024,1792]{2,1,0:T(8,128)(2,1)}) %all-gather.2.cloned.1.call-update) | async-done | bytes 11010064 | tf_op jit(solution)/shard_map/all_gather | solution.py:60
  181.6 0.0 copy-start.4
  181.6 0.0 copy-start.5
  181.6 7.0 %fusion.1 = f32[1024,1024]{1,0:T(8,128)S(1)} fusion(bf16[1024,896]{1,0:T(8,128)(2,1)} %get-tuple-element.43, bf16[1024,896]{1,0:T(8,128)(2,1)} %get-tuple-element.29, bf16[3,1024,1792]{2,1,0:T(8,128)(2,1)} %all-gather.2.cloned.1.call-done), kind=kOutput, calls=%fused_computation.8 | convolution fusion | flops 3765436416 | bytes 11534336 | tf_op jit(solution)/shard_map/dot_general | solution.py:71
  188.6 0.0 copy-done.4
  188.6 0.0 copy-done.5
  188.6 7.2 %add_convert_fusion = bf16[1024,1024]{1,0:T(8,128)(2,1)} fusion(f32[1024,1024]{1,0:T(8,128)S(1)} %fusion.1, bf16[1024,896]{1,0:T(8,128)(2,1)S(1)} %copy-done.5, bf16[1024,896]{1,0:T(8,128)(2,1)S(1)} %copy-done.4, bf16[3,1024,1792]{2,1,0:T(8,128)(2,1)} %all-gather.2.cloned.1.call-done), kind=kOutput, calls=%fused_computation.1 | convolution fusion | flops 3767533568 | bytes 13631488 | tf_op jit(solution)/shard_map/dot_general | solution.py:74
  195.9 5.7 %all-to-all-start.2 = ((bf16[8,128,1024]{2,1,0:T(8,128)(2,1)}), bf16[8,128,1024]{2,1,0:T(8,128)(2,1)S(1)}, u32[]{:S(2)}, u32[]{:S(2)}) async-start(bf16[8,128,1024]{2,1,0:T(8,128)(2,1)} %bitcast.30), calls=%async_computation.3 | async-start | bytes 4194304 | tf_op jit(solution)/shard_map/all_to_all | solution.py:80
  201.6 3.6 %slice_bitcast_fusion.3 = (bf16[1024,1792]{1,0:T(8,128)(2,1)S(1)}, bf16[1024,1792]{1,0:T(8,128)(2,1)S(1)}) fusion(bf16[3,1024,1792]{2,1,0:T(8,128)(2,1)} %all-gather.2.cloned.1.call-done), kind=kLoop, calls=%fused_computation.7 | loop fusion | bytes 14680064 | tf_op jit(solution)/shard_map/squeeze | solution.py:72
  205.2 4.0 %fusion.8 = bf16[1024,896]{1,0:T(8,128)(2,1)S(1)} fusion(bf16[1024,1024]{1,0:T(8,128)(2,1)} %bitcast.1, bf16[1024,1792]{1,0:T(8,128)(2,1)S(1)} %get-tuple-element.27), kind=kOutput, calls=%fused_computation.17 | convolution fusion | flops 1879048192 | bytes 5767168 | tf_op jit(solution)/shard_map/dot_general | solution.py:85
  209.2 0.0 copy-start.3
  209.2 4.2 %fusion.12 = bf16[1024,896]{1,0:T(8,128)(2,1)S(1)} fusion(bf16[1024,1024]{1,0:T(8,128)(2,1)} %bitcast.1, bf16[1024,1792]{1,0:T(8,128)(2,1)S(1)} %get-tuple-element.27), kind=kOutput, calls=%fused_computation.21 | convolution fusion | flops 1879048192 | bytes 5767168 | tf_op jit(solution)/shard_map/dot_general | solution.py:85
  213.4 0.0 copy-done.3
  213.4 3.7 %add_convert_fusion.2 = bf16[1024,896]{1,0:T(8,128)(2,1)} fusion(bf16[1024,896]{1,0:T(8,128)(2,1)S(1)} %fusion.12, bf16[1024,1024]{1,0:T(8,128)(2,1)S(1)} %bitcast.28, bf16[1024,1792]{1,0:T(8,128)(2,1)S(1)} %get-tuple-element.26), kind=kOutput, calls=%fused_computation.16 | convolution fusion | flops 1883635712 | bytes 7602176 | tf_op jit(solution)/shard_map/dot_general | solution.py:84
  217.1 3.7 %add_convert_fusion.1 = bf16[1024,896]{1,0:T(8,128)(2,1)} fusion(bf16[1024,896]{1,0:T(8,128)(2,1)S(1)} %fusion.8, bf16[1024,1024]{1,0:T(8,128)(2,1)S(1)} %bitcast.29, bf16[1024,1792]{1,0:T(8,128)(2,1)S(1)} %get-tuple-element.26), kind=kOutput, calls=%fused_computation.15 | convolution fusion | flops 1883635712 | bytes 7602176 | tf_op jit(solution)/shard_map/dot_general | solution.py:84
  220.9 10.3 %all-to-all-done.2 = bf16[8,128,1024]{2,1,0:T(8,128)(2,1)S(1)} async-done(((bf16[8,128,1024]{2,1,0:T(8,128)(2,1)}), bf16[8,128,1024]{2,1,0:T(8,128)(2,1)S(1)}, u32[]{:S(2)}, u32[]{:S(2)}) %all-to-all-start.2) | async-done | bytes 2097184 | tf_op jit(solution)/shard_map/all_to_all | solution.py:80
  231.2 1.1 reduce_sum.12
  (1 shorter events, 0.0 us)
Async XLA Ops:
  7.2 96.8 %reduce-scatter.2.cloned.1.call-start = ((), (), s32[]{:S(2)}) async-start(), calls=%async_computation.4 | async-start | bytes 8257536 | tf_op jit(solution)/shard_map/reduce_scatter | solution.py:29
  7.2 32.0 %copy-start = (bf16[1024,1792]{1,0:T(8,128)(2,1)S(1)}, bf16[1024,1792]{1,0:T(8,128)(2,1)}, u32[]{:S(2)}) copy-start(bf16[1024,1792]{1,0:T(8,128)(2,1)} %param.6) | copy-start | bytes 11010052
  39.2 4.2 %copy-start.2 = (bf16[8,128,1024]{2,1,0:T(8,128)(2,1)}, bf16[8,128,1024]{2,1,0:T(8,128)(2,1)S(1)}, u32[]{:S(2)}) copy-start(bf16[8,128,1024]{2,1,0:T(8,128)(2,1)S(1)} %all_to_all.23) | copy-start | bytes 6291460
  39.2 4.2 %copy-start.1 = (bf16[1024,1792]{1,0:T(8,128)(2,1)S(1)}, bf16[1024,1792]{1,0:T(8,128)(2,1)}, u32[]{:S(2)}) copy-start(bf16[1024,1792]{1,0:T(8,128)(2,1)} %param.5) | copy-start | bytes 11010052
  54.4 0.9 copy-start.7
  55.3 16.3 %copy-start.6 = (bf16[128,1792]{1,0:T(8,128)(2,1)S(1)}, bf16[128,1792]{1,0:T(8,128)(2,1)}, u32[]{:S(2)}) copy-start(bf16[128,1792]{1,0:T(8,128)(2,1)} %param.7) | copy-start | bytes 1376260
  55.3 8.1 %collective-permute-start = (bf16[128,1024]{1,0:T(8,128)(2,1)S(1)}, bf16[128,1024]{1,0:T(8,128)(2,1)S(1)}, u32[]{:S(2)}, u32[]{:S(2)}) collective-permute-start(bf16[128,1024]{1,0:T(8,128)(2,1)S(1)} %copy-done.7), channel_id=1, source_target_pairs={{0,1},{1,0},{2,3},{3,2},{4,5},{5,4},{6,7},{7,6},{8,9},{9,8},{10,11... | collective-permute-start | bytes 786440 | tf_op jit(solution)/shard_map/ppermute | solution.py:25
  65.1 29.3 %all-to-all-start.1 = ((bf16[8,128,1024]{2,1,0:T(8,128)(2,1)}), bf16[8,128,1024]{2,1,0:T(8,128)(2,1)}, u32[]{:S(2)}, u32[]{:S(2)}) async-start(bf16[8,128,1024]{2,1,0:T(8,128)(2,1)} %tile.5), calls=%async_computation.2 | async-start | bytes 4194304 | tf_op jit(solution)/shard_map/all_to_all | solution.py:23
  71.6 110.0 %all-gather.2.cloned.1.call-start = ((), (), s32[]{:S(2)}) async-start(), calls=%async_computation.5 | async-start | bytes 12386304 | tf_op jit(solution)/shard_map/all_gather | solution.py:60
  105.6 13.1 %collective-permute-start.1 = (bf16[128,1792]{1,0:T(8,128)(2,1)S(1)}, bf16[128,1792]{1,0:T(8,128)(2,1)S(1)}, u32[]{:S(2)}, u32[]{:S(2)}) collective-permute-start(bf16[128,1792]{1,0:T(8,128)(2,1)S(1)} %get-tuple-element.21), channel_id=1, source_target_pairs={{0,1},{1,0},{2,3},{3,2},{4,5},{5,4},{6,7},{7,6},{8,9},{9,8},{10,11... | collective-permute-start | bytes 1376264 | tf_op jit(solution)/shard_map/ppermute | solution.py:56
  181.6 7.0 %copy-start.4 = (bf16[1024,896]{1,0:T(8,128)(2,1)S(1)}, bf16[1024,896]{1,0:T(8,128)(2,1)}, u32[]{:S(2)}) copy-start(bf16[1024,896]{1,0:T(8,128)(2,1)} %get-tuple-element.28) | copy-start | bytes 5505028
  181.6 7.0 %copy-start.5 = (bf16[1024,896]{1,0:T(8,128)(2,1)S(1)}, bf16[1024,896]{1,0:T(8,128)(2,1)}, u32[]{:S(2)}) copy-start(bf16[1024,896]{1,0:T(8,128)(2,1)} %get-tuple-element.44) | copy-start | bytes 5505028
  195.9 35.4 %all-to-all-start.2 = ((bf16[8,128,1024]{2,1,0:T(8,128)(2,1)}), bf16[8,128,1024]{2,1,0:T(8,128)(2,1)S(1)}, u32[]{:S(2)}, u32[]{:S(2)}) async-start(bf16[8,128,1024]{2,1,0:T(8,128)(2,1)} %bitcast.30), calls=%async_computation.3 | async-start | bytes 4194304 | tf_op jit(solution)/shard_map/all_to_all | solution.py:80
  209.2 4.2 %copy-start.3 = (bf16[8,128,1024]{2,1,0:T(8,128)(2,1)S(1)}, bf16[8,128,1024]{2,1,0:T(8,128)(2,1)}, u32[]{:S(2)}) copy-start(bf16[8,128,1024]{2,1,0:T(8,128)(2,1)} %copy-done.2) | copy-start | bytes 6291460
Sparse Core Ops, SparseCore 0:
  54.5 49.4 reduce-scatter.1
  120.2 61.4 all-gather.1

commit v17 on v14

--- a/solution.py
+++ b/solution.py
@@ -34,12 +34,12 @@
     )
     gathered_partner = gather_col(partner_tokens)
     joined, gathered_partner = lax.optimization_barrier((joined, gathered_partner))
-    joined = joined.astype(jnp.float32)
     gate = joined[:, :width]
     up = joined[:, width:]
-    upstream = cotangent.astype(jnp.float32)
+    upstream = cotangent
 
     def grads(gate, up, upstream):
+        gate, up, upstream = (x.astype(jnp.float32) for x in (gate, up, upstream))
         sigma = jax.nn.sigmoid(gate)
         active = gate * sigma
         grad_gate = (upstream * up * sigma * (1.0 + gate * (1.0 - sigma))).astype(jnp.bfloat16)
@@ -55,6 +55,7 @@
     )
     partner_gate, partner_up = jnp.split(lax.ppermute(payload, "dep", pair), 2, axis=1)
     grad_gate_own, grad_up_own = grads(gate_own, up_own, up_stream_own)
+    gate, up = gate.astype(jnp.float32), up.astype(jnp.float32)
     hidden = (gate * jax.nn.sigmoid(gate) * up).astype(jnp.bfloat16)
     gate_own, up_own, gate_other, up_other = grad_gate_own, grad_up_own, grad_gate_other, grad_up_other
     full = lax.all_gather(

time: 239 us -> 238 us (level)
    ppermute x1, waiting for transfers between devices: 9.66 us -> 6.83 us  [on_device(): lax.ppermute(payload, 'dep', pair)]
    dynamic_slice x1 -> x3, local copies, waits for them, and re-layouts: 6.37 us -> 5.86 us  [halves(): own = lax.dynamic_slice_in_dim(x, dep * half, half, axis=1)]
  transfers between devices with their start and end apart: 6 -> 6, of which waited for: 6 -> 6; matrix products, arithmetic and copies ran while one was open for 12% -> 13% of each run, Pallas kernels for 0% -> 0%
where the time goes in v17:
time: 238 us
  waiting for transfers between devices  110 us (46%)
  matrix products  41.6 us (17%)
  blocking collectives  30.9 us (13%)
  starting transfers between devices  17.7 us (7%)
  between operations  14.2 us (6%)
  local copies, waits for them, and re-layouts  13.2 us (6%)
  other arithmetic  9.78 us (4%)
    all_gather x1, waiting for transfers between devices, on_device(): lax.all_gather(jnp.concatenate([gate_own, up_own, gate_other, up_other, p...  54.8 us
    all_to_all x1, blocking collectives, gather_col(): return lax.all_to_all(jnp.tile(block, (n_col, 1)), 'col', 0, 0, tiled=True)  30.9 us
    all_to_all x1, waiting for transfers between devices, gather_col(): return lax.all_to_all(jnp.tile(block, (n_col, 1)), 'col', 0, 0, tiled=True)  22.6 us
    dot_general x1, matrix products, on_device(): lax.dot_general(full[:, :2 * width], weights, transposed, preferred_eleme...  12.9 us
    dot_general x2, matrix products, weight_grad(): lax.dot_general(gathered_partner, partner, contract, preferred_element_ty...  10.4 us
    reduce_scatter x1, waiting for transfers between devices, on_device(): lax.psum_scatter(jnp.concatenate([first, second], axis=1).astype(jnp.bflo...  10.4 us
    all_to_all x1, waiting for transfers between devices, on_device(): parts = lax.all_to_all(term, 'col', 0, 0, tiled=True)  10.4 us
    dot_general x2, matrix products, weight_grad(): lax.dot_general(gathered, own, contract, preferred_element_type=jnp.float32)  8.74 us
  transfers between devices with their start and end apart: 6, of which 6 were waited for; matrix products, arithmetic and copies ran while one was open for 13% of the time, Pallas kernels for 0%

profile of v17, /device:TPU:6, one launch (start us, length us, event | category | flops | bytes accessed | tf_op | source)
XLA Modules:
  0.0 237.5 jit_solution(15468545211119573866)
XLA Ops:
  7.2 0.0 reduce-scatter.2.cloned.1.call-start
  7.2 1.2 tile.4
  8.4 0.0 copy-start
  8.4 30.9 %all_to_all.23 = bf16[8,128,1024]{2,1,0:T(8,128)(2,1)S(1)} all-to-all(bf16[8,128,1024]{2,1,0:T(8,128)(2,1)S(1)} %tile.4), channel_id=1, replica_groups=mesh['row'=8,'col'=8,'dep'=2] {'col'}, dimensions={0} | all-to-all | bytes 4194304 | tf_op jit(solution)/shard_map/all_to_all | solution.py:23
  39.4 0.0 copy-start.2
  39.4 0.0 copy-done
  39.4 0.0 copy-start.1
  39.4 4.2 %convolution_convert_fusion = bf16[1024,1792]{1,0:T(8,128)(2,1)S(1)} fusion(bf16[1024,1024]{1,0:T(8,128)(2,1)S(1)} %bitcast.11, bf16[1024,1792]{1,0:T(8,128)(2,1)S(1)} %copy-done), kind=kOutput, calls=%fused_computation.10 | convolution fusion | flops 3759931392 | bytes 9437184 | tf_op jit(solution)/shard_map/dot_general | solution.py:28
  43.5 0.0 copy-done.2
  43.5 0.0 copy-done.1
  43.5 5.4 %convolution_convert_fusion.1 = bf16[1024,1792]{1,0:T(8,128)(2,1)} fusion(bf16[1024,1024]{1,0:T(8,128)(2,1)S(1)} %bitcast.12, bf16[1024,1792]{1,0:T(8,128)(2,1)S(1)} %copy-done.1), kind=kOutput, calls=%fused_computation.11 | convolution fusion | flops 3759931392 | bytes 9437184 | tf_op jit(solution)/shard_map/dot_general | solution.py:27
  48.9 5.5 %pad_maximum_fusion = bf16[1024,3584]{1,0:T(8,128)(2,1)} fusion(bf16[1024,1792]{1,0:T(8,128)(2,1)S(1)} %convolution_convert_fusion, bf16[1024,1792]{1,0:T(8,128)(2,1)} %convolution_convert_fusion.1), kind=kLoop, calls=%fused_computation.2 | loop fusion | flops 14680064 | bytes 14680064 | tf_op jit(solution)/shard_map/concatenate | solution.py:30
  54.5 0.0 copy-start.7
  54.5 0.0 reduce-scatter.2.cloned.1.call-update
  54.5 0.9 copy-done.7
  55.4 2.9 %collective-permute-start = (bf16[128,1024]{1,0:T(8,128)(2,1)S(1)}, bf16[128,1024]{1,0:T(8,128)(2,1)S(1)}, u32[]{:S(2)}, u32[]{:S(2)}) collective-permute-start(bf16[128,1024]{1,0:T(8,128)(2,1)S(1)} %copy-done.7), channel_id=1, source_target_pairs={{0,1},{1,0},{2,3},{3,2},{4,5},{5,4},{6,7},{7,6},{8,9},{9,8},{10,11... | collective-permute-start | bytes 786440 | tf_op jit(solution)/shard_map/ppermute | solution.py:25
  58.3 5.2 %collective-permute-done = bf16[128,1024]{1,0:T(8,128)(2,1)S(1)} collective-permute-done((bf16[128,1024]{1,0:T(8,128)(2,1)S(1)}, bf16[128,1024]{1,0:T(8,128)(2,1)S(1)}, u32[]{:S(2)}, u32[]{:S(2)}) %collective-permute-start) | collective-permute-done | bytes 262176 | tf_op jit(solution)/shard_map/ppermute | solution.py:25
  63.5 1.6 tile.5
  65.1 0.0 copy-start.6
  65.1 5.9 %all-to-all-start.1 = ((bf16[8,128,1024]{2,1,0:T(8,128)(2,1)}), bf16[8,128,1024]{2,1,0:T(8,128)(2,1)S(1)}, u32[]{:S(2)}, u32[]{:S(2)}) async-start(bf16[8,128,1024]{2,1,0:T(8,128)(2,1)} %tile.5), calls=%async_computation.2 | async-start | bytes 4194304 | tf_op jit(solution)/shard_map/all_to_all | solution.py:23
  71.1 0.0 all-gather.2.cloned.1.call-start
  71.1 0.0 copy-done.6
  71.1 22.6 %all-to-all-done.1 = bf16[8,128,1024]{2,1,0:T(8,128)(2,1)S(1)} async-done(((bf16[8,128,1024]{2,1,0:T(8,128)(2,1)}), bf16[8,128,1024]{2,1,0:T(8,128)(2,1)S(1)}, u32[]{:S(2)}, u32[]{:S(2)}) %all-to-all-start.1) | async-done | bytes 2097184 | tf_op jit(solution)/shard_map/all_to_all | solution.py:23
  93.7 0.0 copy-start.4
  93.7 10.4 %reduce-scatter.2.cloned.1.call-done = bf16[128,3584]{1,0:T(8,128)(2,1)} async-done(((bf16[1024,3584]{1,0:T(8,128)(2,1)}), bf16[128,3584]{1,0:T(8,128)(2,1)}) %reduce-scatter.2.cloned.1.call-update) | async-done | bytes 917520 | tf_op jit(solution)/shard_map/reduce_scatter | solution.py:29
  104.1 0.0 copy-done.4
  104.1 1.2 fusion.50
  105.4 0.3 fusion.33
  105.7 3.1 %collective-permute-start.1 = (bf16[128,1792]{1,0:T(8,128)(2,1)S(1)}, bf16[128,1792]{1,0:T(8,128)(2,1)S(1)}, u32[]{:S(2)}, u32[]{:S(2)}) collective-permute-start(bf16[128,1792]{1,0:T(8,128)(2,1)S(1)} %pad_maximum_fusion.1), channel_id=1, source_target_pairs={{0,1},{1,0},{2,3},{3,2},{4,5},{5,4},{6,7},{7,6},{8,9},{9,8},{10,11... | collective-permute-start | bytes 1376264 | tf_op jit(solution)/shard_map/ppermute | solution.py:56
  108.8 0.9 fusion.48
  109.7 0.8 fusion.47
  110.6 0.7 constant_dynamic-update-slice_fusion.2
  111.3 0.7 constant_dynamic-update-slice_fusion.1
  112.0 6.8 %collective-permute-done.1 = bf16[128,1792]{1,0:T(8,128)(2,1)S(1)} collective-permute-done((bf16[128,1792]{1,0:T(8,128)(2,1)S(1)}, bf16[128,1792]{1,0:T(8,128)(2,1)S(1)}, u32[]{:S(2)}, u32[]{:S(2)}) %collective-permute-start.1) | collective-permute-done | bytes 458784 | tf_op jit(solution)/shard_map/ppermute | solution.py:56
  118.9 0.8 constant_dynamic-update-slice_fusion
  119.7 0.0 all-gather.2.cloned.1.call-update
  119.7 5.8 %constant_dynamic-slice_fusion.1 = (bf16[1024,896]{1,0:T(8,128)(2,1)S(1)}, bf16[1024,896]{1,0:T(8,128)(2,1)}, bf16[1024,896]{1,0:T(8,128)(2,1)}, bf16[1024,896]{1,0:T(8,128)(2,1)}) fusion(bf16[1024,1792]{1,0:T(8,128)(2,1)} %param.6, s32[]{:T(128)S(6)} %select_n.5, s32[]{:T(128)S(6)} %select_n.4, bf16[1024,1792]{1,0:T(8,128)(2,1)} %param.5), kind=kLoop, calls=%fused_computation.63 | loop fusion | bytes 14680072 | tf_op jit(solution)/shard_map/dynamic_slice | solution.py:8
  125.5 1.0 fusion.30
  126.6 54.8 %all-gather.2.cloned.1.call-done = bf16[1024,5376]{1,0:T(8,128)(2,1)} async-done(((bf16[128,5376]{1,0:T(8,128)(2,1)}), bf16[1024,5376]{1,0:T(8,128)(2,1)}) %all-gather.2.cloned.1.call-update) | async-done | bytes 11010064 | tf_op jit(solution)/shard_map/all_gather | solution.py:61
  181.3 12.9 %fusion.9 = bf16[1024,1024]{1,0:T(8,128)(2,1)} fusion(bf16[1024,896]{1,0:T(8,128)(2,1)} %get-tuple-element.29, bf16[1024,896]{1,0:T(8,128)(2,1)} %get-tuple-element.36, bf16[1024,896]{1,0:T(8,128)(2,1)S(1)} %get-tuple-element.28, bf16[1024,896]{1,0:T(8,128)(2,1)} %get-tuple-element.37, bf16[1024,5376]{1,0:T(8,128)(2,1)} %all-gather.2.cloned.1.call-done), kind=kOutput, calls=%fused_computation.14 | convolution fusion | flops 7546601472 | bytes 16777216 | tf_op jit(solution)/shard_map/dot_general | solution.py:71
  194.2 5.7 %all-to-all-start.2 = ((bf16[8,128,1024]{2,1,0:T(8,128)(2,1)}), bf16[8,128,1024]{2,1,0:T(8,128)(2,1)S(1)}, u32[]{:S(2)}, u32[]{:S(2)}) async-start(bf16[8,128,1024]{2,1,0:T(8,128)(2,1)} %bitcast.17), calls=%async_computation.3 | async-start | bytes 4194304 | tf_op jit(solution)/shard_map/all_to_all | solution.py:76
  200.0 0.0 copy-start.3
  200.0 4.7 %fusion.16 = bf16[1024,896]{1,0:T(8,128)(2,1)S(1)} fusion(bf16[1024,1024]{1,0:T(8,128)(2,1)} %bitcast.13, bf16[1024,5376]{1,0:T(8,128)(2,1)} %all-gather.2.cloned.1.call-done), kind=kOutput, calls=%fused_computation.17 | convolution fusion | flops 1879048192 | bytes 5767168 | tf_op jit(solution)/shard_map/dot_general | solution.py:80
  204.6 0.0 copy-done.3
  204.7 0.0 copy-start.5
  204.7 4.1 %fusion.20 = bf16[1024,896]{1,0:T(8,128)(2,1)S(1)} fusion(bf16[1024,1024]{1,0:T(8,128)(2,1)S(1)} %bitcast.14, bf16[1024,5376]{1,0:T(8,128)(2,1)} %all-gather.2.cloned.1.call-done), kind=kOutput, calls=%fused_computation.21 | convolution fusion | flops 1879048192 | bytes 5767168 | tf_op jit(solution)/shard_map/dot_general | solution.py:80
  208.7 0.0 copy-done.5
  208.8 5.2 %add_convert_fusion.1 = bf16[1024,896]{1,0:T(8,128)(2,1)} fusion(bf16[1024,896]{1,0:T(8,128)(2,1)S(1)} %fusion.20, bf16[1024,1024]{1,0:T(8,128)(2,1)S(1)} %bitcast.15, bf16[1024,5376]{1,0:T(8,128)(2,1)} %all-gather.2.cloned.1.call-done), kind=kOutput, calls=%fused_computation.13 | convolution fusion | flops 1883635712 | bytes 7602176 | tf_op jit(solution)/shard_map/dot_general | solution.py:81
  214.0 5.2 %add_convert_fusion = bf16[1024,896]{1,0:T(8,128)(2,1)} fusion(bf16[1024,896]{1,0:T(8,128)(2,1)S(1)} %fusion.16, bf16[1024,1024]{1,0:T(8,128)(2,1)S(1)} %bitcast.16, bf16[1024,5376]{1,0:T(8,128)(2,1)} %all-gather.2.cloned.1.call-done), kind=kOutput, calls=%fused_computation.12 | convolution fusion | flops 1883635712 | bytes 7602176 | tf_op jit(solution)/shard_map/dot_general | solution.py:81
  219.2 10.4 %all-to-all-done.2 = bf16[8,128,1024]{2,1,0:T(8,128)(2,1)S(1)} async-done(((bf16[8,128,1024]{2,1,0:T(8,128)(2,1)}), bf16[8,128,1024]{2,1,0:T(8,128)(2,1)S(1)}, u32[]{:S(2)}, u32[]{:S(2)}) %all-to-all-start.2) | async-done | bytes 2097184 | tf_op jit(solution)/shard_map/all_to_all | solution.py:76
  229.6 1.1 reduce_sum.12
  (3 shorter events, 0.1 us)
Async XLA Ops:
  7.2 96.9 %reduce-scatter.2.cloned.1.call-start = ((), (), s32[]{:S(2)}) async-start(), calls=%async_computation.4 | async-start | bytes 8257536 | tf_op jit(solution)/shard_map/reduce_scatter | solution.py:29
  8.4 30.9 %copy-start = (bf16[1024,1792]{1,0:T(8,128)(2,1)S(1)}, bf16[1024,1792]{1,0:T(8,128)(2,1)}, u32[]{:S(2)}) copy-start(bf16[1024,1792]{1,0:T(8,128)(2,1)} %param.6) | copy-start | bytes 11010052
  39.4 4.2 %copy-start.2 = (bf16[8,128,1024]{2,1,0:T(8,128)(2,1)}, bf16[8,128,1024]{2,1,0:T(8,128)(2,1)S(1)}, u32[]{:S(2)}) copy-start(bf16[8,128,1024]{2,1,0:T(8,128)(2,1)S(1)} %all_to_all.23) | copy-start | bytes 6291460
  39.4 4.2 %copy-start.1 = (bf16[1024,1792]{1,0:T(8,128)(2,1)S(1)}, bf16[1024,1792]{1,0:T(8,128)(2,1)}, u32[]{:S(2)}) copy-start(bf16[1024,1792]{1,0:T(8,128)(2,1)} %param.5) | copy-start | bytes 11010052
  54.5 0.9 copy-start.7
  55.4 8.1 %collective-permute-start = (bf16[128,1024]{1,0:T(8,128)(2,1)S(1)}, bf16[128,1024]{1,0:T(8,128)(2,1)S(1)}, u32[]{:S(2)}, u32[]{:S(2)}) collective-permute-start(bf16[128,1024]{1,0:T(8,128)(2,1)S(1)} %copy-done.7), channel_id=1, source_target_pairs={{0,1},{1,0},{2,3},{3,2},{4,5},{5,4},{6,7},{7,6},{8,9},{9,8},{10,11... | collective-permute-start | bytes 786440 | tf_op jit(solution)/shard_map/ppermute | solution.py:25
  65.1 5.9 %copy-start.6 = (bf16[128,1792]{1,0:T(8,128)(2,1)S(1)}, bf16[128,1792]{1,0:T(8,128)(2,1)}, u32[]{:S(2)}) copy-start(bf16[128,1792]{1,0:T(8,128)(2,1)} %param.7) | copy-start | bytes 1376260
  65.1 28.5 %all-to-all-start.1 = ((bf16[8,128,1024]{2,1,0:T(8,128)(2,1)}), bf16[8,128,1024]{2,1,0:T(8,128)(2,1)S(1)}, u32[]{:S(2)}, u32[]{:S(2)}) async-start(bf16[8,128,1024]{2,1,0:T(8,128)(2,1)} %tile.5), calls=%async_computation.2 | async-start | bytes 4194304 | tf_op jit(solution)/shard_map/all_to_all | solution.py:23
  71.1 110.3 %all-gather.2.cloned.1.call-start = ((), (), s32[]{:S(2)}) async-start(), calls=%async_computation.5 | async-start | bytes 12386304 | tf_op jit(solution)/shard_map/all_gather | solution.py:61
  93.7 10.4 %copy-start.4 = (bf16[8,128,1024]{2,1,0:T(8,128)(2,1)}, bf16[8,128,1024]{2,1,0:T(8,128)(2,1)S(1)}, u32[]{:S(2)}) copy-start(bf16[8,128,1024]{2,1,0:T(8,128)(2,1)S(1)} %all-to-all-done.1) | copy-start | bytes 6291460
  105.7 13.2 %collective-permute-start.1 = (bf16[128,1792]{1,0:T(8,128)(2,1)S(1)}, bf16[128,1792]{1,0:T(8,128)(2,1)S(1)}, u32[]{:S(2)}, u32[]{:S(2)}) collective-permute-start(bf16[128,1792]{1,0:T(8,128)(2,1)S(1)} %pad_maximum_fusion.1), channel_id=1, source_target_pairs={{0,1},{1,0},{2,3},{3,2},{4,5},{5,4},{6,7},{7,6},{8,9},{9,8},{10,11... | collective-permute-start | bytes 1376264 | tf_op jit(solution)/shard_map/ppermute | solution.py:56
  194.2 35.3 %all-to-all-start.2 = ((bf16[8,128,1024]{2,1,0:T(8,128)(2,1)}), bf16[8,128,1024]{2,1,0:T(8,128)(2,1)S(1)}, u32[]{:S(2)}, u32[]{:S(2)}) async-start(bf16[8,128,1024]{2,1,0:T(8,128)(2,1)} %bitcast.17), calls=%async_computation.3 | async-start | bytes 4194304 | tf_op jit(solution)/shard_map/all_to_all | solution.py:76
  200.0 4.7 %copy-start.3 = (bf16[8,128,1024]{2,1,0:T(8,128)(2,1)S(1)}, bf16[8,128,1024]{2,1,0:T(8,128)(2,1)}, u32[]{:S(2)}) copy-start(bf16[8,128,1024]{2,1,0:T(8,128)(2,1)} %copy-done.2) | copy-start | bytes 6291460
  204.7 4.1 %copy-start.5 = (bf16[8,128,1024]{2,1,0:T(8,128)(2,1)S(1)}, bf16[8,128,1024]{2,1,0:T(8,128)(2,1)}, u32[]{:S(2)}) copy-start(bf16[8,128,1024]{2,1,0:T(8,128)(2,1)} %copy-done.4) | copy-start | bytes 6291460
Sparse Core Ops, SparseCore 0:
  54.6 49.4 reduce-scatter.1
  119.9 61.4 all-gather.1
